TPU v7x, 512 devices: a whole 4x8x8 slice. The times are simulated.
512 devices in a mesh: aux: 16 (over z, x_lo), ao: 32 (over y, x_hi, core).
Axes of the slice: x: 4 (x_hi: 2, x_lo: 2; x = x_hi * 2 + x_lo), y: 8, z: 8, core: 2. Of those that a mesh axis runs over, the one named last changes fastest.
Arguments:
- soc_ints: bfloat16 [2048, 3, 16, 8192], P('aux', None, None, 'ao'), may hold values from -6 to 6
- cou_ints: bfloat16 [2048, 16, 8192], P('aux', None, 'ao'), may hold values from -6 to 6
- coef_t: bfloat16 [16, 8192], P(None, 'ao'), may hold values from -0.0625 to 0.0625
- active_rdm: float32 [16, 16], replicated, may hold values from -3 to 3
- spin_dens: bfloat16 [320, 256], P('ao'), may hold values from -6 to 6
- pair_list: int32 [320, 2], replicated, may hold values from 0 to 23
- owner_map: int32 [320], P('ao'), may hold values from 0 to 319, each once
- state_count: int32 [24], replicated, may hold values from 8 to 16, as said below
Outputs:
- soc_elems: float32 [3, 320], P(None, 'ao')
Inputs may be any that keep to these rules, and one draw needn't show every extreme that they name: `state_count`: each state's count of live active orbitals; some state has all 16. `owner_map`: every pair appears in exactly one slot.
All inputs are finite; a program needn't handle non-finite values.
Results may differ from a plain program's by a relative error of at most 0.0003.
Values may be sent and summed in bfloat16 or wider, within the bound.
No kernel may reach another device: no remote copies, remote signals or barrier semaphores. Data moves between devices by JAX's collectives and lax.ppermute only.
A program may use at most 64 MiB of HBM per device.

v0:
```python
import jax
import jax.numpy as jnp
from jax import lax
from jax.sharding import PartitionSpec as P


def mean_field(soc_rows, cou_rows, active_rdm, scale):
    count = soc_rows.shape[0]
    width = active_rdm.shape[0]
    high = lax.Precision.HIGHEST
    fitted = jnp.dot(cou_rows, active_rdm.reshape(-1), precision=high)
    direct = jnp.einsum("p,pxk->xk", fitted, soc_rows, precision=high)
    folded = jnp.einsum(
        "vw,pwu->pvu", active_rdm, cou_rows.reshape(count, width, width), precision=high
    )
    crossed = jnp.einsum(
        "pxtv,pvu->xtu", soc_rows.reshape(count, 3, width, width), folded, precision=high
    )
    return (direct - 1.5 * crossed.reshape(3, width * width)) * scale


def transform(soc_ints, cou_ints, coef_t, count):
    width = coef_t.shape[0]
    span = soc_ints.shape[-1]
    soc_mo = jnp.einsum(
        "rn,un->ru", soc_ints.reshape(-1, span), coef_t, preferred_element_type=jnp.float32
    )
    cou_mo = jnp.einsum(
        "rn,un->ru", cou_ints.reshape(-1, span), coef_t, preferred_element_type=jnp.float32
    )
    return jnp.concatenate(
        [soc_mo.reshape(count, 3 * width * width), cou_mo.reshape(count, width * width)], axis=1
    )


def contract(field, dens_rows, pair_ids, pair_list, state_count, width):
    cells = width * width
    bra_state = jnp.take(pair_list[:, 0], pair_ids, axis=0)
    ket_state = jnp.take(pair_list[:, 1], pair_ids, axis=0)
    states = jnp.arange(state_count.shape[0], dtype=jnp.int32)
    bra_count = jnp.sum(
        jnp.where(bra_state[:, None] == states[None, :], state_count[None, :], 0), axis=1
    )
    ket_count = jnp.sum(
        jnp.where(ket_state[:, None] == states[None, :], state_count[None, :], 0), axis=1
    )
    live = jnp.minimum(bra_count, ket_count)
    cell = jnp.arange(cells, dtype=jnp.int32)
    inside = (cell[None, :] // width < live[:, None]) & (cell[None, :] % width < live[:, None])
    dens = jnp.where(inside, dens_rows.astype(jnp.float32), jnp.float32(0.0))
    return jnp.dot(field, dens.T, precision=lax.Precision.HIGHEST) / width


def on_device(soc_ints, cou_ints, coef_t, active_rdm, spin_dens, pair_list, owner_map, state_count):
    width = coef_t.shape[0]
    cells = width * width
    slab_rows = soc_ints.shape[0]
    total_aux = slab_rows * lax.axis_size("aux")
    scale = 1.0 / (8.0 * jnp.sqrt(jnp.float32(total_aux)))
    partial_rows = transform(soc_ints, cou_ints, coef_t, slab_rows)
    summed = lax.psum(partial_rows, "ao")
    local_field = mean_field(
        summed[:, : 3 * cells].reshape(slab_rows, 3, cells),
        summed[:, 3 * cells :],
        active_rdm,
        scale,
    )
    field = lax.psum(local_field, "aux")
    every_dens = lax.all_gather(spin_dens, "ao", axis=0, tiled=True)
    picked = jnp.take(every_dens, owner_map, axis=0)
    result = contract(field, picked, owner_map, pair_list, state_count, width)
    return result


def solution(mesh):
    return jax.shard_map(
        on_device,
        mesh=mesh,
        in_specs=(
            P("aux", None, None, "ao"),
            P("aux", None, "ao"),
            P(None, "ao"),
            P(),
            P("ao", None),
            P(),
            P("ao"),
            P(),
        ),
        out_specs=P(None, "ao"),
        check_vma=False,
    )
```

profile of v0, /device:TPU:32, one launch (start us, length us, event | category | flops | bytes accessed | tf_op | source)
XLA Modules:
  0.0 356.4 jit_solution(15749440203220310827)
XLA Ops:
  6.5 1.9 copy-done
  8.4 3.3 fusion.24
  11.7 2.8 reshape.95
  14.6 0.0 copy-start.1
  14.6 2.6 fusion.25
  17.2 2.3 reshape.97
  19.5 1.8 pad_maximum_fusion
  21.2 0.0 all-reduce.2.cloned.1.call-update
  21.2 0.7 compare_select_fusion
  21.9 0.8 slice_reduce_fusion
  22.7 0.7 gather_fusion.1
  23.4 0.7 broadcast_select_fusion.1
  24.0 0.7 gather_fusion.2
  24.7 0.6 reshape.134
  25.3 40.4 %all-gather = bf16[32,10,256]{2,1,0:T(8,128)(2,1)S(1)} all-gather(bf16[1,10,256]{2,1,0:T(8,128)(2,1)} %bitcast.40), channel_id=1, replica_groups=mesh['aux'=16,'ao'=32] {'ao'}, dimensions={0}, use_global_device_ids=true | all-gather | bytes 168960 | tf_op jit(solution)/shard_map/all_gather | solution.py:69
  65.7 0.7 reshape.129
  66.4 1.5 gather_fusion
  68.0 0.8 select_reduce_fusion
  68.8 0.5 min.7
  69.4 0.6 and_select_fusion
  70.0 231.9 %all-reduce.2.cloned.1.call-done = f32[128,1024]{1,0:T(8,128)} async-done(((f32[128,1024]{1,0:T(8,128)}), f32[128,1024]{1,0:T(8,128)}) %all-reduce.2.cloned.1.call-update) | async-done | bytes 524304 | tf_op jit(solution)/shard_map/psum | solution.py:61
  301.8 1.8 slice.23
  303.6 1.1 copy.25
  304.7 1.6 slice.22
  306.3 1.6 copy.27
  308.0 1.2 convolution_bitcast_fusion
  309.1 1.1 fusion
  310.3 0.8 mul.17
  311.1 1.1 convolution_bitcast_fusion.2
  312.2 0.4 fusion.26
  312.6 35.5 %psum.15 = f32[3,256]{1,0:T(4,128)S(1)} all-reduce(f32[3,256]{1,0:T(4,128)S(1)} %fusion.17), channel_id=1, replica_groups=mesh['aux'=16,'ao'=32] {'aux'}, use_global_device_ids=true, to_apply=%region_1.0 | all-reduce | flops 768 | bytes 6144 | tf_op jit(solution)/shard_map/psum | solution.py:68
  348.1 1.5 convolution_multiply_fusion
  (10 shorter events, 0.0 us)
Async XLA Ops:
  6.5 1.9 copy-start
  6.5 295.3 %all-reduce.2.cloned.1.call-start = ((), (), s32[]{:S(2)}) async-start(), calls=%async_computation | async-start | bytes 1048576 | tf_op jit(solution)/shard_map/psum | solution.py:61
  11.7 2.8 copy-start.2
  14.6 10.1 %copy-start.1 = (f32[16,16]{1,0:T(8,128)S(1)}, f32[16,16]{1,0:T(8,128)}, u32[]{:S(2)}) copy-start(f32[16,16]{1,0:T(8,128)} %param.13) | copy-start | bytes 3076
  24.0 43.9 %copy-start.3 = (pred[10]{0:T(512)(128)(4,1)}, pred[10]{0:T(512)(128)(4,1)S(1)}, u32[]{:S(2)}) copy-start(pred[10]{0:T(512)(128)(4,1)S(1)} %get-tuple-element.11) | copy-start | bytes 34
Sparse Core Ops, SparseCore 0:
  21.4 280.3 all-reduce.1
where the time goes:
time: 357 us; the launch traced here: 356 us
  waiting for transfers between devices  232 us (65%)
  blocking collectives  75.8 us (21%)
  local copies, waits for them, and re-layouts  18.9 us (5%)
  between operations  13.5 us (4%)
  matrix products  11.2 us (3%)
  other arithmetic  5.09 us (1%)
    psum x1, waiting for transfers between devices, on_device(): summed = lax.psum(partial_rows, 'ao')  232 us
    all_gather x1, blocking collectives, on_device(): every_dens = lax.all_gather(spin_dens, 'ao', axis=0, tiled=True)  40.4 us
    psum x1, blocking collectives, on_device(): field = lax.psum(local_field, 'aux')  35.5 us
  transfers between devices with their start and end apart: 1, of which 1 were waited for; matrix products, arithmetic and copies ran while one was open for 2% of the time, Pallas kernels for 0%

commit v1 on v0

v1 whole, which is shorter than its diff:
```python
import jax
import jax.numpy as jnp
import numpy as np
from jax import lax
from jax.sharding import Mesh
from jax.sharding import PartitionSpec as P

AUX = ("z", "xlo")
AO = ("y", "xhi", "core")
HIGH = lax.Precision.HIGHEST


def butterfly_sum(value, rounds):
    for axis, size in rounds:
        step = 1
        while step < size:
            pairs = [(i, i ^ step) for i in range(size)]
            value = value + lax.ppermute(value, axis, pairs)
            step *= 2
    return value


def butterfly_gather(value, rounds):
    for axis, size in rounds:
        step = 1
        while step < size:
            pairs = [(i, i ^ step) for i in range(size)]
            value = jnp.concatenate([value, lax.ppermute(value, axis, pairs)], axis=0)
            step *= 2
    return value


AO_ROUNDS = (("core", 2), ("xhi", 2), ("y", 8))
AUX_ROUNDS = (("xlo", 2), ("z", 8))


def on_device(soc_ints, cou_ints, coef_t, active_rdm, spin_dens, pair_list, owner_map, state_count):
    width = coef_t.shape[0]
    cells = width * width
    rows = soc_ints.shape[0]
    n_aux = lax.axis_size("z") * lax.axis_size("xlo")
    scale = 1.0 / (8.0 * jnp.sqrt(jnp.float32(rows * n_aux)))

    cou_part = jnp.einsum(
        "ptn,un->ptu", cou_ints, coef_t, preferred_element_type=jnp.float32
    ).reshape(rows, cells)
    cou_mo = butterfly_sum(cou_part, AO_ROUNDS)

    soc_part = jnp.einsum(
        "pxtn,un->xtpu", soc_ints, coef_t, preferred_element_type=jnp.float32
    ).reshape(3 * width, rows * width)

    fitted = jnp.dot(cou_mo, active_rdm.reshape(-1), precision=HIGH)
    folded = jnp.einsum("vw,pwu->pvu", active_rdm, cou_mo.reshape(rows, width, width), precision=HIGH)
    eye = jnp.eye(width, dtype=jnp.float32)
    weight = fitted[:, None, None] * eye[None] - 1.5 * folded
    field_part = jnp.dot(soc_part, weight.reshape(rows * width, width), precision=HIGH)
    field_part = (field_part * scale).reshape(3, cells)
    field = butterfly_sum(field_part, AO_ROUNDS + AUX_ROUNDS)

    me = (lax.axis_index("y") * 4 + lax.axis_index("xhi") * 2 + lax.axis_index("core")).astype(jnp.int32)
    block = spin_dens.shape[0]
    every_dens = butterfly_gather(spin_dens, AO_ROUNDS)
    where = (owner_map // block) ^ me
    picked = jnp.take(every_dens, where * block + owner_map % block, axis=0)

    bra = jnp.take(state_count, jnp.take(pair_list[:, 0], owner_map, axis=0), axis=0)
    ket = jnp.take(state_count, jnp.take(pair_list[:, 1], owner_map, axis=0), axis=0)
    live = jnp.minimum(bra, ket)
    cell = jnp.arange(cells, dtype=jnp.int32)
    inside = (cell[None, :] // width < live[:, None]) & (cell[None, :] % width < live[:, None])
    dens = jnp.where(inside, picked.astype(jnp.float32), jnp.float32(0.0))
    return jnp.dot(field, dens.T, precision=HIGH) / width


def solution(mesh):
    devices = np.asarray(mesh.devices).reshape(8, 2, 8, 2, 2)
    fine = Mesh(devices, AUX + AO)
    return jax.shard_map(
        on_device,
        mesh=fine,
        in_specs=(
            P(AUX, None, None, AO),
            P(AUX, None, AO),
            P(None, AO),
            P(),
            P(AO, None),
            P(),
            P(AO),
            P(),
        ),
        out_specs=P(None, AO),
        check_vma=False,
    )
```

time: 357 us -> 132 us (0.37)
  the two profiles are of different devices: /device:TPU:32 before, /device:TPU:56 now
where the time goes in v1:
time: 132 us; the launch traced here: 131 us
  starting transfers between devices  76.1 us (58%)
  local copies, waits for them, and re-layouts  20.4 us (15%)
  waiting for transfers between devices  18.7 us (14%)
  matrix products  9.07 us (7%)
  other arithmetic  5.88 us (4%)
    ppermute x14, starting transfers between devices, butterfly_sum(): value = value + lax.ppermute(value, axis, pairs)  58 us
    ppermute x14, waiting for transfers between devices, butterfly_sum(): value = value + lax.ppermute(value, axis, pairs)  18.7 us
    ppermute x5, starting transfers between devices, butterfly_gather(): value = jnp.concatenate([value, lax.ppermute(value, axis, pairs)], axis=0)  18.2 us
    reshape x1, local copies, waits for them, and re-layouts, on_device(): soc_part = jnp.einsum('pxtn,un->xtpu', soc_ints, coef_t, preferred_elemen...  3.79 us
    dot_general x1, matrix products, on_device(): jnp.einsum('ptn,un->ptu', cou_ints, coef_t, preferred_element_type=jnp.fl...  2.77 us
  transfers between devices with their start and end apart: 19, of which 9 were waited for; matrix products, arithmetic and copies ran while one was open for 23% of the time, Pallas kernels for 0%

profile of v1, /device:TPU:56, one launch (start us, length us, event | category | flops | bytes accessed | tf_op | source)
XLA Modules:
  0.0 130.6 jit_solution(10038370697815532887)
XLA Ops:
  0.0 2.8 %fusion.16 = f32[128,16,16]{2,1,0:T(8,128)} fusion(bf16[128,16,256]{2,1,0:T(8,128)(2,1)} %param.13, bf16[16,256]{1,0:T(8,128)(2,1)} %param.14), kind=kOutput, calls=%fused_computation.25 | convolution fusion | flops 16777216 | bytes 1187840 | tf_op jit(solution)/shard_map/ptn,un->ptu/dot_general | solution.py:44
  4.4 2.0 %collective-permute-start = (f32[128,256]{0,1:T(8,128)S(1)}, f32[128,256]{0,1:T(8,128)S(1)}, u32[]{:S(2)}, u32[]{:S(2)}) collective-permute-start(f32[128,256]{0,1:T(8,128)S(1)} %bitcast.32), channel_id=1, source_target_pairs={{0,1},{1,0},{2,3},{3,2},{4,5},{5,4},{6,7},{7,6},{8,9},{9,8},{10,11... | collective-permute-start | bytes 393224 | tf_op jit(solution)/shard_map/ppermute | solution.py:18
  7.8 4.9 %collective-permute-start.1 = (f32[128,256]{0,1:T(8,128)S(1)}, f32[128,256]{0,1:T(8,128)S(1)}, u32[]{:S(2)}, u32[]{:S(2)}) collective-permute-start(f32[128,256]{0,1:T(8,128)S(1)} %bitcast_add_fusion), channel_id=1, source_target_pairs={{0,2},{2,0},{1,3},{3,1},{4,6},{6,4},{5,7},{7,5},{8,10},{10,8},{9,1... | collective-permute-start | bytes 393224 | tf_op jit(solution)/shard_map/ppermute | solution.py:18
  12.7 1.9 %collective-permute-start.14 = (bf16[10,256]{1,0:T(8,128)(2,1)S(1)}, bf16[10,256]{1,0:T(8,128)(2,1)}, u32[]{:S(2)}, u32[]{:S(2)}) collective-permute-start(bf16[10,256]{1,0:T(8,128)(2,1)S(1)} %copy-done.2), channel_id=1, source_target_pairs={{0,1},{1,0},{2,3},{3,2},{4,5},{5,4},{6,7},{7,6},{8,9},{9,8},{10,11... | collective-permute-start | bytes 15368 | tf_op jit(solution)/shard_map/ppermute | solution.py:28
  14.7 2.1 %collective-permute-done.1 = f32[128,256]{0,1:T(8,128)S(1)} collective-permute-done((f32[128,256]{0,1:T(8,128)S(1)}, f32[128,256]{0,1:T(8,128)S(1)}, u32[]{:S(2)}, u32[]{:S(2)}) %collective-permute-start.1) | collective-permute-done | bytes 131104 | tf_op jit(solution)/shard_map/ppermute | solution.py:18
  16.7 3.3 %collective-permute-start.2 = (f32[128,256]{0,1:T(8,128)S(1)}, f32[128,256]{0,1:T(8,128)S(1)}, u32[]{:S(2)}, u32[]{:S(2)}) collective-permute-start(f32[128,256]{0,1:T(8,128)S(1)} %add.86), channel_id=1, source_target_pairs={{0,4},{4,0},{8,12},{12,8},{16,20},{20,16},{24,28},{28,24},{1,5},{5... | collective-permute-start | bytes 393224 | tf_op jit(solution)/shard_map/ppermute | solution.py:18
  20.0 1.8 %fusion.2 = f32[3,16,128,16]{2,3,1,0:T(8,128)S(1)} fusion(bf16[128,3,16,256]{3,2,1,0:T(8,128)(2,1)S(1)} %copy-done, bf16[16,256]{1,0:T(8,128)(2,1)S(1)} %copy-done.3), kind=kOutput, calls=%fused_computation.7 | convolution fusion | flops 50331648 | bytes 3547136 | tf_op jit(solution)/shard_map/pxtn,un->xtpu/dot_general | solution.py:49
  21.8 1.8 %collective-permute-done.2 = f32[128,256]{0,1:T(8,128)S(1)} collective-permute-done((f32[128,256]{0,1:T(8,128)S(1)}, f32[128,256]{0,1:T(8,128)S(1)}, u32[]{:S(2)}, u32[]{:S(2)}) %collective-permute-start.2) | collective-permute-done | bytes 131104 | tf_op jit(solution)/shard_map/ppermute | solution.py:18
  23.6 4.0 %collective-permute-start.3 = (f32[128,256]{0,1:T(8,128)S(1)}, f32[128,256]{0,1:T(8,128)S(1)}, u32[]{:S(2)}, u32[]{:S(2)}) collective-permute-start(f32[128,256]{0,1:T(8,128)S(1)} %add.87), channel_id=1, source_target_pairs={{0,8},{4,12},{8,0},{12,4},{16,24},{20,28},{24,16},{28,20},{1,9},{5... | collective-permute-start | bytes 393224 | tf_op jit(solution)/shard_map/ppermute | solution.py:18
  27.7 5.1 %collective-permute-done.3 = f32[128,256]{0,1:T(8,128)S(1)} collective-permute-done((f32[128,256]{0,1:T(8,128)S(1)}, f32[128,256]{0,1:T(8,128)S(1)}, u32[]{:S(2)}, u32[]{:S(2)}) %collective-permute-start.3) | collective-permute-done | bytes 131104 | tf_op jit(solution)/shard_map/ppermute | solution.py:18
  33.5 6.7 %collective-permute-start.4 = (f32[128,256]{0,1:T(8,128)}, f32[128,256]{0,1:T(8,128)}, u32[]{:S(2)}, u32[]{:S(2)}) collective-permute-start(f32[128,256]{0,1:T(8,128)} %add.88), channel_id=1, source_target_pairs={{0,16},{4,20},{8,24},{12,28},{16,0},{20,4},{24,8},{28,12},{1,17},{... | collective-permute-start | bytes 393224 | tf_op jit(solution)/shard_map/ppermute | solution.py:18
  43.5 2.2 %copy.12 = f32[3,16,128,16]{3,2,1,0:T(8,128)} copy(f32[3,16,128,16]{2,3,1,0:T(8,128)S(1)} %fusion.2) | data formatting | bytes 786432 | tf_op jit(solution)/shard_map/pxtn,un->xtpu/transpose | solution.py:49
  45.6 3.8 %reshape.95 = f32[48,2048]{1,0:T(8,128)S(1)} reshape(f32[3,16,128,16]{3,2,1,0:T(8,128)} %copy.12) | data formatting | bytes 786432 | tf_op jit(solution)/shard_map/reshape | solution.py:51
  51.4 1.7 %multiply_subtract_fusion = f32[128,16,16]{0,1,2:T(8,128)} fusion(f32[128,16,16]{0,2,1:T(8,128)S(1)} %bitcast.31, f32[16,16]{0,1:T(8,128)S(1)} %fusion.24, f32[128]{0:T(128)S(1)} %convolution_bitcast_fusion, f32[16,16]{1,0:T(8,128)} %param.15), kind=kOutput, calls=%fused_computation.14 | convolution fusion | flops 6389760 | bytes 264704 | tf_op jit(solution)/shard_map/vw,pwu->pvu/dot_general | solution.py:54
  53.0 2.2 %copy.15 = f32[128,16,16]{1,0,2:T(8,128)} copy(f32[128,16,16]{0,1,2:T(8,128)} %multiply_subtract_fusion) | data formatting | bytes 262144 | tf_op jit(solution)/shard_map/sub | solution.py:56
  55.3 2.5 %reshape.99 = f32[2048,16]{0,1:T(8,128)} reshape(f32[128,16,16]{1,0,2:T(8,128)} %copy.15) | data formatting | bytes 262144 | tf_op jit(solution)/shard_map/reshape | solution.py:57
  57.8 1.9 %convolution_multiply_fusion.1 = f32[48,16]{0,1:T(8,128)} fusion(f32[48,2048]{1,0:T(8,128)S(1)} %reshape.95, f32[2048,16]{0,1:T(8,128)} %reshape.99), kind=kOutput, calls=%fused_computation.10 | convolution fusion | flops 18875136 | bytes 527360 | tf_op jit(solution)/shard_map/dot_general | solution.py:57
  60.6 1.9 %collective-permute-start.5 = (f32[3,256]{1,0:T(4,128)S(1)}, f32[3,256]{1,0:T(4,128)S(1)}, u32[]{:S(2)}, u32[]{:S(2)}) collective-permute-start(f32[3,256]{1,0:T(4,128)S(1)} %reshape.100), channel_id=1, source_target_pairs={{0,1},{1,0},{2,3},{3,2},{4,5},{5,4},{6,7},{7,6},{8,9},{9,8},{10,11... | collective-permute-start | bytes 9224 | tf_op jit(solution)/shard_map/ppermute | solution.py:18
  63.6 2.9 %collective-permute-start.6 = (f32[3,256]{1,0:T(4,128)S(1)}, f32[3,256]{1,0:T(4,128)S(1)}, u32[]{:S(2)}, u32[]{:S(2)}) collective-permute-start(f32[3,256]{1,0:T(4,128)S(1)} %add.90), channel_id=1, source_target_pairs={{0,2},{2,0},{1,3},{3,1},{4,6},{6,4},{5,7},{7,5},{8,10},{10,8},{9,1... | collective-permute-start | bytes 9224 | tf_op jit(solution)/shard_map/ppermute | solution.py:18
  67.8 2.8 %collective-permute-done.6 = f32[3,256]{1,0:T(4,128)S(1)} collective-permute-done((f32[3,256]{1,0:T(4,128)S(1)}, f32[3,256]{1,0:T(4,128)S(1)}, u32[]{:S(2)}, u32[]{:S(2)}) %collective-permute-start.6) | collective-permute-done | bytes 3104 | tf_op jit(solution)/shard_map/ppermute | solution.py:18
  70.6 2.6 %collective-permute-start.7 = (f32[3,256]{1,0:T(4,128)S(1)}, f32[3,256]{1,0:T(4,128)S(1)}, u32[]{:S(2)}, u32[]{:S(2)}) collective-permute-start(f32[3,256]{1,0:T(4,128)S(1)} %add.91), channel_id=1, source_target_pairs={{0,4},{4,0},{8,12},{12,8},{16,20},{20,16},{24,28},{28,24},{1,5},{5... | collective-permute-start | bytes 9224 | tf_op jit(solution)/shard_map/ppermute | solution.py:18
  73.9 2.8 %collective-permute-start.15 = (bf16[20,256]{1,0:T(8,128)(2,1)S(1)}, bf16[20,256]{1,0:T(8,128)(2,1)S(1)}, u32[]{:S(2)}, u32[]{:S(2)}) collective-permute-start(bf16[20,256]{1,0:T(8,128)(2,1)S(1)} %pad_maximum_fusion.2), channel_id=1, source_target_pairs={{0,2},{2,0},{1,3},{3,1},{4,6},{6,4},{5,7},{7,5},{8,10},{10,8},{9,1... | collective-permute-start | bytes 30728 | tf_op jit(solution)/shard_map/ppermute | solution.py:28
  76.7 5.3 %collective-permute-start.8 = (f32[3,256]{1,0:T(4,128)S(1)}, f32[3,256]{1,0:T(4,128)S(1)}, u32[]{:S(2)}, u32[]{:S(2)}) collective-permute-start(f32[3,256]{1,0:T(4,128)S(1)} %add.92), channel_id=1, source_target_pairs={{0,8},{4,12},{8,0},{12,4},{16,24},{20,28},{24,16},{28,20},{1,9},{5... | collective-permute-start | bytes 9224 | tf_op jit(solution)/shard_map/ppermute | solution.py:18
  83.6 4.5 %collective-permute-start.9 = (f32[3,256]{1,0:T(4,128)S(1)}, f32[3,256]{1,0:T(4,128)S(1)}, u32[]{:S(2)}, u32[]{:S(2)}) collective-permute-start(f32[3,256]{1,0:T(4,128)S(1)} %add.93), channel_id=1, source_target_pairs={{0,16},{4,20},{8,24},{12,28},{16,0},{20,4},{24,8},{28,12},{1,17},{... | collective-permute-start | bytes 9224 | tf_op jit(solution)/shard_map/ppermute | solution.py:18
  88.9 3.4 %collective-permute-start.16 = (bf16[40,256]{1,0:T(8,128)(2,1)S(1)}, bf16[40,256]{1,0:T(8,128)(2,1)S(1)}, u32[]{:S(2)}, u32[]{:S(2)}) collective-permute-start(bf16[40,256]{1,0:T(8,128)(2,1)S(1)} %pad_maximum_fusion.1), channel_id=1, source_target_pairs={{0,4},{4,0},{8,12},{12,8},{16,20},{20,16},{24,28},{28,24},{1,5},{5... | collective-permute-start | bytes 61448 | tf_op jit(solution)/shard_map/ppermute | solution.py:28
  93.0 1.9 %collective-permute-start.10 = (f32[3,256]{1,0:T(4,128)S(1)}, f32[3,256]{1,0:T(4,128)S(1)}, u32[]{:S(2)}, u32[]{:S(2)}) collective-permute-start(f32[3,256]{1,0:T(4,128)S(1)} %add.94), channel_id=1, source_target_pairs={{0,32},{32,0},{1,33},{33,1},{2,34},{34,2},{3,35},{35,3},{4,36},{36... | collective-permute-start | bytes 9224 | tf_op jit(solution)/shard_map/ppermute | solution.py:18
  95.6 2.9 %collective-permute-done.10 = f32[3,256]{1,0:T(4,128)S(1)} collective-permute-done((f32[3,256]{1,0:T(4,128)S(1)}, f32[3,256]{1,0:T(4,128)S(1)}, u32[]{:S(2)}, u32[]{:S(2)}) %collective-permute-start.10) | collective-permute-done | bytes 3104 | tf_op jit(solution)/shard_map/ppermute | solution.py:18
  98.5 3.5 %collective-permute-start.11 = (f32[3,256]{1,0:T(4,128)S(1)}, f32[3,256]{1,0:T(4,128)S(1)}, u32[]{:S(2)}, u32[]{:S(2)}) collective-permute-start(f32[3,256]{1,0:T(4,128)S(1)} %add.95), channel_id=1, source_target_pairs={{0,64},{64,0},{128,192},{192,128},{256,320},{320,256},{384,448},{4... | collective-permute-start | bytes 9224 | tf_op jit(solution)/shard_map/ppermute | solution.py:18
  102.8 3.4 %collective-permute-start.17 = (bf16[80,256]{1,0:T(8,128)(2,1)S(1)}, bf16[80,256]{1,0:T(8,128)(2,1)S(1)}, u32[]{:S(2)}, u32[]{:S(2)}) collective-permute-start(bf16[80,256]{1,0:T(8,128)(2,1)S(1)} %pad_maximum_fusion), channel_id=1, source_target_pairs={{0,8},{4,12},{8,0},{12,4},{16,24},{20,28},{24,16},{28,20},{1,9},{5... | collective-permute-start | bytes 122888 | tf_op jit(solution)/shard_map/ppermute | solution.py:28
  106.2 6.1 %collective-permute-start.12 = (f32[3,256]{1,0:T(4,128)S(1)}, f32[3,256]{1,0:T(4,128)S(1)}, u32[]{:S(2)}, u32[]{:S(2)}) collective-permute-start(f32[3,256]{1,0:T(4,128)S(1)} %add.96), channel_id=1, source_target_pairs={{0,128},{64,192},{128,0},{192,64},{256,384},{320,448},{384,256},{4... | collective-permute-start | bytes 9224 | tf_op jit(solution)/shard_map/ppermute | solution.py:18
  113.3 6.7 %collective-permute-start.18 = (bf16[160,256]{1,0:T(8,128)(2,1)S(1)}, bf16[160,256]{1,0:T(8,128)(2,1)S(1)}, u32[]{:S(2)}, u32[]{:S(2)}) collective-permute-start(bf16[160,256]{1,0:T(8,128)(2,1)S(1)} %concatenate.22), channel_id=1, source_target_pairs={{0,16},{4,20},{8,24},{12,28},{16,0},{20,4},{24,8},{28,12},{1,17},{... | collective-permute-start | bytes 245768 | tf_op jit(solution)/shard_map/ppermute | solution.py:28
  120.0 8.2 %collective-permute-start.13 = (f32[3,256]{1,0:T(4,128)S(1)}, f32[3,256]{1,0:T(4,128)S(1)}, u32[]{:S(2)}, u32[]{:S(2)}) collective-permute-start(f32[3,256]{1,0:T(4,128)S(1)} %add.97), channel_id=1, source_target_pairs={{0,256},{64,320},{128,384},{192,448},{256,0},{320,64},{384,128},{4... | collective-permute-start | bytes 9224 | tf_op jit(solution)/shard_map/ppermute | solution.py:18
  (65 shorter events, 20.7 us)
Async XLA Ops:
  0.0 20.0 %copy-start = (bf16[128,3,16,256]{3,2,1,0:T(8,128)(2,1)S(1)}, bf16[128,3,16,256]{3,2,1,0:T(8,128)(2,1)}, u32[]{:S(2)}) copy-start(bf16[128,3,16,256]{3,2,1,0:T(8,128)(2,1)} %param.12) | copy-start | bytes 9437188
  0.0 20.0 %copy-start.3 = (bf16[16,256]{1,0:T(8,128)(2,1)S(1)}, bf16[16,256]{1,0:T(8,128)(2,1)}, u32[]{:S(2)}) copy-start(bf16[16,256]{1,0:T(8,128)(2,1)} %param.14) | copy-start | bytes 24580
  0.0 12.7 %copy-start.2 = (bf16[10,256]{1,0:T(8,128)(2,1)S(1)}, bf16[10,256]{1,0:T(8,128)(2,1)}, u32[]{:S(2)}) copy-start(bf16[10,256]{1,0:T(8,128)(2,1)} %param.16) | copy-start | bytes 15364
  4.4 23.3 %copy-start.5 = (s32[10]{0:T(128)S(1)}, s32[10]{0:T(128)}, u32[]{:S(2)}) copy-start(s32[10]{0:T(128)} %param.18) | copy-start | bytes 124
  4.4 23.3 %copy-start.4 = (s32[320,2]{0,1:T(2,128)S(1)}, s32[320,2]{0,1:T(2,128)}, u32[]{:S(2)}) copy-start(s32[320,2]{0,1:T(2,128)} %param.17) | copy-start | bytes 7684
  4.4 3.4 %collective-permute-start = (f32[128,256]{0,1:T(8,128)S(1)}, f32[128,256]{0,1:T(8,128)S(1)}, u32[]{:S(2)}, u32[]{:S(2)}) collective-permute-start(f32[128,256]{0,1:T(8,128)S(1)} %bitcast.32), channel_id=1, source_target_pairs={{0,1},{1,0},{2,3},{3,2},{4,5},{5,4},{6,7},{7,6},{8,9},{9,8},{10,11... | collective-permute-start | bytes 393224 | tf_op jit(solution)/shard_map/ppermute | solution.py:18
  7.8 8.9 %collective-permute-start.1 = (f32[128,256]{0,1:T(8,128)S(1)}, f32[128,256]{0,1:T(8,128)S(1)}, u32[]{:S(2)}, u32[]{:S(2)}) collective-permute-start(f32[128,256]{0,1:T(8,128)S(1)} %bitcast_add_fusion), channel_id=1, source_target_pairs={{0,2},{2,0},{1,3},{3,1},{4,6},{6,4},{5,7},{7,5},{8,10},{10,8},{9,1... | collective-permute-start | bytes 393224 | tf_op jit(solution)/shard_map/ppermute | solution.py:18
  12.7 60.5 %collective-permute-start.14 = (bf16[10,256]{1,0:T(8,128)(2,1)S(1)}, bf16[10,256]{1,0:T(8,128)(2,1)}, u32[]{:S(2)}, u32[]{:S(2)}) collective-permute-start(bf16[10,256]{1,0:T(8,128)(2,1)S(1)} %copy-done.2), channel_id=1, source_target_pairs={{0,1},{1,0},{2,3},{3,2},{4,5},{5,4},{6,7},{7,6},{8,9},{9,8},{10,11... | collective-permute-start | bytes 15368 | tf_op jit(solution)/shard_map/ppermute | solution.py:28
  16.7 6.9 %collective-permute-start.2 = (f32[128,256]{0,1:T(8,128)S(1)}, f32[128,256]{0,1:T(8,128)S(1)}, u32[]{:S(2)}, u32[]{:S(2)}) collective-permute-start(f32[128,256]{0,1:T(8,128)S(1)} %add.86), channel_id=1, source_target_pairs={{0,4},{4,0},{8,12},{12,8},{16,20},{20,16},{24,28},{28,24},{1,5},{5... | collective-permute-start | bytes 393224 | tf_op jit(solution)/shard_map/ppermute | solution.py:18
  23.6 9.2 %collective-permute-start.3 = (f32[128,256]{0,1:T(8,128)S(1)}, f32[128,256]{0,1:T(8,128)S(1)}, u32[]{:S(2)}, u32[]{:S(2)}) collective-permute-start(f32[128,256]{0,1:T(8,128)S(1)} %add.87), channel_id=1, source_target_pairs={{0,8},{4,12},{8,0},{12,4},{16,24},{20,28},{24,16},{28,20},{1,9},{5... | collective-permute-start | bytes 393224 | tf_op jit(solution)/shard_map/ppermute | solution.py:18
  33.5 16.8 %collective-permute-start.4 = (f32[128,256]{0,1:T(8,128)}, f32[128,256]{0,1:T(8,128)}, u32[]{:S(2)}, u32[]{:S(2)}) collective-permute-start(f32[128,256]{0,1:T(8,128)} %add.88), channel_id=1, source_target_pairs={{0,16},{4,20},{8,24},{12,28},{16,0},{20,4},{24,8},{28,12},{1,17},{... | collective-permute-start | bytes 393224 | tf_op jit(solution)/shard_map/ppermute | solution.py:18
  45.6 20.9 %copy-start.1 = (s32[24]{0:T(128)S(1)}, s32[24]{0:T(128)}, u32[]{:S(2)}) copy-start(s32[24]{0:T(128)} %param.19) | copy-start | bytes 292
  60.6 3.0 %collective-permute-start.5 = (f32[3,256]{1,0:T(4,128)S(1)}, f32[3,256]{1,0:T(4,128)S(1)}, u32[]{:S(2)}, u32[]{:S(2)}) collective-permute-start(f32[3,256]{1,0:T(4,128)S(1)} %reshape.100), channel_id=1, source_target_pairs={{0,1},{1,0},{2,3},{3,2},{4,5},{5,4},{6,7},{7,6},{8,9},{9,8},{10,11... | collective-permute-start | bytes 9224 | tf_op jit(solution)/shard_map/ppermute | solution.py:18
  63.6 7.0 %collective-permute-start.6 = (f32[3,256]{1,0:T(4,128)S(1)}, f32[3,256]{1,0:T(4,128)S(1)}, u32[]{:S(2)}, u32[]{:S(2)}) collective-permute-start(f32[3,256]{1,0:T(4,128)S(1)} %add.90), channel_id=1, source_target_pairs={{0,2},{2,0},{1,3},{3,1},{4,6},{6,4},{5,7},{7,5},{8,10},{10,8},{9,1... | collective-permute-start | bytes 9224 | tf_op jit(solution)/shard_map/ppermute | solution.py:18
  70.6 6.1 %collective-permute-start.7 = (f32[3,256]{1,0:T(4,128)S(1)}, f32[3,256]{1,0:T(4,128)S(1)}, u32[]{:S(2)}, u32[]{:S(2)}) collective-permute-start(f32[3,256]{1,0:T(4,128)S(1)} %add.91), channel_id=1, source_target_pairs={{0,4},{4,0},{8,12},{12,8},{16,20},{20,16},{24,28},{28,24},{1,5},{5... | collective-permute-start | bytes 9224 | tf_op jit(solution)/shard_map/ppermute | solution.py:18
  73.9 14.2 %collective-permute-start.15 = (bf16[20,256]{1,0:T(8,128)(2,1)S(1)}, bf16[20,256]{1,0:T(8,128)(2,1)S(1)}, u32[]{:S(2)}, u32[]{:S(2)}) collective-permute-start(bf16[20,256]{1,0:T(8,128)(2,1)S(1)} %pad_maximum_fusion.2), channel_id=1, source_target_pairs={{0,2},{2,0},{1,3},{3,1},{4,6},{6,4},{5,7},{7,5},{8,10},{10,8},{9,1... | collective-permute-start | bytes 30728 | tf_op jit(solution)/shard_map/ppermute | solution.py:28
  76.7 6.9 %collective-permute-start.8 = (f32[3,256]{1,0:T(4,128)S(1)}, f32[3,256]{1,0:T(4,128)S(1)}, u32[]{:S(2)}, u32[]{:S(2)}) collective-permute-start(f32[3,256]{1,0:T(4,128)S(1)} %add.92), channel_id=1, source_target_pairs={{0,8},{4,12},{8,0},{12,4},{16,24},{20,28},{24,16},{28,20},{1,9},{5... | collective-permute-start | bytes 9224 | tf_op jit(solution)/shard_map/ppermute | solution.py:18
  83.6 9.4 %collective-permute-start.9 = (f32[3,256]{1,0:T(4,128)S(1)}, f32[3,256]{1,0:T(4,128)S(1)}, u32[]{:S(2)}, u32[]{:S(2)}) collective-permute-start(f32[3,256]{1,0:T(4,128)S(1)} %add.93), channel_id=1, source_target_pairs={{0,16},{4,20},{8,24},{12,28},{16,0},{20,4},{24,8},{28,12},{1,17},{... | collective-permute-start | bytes 9224 | tf_op jit(solution)/shard_map/ppermute | solution.py:18
  88.9 13.2 %collective-permute-start.16 = (bf16[40,256]{1,0:T(8,128)(2,1)S(1)}, bf16[40,256]{1,0:T(8,128)(2,1)S(1)}, u32[]{:S(2)}, u32[]{:S(2)}) collective-permute-start(bf16[40,256]{1,0:T(8,128)(2,1)S(1)} %pad_maximum_fusion.1), channel_id=1, source_target_pairs={{0,4},{4,0},{8,12},{12,8},{16,20},{20,16},{24,28},{28,24},{1,5},{5... | collective-permute-start | bytes 61448 | tf_op jit(solution)/shard_map/ppermute | solution.py:28
  93.0 5.5 %collective-permute-start.10 = (f32[3,256]{1,0:T(4,128)S(1)}, f32[3,256]{1,0:T(4,128)S(1)}, u32[]{:S(2)}, u32[]{:S(2)}) collective-permute-start(f32[3,256]{1,0:T(4,128)S(1)} %add.94), channel_id=1, source_target_pairs={{0,32},{32,0},{1,33},{33,1},{2,34},{34,2},{3,35},{35,3},{4,36},{36... | collective-permute-start | bytes 9224 | tf_op jit(solution)/shard_map/ppermute | solution.py:18
  98.5 7.6 %collective-permute-start.11 = (f32[3,256]{1,0:T(4,128)S(1)}, f32[3,256]{1,0:T(4,128)S(1)}, u32[]{:S(2)}, u32[]{:S(2)}) collective-permute-start(f32[3,256]{1,0:T(4,128)S(1)} %add.95), channel_id=1, source_target_pairs={{0,64},{64,0},{128,192},{192,128},{256,320},{320,256},{384,448},{4... | collective-permute-start | bytes 9224 | tf_op jit(solution)/shard_map/ppermute | solution.py:18
  102.8 9.5 %collective-permute-start.17 = (bf16[80,256]{1,0:T(8,128)(2,1)S(1)}, bf16[80,256]{1,0:T(8,128)(2,1)S(1)}, u32[]{:S(2)}, u32[]{:S(2)}) collective-permute-start(bf16[80,256]{1,0:T(8,128)(2,1)S(1)} %pad_maximum_fusion), channel_id=1, source_target_pairs={{0,8},{4,12},{8,0},{12,4},{16,24},{20,28},{24,16},{28,20},{1,9},{5... | collective-permute-start | bytes 122888 | tf_op jit(solution)/shard_map/ppermute | solution.py:28
  106.2 13.8 %collective-permute-start.12 = (f32[3,256]{1,0:T(4,128)S(1)}, f32[3,256]{1,0:T(4,128)S(1)}, u32[]{:S(2)}, u32[]{:S(2)}) collective-permute-start(f32[3,256]{1,0:T(4,128)S(1)} %add.96), channel_id=1, source_target_pairs={{0,128},{64,192},{128,0},{192,64},{256,384},{320,448},{384,256},{4... | collective-permute-start | bytes 9224 | tf_op jit(solution)/shard_map/ppermute | solution.py:18
  113.3 15.0 %collective-permute-start.18 = (bf16[160,256]{1,0:T(8,128)(2,1)S(1)}, bf16[160,256]{1,0:T(8,128)(2,1)S(1)}, u32[]{:S(2)}, u32[]{:S(2)}) collective-permute-start(bf16[160,256]{1,0:T(8,128)(2,1)S(1)} %concatenate.22), channel_id=1, source_target_pairs={{0,16},{4,20},{8,24},{12,28},{16,0},{20,4},{24,8},{28,12},{1,17},{... | collective-permute-start | bytes 245768 | tf_op jit(solution)/shard_map/ppermute | solution.py:28
  120.0 9.8 %collective-permute-start.13 = (f32[3,256]{1,0:T(4,128)S(1)}, f32[3,256]{1,0:T(4,128)S(1)}, u32[]{:S(2)}, u32[]{:S(2)}) collective-permute-start(f32[3,256]{1,0:T(4,128)S(1)} %add.97), channel_id=1, source_target_pairs={{0,256},{64,320},{128,384},{192,448},{256,0},{320,64},{384,128},{4... | collective-permute-start | bytes 9224 | tf_op jit(solution)/shard_map/ppermute | solution.py:18

commit v2 on v1

v2 whole, which is shorter than its diff:
```python
import jax
import jax.numpy as jnp
import numpy as np
from jax import lax
from jax.sharding import Mesh
from jax.sharding import PartitionSpec as P

AUX = ("z", "xlo")
AO = ("y", "xhi", "core")
HIGH = lax.Precision.HIGHEST
AO_ROUNDS = (("core", 2), ("xhi", 2), ("y", 8))
AUX_ROUNDS = (("xlo", 2), ("z", 8))


def partners(size, step):
    return [(i, i ^ step) for i in range(size)]


def butterfly_sum(value, rounds):
    for axis, size in rounds:
        step = 1
        while step < size:
            value = value + lax.ppermute(value, axis, partners(size, step))
            step *= 2
    return value


def butterfly_sum_gather(total, blocks, rounds):
    for axis, size in rounds:
        step = 1
        while step < size:
            pairs = partners(size, step)
            total = total + lax.ppermute(total, axis, pairs)
            blocks = jnp.concatenate([blocks, lax.ppermute(blocks, axis, pairs)], axis=0)
            total, blocks = lax.optimization_barrier((total, blocks))
            step *= 2
    return total, blocks


def on_device(soc_ints, cou_ints, coef_t, active_rdm, spin_dens, pair_list, owner_map, state_count):
    width = coef_t.shape[0]
    cells = width * width
    rows = soc_ints.shape[0]
    n_aux = lax.axis_size("z") * lax.axis_size("xlo")
    scale = 1.0 / (8.0 * jnp.sqrt(jnp.float32(rows * n_aux)))

    cou_part = jnp.einsum("un,ptn->upt", coef_t, cou_ints, preferred_element_type=jnp.float32)
    fitted = jnp.einsum("upt,tu->p", cou_part, active_rdm, precision=HIGH)
    folded = jnp.einsum("upw,vw->uvp", cou_part, active_rdm, precision=HIGH)
    eye = jnp.eye(width, dtype=jnp.float32)
    weight = (eye[:, :, None] * fitted[None, None, :] - 1.5 * folded).reshape(width, width * rows)
    weight, every_dens = butterfly_sum_gather(weight, spin_dens, AO_ROUNDS)

    soc_part = jnp.einsum(
        "vn,pkn->vpk", coef_t, soc_ints.reshape(rows, 3 * width, -1), preferred_element_type=jnp.float32
    ).reshape(width * rows, 3 * width)
    field_part = jnp.dot(weight, soc_part, precision=HIGH) * scale
    field = butterfly_sum(field_part, AO_ROUNDS + AUX_ROUNDS)

    me = (lax.axis_index("y") * 4 + lax.axis_index("xhi") * 2 + lax.axis_index("core")).astype(jnp.int32)
    block = spin_dens.shape[0]
    where = (owner_map // block) ^ me
    picked = jnp.take(every_dens, where * block + owner_map % block, axis=0)

    bra = jnp.take(state_count, jnp.take(pair_list[:, 0], owner_map, axis=0), axis=0)
    ket = jnp.take(state_count, jnp.take(pair_list[:, 1], owner_map, axis=0), axis=0)
    live = jnp.minimum(bra, ket)
    cell = jnp.arange(cells, dtype=jnp.int32)
    inside = (cell[None, :] // width < live[:, None]) & (cell[None, :] % width < live[:, None])
    dens = jnp.where(inside, picked.astype(jnp.float32), jnp.float32(0.0))
    return jnp.einsum(
        "uxt,stu->xs", field.reshape(width, 3, width), dens.reshape(-1, width, width), precision=HIGH
    ) / width


def solution(mesh):
    devices = np.asarray(mesh.devices).reshape(8, 2, 8, 2, 2)
    fine = Mesh(devices, AUX + AO)
    return jax.shard_map(
        on_device,
        mesh=fine,
        in_specs=(
            P(AUX, None, None, AO),
            P(AUX, None, AO),
            P(None, AO),
            P(),
            P(AO, None),
            P(),
            P(AO),
            P(),
        ),
        out_specs=P(None, AO),
        check_vma=False,
    )
```

time: 132 us -> 126 us (0.955)
  the two profiles are of different devices: /device:TPU:56 before, /device:TPU:16 now
where the time goes in v2:
time: 126 us
  starting transfers between devices  69.2 us (55%)
  waiting for transfers between devices  44.1 us (35%)
  matrix products  7.1 us (6%)
  local copies, waits for them, and re-layouts  3.63 us (3%)
    ppermute x9, starting transfers between devices, butterfly_sum(): value = value + lax.ppermute(value, axis, partners(size, step))  35.2 us
    ppermute x9, waiting for transfers between devices, butterfly_sum(): value = value + lax.ppermute(value, axis, partners(size, step))  22.1 us
    ppermute x5, starting transfers between devices, butterfly_sum_gather(): lax.ppermute(blocks, axis, pairs)  17.4 us
    ppermute x5, starting transfers between devices, butterfly_sum_gather(): total = total + lax.ppermute(total, axis, pairs)  16.6 us
    ppermute x5, waiting for transfers between devices, butterfly_sum_gather(): total = total + lax.ppermute(total, axis, pairs)  15.5 us
    ppermute x5, waiting for transfers between devices, butterfly_sum_gather(): lax.ppermute(blocks, axis, pairs)  6.48 us
  transfers between devices with their start and end apart: 19, of which 15 were waited for; matrix products, arithmetic and copies ran while one was open for 5% of the time, Pallas kernels for 0%

profile of v2, /device:TPU:16, one launch (start us, length us, event | category | flops | bytes accessed | tf_op | source)
XLA Modules:
  0.0 125.5 jit_solution(4578066246643815916)
XLA Ops:
  0.0 2.1 %fusion.5 = f32[16,128,16]{1,0,2:T(8,128)S(1)} fusion(bf16[128,16,256]{2,1,0:T(8,128)(2,1)} %param.13, bf16[16,256]{1,0:T(8,128)(2,1)} %param.14), kind=kOutput, calls=%fused_computation.14 | convolution fusion | flops 16777216 | bytes 1187840 | tf_op jit(solution)/shard_map/un,ptn->upt/dot_general | solution.py:47
  4.1 1.9 %collective-permute-start = (f32[16,2048]{1,0:T(8,128)S(1)}, f32[16,2048]{1,0:T(8,128)S(1)}, u32[]{:S(2)}, u32[]{:S(2)}) collective-permute-start(f32[16,2048]{1,0:T(8,128)S(1)} %bitcast.42), channel_id=1, source_target_pairs={{0,1},{1,0},{2,3},{3,2},{4,5},{5,4},{6,7},{7,6},{8,9},{9,8},{10,11... | collective-permute-start | bytes 393224 | tf_op jit(solution)/shard_map/ppermute | solution.py:33
  6.0 2.4 %collective-permute-start.1 = (bf16[10,256]{1,0:T(8,128)(2,1)}, bf16[10,256]{1,0:T(8,128)(2,1)S(1)}, u32[]{:S(2)}, u32[]{:S(2)}) collective-permute-start(bf16[10,256]{1,0:T(8,128)(2,1)} %param.16), channel_id=1, source_target_pairs={{0,1},{1,0},{2,3},{3,2},{4,5},{5,4},{6,7},{7,6},{8,9},{9,8},{10,11... | collective-permute-start | bytes 15368 | tf_op jit(solution)/shard_map/ppermute | solution.py:34
  10.2 4.9 %collective-permute-start.2 = (f32[16,2048]{1,0:T(8,128)S(1)}, f32[16,2048]{1,0:T(8,128)S(1)}, u32[]{:S(2)}, u32[]{:S(2)}) collective-permute-start(f32[16,2048]{1,0:T(8,128)S(1)} %fusion.21), channel_id=1, source_target_pairs={{0,2},{2,0},{1,3},{3,1},{4,6},{6,4},{5,7},{7,5},{8,10},{10,8},{9,1... | collective-permute-start | bytes 393224 | tf_op jit(solution)/shard_map/ppermute | solution.py:33
  15.2 2.4 %collective-permute-start.3 = (bf16[20,256]{1,0:T(8,128)(2,1)S(1)}, bf16[20,256]{1,0:T(8,128)(2,1)S(1)}, u32[]{:S(2)}, u32[]{:S(2)}) collective-permute-start(bf16[20,256]{1,0:T(8,128)(2,1)S(1)} %pad_maximum_fusion.4), channel_id=1, source_target_pairs={{0,2},{2,0},{1,3},{3,1},{4,6},{6,4},{5,7},{7,5},{8,10},{10,8},{9,1... | collective-permute-start | bytes 30728 | tf_op jit(solution)/shard_map/ppermute | solution.py:34
  17.6 4.7 %collective-permute-done.3 = bf16[20,256]{1,0:T(8,128)(2,1)S(1)} collective-permute-done((bf16[20,256]{1,0:T(8,128)(2,1)S(1)}, bf16[20,256]{1,0:T(8,128)(2,1)S(1)}, u32[]{:S(2)}, u32[]{:S(2)}) %collective-permute-start.3) | collective-permute-done | bytes 10272 | tf_op jit(solution)/shard_map/ppermute | solution.py:34
  22.3 3.5 %collective-permute-start.5 = (bf16[40,256]{1,0:T(8,128)(2,1)S(1)}, bf16[40,256]{1,0:T(8,128)(2,1)S(1)}, u32[]{:S(2)}, u32[]{:S(2)}) collective-permute-start(bf16[40,256]{1,0:T(8,128)(2,1)S(1)} %pad_maximum_fusion.3), channel_id=1, source_target_pairs={{0,4},{4,0},{8,12},{12,8},{16,20},{20,16},{24,28},{28,24},{1,5},{5... | collective-permute-start | bytes 61448 | tf_op jit(solution)/shard_map/ppermute | solution.py:34
  25.8 2.4 %collective-permute-start.4 = (f32[16,2048]{1,0:T(8,128)S(1)}, f32[16,2048]{1,0:T(8,128)S(1)}, u32[]{:S(2)}, u32[]{:S(2)}) collective-permute-start(f32[16,2048]{1,0:T(8,128)S(1)} %add.90), channel_id=1, source_target_pairs={{0,4},{4,0},{8,12},{12,8},{16,20},{20,16},{24,28},{28,24},{1,5},{5... | collective-permute-start | bytes 393224 | tf_op jit(solution)/shard_map/ppermute | solution.py:33
  28.2 4.5 %collective-permute-done.4 = f32[16,2048]{1,0:T(8,128)S(1)} collective-permute-done((f32[16,2048]{1,0:T(8,128)S(1)}, f32[16,2048]{1,0:T(8,128)S(1)}, u32[]{:S(2)}, u32[]{:S(2)}) %collective-permute-start.4) | collective-permute-done | bytes 131104 | tf_op jit(solution)/shard_map/ppermute | solution.py:33
  32.7 3.4 %collective-permute-start.7 = (bf16[80,256]{1,0:T(8,128)(2,1)S(1)}, bf16[80,256]{1,0:T(8,128)(2,1)S(1)}, u32[]{:S(2)}, u32[]{:S(2)}) collective-permute-start(bf16[80,256]{1,0:T(8,128)(2,1)S(1)} %pad_maximum_fusion.2), channel_id=1, source_target_pairs={{0,8},{4,12},{8,0},{12,4},{16,24},{20,28},{24,16},{28,20},{1,9},{5... | collective-permute-start | bytes 122888 | tf_op jit(solution)/shard_map/ppermute | solution.py:34
  36.1 3.3 %collective-permute-start.6 = (f32[16,2048]{1,0:T(8,128)S(1)}, f32[16,2048]{1,0:T(8,128)S(1)}, u32[]{:S(2)}, u32[]{:S(2)}) collective-permute-start(f32[16,2048]{1,0:T(8,128)S(1)} %add.91), channel_id=1, source_target_pairs={{0,8},{4,12},{8,0},{12,4},{16,24},{20,28},{24,16},{28,20},{1,9},{5... | collective-permute-start | bytes 393224 | tf_op jit(solution)/shard_map/ppermute | solution.py:33
  39.5 1.8 %fusion = f32[16,128,48]{1,0,2:T(8,128)S(1)} fusion(bf16[128,48,256]{2,1,0:T(8,128)(2,1)S(1)} %bitcast.38, bf16[16,256]{1,0:T(8,128)(2,1)S(1)} %copy-done.2), kind=kOutput, calls=%fused_computation.5 | convolution fusion | flops 50331648 | bytes 3547136 | tf_op jit(solution)/shard_map/vn,pkn->vpk/dot_general | solution.py:54
  41.2 2.7 %collective-permute-done.6 = f32[16,2048]{1,0:T(8,128)S(1)} collective-permute-done((f32[16,2048]{1,0:T(8,128)S(1)}, f32[16,2048]{1,0:T(8,128)S(1)}, u32[]{:S(2)}, u32[]{:S(2)}) %collective-permute-start.6) | collective-permute-done | bytes 131104 | tf_op jit(solution)/shard_map/ppermute | solution.py:33
  44.0 5.7 %collective-permute-start.9 = (bf16[160,256]{1,0:T(8,128)(2,1)S(1)}, bf16[160,256]{1,0:T(8,128)(2,1)S(1)}, u32[]{:S(2)}, u32[]{:S(2)}) collective-permute-start(bf16[160,256]{1,0:T(8,128)(2,1)S(1)} %pad_maximum_fusion.1), channel_id=1, source_target_pairs={{0,16},{4,20},{8,24},{12,28},{16,0},{20,4},{24,8},{28,12},{1,17},{... | collective-permute-start | bytes 245768 | tf_op jit(solution)/shard_map/ppermute | solution.py:34
  49.7 4.1 %collective-permute-start.8 = (f32[16,2048]{1,0:T(8,128)S(1)}, f32[16,2048]{1,0:T(8,128)S(1)}, u32[]{:S(2)}, u32[]{:S(2)}) collective-permute-start(f32[16,2048]{1,0:T(8,128)S(1)} %add.92), channel_id=1, source_target_pairs={{0,16},{4,20},{8,24},{12,28},{16,0},{20,4},{24,8},{28,12},{1,17},{... | collective-permute-start | bytes 393224 | tf_op jit(solution)/shard_map/ppermute | solution.py:33
  54.5 8.3 %collective-permute-done.8 = f32[16,2048]{1,0:T(8,128)S(1)} collective-permute-done((f32[16,2048]{1,0:T(8,128)S(1)}, f32[16,2048]{1,0:T(8,128)S(1)}, u32[]{:S(2)}, u32[]{:S(2)}) %collective-permute-start.8) | collective-permute-done | bytes 131104 | tf_op jit(solution)/shard_map/ppermute | solution.py:33
  63.4 1.9 %collective-permute-start.10 = (f32[16,48]{1,0:T(8,128)S(1)}, f32[16,48]{1,0:T(8,128)S(1)}, u32[]{:S(2)}, u32[]{:S(2)}) collective-permute-start(f32[16,48]{1,0:T(8,128)S(1)} %convolution_multiply_fusion.1), channel_id=1, source_target_pairs={{0,1},{1,0},{2,3},{3,2},{4,5},{5,4},{6,7},{7,6},{8,9},{9,8},{10,11... | collective-permute-start | bytes 9224 | tf_op jit(solution)/shard_map/ppermute | solution.py:23
  66.5 1.9 %collective-permute-start.11 = (f32[16,48]{1,0:T(8,128)S(1)}, f32[16,48]{1,0:T(8,128)S(1)}, u32[]{:S(2)}, u32[]{:S(2)}) collective-permute-start(f32[16,48]{1,0:T(8,128)S(1)} %add.94), channel_id=1, source_target_pairs={{0,2},{2,0},{1,3},{3,1},{4,6},{6,4},{5,7},{7,5},{8,10},{10,8},{9,1... | collective-permute-start | bytes 9224 | tf_op jit(solution)/shard_map/ppermute | solution.py:23
  69.7 3.8 %collective-permute-done.11 = f32[16,48]{1,0:T(8,128)S(1)} collective-permute-done((f32[16,48]{1,0:T(8,128)S(1)}, f32[16,48]{1,0:T(8,128)S(1)}, u32[]{:S(2)}, u32[]{:S(2)}) %collective-permute-start.11) | collective-permute-done | bytes 3104 | tf_op jit(solution)/shard_map/ppermute | solution.py:23
  73.5 2.2 %collective-permute-start.12 = (f32[16,48]{1,0:T(8,128)S(1)}, f32[16,48]{1,0:T(8,128)S(1)}, u32[]{:S(2)}, u32[]{:S(2)}) collective-permute-start(f32[16,48]{1,0:T(8,128)S(1)} %add.95), channel_id=1, source_target_pairs={{0,4},{4,0},{8,12},{12,8},{16,20},{20,16},{24,28},{28,24},{1,5},{5... | collective-permute-start | bytes 9224 | tf_op jit(solution)/shard_map/ppermute | solution.py:23
  75.7 3.3 %collective-permute-done.12 = f32[16,48]{1,0:T(8,128)S(1)} collective-permute-done((f32[16,48]{1,0:T(8,128)S(1)}, f32[16,48]{1,0:T(8,128)S(1)}, u32[]{:S(2)}, u32[]{:S(2)}) %collective-permute-start.12) | collective-permute-done | bytes 3104 | tf_op jit(solution)/shard_map/ppermute | solution.py:23
  79.0 2.8 %collective-permute-start.13 = (f32[16,48]{1,0:T(8,128)S(1)}, f32[16,48]{1,0:T(8,128)S(1)}, u32[]{:S(2)}, u32[]{:S(2)}) collective-permute-start(f32[16,48]{1,0:T(8,128)S(1)} %add.96), channel_id=1, source_target_pairs={{0,8},{4,12},{8,0},{12,4},{16,24},{20,28},{24,16},{28,20},{1,9},{5... | collective-permute-start | bytes 9224 | tf_op jit(solution)/shard_map/ppermute | solution.py:23
  83.2 2.2 %collective-permute-done.13 = f32[16,48]{1,0:T(8,128)S(1)} collective-permute-done((f32[16,48]{1,0:T(8,128)S(1)}, f32[16,48]{1,0:T(8,128)S(1)}, u32[]{:S(2)}, u32[]{:S(2)}) %collective-permute-start.13) | collective-permute-done | bytes 3104 | tf_op jit(solution)/shard_map/ppermute | solution.py:23
  85.5 5.0 %collective-permute-start.14 = (f32[16,48]{1,0:T(8,128)S(1)}, f32[16,48]{1,0:T(8,128)S(1)}, u32[]{:S(2)}, u32[]{:S(2)}) collective-permute-start(f32[16,48]{1,0:T(8,128)S(1)} %add.97), channel_id=1, source_target_pairs={{0,16},{4,20},{8,24},{12,28},{16,0},{20,4},{24,8},{28,12},{1,17},{... | collective-permute-start | bytes 9224 | tf_op jit(solution)/shard_map/ppermute | solution.py:23
  90.5 4.4 %collective-permute-done.14 = f32[16,48]{1,0:T(8,128)S(1)} collective-permute-done((f32[16,48]{1,0:T(8,128)S(1)}, f32[16,48]{1,0:T(8,128)S(1)}, u32[]{:S(2)}, u32[]{:S(2)}) %collective-permute-start.14) | collective-permute-done | bytes 3104 | tf_op jit(solution)/shard_map/ppermute | solution.py:23
  94.9 2.1 %collective-permute-start.15 = (f32[16,48]{1,0:T(8,128)S(1)}, f32[16,48]{1,0:T(8,128)S(1)}, u32[]{:S(2)}, u32[]{:S(2)}) collective-permute-start(f32[16,48]{1,0:T(8,128)S(1)} %add.98), channel_id=1, source_target_pairs={{0,32},{32,0},{1,33},{33,1},{2,34},{34,2},{3,35},{35,3},{4,36},{36... | collective-permute-start | bytes 9224 | tf_op jit(solution)/shard_map/ppermute | solution.py:23
  97.1 3.4 %collective-permute-done.15 = f32[16,48]{1,0:T(8,128)S(1)} collective-permute-done((f32[16,48]{1,0:T(8,128)S(1)}, f32[16,48]{1,0:T(8,128)S(1)}, u32[]{:S(2)}, u32[]{:S(2)}) %collective-permute-start.15) | collective-permute-done | bytes 3104 | tf_op jit(solution)/shard_map/ppermute | solution.py:23
  100.5 3.9 %collective-permute-start.16 = (f32[16,48]{1,0:T(8,128)S(1)}, f32[16,48]{1,0:T(8,128)S(1)}, u32[]{:S(2)}, u32[]{:S(2)}) collective-permute-start(f32[16,48]{1,0:T(8,128)S(1)} %add.99), channel_id=1, source_target_pairs={{0,64},{64,0},{128,192},{192,128},{256,320},{320,256},{384,448},{4... | collective-permute-start | bytes 9224 | tf_op jit(solution)/shard_map/ppermute | solution.py:23
  104.4 1.6 %collective-permute-done.16 = f32[16,48]{1,0:T(8,128)S(1)} collective-permute-done((f32[16,48]{1,0:T(8,128)S(1)}, f32[16,48]{1,0:T(8,128)S(1)}, u32[]{:S(2)}, u32[]{:S(2)}) %collective-permute-start.16) | collective-permute-done | bytes 3104 | tf_op jit(solution)/shard_map/ppermute | solution.py:23
  106.0 6.1 %collective-permute-start.17 = (f32[16,48]{1,0:T(8,128)S(1)}, f32[16,48]{1,0:T(8,128)S(1)}, u32[]{:S(2)}, u32[]{:S(2)}) collective-permute-start(f32[16,48]{1,0:T(8,128)S(1)} %add.100), channel_id=1, source_target_pairs={{0,128},{64,192},{128,0},{192,64},{256,384},{320,448},{384,256},{4... | collective-permute-start | bytes 9224 | tf_op jit(solution)/shard_map/ppermute | solution.py:23
  113.7 9.3 %collective-permute-start.18 = (f32[16,48]{1,0:T(8,128)S(1)}, f32[16,48]{1,0:T(8,128)S(1)}, u32[]{:S(2)}, u32[]{:S(2)}) collective-permute-start(f32[16,48]{1,0:T(8,128)S(1)} %add.101), channel_id=1, source_target_pairs={{0,256},{64,320},{128,384},{192,448},{256,0},{320,64},{384,128},{4... | collective-permute-start | bytes 9224 | tf_op jit(solution)/shard_map/ppermute | solution.py:23
  123.2 1.4 %collective-permute-done.18 = f32[16,48]{1,0:T(8,128)S(1)} collective-permute-done((f32[16,48]{1,0:T(8,128)S(1)}, f32[16,48]{1,0:T(8,128)S(1)}, u32[]{:S(2)}, u32[]{:S(2)}) %collective-permute-start.18) | collective-permute-done | bytes 3104 | tf_op jit(solution)/shard_map/ppermute | solution.py:23
  (61 shorter events, 11.8 us)
Async XLA Ops:
  0.0 39.4 %copy-start = (bf16[128,3,16,256]{3,2,1,0:T(8,128)(2,1)S(1)}, bf16[128,3,16,256]{3,2,1,0:T(8,128)(2,1)}, u32[]{:S(2)}) copy-start(bf16[128,3,16,256]{3,2,1,0:T(8,128)(2,1)} %param.12) | copy-start | bytes 9437188
  0.0 39.4 %copy-start.2 = (bf16[16,256]{1,0:T(8,128)(2,1)S(1)}, bf16[16,256]{1,0:T(8,128)(2,1)}, u32[]{:S(2)}) copy-start(bf16[16,256]{1,0:T(8,128)(2,1)} %param.14) | copy-start | bytes 24580
  2.1 51.7 %copy-start.4 = (s32[10]{0:T(128)S(1)}, s32[10]{0:T(128)}, u32[]{:S(2)}) copy-start(s32[10]{0:T(128)} %param.18) | copy-start | bytes 124
  4.1 6.1 %collective-permute-start = (f32[16,2048]{1,0:T(8,128)S(1)}, f32[16,2048]{1,0:T(8,128)S(1)}, u32[]{:S(2)}, u32[]{:S(2)}) collective-permute-start(f32[16,2048]{1,0:T(8,128)S(1)} %bitcast.42), channel_id=1, source_target_pairs={{0,1},{1,0},{2,3},{3,2},{4,5},{5,4},{6,7},{7,6},{8,9},{9,8},{10,11... | collective-permute-start | bytes 393224 | tf_op jit(solution)/shard_map/ppermute | solution.py:33
  6.0 3.4 %collective-permute-start.1 = (bf16[10,256]{1,0:T(8,128)(2,1)}, bf16[10,256]{1,0:T(8,128)(2,1)S(1)}, u32[]{:S(2)}, u32[]{:S(2)}) collective-permute-start(bf16[10,256]{1,0:T(8,128)(2,1)} %param.16), channel_id=1, source_target_pairs={{0,1},{1,0},{2,3},{3,2},{4,5},{5,4},{6,7},{7,6},{8,9},{9,8},{10,11... | collective-permute-start | bytes 15368 | tf_op jit(solution)/shard_map/ppermute | solution.py:34
  10.2 55.1 %copy-start.3 = (s32[320,2]{0,1:T(2,128)S(1)}, s32[320,2]{0,1:T(2,128)}, u32[]{:S(2)}) copy-start(s32[320,2]{0,1:T(2,128)} %param.17) | copy-start | bytes 7684
  10.2 12.0 %collective-permute-start.2 = (f32[16,2048]{1,0:T(8,128)S(1)}, f32[16,2048]{1,0:T(8,128)S(1)}, u32[]{:S(2)}, u32[]{:S(2)}) collective-permute-start(f32[16,2048]{1,0:T(8,128)S(1)} %fusion.21), channel_id=1, source_target_pairs={{0,2},{2,0},{1,3},{3,1},{4,6},{6,4},{5,7},{7,5},{8,10},{10,8},{9,1... | collective-permute-start | bytes 393224 | tf_op jit(solution)/shard_map/ppermute | solution.py:33
  15.2 7.1 %collective-permute-start.3 = (bf16[20,256]{1,0:T(8,128)(2,1)S(1)}, bf16[20,256]{1,0:T(8,128)(2,1)S(1)}, u32[]{:S(2)}, u32[]{:S(2)}) collective-permute-start(bf16[20,256]{1,0:T(8,128)(2,1)S(1)} %pad_maximum_fusion.4), channel_id=1, source_target_pairs={{0,2},{2,0},{1,3},{3,1},{4,6},{6,4},{5,7},{7,5},{8,10},{10,8},{9,1... | collective-permute-start | bytes 30728 | tf_op jit(solution)/shard_map/ppermute | solution.py:34
  22.3 5.9 %collective-permute-start.5 = (bf16[40,256]{1,0:T(8,128)(2,1)S(1)}, bf16[40,256]{1,0:T(8,128)(2,1)S(1)}, u32[]{:S(2)}, u32[]{:S(2)}) collective-permute-start(bf16[40,256]{1,0:T(8,128)(2,1)S(1)} %pad_maximum_fusion.3), channel_id=1, source_target_pairs={{0,4},{4,0},{8,12},{12,8},{16,20},{20,16},{24,28},{28,24},{1,5},{5... | collective-permute-start | bytes 61448 | tf_op jit(solution)/shard_map/ppermute | solution.py:34
  25.8 6.9 %collective-permute-start.4 = (f32[16,2048]{1,0:T(8,128)S(1)}, f32[16,2048]{1,0:T(8,128)S(1)}, u32[]{:S(2)}, u32[]{:S(2)}) collective-permute-start(f32[16,2048]{1,0:T(8,128)S(1)} %add.90), channel_id=1, source_target_pairs={{0,4},{4,0},{8,12},{12,8},{16,20},{20,16},{24,28},{28,24},{1,5},{5... | collective-permute-start | bytes 393224 | tf_op jit(solution)/shard_map/ppermute | solution.py:33
  32.7 8.6 %collective-permute-start.7 = (bf16[80,256]{1,0:T(8,128)(2,1)S(1)}, bf16[80,256]{1,0:T(8,128)(2,1)S(1)}, u32[]{:S(2)}, u32[]{:S(2)}) collective-permute-start(bf16[80,256]{1,0:T(8,128)(2,1)S(1)} %pad_maximum_fusion.2), channel_id=1, source_target_pairs={{0,8},{4,12},{8,0},{12,4},{16,24},{20,28},{24,16},{28,20},{1,9},{5... | collective-permute-start | bytes 122888 | tf_op jit(solution)/shard_map/ppermute | solution.py:34
  36.1 7.9 %collective-permute-start.6 = (f32[16,2048]{1,0:T(8,128)S(1)}, f32[16,2048]{1,0:T(8,128)S(1)}, u32[]{:S(2)}, u32[]{:S(2)}) collective-permute-start(f32[16,2048]{1,0:T(8,128)S(1)} %add.91), channel_id=1, source_target_pairs={{0,8},{4,12},{8,0},{12,4},{16,24},{20,28},{24,16},{28,20},{1,9},{5... | collective-permute-start | bytes 393224 | tf_op jit(solution)/shard_map/ppermute | solution.py:33
  39.5 42.4 %copy-start.1 = (s32[24]{0:T(128)S(1)}, s32[24]{0:T(128)}, u32[]{:S(2)}) copy-start(s32[24]{0:T(128)} %param.19) | copy-start | bytes 292
  44.0 10.6 %collective-permute-start.9 = (bf16[160,256]{1,0:T(8,128)(2,1)S(1)}, bf16[160,256]{1,0:T(8,128)(2,1)S(1)}, u32[]{:S(2)}, u32[]{:S(2)}) collective-permute-start(bf16[160,256]{1,0:T(8,128)(2,1)S(1)} %pad_maximum_fusion.1), channel_id=1, source_target_pairs={{0,16},{4,20},{8,24},{12,28},{16,0},{20,4},{24,8},{28,12},{1,17},{... | collective-permute-start | bytes 245768 | tf_op jit(solution)/shard_map/ppermute | solution.py:34
  49.7 13.2 %collective-permute-start.8 = (f32[16,2048]{1,0:T(8,128)S(1)}, f32[16,2048]{1,0:T(8,128)S(1)}, u32[]{:S(2)}, u32[]{:S(2)}) collective-permute-start(f32[16,2048]{1,0:T(8,128)S(1)} %add.92), channel_id=1, source_target_pairs={{0,16},{4,20},{8,24},{12,28},{16,0},{20,4},{24,8},{28,12},{1,17},{... | collective-permute-start | bytes 393224 | tf_op jit(solution)/shard_map/ppermute | solution.py:33
  63.4 3.1 %collective-permute-start.10 = (f32[16,48]{1,0:T(8,128)S(1)}, f32[16,48]{1,0:T(8,128)S(1)}, u32[]{:S(2)}, u32[]{:S(2)}) collective-permute-start(f32[16,48]{1,0:T(8,128)S(1)} %convolution_multiply_fusion.1), channel_id=1, source_target_pairs={{0,1},{1,0},{2,3},{3,2},{4,5},{5,4},{6,7},{7,6},{8,9},{9,8},{10,11... | collective-permute-start | bytes 9224 | tf_op jit(solution)/shard_map/ppermute | solution.py:23
  66.5 7.0 %collective-permute-start.11 = (f32[16,48]{1,0:T(8,128)S(1)}, f32[16,48]{1,0:T(8,128)S(1)}, u32[]{:S(2)}, u32[]{:S(2)}) collective-permute-start(f32[16,48]{1,0:T(8,128)S(1)} %add.94), channel_id=1, source_target_pairs={{0,2},{2,0},{1,3},{3,1},{4,6},{6,4},{5,7},{7,5},{8,10},{10,8},{9,1... | collective-permute-start | bytes 9224 | tf_op jit(solution)/shard_map/ppermute | solution.py:23
  73.5 5.5 %collective-permute-start.12 = (f32[16,48]{1,0:T(8,128)S(1)}, f32[16,48]{1,0:T(8,128)S(1)}, u32[]{:S(2)}, u32[]{:S(2)}) collective-permute-start(f32[16,48]{1,0:T(8,128)S(1)} %add.95), channel_id=1, source_target_pairs={{0,4},{4,0},{8,12},{12,8},{16,20},{20,16},{24,28},{28,24},{1,5},{5... | collective-permute-start | bytes 9224 | tf_op jit(solution)/shard_map/ppermute | solution.py:23
  79.0 6.4 %collective-permute-start.13 = (f32[16,48]{1,0:T(8,128)S(1)}, f32[16,48]{1,0:T(8,128)S(1)}, u32[]{:S(2)}, u32[]{:S(2)}) collective-permute-start(f32[16,48]{1,0:T(8,128)S(1)} %add.96), channel_id=1, source_target_pairs={{0,8},{4,12},{8,0},{12,4},{16,24},{20,28},{24,16},{28,20},{1,9},{5... | collective-permute-start | bytes 9224 | tf_op jit(solution)/shard_map/ppermute | solution.py:23
  85.5 9.4 %collective-permute-start.14 = (f32[16,48]{1,0:T(8,128)S(1)}, f32[16,48]{1,0:T(8,128)S(1)}, u32[]{:S(2)}, u32[]{:S(2)}) collective-permute-start(f32[16,48]{1,0:T(8,128)S(1)} %add.97), channel_id=1, source_target_pairs={{0,16},{4,20},{8,24},{12,28},{16,0},{20,4},{24,8},{28,12},{1,17},{... | collective-permute-start | bytes 9224 | tf_op jit(solution)/shard_map/ppermute | solution.py:23
  94.9 5.5 %collective-permute-start.15 = (f32[16,48]{1,0:T(8,128)S(1)}, f32[16,48]{1,0:T(8,128)S(1)}, u32[]{:S(2)}, u32[]{:S(2)}) collective-permute-start(f32[16,48]{1,0:T(8,128)S(1)} %add.98), channel_id=1, source_target_pairs={{0,32},{32,0},{1,33},{33,1},{2,34},{34,2},{3,35},{35,3},{4,36},{36... | collective-permute-start | bytes 9224 | tf_op jit(solution)/shard_map/ppermute | solution.py:23
  100.5 5.5 %collective-permute-start.16 = (f32[16,48]{1,0:T(8,128)S(1)}, f32[16,48]{1,0:T(8,128)S(1)}, u32[]{:S(2)}, u32[]{:S(2)}) collective-permute-start(f32[16,48]{1,0:T(8,128)S(1)} %add.99), channel_id=1, source_target_pairs={{0,64},{64,0},{128,192},{192,128},{256,320},{320,256},{384,448},{4... | collective-permute-start | bytes 9224 | tf_op jit(solution)/shard_map/ppermute | solution.py:23
  106.0 7.7 %collective-permute-start.17 = (f32[16,48]{1,0:T(8,128)S(1)}, f32[16,48]{1,0:T(8,128)S(1)}, u32[]{:S(2)}, u32[]{:S(2)}) collective-permute-start(f32[16,48]{1,0:T(8,128)S(1)} %add.100), channel_id=1, source_target_pairs={{0,128},{64,192},{128,0},{192,64},{256,384},{320,448},{384,256},{4... | collective-permute-start | bytes 9224 | tf_op jit(solution)/shard_map/ppermute | solution.py:23
  113.7 10.9 %collective-permute-start.18 = (f32[16,48]{1,0:T(8,128)S(1)}, f32[16,48]{1,0:T(8,128)S(1)}, u32[]{:S(2)}, u32[]{:S(2)}) collective-permute-start(f32[16,48]{1,0:T(8,128)S(1)} %add.101), channel_id=1, source_target_pairs={{0,256},{64,320},{128,384},{192,448},{256,0},{320,64},{384,128},{4... | collective-permute-start | bytes 9224 | tf_op jit(solution)/shard_map/ppermute | solution.py:23

commit v3 on v2

--- a/solution.py
+++ b/solution.py
@@ -26,13 +26,13 @@
 
 
 def butterfly_sum_gather(total, blocks, rounds):
+    count = total.shape[0]
     for axis, size in rounds:
         step = 1
         while step < size:
-            pairs = partners(size, step)
-            total = total + lax.ppermute(total, axis, pairs)
-            blocks = jnp.concatenate([blocks, lax.ppermute(blocks, axis, pairs)], axis=0)
-            total, blocks = lax.optimization_barrier((total, blocks))
+            got = lax.ppermute(jnp.concatenate([total, blocks], axis=0), axis, partners(size, step))
+            total = total + got[:count]
+            blocks = jnp.concatenate([blocks, got[count:]], axis=0)
             step *= 2
     return total, blocks
 
@@ -49,7 +49,12 @@
     folded = jnp.einsum("upw,vw->uvp", cou_part, active_rdm, precision=HIGH)
     eye = jnp.eye(width, dtype=jnp.float32)
     weight = (eye[:, :, None] * fitted[None, None, :] - 1.5 * folded).reshape(width, width * rows)
-    weight, every_dens = butterfly_sum_gather(weight, spin_dens, AO_ROUNDS)
+    block = spin_dens.shape[0]
+    slot = -(-block // width) * width
+    lane = weight.shape[1]
+    own_dens = jnp.pad(spin_dens.astype(jnp.float32), ((0, slot - block), (0, 0))).reshape(-1, lane)
+    weight, every_dens = butterfly_sum_gather(weight, own_dens, AO_ROUNDS)
+    every_dens = every_dens.reshape(-1, cells)
 
     soc_part = jnp.einsum(
         "vn,pkn->vpk", coef_t, soc_ints.reshape(rows, 3 * width, -1), preferred_element_type=jnp.float32
@@ -58,16 +63,15 @@
     field = butterfly_sum(field_part, AO_ROUNDS + AUX_ROUNDS)
 
     me = (lax.axis_index("y") * 4 + lax.axis_index("xhi") * 2 + lax.axis_index("core")).astype(jnp.int32)
-    block = spin_dens.shape[0]
     where = (owner_map // block) ^ me
-    picked = jnp.take(every_dens, where * block + owner_map % block, axis=0)
+    picked = jnp.take(every_dens, where * slot + owner_map % block, axis=0)
 
     bra = jnp.take(state_count, jnp.take(pair_list[:, 0], owner_map, axis=0), axis=0)
     ket = jnp.take(state_count, jnp.take(pair_list[:, 1], owner_map, axis=0), axis=0)
     live = jnp.minimum(bra, ket)
     cell = jnp.arange(cells, dtype=jnp.int32)
     inside = (cell[None, :] // width < live[:, None]) & (cell[None, :] % width < live[:, None])
-    dens = jnp.where(inside, picked.astype(jnp.float32), jnp.float32(0.0))
+    dens = jnp.where(inside, picked, jnp.float32(0.0))
     return jnp.einsum(
         "uxt,stu->xs", field.reshape(width, 3, width), dens.reshape(-1, width, width), precision=HIGH
     ) / width

time: 126 us -> 145 us (1.15)
  the two profiles are of different devices: /device:TPU:16 before, /device:TPU:6 now
where the time goes in v3:
time: 145 us; the launch traced here: 144 us
  starting transfers between devices  58.1 us (40%)
  waiting for transfers between devices  56.9 us (39%)
  local copies, waits for them, and re-layouts  18.3 us (13%)
  matrix products  7.01 us (5%)
  other arithmetic  3.22 us (2%)
    ppermute x5, waiting for transfers between devices, butterfly_sum_gather(): lax.ppermute(jnp.concatenate([total, blocks], axis=0), axis, partners(siz...  39.1 us
    ppermute x9, starting transfers between devices, butterfly_sum(): value = value + lax.ppermute(value, axis, partners(size, step))  37.1 us
    ppermute x5, starting transfers between devices, butterfly_sum_gather(): lax.ppermute(jnp.concatenate([total, blocks], axis=0), axis, partners(siz...  20.9 us
    ppermute x9, waiting for transfers between devices, butterfly_sum(): value = value + lax.ppermute(value, axis, partners(size, step))  17.8 us
    concatenate x2, local copies, waits for them, and re-layouts, butterfly_sum_gather(): jnp.concatenate([total, blocks], axis=0)  6.16 us
    concatenate x1, local copies, waits for them, and re-layouts, butterfly_sum_gather(): blocks = jnp.concatenate([blocks, got[count:]], axis=0)  3.59 us
  transfers between devices with their start and end apart: 14, of which 13 were waited for; matrix products, arithmetic and copies ran while one was open for 11% of the time, Pallas kernels for 0%

profile of v3, /device:TPU:6, one launch (start us, length us, event | category | flops | bytes accessed | tf_op | source)
XLA Modules:
  0.0 144.0 jit_solution(1772902179860016062)
XLA Ops:
  0.9 2.0 %fusion.5 = f32[16,128,16]{1,0,2:T(8,128)S(1)} fusion(bf16[128,16,256]{2,1,0:T(8,128)(2,1)} %param.13, bf16[16,256]{1,0:T(8,128)(2,1)} %param.14), kind=kOutput, calls=%fused_computation.14 | convolution fusion | flops 16777216 | bytes 1187840 | tf_op jit(solution)/shard_map/un,ptn->upt/dot_general | solution.py:47
  4.9 1.9 %collective-permute-start = (f32[18,2048]{1,0:T(8,128)S(1)}, f32[18,2048]{1,0:T(8,128)S(1)}, u32[]{:S(2)}, u32[]{:S(2)}) collective-permute-start(f32[18,2048]{1,0:T(8,128)S(1)} %pad_maximum_fusion), channel_id=1, source_target_pairs={{0,1},{1,0},{2,3},{3,2},{4,5},{5,4},{6,7},{7,6},{8,9},{9,8},{10,11... | collective-permute-start | bytes 442376 | tf_op jit(solution)/shard_map/ppermute | solution.py:33
  6.8 1.4 collective-permute-done
  8.4 3.3 %collective-permute-start.1 = (f32[20,2048]{1,0:T(8,128)S(1)}, f32[20,2048]{1,0:T(8,128)S(1)}, u32[]{:S(2)}, u32[]{:S(2)}) collective-permute-start(f32[20,2048]{1,0:T(8,128)S(1)} %pad_maximum_fusion.1), channel_id=1, source_target_pairs={{0,2},{2,0},{1,3},{3,1},{4,6},{6,4},{5,7},{7,5},{8,10},{10,8},{9,1... | collective-permute-start | bytes 491528 | tf_op jit(solution)/shard_map/ppermute | solution.py:33
  11.7 7.0 %collective-permute-done.1 = f32[20,2048]{1,0:T(8,128)S(1)} collective-permute-done((f32[20,2048]{1,0:T(8,128)S(1)}, f32[20,2048]{1,0:T(8,128)S(1)}, u32[]{:S(2)}, u32[]{:S(2)}) %collective-permute-start.1) | collective-permute-done | bytes 163872 | tf_op jit(solution)/shard_map/ppermute | solution.py:33
  18.8 3.5 %collective-permute-start.2 = (f32[24,2048]{1,0:T(8,128)S(1)}, f32[24,2048]{1,0:T(8,128)S(1)}, u32[]{:S(2)}, u32[]{:S(2)}) collective-permute-start(f32[24,2048]{1,0:T(8,128)S(1)} %pad_maximum_fusion.2), channel_id=1, source_target_pairs={{0,4},{4,0},{8,12},{12,8},{16,20},{20,16},{24,28},{28,24},{1,5},{5... | collective-permute-start | bytes 589832 | tf_op jit(solution)/shard_map/ppermute | solution.py:33
  22.3 4.5 %collective-permute-done.2 = f32[24,2048]{1,0:T(8,128)S(1)} collective-permute-done((f32[24,2048]{1,0:T(8,128)S(1)}, f32[24,2048]{1,0:T(8,128)S(1)}, u32[]{:S(2)}, u32[]{:S(2)}) %collective-permute-start.2) | collective-permute-done | bytes 196640 | tf_op jit(solution)/shard_map/ppermute | solution.py:33
  26.8 1.9 %concatenate.33 = f32[32,2048]{1,0:T(8,128)} concatenate(f32[16,2048]{1,0:T(8,128)S(1)} %slice_add_fusion.3, f32[2,2048]{1,0:T(2,128)S(1)} %reshape.134, f32[2,2048]{1,0:T(2,128)S(1)} %slice.59, f32[4,2048]{1,0:T(4,128)S(1)} %slice.61, f32[8,2048]{1,0:T(8,128)S(1)} %slice.63), dimensions={0} | concatenate | bytes 524288 | tf_op jit(solution)/shard_map/concatenate | solution.py:33
  28.8 4.5 %collective-permute-start.3 = (f32[32,2048]{1,0:T(8,128)}, f32[32,2048]{1,0:T(8,128)S(1)}, u32[]{:S(2)}, u32[]{:S(2)}) collective-permute-start(f32[32,2048]{1,0:T(8,128)} %concatenate.33), channel_id=1, source_target_pairs={{0,8},{4,12},{8,0},{12,4},{16,24},{20,28},{24,16},{28,20},{1,9},{5... | collective-permute-start | bytes 786440 | tf_op jit(solution)/shard_map/ppermute | solution.py:33
  33.3 10.7 %collective-permute-done.3 = f32[32,2048]{1,0:T(8,128)S(1)} collective-permute-done((f32[32,2048]{1,0:T(8,128)}, f32[32,2048]{1,0:T(8,128)S(1)}, u32[]{:S(2)}, u32[]{:S(2)}) %collective-permute-start.3) | collective-permute-done | bytes 262176 | tf_op jit(solution)/shard_map/ppermute | solution.py:33
  44.1 4.2 %concatenate.34 = f32[48,2048]{1,0:T(8,128)} concatenate(f32[16,2048]{1,0:T(8,128)S(1)} %get-tuple-element.12, f32[2,2048]{1,0:T(2,128)} %copy-done.6, f32[2,2048]{1,0:T(2,128)} %copy-done.8, f32[4,2048]{1,0:T(4,128)} %copy-done.4, f32[8,2048]{1,0:T(8,128)} %copy-done.2, f32[16,2048]{1,0:T(8,128)S(1)} %get-tuple-element.11), dimensions={0} | concatenate | bytes 786432 | tf_op jit(solution)/shard_map/concatenate | solution.py:33
  48.3 7.7 %collective-permute-start.4 = (f32[48,2048]{1,0:T(8,128)}, f32[48,2048]{1,0:T(8,128)S(1)}, u32[]{:S(2)}, u32[]{:S(2)}) collective-permute-start(f32[48,2048]{1,0:T(8,128)} %concatenate.34), channel_id=1, source_target_pairs={{0,16},{4,20},{8,24},{12,28},{16,0},{20,4},{24,8},{28,12},{1,17},{... | collective-permute-start | bytes 1179656 | tf_op jit(solution)/shard_map/ppermute | solution.py:33
  56.7 1.8 %fusion = f32[16,128,48]{1,0,2:T(8,128)S(1)} fusion(bf16[128,48,256]{2,1,0:T(8,128)(2,1)S(1)} %bitcast.37, bf16[16,256]{1,0:T(8,128)(2,1)S(1)} %copy-done.11), kind=kOutput, calls=%fused_computation.5 | convolution fusion | flops 50331648 | bytes 3547136 | tf_op jit(solution)/shard_map/vn,pkn->vpk/dot_general | solution.py:59
  58.5 15.4 %collective-permute-done.4 = f32[48,2048]{1,0:T(8,128)S(1)} collective-permute-done((f32[48,2048]{1,0:T(8,128)}, f32[48,2048]{1,0:T(8,128)S(1)}, u32[]{:S(2)}, u32[]{:S(2)}) %collective-permute-start.4) | collective-permute-done | bytes 393248 | tf_op jit(solution)/shard_map/ppermute | solution.py:33
  74.6 1.9 %collective-permute-start.5 = (f32[16,48]{1,0:T(8,128)S(1)}, f32[16,48]{1,0:T(8,128)S(1)}, u32[]{:S(2)}, u32[]{:S(2)}) collective-permute-start(f32[16,48]{1,0:T(8,128)S(1)} %convolution_multiply_fusion.1), channel_id=1, source_target_pairs={{0,1},{1,0},{2,3},{3,2},{4,5},{5,4},{6,7},{7,6},{8,9},{9,8},{10,11... | collective-permute-start | bytes 9224 | tf_op jit(solution)/shard_map/ppermute | solution.py:23
  77.7 3.3 %collective-permute-start.6 = (f32[16,48]{1,0:T(8,128)S(1)}, f32[16,48]{1,0:T(8,128)S(1)}, u32[]{:S(2)}, u32[]{:S(2)}) collective-permute-start(f32[16,48]{1,0:T(8,128)S(1)} %add.96), channel_id=1, source_target_pairs={{0,2},{2,0},{1,3},{3,1},{4,6},{6,4},{5,7},{7,5},{8,10},{10,8},{9,1... | collective-permute-start | bytes 9224 | tf_op jit(solution)/shard_map/ppermute | solution.py:23
  82.4 2.4 %collective-permute-done.6 = f32[16,48]{1,0:T(8,128)S(1)} collective-permute-done((f32[16,48]{1,0:T(8,128)S(1)}, f32[16,48]{1,0:T(8,128)S(1)}, u32[]{:S(2)}, u32[]{:S(2)}) %collective-permute-start.6) | collective-permute-done | bytes 3104 | tf_op jit(solution)/shard_map/ppermute | solution.py:23
  84.7 1.9 %collective-permute-start.7 = (f32[16,48]{1,0:T(8,128)S(1)}, f32[16,48]{1,0:T(8,128)S(1)}, u32[]{:S(2)}, u32[]{:S(2)}) collective-permute-start(f32[16,48]{1,0:T(8,128)S(1)} %add.97), channel_id=1, source_target_pairs={{0,4},{4,0},{8,12},{12,8},{16,20},{20,16},{24,28},{28,24},{1,5},{5... | collective-permute-start | bytes 9224 | tf_op jit(solution)/shard_map/ppermute | solution.py:23
  87.3 3.0 %collective-permute-done.7 = f32[16,48]{1,0:T(8,128)S(1)} collective-permute-done((f32[16,48]{1,0:T(8,128)S(1)}, f32[16,48]{1,0:T(8,128)S(1)}, u32[]{:S(2)}, u32[]{:S(2)}) %collective-permute-start.7) | collective-permute-done | bytes 3104 | tf_op jit(solution)/shard_map/ppermute | solution.py:23
  90.3 3.0 %collective-permute-start.8 = (f32[16,48]{1,0:T(8,128)S(1)}, f32[16,48]{1,0:T(8,128)S(1)}, u32[]{:S(2)}, u32[]{:S(2)}) collective-permute-start(f32[16,48]{1,0:T(8,128)S(1)} %add.98), channel_id=1, source_target_pairs={{0,8},{4,12},{8,0},{12,4},{16,24},{20,28},{24,16},{28,20},{1,9},{5... | collective-permute-start | bytes 9224 | tf_op jit(solution)/shard_map/ppermute | solution.py:23
  94.6 2.1 %collective-permute-done.8 = f32[16,48]{1,0:T(8,128)S(1)} collective-permute-done((f32[16,48]{1,0:T(8,128)S(1)}, f32[16,48]{1,0:T(8,128)S(1)}, u32[]{:S(2)}, u32[]{:S(2)}) %collective-permute-start.8) | collective-permute-done | bytes 3104 | tf_op jit(solution)/shard_map/ppermute | solution.py:23
  96.7 4.9 %collective-permute-start.9 = (f32[16,48]{1,0:T(8,128)S(1)}, f32[16,48]{1,0:T(8,128)S(1)}, u32[]{:S(2)}, u32[]{:S(2)}) collective-permute-start(f32[16,48]{1,0:T(8,128)S(1)} %add.99), channel_id=1, source_target_pairs={{0,16},{4,20},{8,24},{12,28},{16,0},{20,4},{24,8},{28,12},{1,17},{... | collective-permute-start | bytes 9224 | tf_op jit(solution)/shard_map/ppermute | solution.py:23
  101.6 4.5 %collective-permute-done.9 = f32[16,48]{1,0:T(8,128)S(1)} collective-permute-done((f32[16,48]{1,0:T(8,128)S(1)}, f32[16,48]{1,0:T(8,128)S(1)}, u32[]{:S(2)}, u32[]{:S(2)}) %collective-permute-start.9) | collective-permute-done | bytes 3104 | tf_op jit(solution)/shard_map/ppermute | solution.py:23
  106.2 5.0 %collective-permute-start.10 = (f32[16,48]{1,0:T(8,128)S(1)}, f32[16,48]{1,0:T(8,128)S(1)}, u32[]{:S(2)}, u32[]{:S(2)}) collective-permute-start(f32[16,48]{1,0:T(8,128)S(1)} %add.100), channel_id=1, source_target_pairs={{0,32},{32,0},{1,33},{33,1},{2,34},{34,2},{3,35},{35,3},{4,36},{36... | collective-permute-start | bytes 9224 | tf_op jit(solution)/shard_map/ppermute | solution.py:23
  112.8 3.2 %collective-permute-start.11 = (f32[16,48]{1,0:T(8,128)S(1)}, f32[16,48]{1,0:T(8,128)S(1)}, u32[]{:S(2)}, u32[]{:S(2)}) collective-permute-start(f32[16,48]{1,0:T(8,128)S(1)} %add.101), channel_id=1, source_target_pairs={{0,64},{64,0},{128,192},{192,128},{256,320},{320,256},{384,448},{4... | collective-permute-start | bytes 9224 | tf_op jit(solution)/shard_map/ppermute | solution.py:23
  116.0 2.4 %collective-permute-done.11 = f32[16,48]{1,0:T(8,128)S(1)} collective-permute-done((f32[16,48]{1,0:T(8,128)S(1)}, f32[16,48]{1,0:T(8,128)S(1)}, u32[]{:S(2)}, u32[]{:S(2)}) %collective-permute-start.11) | collective-permute-done | bytes 3104 | tf_op jit(solution)/shard_map/ppermute | solution.py:23
  118.4 5.3 %collective-permute-start.12 = (f32[16,48]{1,0:T(8,128)S(1)}, f32[16,48]{1,0:T(8,128)S(1)}, u32[]{:S(2)}, u32[]{:S(2)}) collective-permute-start(f32[16,48]{1,0:T(8,128)S(1)} %add.102), channel_id=1, source_target_pairs={{0,128},{64,192},{128,0},{192,64},{256,384},{320,448},{384,256},{4... | collective-permute-start | bytes 9224 | tf_op jit(solution)/shard_map/ppermute | solution.py:23
  123.7 1.7 %slice.67 = f32[32,2048]{1,0:T(8,128)} slice(f32[48,2048]{1,0:T(8,128)} %copy-done.10), slice={[16:48], [0:2048]} | slice | bytes 524288 | tf_op jit(solution)/shard_map/slice | solution.py:35
  125.4 3.6 %concatenate.35 = f32[64,2048]{1,0:T(8,128)} concatenate(f32[2,2048]{1,0:T(2,128)S(1)} %copy-done.7, f32[2,2048]{1,0:T(2,128)S(1)} %copy-done.9, f32[4,2048]{1,0:T(4,128)S(1)} %copy-done.5, f32[8,2048]{1,0:T(8,128)S(1)} %copy-done.3, f32[16,2048]{1,0:T(8,128)S(1)} %get-tuple-element.11, f32[32,2048]{1,0:T(8,128)} %slice.67), dimensions={0} | concatenate | bytes 1048576 | tf_op jit(solution)/shard_map/concatenate | solution.py:35
  129.0 1.9 %reshape.132 = f32[512,256]{1,0:T(8,128)} reshape(f32[64,2048]{1,0:T(8,128)} %concatenate.35) | data formatting | bytes 1048576 | tf_op jit(solution)/shard_map/reshape | solution.py:57
  130.9 1.6 %gather_fusion = f32[10,256]{1,0:T(8,128)S(1)} fusion(f32[512,256]{1,0:T(8,128)} %reshape.132, s32[1024]{0:T(1024)S(1)} %pad_clamp_fusion), kind=kCustom, calls=%fused_computation.4 | custom fusion | bytes 20520 | tf_op jit(solution)/shard_map/jit(_take)/gather | solution.py:67
  132.6 8.8 %collective-permute-start.13 = (f32[16,48]{1,0:T(8,128)S(1)}, f32[16,48]{1,0:T(8,128)S(1)}, u32[]{:S(2)}, u32[]{:S(2)}) collective-permute-start(f32[16,48]{1,0:T(8,128)S(1)} %add.103), channel_id=1, source_target_pairs={{0,256},{64,320},{128,384},{192,448},{256,0},{320,64},{384,128},{4... | collective-permute-start | bytes 9224 | tf_op jit(solution)/shard_map/ppermute | solution.py:23
  (74 shorter events, 13.3 us)
Async XLA Ops:
  0.0 56.7 %copy-start = (bf16[128,3,16,256]{3,2,1,0:T(8,128)(2,1)S(1)}, bf16[128,3,16,256]{3,2,1,0:T(8,128)(2,1)}, u32[]{:S(2)}) copy-start(bf16[128,3,16,256]{3,2,1,0:T(8,128)(2,1)} %param.12) | copy-start | bytes 9437188
  0.9 32.4 %copy-start.6 = (f32[2,2048]{1,0:T(2,128)}, f32[2,2048]{1,0:T(2,128)S(1)}, u32[]{:S(2)}) copy-start(f32[2,2048]{1,0:T(2,128)S(1)} %reshape.134) | copy-start | bytes 49156
  0.9 55.8 %copy-start.11 = (bf16[16,256]{1,0:T(8,128)(2,1)S(1)}, bf16[16,256]{1,0:T(8,128)(2,1)}, u32[]{:S(2)}) copy-start(bf16[16,256]{1,0:T(8,128)(2,1)} %param.14) | copy-start | bytes 24580
  4.9 3.3 %collective-permute-start = (f32[18,2048]{1,0:T(8,128)S(1)}, f32[18,2048]{1,0:T(8,128)S(1)}, u32[]{:S(2)}, u32[]{:S(2)}) collective-permute-start(f32[18,2048]{1,0:T(8,128)S(1)} %pad_maximum_fusion), channel_id=1, source_target_pairs={{0,1},{1,0},{2,3},{3,2},{4,5},{5,4},{6,7},{7,6},{8,9},{9,8},{10,11... | collective-permute-start | bytes 442376 | tf_op jit(solution)/shard_map/ppermute | solution.py:33
  8.3 25.0 %copy-start.8 = (f32[2,2048]{1,0:T(2,128)}, f32[2,2048]{1,0:T(2,128)S(1)}, u32[]{:S(2)}) copy-start(f32[2,2048]{1,0:T(2,128)S(1)} %slice.59) | copy-start | bytes 49156
  8.4 10.3 %collective-permute-start.1 = (f32[20,2048]{1,0:T(8,128)S(1)}, f32[20,2048]{1,0:T(8,128)S(1)}, u32[]{:S(2)}, u32[]{:S(2)}) collective-permute-start(f32[20,2048]{1,0:T(8,128)S(1)} %pad_maximum_fusion.1), channel_id=1, source_target_pairs={{0,2},{2,0},{1,3},{3,1},{4,6},{6,4},{5,7},{7,5},{8,10},{10,8},{9,1... | collective-permute-start | bytes 491528 | tf_op jit(solution)/shard_map/ppermute | solution.py:33
  18.7 14.6 %copy-start.4 = (f32[4,2048]{1,0:T(4,128)}, f32[4,2048]{1,0:T(4,128)S(1)}, u32[]{:S(2)}) copy-start(f32[4,2048]{1,0:T(4,128)S(1)} %slice.61) | copy-start | bytes 98308
  18.8 8.0 %collective-permute-start.2 = (f32[24,2048]{1,0:T(8,128)S(1)}, f32[24,2048]{1,0:T(8,128)S(1)}, u32[]{:S(2)}, u32[]{:S(2)}) collective-permute-start(f32[24,2048]{1,0:T(8,128)S(1)} %pad_maximum_fusion.2), channel_id=1, source_target_pairs={{0,4},{4,0},{8,12},{12,8},{16,20},{20,16},{24,28},{28,24},{1,5},{5... | collective-permute-start | bytes 589832 | tf_op jit(solution)/shard_map/ppermute | solution.py:33
  26.8 49.8 %copy-start.12 = (s32[320,2]{0,1:T(2,128)S(1)}, s32[320,2]{0,1:T(2,128)}, u32[]{:S(2)}) copy-start(s32[320,2]{0,1:T(2,128)} %param.17) | copy-start | bytes 7684
  26.8 6.5 %copy-start.2 = (f32[8,2048]{1,0:T(8,128)}, f32[8,2048]{1,0:T(8,128)S(1)}, u32[]{:S(2)}) copy-start(f32[8,2048]{1,0:T(8,128)S(1)} %slice.63) | copy-start | bytes 196612
  28.8 15.2 %collective-permute-start.3 = (f32[32,2048]{1,0:T(8,128)}, f32[32,2048]{1,0:T(8,128)S(1)}, u32[]{:S(2)}, u32[]{:S(2)}) collective-permute-start(f32[32,2048]{1,0:T(8,128)} %concatenate.33), channel_id=1, source_target_pairs={{0,8},{4,12},{8,0},{12,4},{16,24},{20,28},{24,16},{28,20},{1,9},{5... | collective-permute-start | bytes 786440 | tf_op jit(solution)/shard_map/ppermute | solution.py:33
  44.1 49.2 %copy-start.1 = (s32[24]{0:T(128)S(1)}, s32[24]{0:T(128)}, u32[]{:S(2)}) copy-start(s32[24]{0:T(128)} %param.19) | copy-start | bytes 292
  48.3 25.6 %collective-permute-start.4 = (f32[48,2048]{1,0:T(8,128)}, f32[48,2048]{1,0:T(8,128)S(1)}, u32[]{:S(2)}, u32[]{:S(2)}) collective-permute-start(f32[48,2048]{1,0:T(8,128)} %concatenate.34), channel_id=1, source_target_pairs={{0,16},{4,20},{8,24},{12,28},{16,0},{20,4},{24,8},{28,12},{1,17},{... | collective-permute-start | bytes 1179656 | tf_op jit(solution)/shard_map/ppermute | solution.py:33
  56.7 68.7 %copy-start.3 = (f32[8,2048]{1,0:T(8,128)S(1)}, f32[8,2048]{1,0:T(8,128)}, u32[]{:S(2)}) copy-start(f32[8,2048]{1,0:T(8,128)} %copy-done.2) | copy-start | bytes 196612
  56.7 68.7 %copy-start.5 = (f32[4,2048]{1,0:T(4,128)S(1)}, f32[4,2048]{1,0:T(4,128)}, u32[]{:S(2)}) copy-start(f32[4,2048]{1,0:T(4,128)} %copy-done.4) | copy-start | bytes 98308
  56.7 68.7 %copy-start.7 = (f32[2,2048]{1,0:T(2,128)S(1)}, f32[2,2048]{1,0:T(2,128)}, u32[]{:S(2)}) copy-start(f32[2,2048]{1,0:T(2,128)} %copy-done.6) | copy-start | bytes 49156
  56.7 68.7 %copy-start.9 = (f32[2,2048]{1,0:T(2,128)S(1)}, f32[2,2048]{1,0:T(2,128)}, u32[]{:S(2)}) copy-start(f32[2,2048]{1,0:T(2,128)} %copy-done.8) | copy-start | bytes 49156
  73.9 0.7 copy-start.10
  74.6 3.1 %collective-permute-start.5 = (f32[16,48]{1,0:T(8,128)S(1)}, f32[16,48]{1,0:T(8,128)S(1)}, u32[]{:S(2)}, u32[]{:S(2)}) collective-permute-start(f32[16,48]{1,0:T(8,128)S(1)} %convolution_multiply_fusion.1), channel_id=1, source_target_pairs={{0,1},{1,0},{2,3},{3,2},{4,5},{5,4},{6,7},{7,6},{8,9},{9,8},{10,11... | collective-permute-start | bytes 9224 | tf_op jit(solution)/shard_map/ppermute | solution.py:23
  77.7 7.0 %collective-permute-start.6 = (f32[16,48]{1,0:T(8,128)S(1)}, f32[16,48]{1,0:T(8,128)S(1)}, u32[]{:S(2)}, u32[]{:S(2)}) collective-permute-start(f32[16,48]{1,0:T(8,128)S(1)} %add.96), channel_id=1, source_target_pairs={{0,2},{2,0},{1,3},{3,1},{4,6},{6,4},{5,7},{7,5},{8,10},{10,8},{9,1... | collective-permute-start | bytes 9224 | tf_op jit(solution)/shard_map/ppermute | solution.py:23
  84.7 5.5 %collective-permute-start.7 = (f32[16,48]{1,0:T(8,128)S(1)}, f32[16,48]{1,0:T(8,128)S(1)}, u32[]{:S(2)}, u32[]{:S(2)}) collective-permute-start(f32[16,48]{1,0:T(8,128)S(1)} %add.97), channel_id=1, source_target_pairs={{0,4},{4,0},{8,12},{12,8},{16,20},{20,16},{24,28},{28,24},{1,5},{5... | collective-permute-start | bytes 9224 | tf_op jit(solution)/shard_map/ppermute | solution.py:23
  90.3 6.4 %collective-permute-start.8 = (f32[16,48]{1,0:T(8,128)S(1)}, f32[16,48]{1,0:T(8,128)S(1)}, u32[]{:S(2)}, u32[]{:S(2)}) collective-permute-start(f32[16,48]{1,0:T(8,128)S(1)} %add.98), channel_id=1, source_target_pairs={{0,8},{4,12},{8,0},{12,4},{16,24},{20,28},{24,16},{28,20},{1,9},{5... | collective-permute-start | bytes 9224 | tf_op jit(solution)/shard_map/ppermute | solution.py:23
  96.7 9.4 %collective-permute-start.9 = (f32[16,48]{1,0:T(8,128)S(1)}, f32[16,48]{1,0:T(8,128)S(1)}, u32[]{:S(2)}, u32[]{:S(2)}) collective-permute-start(f32[16,48]{1,0:T(8,128)S(1)} %add.99), channel_id=1, source_target_pairs={{0,16},{4,20},{8,24},{12,28},{16,0},{20,4},{24,8},{28,12},{1,17},{... | collective-permute-start | bytes 9224 | tf_op jit(solution)/shard_map/ppermute | solution.py:23
  106.2 6.6 %collective-permute-start.10 = (f32[16,48]{1,0:T(8,128)S(1)}, f32[16,48]{1,0:T(8,128)S(1)}, u32[]{:S(2)}, u32[]{:S(2)}) collective-permute-start(f32[16,48]{1,0:T(8,128)S(1)} %add.100), channel_id=1, source_target_pairs={{0,32},{32,0},{1,33},{33,1},{2,34},{34,2},{3,35},{35,3},{4,36},{36... | collective-permute-start | bytes 9224 | tf_op jit(solution)/shard_map/ppermute | solution.py:23
  112.8 5.6 %collective-permute-start.11 = (f32[16,48]{1,0:T(8,128)S(1)}, f32[16,48]{1,0:T(8,128)S(1)}, u32[]{:S(2)}, u32[]{:S(2)}) collective-permute-start(f32[16,48]{1,0:T(8,128)S(1)} %add.101), channel_id=1, source_target_pairs={{0,64},{64,0},{128,192},{192,128},{256,320},{320,256},{384,448},{4... | collective-permute-start | bytes 9224 | tf_op jit(solution)/shard_map/ppermute | solution.py:23
  118.4 14.2 %collective-permute-start.12 = (f32[16,48]{1,0:T(8,128)S(1)}, f32[16,48]{1,0:T(8,128)S(1)}, u32[]{:S(2)}, u32[]{:S(2)}) collective-permute-start(f32[16,48]{1,0:T(8,128)S(1)} %add.102), channel_id=1, source_target_pairs={{0,128},{64,192},{128,0},{192,64},{256,384},{320,448},{384,256},{4... | collective-permute-start | bytes 9224 | tf_op jit(solution)/shard_map/ppermute | solution.py:23
  132.6 10.4 %collective-permute-start.13 = (f32[16,48]{1,0:T(8,128)S(1)}, f32[16,48]{1,0:T(8,128)S(1)}, u32[]{:S(2)}, u32[]{:S(2)}) collective-permute-start(f32[16,48]{1,0:T(8,128)S(1)} %add.103), channel_id=1, source_target_pairs={{0,256},{64,320},{128,384},{192,448},{256,0},{320,64},{384,128},{4... | collective-permute-start | bytes 9224 | tf_op jit(solution)/shard_map/ppermute | solution.py:23

commit v4 on v3

--- a/solution.py
+++ b/solution.py
@@ -30,9 +30,15 @@
     for axis, size in rounds:
         step = 1
         while step < size:
-            got = lax.ppermute(jnp.concatenate([total, blocks], axis=0), axis, partners(size, step))
-            total = total + got[:count]
-            blocks = jnp.concatenate([blocks, got[count:]], axis=0)
+            high = lax.reduce_precision(total, exponent_bits=8, mantissa_bits=7)
+            low = total - high
+            message = jnp.concatenate(
+                [high.astype(jnp.bfloat16), low.astype(jnp.bfloat16), blocks], axis=0
+            )
+            got = lax.ppermute(message, axis, partners(size, step))
+            sent = got[:count].astype(jnp.float32) + got[count : 2 * count].astype(jnp.float32)
+            total = total + sent
+            blocks = jnp.concatenate([blocks, got[2 * count :]], axis=0)
             step *= 2
     return total, blocks
 
@@ -52,7 +58,7 @@
     block = spin_dens.shape[0]
     slot = -(-block // width) * width
     lane = weight.shape[1]
-    own_dens = jnp.pad(spin_dens.astype(jnp.float32), ((0, slot - block), (0, 0))).reshape(-1, lane)
+    own_dens = jnp.pad(spin_dens, ((0, slot - block), (0, 0))).reshape(-1, lane)
     weight, every_dens = butterfly_sum_gather(weight, own_dens, AO_ROUNDS)
     every_dens = every_dens.reshape(-1, cells)
 
@@ -71,7 +77,7 @@
     live = jnp.minimum(bra, ket)
     cell = jnp.arange(cells, dtype=jnp.int32)
     inside = (cell[None, :] // width < live[:, None]) & (cell[None, :] % width < live[:, None])
-    dens = jnp.where(inside, picked, jnp.float32(0.0))
+    dens = jnp.where(inside, picked.astype(jnp.float32), jnp.float32(0.0))
     return jnp.einsum(
         "uxt,stu->xs", field.reshape(width, 3, width), dens.reshape(-1, width, width), precision=HIGH
     ) / width

time: 145 us -> 136 us (0.938)
  waiting for transfers between devices: 56.9 us -> 45.6 us
  other arithmetic: 3.22 us -> 5.21 us
    ppermute x5, waiting for transfers between devices: 39.1 us -> 29.2 us  [butterfly_sum_gather(): got = lax.ppermute(message, axis, partners(size, step))]
    ppermute x9, waiting for transfers between devices: 17.8 us -> 16.4 us  [butterfly_sum(): value = value + lax.ppermute(value, axis, partners(size, step))]
    concatenate x3 -> x4, local copies, waits for them, and re-layouts: 9.76 us -> 8.59 us  [the longest x3 7.63 us: butterfly_sum_gather(): jnp.concatenate([high.astype(jnp.bfloat16), low.astype(jnp.bfloat16), blo...]
  transfers between devices with their start and end apart: 14 -> 14, of which waited for: 13 -> 13; matrix products, arithmetic and copies ran while one was open for 11% -> 10% of each run, Pallas kernels for 0% -> 0%
where the time goes in v4:
time: 136 us; the launch traced here: 135 us
  starting transfers between devices  58.6 us (43%)
  waiting for transfers between devices  45.6 us (34%)
  local copies, waits for them, and re-layouts  17.7 us (13%)
  matrix products  8.01 us (6%)
  other arithmetic  5.21 us (4%)
    ppermute x9, starting transfers between devices, butterfly_sum(): value = value + lax.ppermute(value, axis, partners(size, step))  37.4 us
    ppermute x5, waiting for transfers between devices, butterfly_sum_gather(): got = lax.ppermute(message, axis, partners(size, step))  29.2 us
    ppermute x5, starting transfers between devices, butterfly_sum_gather(): got = lax.ppermute(message, axis, partners(size, step))  21.2 us
    ppermute x9, waiting for transfers between devices, butterfly_sum(): value = value + lax.ppermute(value, axis, partners(size, step))  16.4 us
    concatenate x3, local copies, waits for them, and re-layouts, butterfly_sum_gather(): jnp.concatenate([high.astype(jnp.bfloat16), low.astype(jnp.bfloat16), blo...  7.63 us
  transfers between devices with their start and end apart: 14, of which 13 were waited for; matrix products, arithmetic and copies ran while one was open for 10% of the time, Pallas kernels for 0%

profile of v4, /device:TPU:6, one launch (start us, length us, event | category | flops | bytes accessed | tf_op | source)
XLA Modules:
  0.0 135.4 jit_solution(13562199542701484795)
XLA Ops:
  0.9 2.0 %fusion.5 = f32[16,128,16]{1,0,2:T(8,128)S(1)} fusion(bf16[128,16,256]{2,1,0:T(8,128)(2,1)} %param.13, bf16[16,256]{1,0:T(8,128)(2,1)} %param.14), kind=kOutput, calls=%fused_computation.14 | convolution fusion | flops 16777216 | bytes 1187840 | tf_op jit(solution)/shard_map/un,ptn->upt/dot_general | solution.py:53
  4.9 1.9 %collective-permute-start = (bf16[34,2048]{1,0:T(8,128)(2,1)S(1)}, bf16[34,2048]{1,0:T(8,128)(2,1)S(1)}, u32[]{:S(2)}, u32[]{:S(2)}) collective-permute-start(bf16[34,2048]{1,0:T(8,128)(2,1)S(1)} %pad_maximum_fusion), channel_id=1, source_target_pairs={{0,1},{1,0},{2,3},{3,2},{4,5},{5,4},{6,7},{7,6},{8,9},{9,8},{10,11... | collective-permute-start | bytes 417800 | tf_op jit(solution)/shard_map/ppermute | solution.py:38
  6.8 1.4 %collective-permute-done = bf16[34,2048]{1,0:T(8,128)(2,1)S(1)} collective-permute-done((bf16[34,2048]{1,0:T(8,128)(2,1)S(1)}, bf16[34,2048]{1,0:T(8,128)(2,1)S(1)}, u32[]{:S(2)}, u32[]{:S(2)}) %collective-permute-start) | collective-permute-done | bytes 139296 | tf_op jit(solution)/shard_map/ppermute | solution.py:38
  8.3 3.3 %collective-permute-start.1 = (bf16[36,2048]{1,0:T(8,128)(2,1)S(1)}, bf16[36,2048]{1,0:T(8,128)(2,1)S(1)}, u32[]{:S(2)}, u32[]{:S(2)}) collective-permute-start(bf16[36,2048]{1,0:T(8,128)(2,1)S(1)} %pad_maximum_fusion.1), channel_id=1, source_target_pairs={{0,2},{2,0},{1,3},{3,1},{4,6},{6,4},{5,7},{7,5},{8,10},{10,8},{9,1... | collective-permute-start | bytes 442376 | tf_op jit(solution)/shard_map/ppermute | solution.py:38
  11.7 6.3 %collective-permute-done.1 = bf16[36,2048]{1,0:T(8,128)(2,1)S(1)} collective-permute-done((bf16[36,2048]{1,0:T(8,128)(2,1)S(1)}, bf16[36,2048]{1,0:T(8,128)(2,1)S(1)}, u32[]{:S(2)}, u32[]{:S(2)}) %collective-permute-start.1) | collective-permute-done | bytes 147488 | tf_op jit(solution)/shard_map/ppermute | solution.py:38
  18.7 1.9 %concatenate.32 = bf16[40,2048]{1,0:T(8,128)(2,1)} concatenate(bf16[16,2048]{1,0:T(8,128)(2,1)S(1)} %get-tuple-element.18, bf16[16,2048]{1,0:T(8,128)(2,1)S(1)} %get-tuple-element.17, bf16[2,2048]{1,0:T(2,128)(2,1)S(1)} %reshape.124, bf16[2,2048]{1,0:T(2,128)(2,1)S(1)} %slice.80, bf16[4,2048]{1,0:T(4,128)(2,1)S(1)} %slice.83), dimensions={0} | concatenate | bytes 327680 | tf_op jit(solution)/shard_map/concatenate | solution.py:35
  20.6 3.6 %collective-permute-start.2 = (bf16[40,2048]{1,0:T(8,128)(2,1)}, bf16[40,2048]{1,0:T(8,128)(2,1)S(1)}, u32[]{:S(2)}, u32[]{:S(2)}) collective-permute-start(bf16[40,2048]{1,0:T(8,128)(2,1)} %concatenate.32), channel_id=1, source_target_pairs={{0,4},{4,0},{8,12},{12,8},{16,20},{20,16},{24,28},{28,24},{1,5},{5... | collective-permute-start | bytes 491528 | tf_op jit(solution)/shard_map/ppermute | solution.py:38
  24.2 4.0 %collective-permute-done.2 = bf16[40,2048]{1,0:T(8,128)(2,1)S(1)} collective-permute-done((bf16[40,2048]{1,0:T(8,128)(2,1)}, bf16[40,2048]{1,0:T(8,128)(2,1)S(1)}, u32[]{:S(2)}, u32[]{:S(2)}) %collective-permute-start.2) | collective-permute-done | bytes 163872 | tf_op jit(solution)/shard_map/ppermute | solution.py:38
  29.1 2.5 %concatenate.33 = bf16[48,2048]{1,0:T(8,128)(2,1)} concatenate(bf16[16,2048]{1,0:T(8,128)(2,1)S(1)} %reduce-precision_convert_fusion.1, bf16[16,2048]{1,0:T(8,128)(2,1)S(1)} %get-tuple-element.11, bf16[2,2048]{1,0:T(2,128)(2,1)S(1)} %reshape.124, bf16[2,2048]{1,0:T(2,128)(2,1)S(1)} %slice.80, bf16[4,2048]{1,0:T(4,128)(2,1)S(1)} %slice.83, bf16[8,2048]{1,0:T(8,128)(2,1)S(1)} %slice.86), dimensions={0} | concatenate | bytes 393216 | tf_op jit(solution)/shard_map/concatenate | solution.py:35
  31.7 4.6 %collective-permute-start.3 = (bf16[48,2048]{1,0:T(8,128)(2,1)}, bf16[48,2048]{1,0:T(8,128)(2,1)S(1)}, u32[]{:S(2)}, u32[]{:S(2)}) collective-permute-start(bf16[48,2048]{1,0:T(8,128)(2,1)} %concatenate.33), channel_id=1, source_target_pairs={{0,8},{4,12},{8,0},{12,4},{16,24},{20,28},{24,16},{28,20},{1,9},{5... | collective-permute-start | bytes 589832 | tf_op jit(solution)/shard_map/ppermute | solution.py:38
  36.3 7.9 %collective-permute-done.3 = bf16[48,2048]{1,0:T(8,128)(2,1)S(1)} collective-permute-done((bf16[48,2048]{1,0:T(8,128)(2,1)}, bf16[48,2048]{1,0:T(8,128)(2,1)S(1)}, u32[]{:S(2)}, u32[]{:S(2)}) %collective-permute-start.3) | collective-permute-done | bytes 196640 | tf_op jit(solution)/shard_map/ppermute | solution.py:38
  45.0 3.2 %concatenate.34 = bf16[64,2048]{1,0:T(8,128)(2,1)} concatenate(bf16[16,2048]{1,0:T(8,128)(2,1)S(1)} %get-tuple-element.16, bf16[16,2048]{1,0:T(8,128)(2,1)S(1)} %get-tuple-element.15, bf16[2,2048]{1,0:T(2,128)(2,1)S(1)} %reshape.124, bf16[2,2048]{1,0:T(2,128)(2,1)S(1)} %slice.80, bf16[4,2048]{1,0:T(4,128)(2,1)S(1)} %slice.83, bf16[8,2048]{1,0:T(8,128)(2,1)S(1)} %slice.86, ...), dimensions={0} | concatenate | bytes 524288 | tf_op jit(solution)/shard_map/concatenate | solution.py:35
  48.1 7.7 %collective-permute-start.4 = (bf16[64,2048]{1,0:T(8,128)(2,1)}, bf16[64,2048]{1,0:T(8,128)(2,1)S(1)}, u32[]{:S(2)}, u32[]{:S(2)}) collective-permute-start(bf16[64,2048]{1,0:T(8,128)(2,1)} %concatenate.34), channel_id=1, source_target_pairs={{0,16},{4,20},{8,24},{12,28},{16,0},{20,4},{24,8},{28,12},{1,17},{... | collective-permute-start | bytes 786440 | tf_op jit(solution)/shard_map/ppermute | solution.py:38
  55.9 1.8 %fusion = f32[16,128,48]{1,0,2:T(8,128)S(1)} fusion(bf16[128,48,256]{2,1,0:T(8,128)(2,1)S(1)} %bitcast.37, bf16[16,256]{1,0:T(8,128)(2,1)S(1)} %copy-done.5), kind=kOutput, calls=%fused_computation.5 | convolution fusion | flops 50331648 | bytes 3547136 | tf_op jit(solution)/shard_map/vn,pkn->vpk/dot_general | solution.py:65
  58.3 9.6 %collective-permute-done.4 = bf16[64,2048]{1,0:T(8,128)(2,1)S(1)} collective-permute-done((bf16[64,2048]{1,0:T(8,128)(2,1)}, bf16[64,2048]{1,0:T(8,128)(2,1)S(1)}, u32[]{:S(2)}, u32[]{:S(2)}) %collective-permute-start.4) | collective-permute-done | bytes 262176 | tf_op jit(solution)/shard_map/ppermute | solution.py:38
  67.9 1.5 %convolution_multiply_fusion.1 = f32[16,48]{1,0:T(8,128)S(1)} fusion(f32[6,8,16,128]{3,2,1,0:T(8,128)S(1)} %bitcast.38, bf16[64,2048]{1,0:T(8,128)(2,1)S(1)} %collective-permute-done.4, f32[16,2048]{1,0:T(8,128)S(1)} %get-tuple-element.12, bf16[48,2048]{1,0:T(8,128)(2,1)} %copy-done.3), kind=kOutput, calls=%fused_computation.10 | convolution fusion | flops 19137280 | bytes 789504 | tf_op jit(solution)/shard_map/dot_general | solution.py:68
  69.3 1.9 %collective-permute-start.5 = (f32[16,48]{1,0:T(8,128)S(1)}, f32[16,48]{1,0:T(8,128)S(1)}, u32[]{:S(2)}, u32[]{:S(2)}) collective-permute-start(f32[16,48]{1,0:T(8,128)S(1)} %convolution_multiply_fusion.1), channel_id=1, source_target_pairs={{0,1},{1,0},{2,3},{3,2},{4,5},{5,4},{6,7},{7,6},{8,9},{9,8},{10,11... | collective-permute-start | bytes 9224 | tf_op jit(solution)/shard_map/ppermute | solution.py:23
  72.4 3.3 %collective-permute-start.6 = (f32[16,48]{1,0:T(8,128)S(1)}, f32[16,48]{1,0:T(8,128)S(1)}, u32[]{:S(2)}, u32[]{:S(2)}) collective-permute-start(f32[16,48]{1,0:T(8,128)S(1)} %add.116), channel_id=1, source_target_pairs={{0,2},{2,0},{1,3},{3,1},{4,6},{6,4},{5,7},{7,5},{8,10},{10,8},{9,1... | collective-permute-start | bytes 9224 | tf_op jit(solution)/shard_map/ppermute | solution.py:23
  77.1 2.4 %collective-permute-done.6 = f32[16,48]{1,0:T(8,128)S(1)} collective-permute-done((f32[16,48]{1,0:T(8,128)S(1)}, f32[16,48]{1,0:T(8,128)S(1)}, u32[]{:S(2)}, u32[]{:S(2)}) %collective-permute-start.6) | collective-permute-done | bytes 3104 | tf_op jit(solution)/shard_map/ppermute | solution.py:23
  79.5 1.9 %collective-permute-start.7 = (f32[16,48]{1,0:T(8,128)S(1)}, f32[16,48]{1,0:T(8,128)S(1)}, u32[]{:S(2)}, u32[]{:S(2)}) collective-permute-start(f32[16,48]{1,0:T(8,128)S(1)} %add.117), channel_id=1, source_target_pairs={{0,4},{4,0},{8,12},{12,8},{16,20},{20,16},{24,28},{28,24},{1,5},{5... | collective-permute-start | bytes 9224 | tf_op jit(solution)/shard_map/ppermute | solution.py:23
  82.0 3.0 %collective-permute-done.7 = f32[16,48]{1,0:T(8,128)S(1)} collective-permute-done((f32[16,48]{1,0:T(8,128)S(1)}, f32[16,48]{1,0:T(8,128)S(1)}, u32[]{:S(2)}, u32[]{:S(2)}) %collective-permute-start.7) | collective-permute-done | bytes 3104 | tf_op jit(solution)/shard_map/ppermute | solution.py:23
  85.0 3.2 %collective-permute-start.8 = (f32[16,48]{1,0:T(8,128)S(1)}, f32[16,48]{1,0:T(8,128)S(1)}, u32[]{:S(2)}, u32[]{:S(2)}) collective-permute-start(f32[16,48]{1,0:T(8,128)S(1)} %add.118), channel_id=1, source_target_pairs={{0,8},{4,12},{8,0},{12,4},{16,24},{20,28},{24,16},{28,20},{1,9},{5... | collective-permute-start | bytes 9224 | tf_op jit(solution)/shard_map/ppermute | solution.py:23
  89.6 1.9 %collective-permute-done.8 = f32[16,48]{1,0:T(8,128)S(1)} collective-permute-done((f32[16,48]{1,0:T(8,128)S(1)}, f32[16,48]{1,0:T(8,128)S(1)}, u32[]{:S(2)}, u32[]{:S(2)}) %collective-permute-start.8) | collective-permute-done | bytes 3104 | tf_op jit(solution)/shard_map/ppermute | solution.py:23
  91.4 4.9 %collective-permute-start.9 = (f32[16,48]{1,0:T(8,128)S(1)}, f32[16,48]{1,0:T(8,128)S(1)}, u32[]{:S(2)}, u32[]{:S(2)}) collective-permute-start(f32[16,48]{1,0:T(8,128)S(1)} %add.119), channel_id=1, source_target_pairs={{0,16},{4,20},{8,24},{12,28},{16,0},{20,4},{24,8},{28,12},{1,17},{... | collective-permute-start | bytes 9224 | tf_op jit(solution)/shard_map/ppermute | solution.py:23
  96.3 4.5 %collective-permute-done.9 = f32[16,48]{1,0:T(8,128)S(1)} collective-permute-done((f32[16,48]{1,0:T(8,128)S(1)}, f32[16,48]{1,0:T(8,128)S(1)}, u32[]{:S(2)}, u32[]{:S(2)}) %collective-permute-start.9) | collective-permute-done | bytes 3104 | tf_op jit(solution)/shard_map/ppermute | solution.py:23
  100.9 5.0 %collective-permute-start.10 = (f32[16,48]{1,0:T(8,128)S(1)}, f32[16,48]{1,0:T(8,128)S(1)}, u32[]{:S(2)}, u32[]{:S(2)}) collective-permute-start(f32[16,48]{1,0:T(8,128)S(1)} %add.120), channel_id=1, source_target_pairs={{0,32},{32,0},{1,33},{33,1},{2,34},{34,2},{3,35},{35,3},{4,36},{36... | collective-permute-start | bytes 9224 | tf_op jit(solution)/shard_map/ppermute | solution.py:23
  107.5 3.1 %collective-permute-start.11 = (f32[16,48]{1,0:T(8,128)S(1)}, f32[16,48]{1,0:T(8,128)S(1)}, u32[]{:S(2)}, u32[]{:S(2)}) collective-permute-start(f32[16,48]{1,0:T(8,128)S(1)} %add.121), channel_id=1, source_target_pairs={{0,64},{64,0},{128,192},{192,128},{256,320},{320,256},{384,448},{4... | collective-permute-start | bytes 9224 | tf_op jit(solution)/shard_map/ppermute | solution.py:23
  111.3 1.8 %collective-permute-done.11 = f32[16,48]{1,0:T(8,128)S(1)} collective-permute-done((f32[16,48]{1,0:T(8,128)S(1)}, f32[16,48]{1,0:T(8,128)S(1)}, u32[]{:S(2)}, u32[]{:S(2)}) %collective-permute-start.11) | collective-permute-done | bytes 3104 | tf_op jit(solution)/shard_map/ppermute | solution.py:23
  113.1 5.3 %collective-permute-start.12 = (f32[16,48]{1,0:T(8,128)S(1)}, f32[16,48]{1,0:T(8,128)}, u32[]{:S(2)}, u32[]{:S(2)}) collective-permute-start(f32[16,48]{1,0:T(8,128)S(1)} %add.122), channel_id=1, source_target_pairs={{0,128},{64,192},{128,0},{192,64},{256,384},{320,448},{384,256},{4... | collective-permute-start | bytes 9224 | tf_op jit(solution)/shard_map/ppermute | solution.py:23
  118.4 1.6 %slice.92 = bf16[32,2048]{1,0:T(8,128)(2,1)} slice(bf16[64,2048]{1,0:T(8,128)(2,1)} %copy-done.4), slice={[32:64], [0:2048]} | slice | bytes 262144 | tf_op jit(solution)/shard_map/slice | solution.py:41
  121.8 1.5 %gather_fusion = bf16[10,256]{1,0:T(8,128)(2,1)S(1)} fusion(bf16[512,256]{1,0:T(8,128)(2,1)} %reshape.128, s32[1024]{0:T(1024)S(1)} %pad_clamp_fusion), kind=kCustom, calls=%fused_computation.4 | custom fusion | bytes 10280 | tf_op jit(solution)/shard_map/jit(_take)/gather | solution.py:73
  124.1 8.7 %collective-permute-start.13 = (f32[16,48]{1,0:T(8,128)S(1)}, f32[16,48]{1,0:T(8,128)S(1)}, u32[]{:S(2)}, u32[]{:S(2)}) collective-permute-start(f32[16,48]{1,0:T(8,128)S(1)} %add.123), channel_id=1, source_target_pairs={{0,256},{64,320},{128,384},{192,448},{256,0},{320,64},{384,128},{4... | collective-permute-start | bytes 9224 | tf_op jit(solution)/shard_map/ppermute | solution.py:23
  (67 shorter events, 17.8 us)
Async XLA Ops:
  0.0 55.9 %copy-start = (bf16[128,3,16,256]{3,2,1,0:T(8,128)(2,1)S(1)}, bf16[128,3,16,256]{3,2,1,0:T(8,128)(2,1)}, u32[]{:S(2)}) copy-start(bf16[128,3,16,256]{3,2,1,0:T(8,128)(2,1)} %param.12) | copy-start | bytes 9437188
  0.0 55.9 %copy-start.5 = (bf16[16,256]{1,0:T(8,128)(2,1)S(1)}, bf16[16,256]{1,0:T(8,128)(2,1)}, u32[]{:S(2)}) copy-start(bf16[16,256]{1,0:T(8,128)(2,1)} %param.14) | copy-start | bytes 24580
  4.9 3.3 %collective-permute-start = (bf16[34,2048]{1,0:T(8,128)(2,1)S(1)}, bf16[34,2048]{1,0:T(8,128)(2,1)S(1)}, u32[]{:S(2)}, u32[]{:S(2)}) collective-permute-start(bf16[34,2048]{1,0:T(8,128)(2,1)S(1)} %pad_maximum_fusion), channel_id=1, source_target_pairs={{0,1},{1,0},{2,3},{3,2},{4,5},{5,4},{6,7},{7,6},{8,9},{9,8},{10,11... | collective-permute-start | bytes 417800 | tf_op jit(solution)/shard_map/ppermute | solution.py:38
  8.3 9.6 %collective-permute-start.1 = (bf16[36,2048]{1,0:T(8,128)(2,1)S(1)}, bf16[36,2048]{1,0:T(8,128)(2,1)S(1)}, u32[]{:S(2)}, u32[]{:S(2)}) collective-permute-start(bf16[36,2048]{1,0:T(8,128)(2,1)S(1)} %pad_maximum_fusion.1), channel_id=1, source_target_pairs={{0,2},{2,0},{1,3},{3,1},{4,6},{6,4},{5,7},{7,5},{8,10},{10,8},{9,1... | collective-permute-start | bytes 442376 | tf_op jit(solution)/shard_map/ppermute | solution.py:38
  18.0 0.7 copy-start.2
  20.6 50.7 %copy-start.6 = (s32[320,2]{0,1:T(2,128)S(1)}, s32[320,2]{0,1:T(2,128)}, u32[]{:S(2)}) copy-start(s32[320,2]{0,1:T(2,128)} %param.17) | copy-start | bytes 7684
  20.6 7.6 %collective-permute-start.2 = (bf16[40,2048]{1,0:T(8,128)(2,1)}, bf16[40,2048]{1,0:T(8,128)(2,1)S(1)}, u32[]{:S(2)}, u32[]{:S(2)}) collective-permute-start(bf16[40,2048]{1,0:T(8,128)(2,1)} %concatenate.32), channel_id=1, source_target_pairs={{0,4},{4,0},{8,12},{12,8},{16,20},{20,16},{24,28},{28,24},{1,5},{5... | collective-permute-start | bytes 491528 | tf_op jit(solution)/shard_map/ppermute | solution.py:38
  31.7 56.5 %copy-start.1 = (s32[24]{0:T(128)S(1)}, s32[24]{0:T(128)}, u32[]{:S(2)}) copy-start(s32[24]{0:T(128)} %param.19) | copy-start | bytes 292
  31.7 12.6 %collective-permute-start.3 = (bf16[48,2048]{1,0:T(8,128)(2,1)}, bf16[48,2048]{1,0:T(8,128)(2,1)S(1)}, u32[]{:S(2)}, u32[]{:S(2)}) collective-permute-start(bf16[48,2048]{1,0:T(8,128)(2,1)} %concatenate.33), channel_id=1, source_target_pairs={{0,8},{4,12},{8,0},{12,4},{16,24},{20,28},{24,16},{28,20},{1,9},{5... | collective-permute-start | bytes 589832 | tf_op jit(solution)/shard_map/ppermute | solution.py:38
  44.3 0.7 copy-start.3
  48.1 19.7 %collective-permute-start.4 = (bf16[64,2048]{1,0:T(8,128)(2,1)}, bf16[64,2048]{1,0:T(8,128)(2,1)S(1)}, u32[]{:S(2)}, u32[]{:S(2)}) collective-permute-start(bf16[64,2048]{1,0:T(8,128)(2,1)} %concatenate.34), channel_id=1, source_target_pairs={{0,16},{4,20},{8,24},{12,28},{16,0},{20,4},{24,8},{28,12},{1,17},{... | collective-permute-start | bytes 786440 | tf_op jit(solution)/shard_map/ppermute | solution.py:38
  55.9 50.1 %copy-start.7 = (s32[10]{0:T(128)S(1)}, s32[10]{0:T(128)}, u32[]{:S(2)}) copy-start(s32[10]{0:T(128)} %param.18) | copy-start | bytes 124
  67.9 1.5 %copy-start.4 = (bf16[64,2048]{1,0:T(8,128)(2,1)}, bf16[64,2048]{1,0:T(8,128)(2,1)S(1)}, u32[]{:S(2)}) copy-start(bf16[64,2048]{1,0:T(8,128)(2,1)S(1)} %collective-permute-done.4) | copy-start | bytes 786436
  69.3 3.1 %collective-permute-start.5 = (f32[16,48]{1,0:T(8,128)S(1)}, f32[16,48]{1,0:T(8,128)S(1)}, u32[]{:S(2)}, u32[]{:S(2)}) collective-permute-start(f32[16,48]{1,0:T(8,128)S(1)} %convolution_multiply_fusion.1), channel_id=1, source_target_pairs={{0,1},{1,0},{2,3},{3,2},{4,5},{5,4},{6,7},{7,6},{8,9},{9,8},{10,11... | collective-permute-start | bytes 9224 | tf_op jit(solution)/shard_map/ppermute | solution.py:23
  72.4 7.0 %collective-permute-start.6 = (f32[16,48]{1,0:T(8,128)S(1)}, f32[16,48]{1,0:T(8,128)S(1)}, u32[]{:S(2)}, u32[]{:S(2)}) collective-permute-start(f32[16,48]{1,0:T(8,128)S(1)} %add.116), channel_id=1, source_target_pairs={{0,2},{2,0},{1,3},{3,1},{4,6},{6,4},{5,7},{7,5},{8,10},{10,8},{9,1... | collective-permute-start | bytes 9224 | tf_op jit(solution)/shard_map/ppermute | solution.py:23
  79.5 5.5 %collective-permute-start.7 = (f32[16,48]{1,0:T(8,128)S(1)}, f32[16,48]{1,0:T(8,128)S(1)}, u32[]{:S(2)}, u32[]{:S(2)}) collective-permute-start(f32[16,48]{1,0:T(8,128)S(1)} %add.117), channel_id=1, source_target_pairs={{0,4},{4,0},{8,12},{12,8},{16,20},{20,16},{24,28},{28,24},{1,5},{5... | collective-permute-start | bytes 9224 | tf_op jit(solution)/shard_map/ppermute | solution.py:23
  85.0 6.4 %collective-permute-start.8 = (f32[16,48]{1,0:T(8,128)S(1)}, f32[16,48]{1,0:T(8,128)S(1)}, u32[]{:S(2)}, u32[]{:S(2)}) collective-permute-start(f32[16,48]{1,0:T(8,128)S(1)} %add.118), channel_id=1, source_target_pairs={{0,8},{4,12},{8,0},{12,4},{16,24},{20,28},{24,16},{28,20},{1,9},{5... | collective-permute-start | bytes 9224 | tf_op jit(solution)/shard_map/ppermute | solution.py:23
  91.4 9.4 %collective-permute-start.9 = (f32[16,48]{1,0:T(8,128)S(1)}, f32[16,48]{1,0:T(8,128)S(1)}, u32[]{:S(2)}, u32[]{:S(2)}) collective-permute-start(f32[16,48]{1,0:T(8,128)S(1)} %add.119), channel_id=1, source_target_pairs={{0,16},{4,20},{8,24},{12,28},{16,0},{20,4},{24,8},{28,12},{1,17},{... | collective-permute-start | bytes 9224 | tf_op jit(solution)/shard_map/ppermute | solution.py:23
  100.9 6.7 %collective-permute-start.10 = (f32[16,48]{1,0:T(8,128)S(1)}, f32[16,48]{1,0:T(8,128)S(1)}, u32[]{:S(2)}, u32[]{:S(2)}) collective-permute-start(f32[16,48]{1,0:T(8,128)S(1)} %add.120), channel_id=1, source_target_pairs={{0,32},{32,0},{1,33},{33,1},{2,34},{34,2},{3,35},{35,3},{4,36},{36... | collective-permute-start | bytes 9224 | tf_op jit(solution)/shard_map/ppermute | solution.py:23
  107.5 5.6 %collective-permute-start.11 = (f32[16,48]{1,0:T(8,128)S(1)}, f32[16,48]{1,0:T(8,128)S(1)}, u32[]{:S(2)}, u32[]{:S(2)}) collective-permute-start(f32[16,48]{1,0:T(8,128)S(1)} %add.121), channel_id=1, source_target_pairs={{0,64},{64,0},{128,192},{192,128},{256,320},{320,256},{384,448},{4... | collective-permute-start | bytes 9224 | tf_op jit(solution)/shard_map/ppermute | solution.py:23
  113.1 10.3 %collective-permute-start.12 = (f32[16,48]{1,0:T(8,128)S(1)}, f32[16,48]{1,0:T(8,128)}, u32[]{:S(2)}, u32[]{:S(2)}) collective-permute-start(f32[16,48]{1,0:T(8,128)S(1)} %add.122), channel_id=1, source_target_pairs={{0,128},{64,192},{128,0},{192,64},{256,384},{320,448},{384,256},{4... | collective-permute-start | bytes 9224 | tf_op jit(solution)/shard_map/ppermute | solution.py:23
  124.1 10.4 %collective-permute-start.13 = (f32[16,48]{1,0:T(8,128)S(1)}, f32[16,48]{1,0:T(8,128)S(1)}, u32[]{:S(2)}, u32[]{:S(2)}) collective-permute-start(f32[16,48]{1,0:T(8,128)S(1)} %add.123), channel_id=1, source_target_pairs={{0,256},{64,320},{128,384},{192,448},{256,0},{320,64},{384,128},{4... | collective-permute-start | bytes 9224 | tf_op jit(solution)/shard_map/ppermute | solution.py:23

commit v5 on v2

--- a/solution.py
+++ b/solution.py
@@ -25,16 +25,21 @@
     return value
 
 
-def butterfly_sum_gather(total, blocks, rounds):
+def halve_and_gather(rows, blocks, rounds):
     for axis, size in rounds:
         step = 1
         while step < size:
             pairs = partners(size, step)
-            total = total + lax.ppermute(total, axis, pairs)
+            half = rows.shape[0] // 2
+            upper = (lax.axis_index(axis) // step) % 2 == 1
+            low, high = rows[:half], rows[half:]
+            keep = jnp.where(upper, high, low)
+            give = jnp.where(upper, low, high)
+            rows = keep + lax.ppermute(give, axis, pairs)
             blocks = jnp.concatenate([blocks, lax.ppermute(blocks, axis, pairs)], axis=0)
-            total, blocks = lax.optimization_barrier((total, blocks))
+            rows, blocks = lax.optimization_barrier((rows, blocks))
             step *= 2
-    return total, blocks
+    return rows, blocks
 
 
 def on_device(soc_ints, cou_ints, coef_t, active_rdm, spin_dens, pair_list, owner_map, state_count):
@@ -44,18 +49,22 @@
     n_aux = lax.axis_size("z") * lax.axis_size("xlo")
     scale = 1.0 / (8.0 * jnp.sqrt(jnp.float32(rows * n_aux)))
 
-    cou_part = jnp.einsum("un,ptn->upt", coef_t, cou_ints, preferred_element_type=jnp.float32)
-    fitted = jnp.einsum("upt,tu->p", cou_part, active_rdm, precision=HIGH)
-    folded = jnp.einsum("upw,vw->uvp", cou_part, active_rdm, precision=HIGH)
+    soc_part = jnp.einsum(
+        "pkn,vn->pkv", soc_ints.reshape(rows, 3 * width, -1), coef_t, preferred_element_type=jnp.float32
+    ).reshape(rows, 3 * cells)
+    cou_part = jnp.einsum("ptn,un->ptu", cou_ints, coef_t, preferred_element_type=jnp.float32)
+    fitted = jnp.einsum("ptu,tu->p", cou_part, active_rdm, precision=HIGH)
+    folded = jnp.einsum("vw,pwu->pvu", active_rdm, cou_part, precision=HIGH)
     eye = jnp.eye(width, dtype=jnp.float32)
-    weight = (eye[:, :, None] * fitted[None, None, :] - 1.5 * folded).reshape(width, width * rows)
-    weight, every_dens = butterfly_sum_gather(weight, spin_dens, AO_ROUNDS)
+    weight = (fitted[:, None, None] * eye[None] - 1.5 * folded).reshape(rows, cells)
 
-    soc_part = jnp.einsum(
-        "vn,pkn->vpk", coef_t, soc_ints.reshape(rows, 3 * width, -1), preferred_element_type=jnp.float32
-    ).reshape(width * rows, 3 * width)
-    field_part = jnp.dot(weight, soc_part, precision=HIGH) * scale
-    field = butterfly_sum(field_part, AO_ROUNDS + AUX_ROUNDS)
+    joined = jnp.concatenate([soc_part, weight], axis=1)
+    share, every_dens = halve_and_gather(joined, spin_dens, AO_ROUNDS)
+    count = share.shape[0]
+    soc_mo = share[:, : 3 * cells].reshape(count, 3, width, width)
+    weight = share[:, 3 * cells :].reshape(count, width, width)
+    field_part = jnp.einsum("pxtv,pvu->xtu", soc_mo, weight, precision=HIGH) * scale
+    field = butterfly_sum(field_part.reshape(3, cells), AO_ROUNDS + AUX_ROUNDS)
 
     me = (lax.axis_index("y") * 4 + lax.axis_index("xhi") * 2 + lax.axis_index("core")).astype(jnp.int32)
     block = spin_dens.shape[0]
@@ -68,9 +77,7 @@
     cell = jnp.arange(cells, dtype=jnp.int32)
     inside = (cell[None, :] // width < live[:, None]) & (cell[None, :] % width < live[:, None])
     dens = jnp.where(inside, picked.astype(jnp.float32), jnp.float32(0.0))
-    return jnp.einsum(
-        "uxt,stu->xs", field.reshape(width, 3, width), dens.reshape(-1, width, width), precision=HIGH
-    ) / width
+    return jnp.dot(field, dens.T, precision=HIGH) / width
 
 
 def solution(mesh):

time: 126 us -> 137 us (1.087)
  the two profiles are of different devices: /device:TPU:16 before, /device:TPU:24 now
where the time goes in v5:
time: 137 us; the launch traced here: 136 us
  starting transfers between devices  69 us (50%)
  waiting for transfers between devices  39.7 us (29%)
  local copies, waits for them, and re-layouts  11 us (8%)
  matrix products  9.05 us (7%)
  other arithmetic  6.53 us (5%)
    ppermute x9, starting transfers between devices, butterfly_sum(): value = value + lax.ppermute(value, axis, partners(size, step))  34.9 us
    ppermute x5, starting transfers between devices, halve_and_gather(): rows = keep + lax.ppermute(give, axis, pairs)  20.7 us
    ppermute x9, waiting for transfers between devices, butterfly_sum(): value = value + lax.ppermute(value, axis, partners(size, step))  20.3 us
    ppermute x5, waiting for transfers between devices, halve_and_gather(): lax.ppermute(blocks, axis, pairs)  16.8 us
    ppermute x5, starting transfers between devices, halve_and_gather(): lax.ppermute(blocks, axis, pairs)  13.4 us
    dot_general x1, matrix products, on_device(): jnp.einsum('ptn,un->ptu', cou_ints, coef_t, preferred_element_type=jnp.fl...  2.77 us
  transfers between devices with their start and end apart: 19, of which 14 were waited for; matrix products, arithmetic and copies ran while one was open for 5% of the time, Pallas kernels for 0%

profile of v5, /device:TPU:24, one launch (start us, length us, event | category | flops | bytes accessed | tf_op | source)
XLA Modules:
  0.0 135.9 jit_solution(4160747421611954945)
XLA Ops:
  0.0 2.8 %fusion.12 = f32[128,16,16]{2,1,0:T(8,128)} fusion(bf16[128,16,256]{2,1,0:T(8,128)(2,1)} %param.13, bf16[16,256]{1,0:T(8,128)(2,1)} %param.14), kind=kOutput, calls=%fused_computation.39 | convolution fusion | flops 16777216 | bytes 1187840 | tf_op jit(solution)/shard_map/ptn,un->ptu/dot_general | solution.py:55
  2.8 1.6 %copy.15 = f32[128,16,16]{0,1,2:T(8,128)S(1)} copy(f32[128,16,16]{2,1,0:T(8,128)} %fusion.12) | data formatting | bytes 262144 | tf_op jit(solution)/shard_map/ptn,un->ptu/dot_general | solution.py:55
  4.5 2.4 %convolution_bitcast_fusion.1 = f32[128]{0:T(128)S(1)} fusion(f32[16,16,1]{1,2,0:T(1,128)S(1)} %bitcast.34, f32[128,16,16]{2,1,0:T(8,128)} %fusion.12), kind=kOutput, calls=%fused_computation.11 | convolution fusion | flops 393216 | bytes 132608 | tf_op jit(solution)/shard_map/ptu,tu->p/dot_general | solution.py:56
  7.9 2.6 %fusion.14 = f32[128,48,16]{1,2,0:T(8,128)} fusion(bf16[128,48,256]{2,1,0:T(8,128)(2,1)S(1)} %bitcast.31, bf16[16,256]{1,0:T(8,128)(2,1)S(1)} %copy-done.3), kind=kOutput, calls=%fused_computation.41 | convolution fusion | flops 50331648 | bytes 3547136 | tf_op jit(solution)/shard_map/pkn,vn->pkv/dot_general | solution.py:52
  10.5 2.4 %copy.21 = f32[128,48,16]{0,2,1:T(8,128)} copy(f32[128,48,16]{1,2,0:T(8,128)} %fusion.14) | data formatting | bytes 786432 | tf_op jit(solution)/shard_map/pkn,vn->pkv/dot_general | solution.py:52
  15.8 1.9 %collective-permute-start = (f32[64,1024]{1,0:T(8,128)}, f32[64,1024]{1,0:T(8,128)}, u32[]{:S(2)}, u32[]{:S(2)}) collective-permute-start(f32[64,1024]{1,0:T(8,128)} %broadcast_select_fusion), channel_id=1, source_target_pairs={{0,1},{1,0},{2,3},{3,2},{4,5},{5,4},{6,7},{7,6},{8,9},{9,8},{10,11... | collective-permute-start | bytes 786440 | tf_op jit(solution)/shard_map/ppermute | solution.py:38
  17.7 2.4 %collective-permute-start.1 = (bf16[10,256]{1,0:T(8,128)(2,1)S(1)}, bf16[10,256]{1,0:T(8,128)(2,1)}, u32[]{:S(2)}, u32[]{:S(2)}) collective-permute-start(bf16[10,256]{1,0:T(8,128)(2,1)S(1)} %copy-done.5), channel_id=1, source_target_pairs={{0,1},{1,0},{2,3},{3,2},{4,5},{5,4},{6,7},{7,6},{8,9},{9,8},{10,11... | collective-permute-start | bytes 15368 | tf_op jit(solution)/shard_map/ppermute | solution.py:39
  23.5 4.9 %collective-permute-start.2 = (f32[32,1024]{1,0:T(8,128)S(1)}, f32[32,1024]{1,0:T(8,128)S(1)}, u32[]{:S(2)}, u32[]{:S(2)}) collective-permute-start(f32[32,1024]{1,0:T(8,128)S(1)} %slice_select_fusion), channel_id=1, source_target_pairs={{0,2},{2,0},{1,3},{3,1},{4,6},{6,4},{5,7},{7,5},{8,10},{10,8},{9,1... | collective-permute-start | bytes 393224 | tf_op jit(solution)/shard_map/ppermute | solution.py:38
  28.5 2.4 %collective-permute-start.3 = (bf16[20,256]{1,0:T(8,128)(2,1)S(1)}, bf16[20,256]{1,0:T(8,128)(2,1)S(1)}, u32[]{:S(2)}, u32[]{:S(2)}) collective-permute-start(bf16[20,256]{1,0:T(8,128)(2,1)S(1)} %pad_maximum_fusion.5), channel_id=1, source_target_pairs={{0,2},{2,0},{1,3},{3,1},{4,6},{6,4},{5,7},{7,5},{8,10},{10,8},{9,1... | collective-permute-start | bytes 30728 | tf_op jit(solution)/shard_map/ppermute | solution.py:39
  30.9 4.6 %collective-permute-done.3 = bf16[20,256]{1,0:T(8,128)(2,1)S(1)} collective-permute-done((bf16[20,256]{1,0:T(8,128)(2,1)S(1)}, bf16[20,256]{1,0:T(8,128)(2,1)S(1)}, u32[]{:S(2)}, u32[]{:S(2)}) %collective-permute-start.3) | collective-permute-done | bytes 10272 | tf_op jit(solution)/shard_map/ppermute | solution.py:39
  36.6 2.4 %collective-permute-start.5 = (bf16[40,256]{1,0:T(8,128)(2,1)S(1)}, bf16[40,256]{1,0:T(8,128)(2,1)S(1)}, u32[]{:S(2)}, u32[]{:S(2)}) collective-permute-start(bf16[40,256]{1,0:T(8,128)(2,1)S(1)} %pad_maximum_fusion.4), channel_id=1, source_target_pairs={{0,4},{4,0},{8,12},{12,8},{16,20},{20,16},{24,28},{28,24},{1,5},{5... | collective-permute-start | bytes 61448 | tf_op jit(solution)/shard_map/ppermute | solution.py:39
  39.0 3.5 %collective-permute-start.4 = (f32[16,1024]{1,0:T(8,128)S(1)}, f32[16,1024]{1,0:T(8,128)S(1)}, u32[]{:S(2)}, u32[]{:S(2)}) collective-permute-start(f32[16,1024]{1,0:T(8,128)S(1)} %slice_select_fusion.1), channel_id=1, source_target_pairs={{0,4},{4,0},{8,12},{12,8},{16,20},{20,16},{24,28},{28,24},{1,5},{5... | collective-permute-start | bytes 196616 | tf_op jit(solution)/shard_map/ppermute | solution.py:38
  42.5 2.6 %collective-permute-done.4 = f32[16,1024]{1,0:T(8,128)S(1)} collective-permute-done((f32[16,1024]{1,0:T(8,128)S(1)}, f32[16,1024]{1,0:T(8,128)S(1)}, u32[]{:S(2)}, u32[]{:S(2)}) %collective-permute-start.4) | collective-permute-done | bytes 65568 | tf_op jit(solution)/shard_map/ppermute | solution.py:38
  45.2 5.0 %collective-permute-start.6 = (f32[8,1024]{1,0:T(8,128)S(1)}, f32[8,1024]{1,0:T(8,128)S(1)}, u32[]{:S(2)}, u32[]{:S(2)}) collective-permute-start(f32[8,1024]{1,0:T(8,128)S(1)} %slice_select_fusion.2), channel_id=1, source_target_pairs={{0,8},{4,12},{8,0},{12,4},{16,24},{20,28},{24,16},{28,20},{1,9},{5... | collective-permute-start | bytes 98312 | tf_op jit(solution)/shard_map/ppermute | solution.py:38
  50.1 1.9 %collective-permute-start.7 = (bf16[80,256]{1,0:T(8,128)(2,1)S(1)}, bf16[80,256]{1,0:T(8,128)(2,1)S(1)}, u32[]{:S(2)}, u32[]{:S(2)}) collective-permute-start(bf16[80,256]{1,0:T(8,128)(2,1)S(1)} %pad_maximum_fusion.3), channel_id=1, source_target_pairs={{0,8},{4,12},{8,0},{12,4},{16,24},{20,28},{24,16},{28,20},{1,9},{5... | collective-permute-start | bytes 122888 | tf_op jit(solution)/shard_map/ppermute | solution.py:39
  52.1 4.8 %collective-permute-done.7 = bf16[80,256]{1,0:T(8,128)(2,1)S(1)} collective-permute-done((bf16[80,256]{1,0:T(8,128)(2,1)S(1)}, bf16[80,256]{1,0:T(8,128)(2,1)S(1)}, u32[]{:S(2)}, u32[]{:S(2)}) %collective-permute-start.7) | collective-permute-done | bytes 40992 | tf_op jit(solution)/shard_map/ppermute | solution.py:39
  57.0 5.5 %collective-permute-start.8 = (f32[4,1024]{1,0:T(4,128)S(1)}, f32[4,1024]{1,0:T(4,128)S(1)}, u32[]{:S(2)}, u32[]{:S(2)}) collective-permute-start(f32[4,1024]{1,0:T(4,128)S(1)} %slice_select_fusion.3), channel_id=1, source_target_pairs={{0,16},{4,20},{8,24},{12,28},{16,0},{20,4},{24,8},{28,12},{1,17},{... | collective-permute-start | bytes 49160 | tf_op jit(solution)/shard_map/ppermute | solution.py:38
  62.4 4.3 %collective-permute-start.9 = (bf16[160,256]{1,0:T(8,128)(2,1)S(1)}, bf16[160,256]{1,0:T(8,128)(2,1)S(1)}, u32[]{:S(2)}, u32[]{:S(2)}) collective-permute-start(bf16[160,256]{1,0:T(8,128)(2,1)S(1)} %pad_maximum_fusion.2), channel_id=1, source_target_pairs={{0,16},{4,20},{8,24},{12,28},{16,0},{20,4},{24,8},{28,12},{1,17},{... | collective-permute-start | bytes 245768 | tf_op jit(solution)/shard_map/ppermute | solution.py:39
  66.8 6.4 %collective-permute-done.9 = bf16[160,256]{1,0:T(8,128)(2,1)S(1)} collective-permute-done((bf16[160,256]{1,0:T(8,128)(2,1)S(1)}, bf16[160,256]{1,0:T(8,128)(2,1)S(1)}, u32[]{:S(2)}, u32[]{:S(2)}) %collective-permute-start.9) | collective-permute-done | bytes 81952 | tf_op jit(solution)/shard_map/ppermute | solution.py:39
  73.7 1.9 %collective-permute-start.10 = (f32[3,256]{1,0:T(4,128)S(1)}, f32[3,256]{1,0:T(4,128)S(1)}, u32[]{:S(2)}, u32[]{:S(2)}) collective-permute-start(f32[3,256]{1,0:T(4,128)S(1)} %reshape.100), channel_id=1, source_target_pairs={{0,1},{1,0},{2,3},{3,2},{4,5},{5,4},{6,7},{7,6},{8,9},{9,8},{10,11... | collective-permute-start | bytes 9224 | tf_op jit(solution)/shard_map/ppermute | solution.py:23
  76.7 2.0 %collective-permute-start.11 = (f32[3,256]{1,0:T(4,128)S(1)}, f32[3,256]{1,0:T(4,128)S(1)}, u32[]{:S(2)}, u32[]{:S(2)}) collective-permute-start(f32[3,256]{1,0:T(4,128)S(1)} %add.116), channel_id=1, source_target_pairs={{0,2},{2,0},{1,3},{3,1},{4,6},{6,4},{5,7},{7,5},{8,10},{10,8},{9,1... | collective-permute-start | bytes 9224 | tf_op jit(solution)/shard_map/ppermute | solution.py:23
  79.5 4.2 %collective-permute-done.11 = f32[3,256]{1,0:T(4,128)S(1)} collective-permute-done((f32[3,256]{1,0:T(4,128)S(1)}, f32[3,256]{1,0:T(4,128)S(1)}, u32[]{:S(2)}, u32[]{:S(2)}) %collective-permute-start.11) | collective-permute-done | bytes 3104 | tf_op jit(solution)/shard_map/ppermute | solution.py:23
  83.7 2.7 %collective-permute-start.12 = (f32[3,256]{1,0:T(4,128)S(1)}, f32[3,256]{1,0:T(4,128)S(1)}, u32[]{:S(2)}, u32[]{:S(2)}) collective-permute-start(f32[3,256]{1,0:T(4,128)S(1)} %add.117), channel_id=1, source_target_pairs={{0,4},{4,0},{8,12},{12,8},{16,20},{20,16},{24,28},{28,24},{1,5},{5... | collective-permute-start | bytes 9224 | tf_op jit(solution)/shard_map/ppermute | solution.py:23
  89.2 1.9 %collective-permute-start.13 = (f32[3,256]{1,0:T(4,128)S(1)}, f32[3,256]{1,0:T(4,128)S(1)}, u32[]{:S(2)}, u32[]{:S(2)}) collective-permute-start(f32[3,256]{1,0:T(4,128)S(1)} %add.118), channel_id=1, source_target_pairs={{0,8},{4,12},{8,0},{12,4},{16,24},{20,28},{24,16},{28,20},{1,9},{5... | collective-permute-start | bytes 9224 | tf_op jit(solution)/shard_map/ppermute | solution.py:23
  91.8 3.8 %collective-permute-done.13 = f32[3,256]{1,0:T(4,128)S(1)} collective-permute-done((f32[3,256]{1,0:T(4,128)S(1)}, f32[3,256]{1,0:T(4,128)S(1)}, u32[]{:S(2)}, u32[]{:S(2)}) %collective-permute-start.13) | collective-permute-done | bytes 3104 | tf_op jit(solution)/shard_map/ppermute | solution.py:23
  95.6 3.8 %collective-permute-start.14 = (f32[3,256]{1,0:T(4,128)S(1)}, f32[3,256]{1,0:T(4,128)S(1)}, u32[]{:S(2)}, u32[]{:S(2)}) collective-permute-start(f32[3,256]{1,0:T(4,128)S(1)} %add.119), channel_id=1, source_target_pairs={{0,16},{4,20},{8,24},{12,28},{16,0},{20,4},{24,8},{28,12},{1,17},{... | collective-permute-start | bytes 9224 | tf_op jit(solution)/shard_map/ppermute | solution.py:23
  100.8 4.2 %collective-permute-done.14 = f32[3,256]{1,0:T(4,128)S(1)} collective-permute-done((f32[3,256]{1,0:T(4,128)S(1)}, f32[3,256]{1,0:T(4,128)S(1)}, u32[]{:S(2)}, u32[]{:S(2)}) %collective-permute-start.14) | collective-permute-done | bytes 3104 | tf_op jit(solution)/shard_map/ppermute | solution.py:23
  105.0 2.7 %collective-permute-start.15 = (f32[3,256]{1,0:T(4,128)S(1)}, f32[3,256]{1,0:T(4,128)S(1)}, u32[]{:S(2)}, u32[]{:S(2)}) collective-permute-start(f32[3,256]{1,0:T(4,128)S(1)} %add.120), channel_id=1, source_target_pairs={{0,32},{32,0},{1,33},{33,1},{2,34},{34,2},{3,35},{35,3},{4,36},{36... | collective-permute-start | bytes 9224 | tf_op jit(solution)/shard_map/ppermute | solution.py:23
  107.8 2.7 %collective-permute-done.15 = f32[3,256]{1,0:T(4,128)S(1)} collective-permute-done((f32[3,256]{1,0:T(4,128)S(1)}, f32[3,256]{1,0:T(4,128)S(1)}, u32[]{:S(2)}, u32[]{:S(2)}) %collective-permute-start.15) | collective-permute-done | bytes 3104 | tf_op jit(solution)/shard_map/ppermute | solution.py:23
  110.5 4.5 %collective-permute-start.16 = (f32[3,256]{1,0:T(4,128)S(1)}, f32[3,256]{1,0:T(4,128)S(1)}, u32[]{:S(2)}, u32[]{:S(2)}) collective-permute-start(f32[3,256]{1,0:T(4,128)S(1)} %add.121), channel_id=1, source_target_pairs={{0,64},{64,0},{128,192},{192,128},{256,320},{320,256},{384,448},{4... | collective-permute-start | bytes 9224 | tf_op jit(solution)/shard_map/ppermute | solution.py:23
  116.6 6.1 %collective-permute-start.17 = (f32[3,256]{1,0:T(4,128)S(1)}, f32[3,256]{1,0:T(4,128)S(1)}, u32[]{:S(2)}, u32[]{:S(2)}) collective-permute-start(f32[3,256]{1,0:T(4,128)S(1)} %add.122), channel_id=1, source_target_pairs={{0,128},{64,192},{128,0},{192,64},{256,384},{320,448},{384,256},{4... | collective-permute-start | bytes 9224 | tf_op jit(solution)/shard_map/ppermute | solution.py:23
  124.3 9.3 %collective-permute-start.18 = (f32[3,256]{1,0:T(4,128)S(1)}, f32[3,256]{1,0:T(4,128)S(1)}, u32[]{:S(2)}, u32[]{:S(2)}) collective-permute-start(f32[3,256]{1,0:T(4,128)S(1)} %add.123), channel_id=1, source_target_pairs={{0,256},{64,320},{128,384},{192,448},{256,0},{320,64},{384,128},{4... | collective-permute-start | bytes 9224 | tf_op jit(solution)/shard_map/ppermute | solution.py:23
  (72 shorter events, 21.1 us)
Async XLA Ops:
  0.0 7.9 %copy-start = (bf16[128,3,16,256]{3,2,1,0:T(8,128)(2,1)S(1)}, bf16[128,3,16,256]{3,2,1,0:T(8,128)(2,1)}, u32[]{:S(2)}) copy-start(bf16[128,3,16,256]{3,2,1,0:T(8,128)(2,1)} %param.12) | copy-start | bytes 9437188
  0.0 7.9 %copy-start.3 = (bf16[16,256]{1,0:T(8,128)(2,1)S(1)}, bf16[16,256]{1,0:T(8,128)(2,1)}, u32[]{:S(2)}) copy-start(bf16[16,256]{1,0:T(8,128)(2,1)} %param.14) | copy-start | bytes 24580
  0.0 4.4 %copy-start.4 = (f32[16,16]{1,0:T(8,128)S(1)}, f32[16,16]{1,0:T(8,128)}, u32[]{:S(2)}) copy-start(f32[16,16]{1,0:T(8,128)} %param.15) | copy-start | bytes 3076
  7.9 9.8 %copy-start.5 = (bf16[10,256]{1,0:T(8,128)(2,1)S(1)}, bf16[10,256]{1,0:T(8,128)(2,1)}, u32[]{:S(2)}) copy-start(bf16[10,256]{1,0:T(8,128)(2,1)} %param.16) | copy-start | bytes 15364
  13.0 86.5 %copy-start.1 = (s32[24]{0:T(128)S(1)}, s32[24]{0:T(128)}, u32[]{:S(2)}) copy-start(s32[24]{0:T(128)} %param.19) | copy-start | bytes 292
  15.8 6.0 %collective-permute-start = (f32[64,1024]{1,0:T(8,128)}, f32[64,1024]{1,0:T(8,128)}, u32[]{:S(2)}, u32[]{:S(2)}) collective-permute-start(f32[64,1024]{1,0:T(8,128)} %broadcast_select_fusion), channel_id=1, source_target_pairs={{0,1},{1,0},{2,3},{3,2},{4,5},{5,4},{6,7},{7,6},{8,9},{9,8},{10,11... | collective-permute-start | bytes 786440 | tf_op jit(solution)/shard_map/ppermute | solution.py:38
  17.7 3.4 %collective-permute-start.1 = (bf16[10,256]{1,0:T(8,128)(2,1)S(1)}, bf16[10,256]{1,0:T(8,128)(2,1)}, u32[]{:S(2)}, u32[]{:S(2)}) collective-permute-start(bf16[10,256]{1,0:T(8,128)(2,1)S(1)} %copy-done.5), channel_id=1, source_target_pairs={{0,1},{1,0},{2,3},{3,2},{4,5},{5,4},{6,7},{7,6},{8,9},{9,8},{10,11... | collective-permute-start | bytes 15368 | tf_op jit(solution)/shard_map/ppermute | solution.py:39
  22.8 0.7 copy-start.2
  23.5 12.0 %collective-permute-start.2 = (f32[32,1024]{1,0:T(8,128)S(1)}, f32[32,1024]{1,0:T(8,128)S(1)}, u32[]{:S(2)}, u32[]{:S(2)}) collective-permute-start(f32[32,1024]{1,0:T(8,128)S(1)} %slice_select_fusion), channel_id=1, source_target_pairs={{0,2},{2,0},{1,3},{3,1},{4,6},{6,4},{5,7},{7,5},{8,10},{10,8},{9,1... | collective-permute-start | bytes 393224 | tf_op jit(solution)/shard_map/ppermute | solution.py:38
  28.5 7.1 %collective-permute-start.3 = (bf16[20,256]{1,0:T(8,128)(2,1)S(1)}, bf16[20,256]{1,0:T(8,128)(2,1)S(1)}, u32[]{:S(2)}, u32[]{:S(2)}) collective-permute-start(bf16[20,256]{1,0:T(8,128)(2,1)S(1)} %pad_maximum_fusion.5), channel_id=1, source_target_pairs={{0,2},{2,0},{1,3},{3,1},{4,6},{6,4},{5,7},{7,5},{8,10},{10,8},{9,1... | collective-permute-start | bytes 30728 | tf_op jit(solution)/shard_map/ppermute | solution.py:39
  36.6 5.9 %collective-permute-start.5 = (bf16[40,256]{1,0:T(8,128)(2,1)S(1)}, bf16[40,256]{1,0:T(8,128)(2,1)S(1)}, u32[]{:S(2)}, u32[]{:S(2)}) collective-permute-start(bf16[40,256]{1,0:T(8,128)(2,1)S(1)} %pad_maximum_fusion.4), channel_id=1, source_target_pairs={{0,4},{4,0},{8,12},{12,8},{16,20},{20,16},{24,28},{28,24},{1,5},{5... | collective-permute-start | bytes 61448 | tf_op jit(solution)/shard_map/ppermute | solution.py:39
  39.0 6.2 %collective-permute-start.4 = (f32[16,1024]{1,0:T(8,128)S(1)}, f32[16,1024]{1,0:T(8,128)S(1)}, u32[]{:S(2)}, u32[]{:S(2)}) collective-permute-start(f32[16,1024]{1,0:T(8,128)S(1)} %slice_select_fusion.1), channel_id=1, source_target_pairs={{0,4},{4,0},{8,12},{12,8},{16,20},{20,16},{24,28},{28,24},{1,5},{5... | collective-permute-start | bytes 196616 | tf_op jit(solution)/shard_map/ppermute | solution.py:38
  45.2 6.9 %collective-permute-start.6 = (f32[8,1024]{1,0:T(8,128)S(1)}, f32[8,1024]{1,0:T(8,128)S(1)}, u32[]{:S(2)}, u32[]{:S(2)}) collective-permute-start(f32[8,1024]{1,0:T(8,128)S(1)} %slice_select_fusion.2), channel_id=1, source_target_pairs={{0,8},{4,12},{8,0},{12,4},{16,24},{20,28},{24,16},{28,20},{1,9},{5... | collective-permute-start | bytes 98312 | tf_op jit(solution)/shard_map/ppermute | solution.py:38
  50.1 6.8 %collective-permute-start.7 = (bf16[80,256]{1,0:T(8,128)(2,1)S(1)}, bf16[80,256]{1,0:T(8,128)(2,1)S(1)}, u32[]{:S(2)}, u32[]{:S(2)}) collective-permute-start(bf16[80,256]{1,0:T(8,128)(2,1)S(1)} %pad_maximum_fusion.3), channel_id=1, source_target_pairs={{0,8},{4,12},{8,0},{12,4},{16,24},{20,28},{24,16},{28,20},{1,9},{5... | collective-permute-start | bytes 122888 | tf_op jit(solution)/shard_map/ppermute | solution.py:39
  57.0 9.8 %collective-permute-start.8 = (f32[4,1024]{1,0:T(4,128)S(1)}, f32[4,1024]{1,0:T(4,128)S(1)}, u32[]{:S(2)}, u32[]{:S(2)}) collective-permute-start(f32[4,1024]{1,0:T(4,128)S(1)} %slice_select_fusion.3), channel_id=1, source_target_pairs={{0,16},{4,20},{8,24},{12,28},{16,0},{20,4},{24,8},{28,12},{1,17},{... | collective-permute-start | bytes 49160 | tf_op jit(solution)/shard_map/ppermute | solution.py:38
  62.4 10.7 %collective-permute-start.9 = (bf16[160,256]{1,0:T(8,128)(2,1)S(1)}, bf16[160,256]{1,0:T(8,128)(2,1)S(1)}, u32[]{:S(2)}, u32[]{:S(2)}) collective-permute-start(bf16[160,256]{1,0:T(8,128)(2,1)S(1)} %pad_maximum_fusion.2), channel_id=1, source_target_pairs={{0,16},{4,20},{8,24},{12,28},{16,0},{20,4},{24,8},{28,12},{1,17},{... | collective-permute-start | bytes 245768 | tf_op jit(solution)/shard_map/ppermute | solution.py:39
  73.7 3.1 %collective-permute-start.10 = (f32[3,256]{1,0:T(4,128)S(1)}, f32[3,256]{1,0:T(4,128)S(1)}, u32[]{:S(2)}, u32[]{:S(2)}) collective-permute-start(f32[3,256]{1,0:T(4,128)S(1)} %reshape.100), channel_id=1, source_target_pairs={{0,1},{1,0},{2,3},{3,2},{4,5},{5,4},{6,7},{7,6},{8,9},{9,8},{10,11... | collective-permute-start | bytes 9224 | tf_op jit(solution)/shard_map/ppermute | solution.py:23
  76.7 7.0 %collective-permute-start.11 = (f32[3,256]{1,0:T(4,128)S(1)}, f32[3,256]{1,0:T(4,128)S(1)}, u32[]{:S(2)}, u32[]{:S(2)}) collective-permute-start(f32[3,256]{1,0:T(4,128)S(1)} %add.116), channel_id=1, source_target_pairs={{0,2},{2,0},{1,3},{3,1},{4,6},{6,4},{5,7},{7,5},{8,10},{10,8},{9,1... | collective-permute-start | bytes 9224 | tf_op jit(solution)/shard_map/ppermute | solution.py:23
  83.7 5.5 %collective-permute-start.12 = (f32[3,256]{1,0:T(4,128)S(1)}, f32[3,256]{1,0:T(4,128)S(1)}, u32[]{:S(2)}, u32[]{:S(2)}) collective-permute-start(f32[3,256]{1,0:T(4,128)S(1)} %add.117), channel_id=1, source_target_pairs={{0,4},{4,0},{8,12},{12,8},{16,20},{20,16},{24,28},{28,24},{1,5},{5... | collective-permute-start | bytes 9224 | tf_op jit(solution)/shard_map/ppermute | solution.py:23
  89.2 6.4 %collective-permute-start.13 = (f32[3,256]{1,0:T(4,128)S(1)}, f32[3,256]{1,0:T(4,128)S(1)}, u32[]{:S(2)}, u32[]{:S(2)}) collective-permute-start(f32[3,256]{1,0:T(4,128)S(1)} %add.118), channel_id=1, source_target_pairs={{0,8},{4,12},{8,0},{12,4},{16,24},{20,28},{24,16},{28,20},{1,9},{5... | collective-permute-start | bytes 9224 | tf_op jit(solution)/shard_map/ppermute | solution.py:23
  95.6 9.4 %collective-permute-start.14 = (f32[3,256]{1,0:T(4,128)S(1)}, f32[3,256]{1,0:T(4,128)S(1)}, u32[]{:S(2)}, u32[]{:S(2)}) collective-permute-start(f32[3,256]{1,0:T(4,128)S(1)} %add.119), channel_id=1, source_target_pairs={{0,16},{4,20},{8,24},{12,28},{16,0},{20,4},{24,8},{28,12},{1,17},{... | collective-permute-start | bytes 9224 | tf_op jit(solution)/shard_map/ppermute | solution.py:23
  105.0 5.5 %collective-permute-start.15 = (f32[3,256]{1,0:T(4,128)S(1)}, f32[3,256]{1,0:T(4,128)S(1)}, u32[]{:S(2)}, u32[]{:S(2)}) collective-permute-start(f32[3,256]{1,0:T(4,128)S(1)} %add.120), channel_id=1, source_target_pairs={{0,32},{32,0},{1,33},{33,1},{2,34},{34,2},{3,35},{35,3},{4,36},{36... | collective-permute-start | bytes 9224 | tf_op jit(solution)/shard_map/ppermute | solution.py:23
  110.5 6.1 %collective-permute-start.16 = (f32[3,256]{1,0:T(4,128)S(1)}, f32[3,256]{1,0:T(4,128)S(1)}, u32[]{:S(2)}, u32[]{:S(2)}) collective-permute-start(f32[3,256]{1,0:T(4,128)S(1)} %add.121), channel_id=1, source_target_pairs={{0,64},{64,0},{128,192},{192,128},{256,320},{320,256},{384,448},{4... | collective-permute-start | bytes 9224 | tf_op jit(solution)/shard_map/ppermute | solution.py:23
  116.6 7.7 %collective-permute-start.17 = (f32[3,256]{1,0:T(4,128)S(1)}, f32[3,256]{1,0:T(4,128)S(1)}, u32[]{:S(2)}, u32[]{:S(2)}) collective-permute-start(f32[3,256]{1,0:T(4,128)S(1)} %add.122), channel_id=1, source_target_pairs={{0,128},{64,192},{128,0},{192,64},{256,384},{320,448},{384,256},{4... | collective-permute-start | bytes 9224 | tf_op jit(solution)/shard_map/ppermute | solution.py:23
  124.3 10.9 %collective-permute-start.18 = (f32[3,256]{1,0:T(4,128)S(1)}, f32[3,256]{1,0:T(4,128)S(1)}, u32[]{:S(2)}, u32[]{:S(2)}) collective-permute-start(f32[3,256]{1,0:T(4,128)S(1)} %add.123), channel_id=1, source_target_pairs={{0,256},{64,320},{128,384},{192,448},{256,0},{320,64},{384,128},{4... | collective-permute-start | bytes 9224 | tf_op jit(solution)/shard_map/ppermute | solution.py:23

commit v6 on v2

--- a/solution.py
+++ b/solution.py
@@ -12,8 +12,15 @@
 AUX_ROUNDS = (("xlo", 2), ("z", 8))
 
 
+def ring_label(position, size):
+    if size < 8:
+        return position
+    return position if position < size // 2 else 3 * size // 2 - 1 - position
+
+
 def partners(size, step):
-    return [(i, i ^ step) for i in range(size)]
+    labels = [ring_label(i, size) for i in range(size)]
+    return [(i, labels.index(labels[i] ^ step)) for i in range(size)]
 
 
 def butterfly_sum(value, rounds):
@@ -57,9 +64,13 @@
     field_part = jnp.dot(weight, soc_part, precision=HIGH) * scale
     field = butterfly_sum(field_part, AO_ROUNDS + AUX_ROUNDS)
 
+    def labelled(device):
+        y = device // 4
+        return jnp.where(y < 4, y, 11 - y) * 4 + device % 4
+
     me = (lax.axis_index("y") * 4 + lax.axis_index("xhi") * 2 + lax.axis_index("core")).astype(jnp.int32)
     block = spin_dens.shape[0]
-    where = (owner_map // block) ^ me
+    where = labelled(owner_map // block) ^ labelled(me)
     picked = jnp.take(every_dens, where * block + owner_map % block, axis=0)
 
     bra = jnp.take(state_count, jnp.take(pair_list[:, 0], owner_map, axis=0), axis=0)

time: 126 us -> 123 us (0.976)
  the two profiles are of different devices: /device:TPU:16 before, /device:TPU:8 now
where the time goes in v6:
time: 123 us; the launch traced here: 122 us
  starting transfers between devices  70.5 us (57%)
  waiting for transfers between devices  39.3 us (32%)
  matrix products  7.1 us (6%)
  local copies, waits for them, and re-layouts  3.63 us (3%)
    ppermute x9, starting transfers between devices, butterfly_sum(): value = value + lax.ppermute(value, axis, partners(size, step))  36.2 us
    ppermute x9, waiting for transfers between devices, butterfly_sum(): value = value + lax.ppermute(value, axis, partners(size, step))  20.7 us
    ppermute x5, starting transfers between devices, butterfly_sum_gather(): lax.ppermute(blocks, axis, pairs)  17.2 us
    ppermute x5, starting transfers between devices, butterfly_sum_gather(): total = total + lax.ppermute(total, axis, pairs)  17.1 us
    ppermute x5, waiting for transfers between devices, butterfly_sum_gather(): total = total + lax.ppermute(total, axis, pairs)  11.8 us
    ppermute x5, waiting for transfers between devices, butterfly_sum_gather(): lax.ppermute(blocks, axis, pairs)  6.76 us
  transfers between devices with their start and end apart: 19, of which 15 were waited for; matrix products, arithmetic and copies ran while one was open for 5% of the time, Pallas kernels for 0%

profile of v6, /device:TPU:8, one launch (start us, length us, event | category | flops | bytes accessed | tf_op | source)
XLA Modules:
  0.0 122.0 jit_solution(590482613600642937)
XLA Ops:
  0.0 2.1 %fusion.5 = f32[16,128,16]{1,0,2:T(8,128)S(1)} fusion(bf16[128,16,256]{2,1,0:T(8,128)(2,1)} %param.13, bf16[16,256]{1,0:T(8,128)(2,1)} %param.14), kind=kOutput, calls=%fused_computation.14 | convolution fusion | flops 16777216 | bytes 1187840 | tf_op jit(solution)/shard_map/un,ptn->upt/dot_general | solution.py:54
  4.1 1.9 %collective-permute-start = (f32[16,2048]{1,0:T(8,128)S(1)}, f32[16,2048]{1,0:T(8,128)S(1)}, u32[]{:S(2)}, u32[]{:S(2)}) collective-permute-start(f32[16,2048]{1,0:T(8,128)S(1)} %bitcast.42), channel_id=1, source_target_pairs={{0,1},{1,0},{2,3},{3,2},{4,5},{5,4},{6,7},{7,6},{8,9},{9,8},{10,11... | collective-permute-start | bytes 393224 | tf_op jit(solution)/shard_map/ppermute | solution.py:40
  6.0 2.4 %collective-permute-start.1 = (bf16[10,256]{1,0:T(8,128)(2,1)}, bf16[10,256]{1,0:T(8,128)(2,1)S(1)}, u32[]{:S(2)}, u32[]{:S(2)}) collective-permute-start(bf16[10,256]{1,0:T(8,128)(2,1)} %param.16), channel_id=1, source_target_pairs={{0,1},{1,0},{2,3},{3,2},{4,5},{5,4},{6,7},{7,6},{8,9},{9,8},{10,11... | collective-permute-start | bytes 15368 | tf_op jit(solution)/shard_map/ppermute | solution.py:41
  10.2 4.9 %collective-permute-start.2 = (f32[16,2048]{1,0:T(8,128)S(1)}, f32[16,2048]{1,0:T(8,128)S(1)}, u32[]{:S(2)}, u32[]{:S(2)}) collective-permute-start(f32[16,2048]{1,0:T(8,128)S(1)} %fusion.23), channel_id=1, source_target_pairs={{0,2},{2,0},{1,3},{3,1},{4,6},{6,4},{5,7},{7,5},{8,10},{10,8},{9,1... | collective-permute-start | bytes 393224 | tf_op jit(solution)/shard_map/ppermute | solution.py:40
  15.2 2.4 %collective-permute-start.3 = (bf16[20,256]{1,0:T(8,128)(2,1)S(1)}, bf16[20,256]{1,0:T(8,128)(2,1)S(1)}, u32[]{:S(2)}, u32[]{:S(2)}) collective-permute-start(bf16[20,256]{1,0:T(8,128)(2,1)S(1)} %pad_maximum_fusion.4), channel_id=1, source_target_pairs={{0,2},{2,0},{1,3},{3,1},{4,6},{6,4},{5,7},{7,5},{8,10},{10,8},{9,1... | collective-permute-start | bytes 30728 | tf_op jit(solution)/shard_map/ppermute | solution.py:41
  17.6 4.7 %collective-permute-done.3 = bf16[20,256]{1,0:T(8,128)(2,1)S(1)} collective-permute-done((bf16[20,256]{1,0:T(8,128)(2,1)S(1)}, bf16[20,256]{1,0:T(8,128)(2,1)S(1)}, u32[]{:S(2)}, u32[]{:S(2)}) %collective-permute-start.3) | collective-permute-done | bytes 10272 | tf_op jit(solution)/shard_map/ppermute | solution.py:41
  22.3 5.1 %collective-permute-start.5 = (bf16[40,256]{1,0:T(8,128)(2,1)S(1)}, bf16[40,256]{1,0:T(8,128)(2,1)S(1)}, u32[]{:S(2)}, u32[]{:S(2)}) collective-permute-start(bf16[40,256]{1,0:T(8,128)(2,1)S(1)} %pad_maximum_fusion.3), channel_id=1, source_target_pairs={{0,4},{4,0},{8,12},{12,8},{16,20},{20,16},{24,28},{28,24},{1,5},{5... | collective-permute-start | bytes 61448 | tf_op jit(solution)/shard_map/ppermute | solution.py:41
  27.4 1.9 %collective-permute-start.4 = (f32[16,2048]{1,0:T(8,128)S(1)}, f32[16,2048]{1,0:T(8,128)S(1)}, u32[]{:S(2)}, u32[]{:S(2)}) collective-permute-start(f32[16,2048]{1,0:T(8,128)S(1)} %add.106), channel_id=1, source_target_pairs={{0,4},{4,0},{8,12},{12,8},{16,20},{20,16},{24,28},{28,24},{1,5},{5... | collective-permute-start | bytes 393224 | tf_op jit(solution)/shard_map/ppermute | solution.py:40
  29.3 4.9 %collective-permute-done.4 = f32[16,2048]{1,0:T(8,128)S(1)} collective-permute-done((f32[16,2048]{1,0:T(8,128)S(1)}, f32[16,2048]{1,0:T(8,128)S(1)}, u32[]{:S(2)}, u32[]{:S(2)}) %collective-permute-start.4) | collective-permute-done | bytes 131104 | tf_op jit(solution)/shard_map/ppermute | solution.py:40
  34.3 1.9 %collective-permute-start.7 = (bf16[80,256]{1,0:T(8,128)(2,1)S(1)}, bf16[80,256]{1,0:T(8,128)(2,1)S(1)}, u32[]{:S(2)}, u32[]{:S(2)}) collective-permute-start(bf16[80,256]{1,0:T(8,128)(2,1)S(1)} %pad_maximum_fusion.2), channel_id=1, source_target_pairs={{0,8},{4,12},{8,0},{12,4},{16,24},{20,28},{24,16},{28,20},{1,9},{5... | collective-permute-start | bytes 122888 | tf_op jit(solution)/shard_map/ppermute | solution.py:41
  36.2 4.8 %collective-permute-start.6 = (f32[16,2048]{1,0:T(8,128)S(1)}, f32[16,2048]{1,0:T(8,128)S(1)}, u32[]{:S(2)}, u32[]{:S(2)}) collective-permute-start(f32[16,2048]{1,0:T(8,128)S(1)} %add.107), channel_id=1, source_target_pairs={{0,8},{4,12},{8,0},{12,4},{16,24},{20,28},{24,16},{28,20},{1,9},{5... | collective-permute-start | bytes 393224 | tf_op jit(solution)/shard_map/ppermute | solution.py:40
  41.1 1.8 %fusion = f32[16,128,48]{1,0,2:T(8,128)S(1)} fusion(bf16[128,48,256]{2,1,0:T(8,128)(2,1)S(1)} %bitcast.38, bf16[16,256]{1,0:T(8,128)(2,1)S(1)} %copy-done.2), kind=kOutput, calls=%fused_computation.5 | convolution fusion | flops 50331648 | bytes 3547136 | tf_op jit(solution)/shard_map/vn,pkn->vpk/dot_general | solution.py:61
  42.8 1.5 %collective-permute-done.6 = f32[16,2048]{1,0:T(8,128)S(1)} collective-permute-done((f32[16,2048]{1,0:T(8,128)S(1)}, f32[16,2048]{1,0:T(8,128)S(1)}, u32[]{:S(2)}, u32[]{:S(2)}) %collective-permute-start.6) | collective-permute-done | bytes 131104 | tf_op jit(solution)/shard_map/ppermute | solution.py:40
  44.4 5.4 %collective-permute-start.9 = (bf16[160,256]{1,0:T(8,128)(2,1)S(1)}, bf16[160,256]{1,0:T(8,128)(2,1)S(1)}, u32[]{:S(2)}, u32[]{:S(2)}) collective-permute-start(bf16[160,256]{1,0:T(8,128)(2,1)S(1)} %pad_maximum_fusion.1), channel_id=1, source_target_pairs={{0,28},{4,24},{8,20},{12,16},{16,12},{20,8},{24,4},{28,0},{1,29},{... | collective-permute-start | bytes 245768 | tf_op jit(solution)/shard_map/ppermute | solution.py:41
  49.8 3.5 %collective-permute-start.8 = (f32[16,2048]{1,0:T(8,128)S(1)}, f32[16,2048]{1,0:T(8,128)S(1)}, u32[]{:S(2)}, u32[]{:S(2)}) collective-permute-start(f32[16,2048]{1,0:T(8,128)S(1)} %add.108), channel_id=1, source_target_pairs={{0,28},{4,24},{8,20},{12,16},{16,12},{20,8},{24,4},{28,0},{1,29},{... | collective-permute-start | bytes 393224 | tf_op jit(solution)/shard_map/ppermute | solution.py:40
  54.3 5.4 %collective-permute-done.8 = f32[16,2048]{1,0:T(8,128)S(1)} collective-permute-done((f32[16,2048]{1,0:T(8,128)S(1)}, f32[16,2048]{1,0:T(8,128)S(1)}, u32[]{:S(2)}, u32[]{:S(2)}) %collective-permute-start.8) | collective-permute-done | bytes 131104 | tf_op jit(solution)/shard_map/ppermute | solution.py:40
  60.2 1.9 %collective-permute-start.10 = (f32[16,48]{1,0:T(8,128)S(1)}, f32[16,48]{1,0:T(8,128)S(1)}, u32[]{:S(2)}, u32[]{:S(2)}) collective-permute-start(f32[16,48]{1,0:T(8,128)S(1)} %convolution_multiply_fusion.1), channel_id=1, source_target_pairs={{0,1},{1,0},{2,3},{3,2},{4,5},{5,4},{6,7},{7,6},{8,9},{9,8},{10,11... | collective-permute-start | bytes 9224 | tf_op jit(solution)/shard_map/ppermute | solution.py:30
  63.3 2.4 %collective-permute-start.11 = (f32[16,48]{1,0:T(8,128)S(1)}, f32[16,48]{1,0:T(8,128)S(1)}, u32[]{:S(2)}, u32[]{:S(2)}) collective-permute-start(f32[16,48]{1,0:T(8,128)S(1)} %add.110), channel_id=1, source_target_pairs={{0,2},{2,0},{1,3},{3,1},{4,6},{6,4},{5,7},{7,5},{8,10},{10,8},{9,1... | collective-permute-start | bytes 9224 | tf_op jit(solution)/shard_map/ppermute | solution.py:30
  67.1 3.3 %collective-permute-done.11 = f32[16,48]{1,0:T(8,128)S(1)} collective-permute-done((f32[16,48]{1,0:T(8,128)S(1)}, f32[16,48]{1,0:T(8,128)S(1)}, u32[]{:S(2)}, u32[]{:S(2)}) %collective-permute-start.11) | collective-permute-done | bytes 3104 | tf_op jit(solution)/shard_map/ppermute | solution.py:30
  70.4 3.2 %collective-permute-start.12 = (f32[16,48]{1,0:T(8,128)S(1)}, f32[16,48]{1,0:T(8,128)S(1)}, u32[]{:S(2)}, u32[]{:S(2)}) collective-permute-start(f32[16,48]{1,0:T(8,128)S(1)} %add.111), channel_id=1, source_target_pairs={{0,4},{4,0},{8,12},{12,8},{16,20},{20,16},{24,28},{28,24},{1,5},{5... | collective-permute-start | bytes 9224 | tf_op jit(solution)/shard_map/ppermute | solution.py:30
  73.5 2.4 %collective-permute-done.12 = f32[16,48]{1,0:T(8,128)S(1)} collective-permute-done((f32[16,48]{1,0:T(8,128)S(1)}, f32[16,48]{1,0:T(8,128)S(1)}, u32[]{:S(2)}, u32[]{:S(2)}) %collective-permute-start.12) | collective-permute-done | bytes 3104 | tf_op jit(solution)/shard_map/ppermute | solution.py:30
  75.9 3.1 %collective-permute-start.13 = (f32[16,48]{1,0:T(8,128)S(1)}, f32[16,48]{1,0:T(8,128)S(1)}, u32[]{:S(2)}, u32[]{:S(2)}) collective-permute-start(f32[16,48]{1,0:T(8,128)S(1)} %add.112), channel_id=1, source_target_pairs={{0,8},{4,12},{8,0},{12,4},{16,24},{20,28},{24,16},{28,20},{1,9},{5... | collective-permute-start | bytes 9224 | tf_op jit(solution)/shard_map/ppermute | solution.py:30
  80.3 2.0 %collective-permute-done.13 = f32[16,48]{1,0:T(8,128)S(1)} collective-permute-done((f32[16,48]{1,0:T(8,128)S(1)}, f32[16,48]{1,0:T(8,128)S(1)}, u32[]{:S(2)}, u32[]{:S(2)}) %collective-permute-start.13) | collective-permute-done | bytes 3104 | tf_op jit(solution)/shard_map/ppermute | solution.py:30
  82.3 3.4 %collective-permute-start.14 = (f32[16,48]{1,0:T(8,128)S(1)}, f32[16,48]{1,0:T(8,128)S(1)}, u32[]{:S(2)}, u32[]{:S(2)}) collective-permute-start(f32[16,48]{1,0:T(8,128)S(1)} %add.113), channel_id=1, source_target_pairs={{0,28},{4,24},{8,20},{12,16},{16,12},{20,8},{24,4},{28,0},{1,29},{... | collective-permute-start | bytes 9224 | tf_op jit(solution)/shard_map/ppermute | solution.py:30
  85.8 5.0 %collective-permute-done.14 = f32[16,48]{1,0:T(8,128)S(1)} collective-permute-done((f32[16,48]{1,0:T(8,128)S(1)}, f32[16,48]{1,0:T(8,128)S(1)}, u32[]{:S(2)}, u32[]{:S(2)}) %collective-permute-start.14) | collective-permute-done | bytes 3104 | tf_op jit(solution)/shard_map/ppermute | solution.py:30
  90.9 2.5 %collective-permute-start.15 = (f32[16,48]{1,0:T(8,128)S(1)}, f32[16,48]{1,0:T(8,128)S(1)}, u32[]{:S(2)}, u32[]{:S(2)}) collective-permute-start(f32[16,48]{1,0:T(8,128)S(1)} %add.114), channel_id=1, source_target_pairs={{0,32},{32,0},{1,33},{33,1},{2,34},{34,2},{3,35},{35,3},{4,36},{36... | collective-permute-start | bytes 9224 | tf_op jit(solution)/shard_map/ppermute | solution.py:30
  93.4 3.0 %collective-permute-done.15 = f32[16,48]{1,0:T(8,128)S(1)} collective-permute-done((f32[16,48]{1,0:T(8,128)S(1)}, f32[16,48]{1,0:T(8,128)S(1)}, u32[]{:S(2)}, u32[]{:S(2)}) %collective-permute-start.15) | collective-permute-done | bytes 3104 | tf_op jit(solution)/shard_map/ppermute | solution.py:30
  96.4 4.3 %collective-permute-start.16 = (f32[16,48]{1,0:T(8,128)S(1)}, f32[16,48]{1,0:T(8,128)S(1)}, u32[]{:S(2)}, u32[]{:S(2)}) collective-permute-start(f32[16,48]{1,0:T(8,128)S(1)} %add.115), channel_id=1, source_target_pairs={{0,64},{64,0},{128,192},{192,128},{256,320},{320,256},{384,448},{4... | collective-permute-start | bytes 9224 | tf_op jit(solution)/shard_map/ppermute | solution.py:30
  100.7 1.6 %collective-permute-done.16 = f32[16,48]{1,0:T(8,128)S(1)} collective-permute-done((f32[16,48]{1,0:T(8,128)S(1)}, f32[16,48]{1,0:T(8,128)S(1)}, u32[]{:S(2)}, u32[]{:S(2)}) %collective-permute-start.16) | collective-permute-done | bytes 3104 | tf_op jit(solution)/shard_map/ppermute | solution.py:30
  102.3 6.1 %collective-permute-start.17 = (f32[16,48]{1,0:T(8,128)S(1)}, f32[16,48]{1,0:T(8,128)S(1)}, u32[]{:S(2)}, u32[]{:S(2)}) collective-permute-start(f32[16,48]{1,0:T(8,128)S(1)} %add.116), channel_id=1, source_target_pairs={{0,128},{64,192},{128,0},{192,64},{256,384},{320,448},{384,256},{4... | collective-permute-start | bytes 9224 | tf_op jit(solution)/shard_map/ppermute | solution.py:30
  110.0 9.4 %collective-permute-start.18 = (f32[16,48]{1,0:T(8,128)S(1)}, f32[16,48]{1,0:T(8,128)S(1)}, u32[]{:S(2)}, u32[]{:S(2)}) collective-permute-start(f32[16,48]{1,0:T(8,128)S(1)} %add.117), channel_id=1, source_target_pairs={{0,448},{64,384},{128,320},{192,256},{256,192},{320,128},{384,64},... | collective-permute-start | bytes 9224 | tf_op jit(solution)/shard_map/ppermute | solution.py:30
  119.6 1.4 %collective-permute-done.18 = f32[16,48]{1,0:T(8,128)S(1)} collective-permute-done((f32[16,48]{1,0:T(8,128)S(1)}, f32[16,48]{1,0:T(8,128)S(1)}, u32[]{:S(2)}, u32[]{:S(2)}) %collective-permute-start.18) | collective-permute-done | bytes 3104 | tf_op jit(solution)/shard_map/ppermute | solution.py:30
  (61 shorter events, 12.1 us)
Async XLA Ops:
  0.0 41.0 %copy-start = (bf16[128,3,16,256]{3,2,1,0:T(8,128)(2,1)S(1)}, bf16[128,3,16,256]{3,2,1,0:T(8,128)(2,1)}, u32[]{:S(2)}) copy-start(bf16[128,3,16,256]{3,2,1,0:T(8,128)(2,1)} %param.12) | copy-start | bytes 9437188
  0.0 41.0 %copy-start.2 = (bf16[16,256]{1,0:T(8,128)(2,1)S(1)}, bf16[16,256]{1,0:T(8,128)(2,1)}, u32[]{:S(2)}) copy-start(bf16[16,256]{1,0:T(8,128)(2,1)} %param.14) | copy-start | bytes 24580
  2.1 51.2 %copy-start.4 = (s32[10]{0:T(128)S(1)}, s32[10]{0:T(128)}, u32[]{:S(2)}) copy-start(s32[10]{0:T(128)} %param.18) | copy-start | bytes 124
  4.1 6.1 %collective-permute-start = (f32[16,2048]{1,0:T(8,128)S(1)}, f32[16,2048]{1,0:T(8,128)S(1)}, u32[]{:S(2)}, u32[]{:S(2)}) collective-permute-start(f32[16,2048]{1,0:T(8,128)S(1)} %bitcast.42), channel_id=1, source_target_pairs={{0,1},{1,0},{2,3},{3,2},{4,5},{5,4},{6,7},{7,6},{8,9},{9,8},{10,11... | collective-permute-start | bytes 393224 | tf_op jit(solution)/shard_map/ppermute | solution.py:40
  6.0 3.4 %collective-permute-start.1 = (bf16[10,256]{1,0:T(8,128)(2,1)}, bf16[10,256]{1,0:T(8,128)(2,1)S(1)}, u32[]{:S(2)}, u32[]{:S(2)}) collective-permute-start(bf16[10,256]{1,0:T(8,128)(2,1)} %param.16), channel_id=1, source_target_pairs={{0,1},{1,0},{2,3},{3,2},{4,5},{5,4},{6,7},{7,6},{8,9},{9,8},{10,11... | collective-permute-start | bytes 15368 | tf_op jit(solution)/shard_map/ppermute | solution.py:41
  10.2 52.0 %copy-start.3 = (s32[320,2]{0,1:T(2,128)S(1)}, s32[320,2]{0,1:T(2,128)}, u32[]{:S(2)}) copy-start(s32[320,2]{0,1:T(2,128)} %param.17) | copy-start | bytes 7684
  10.2 12.0 %collective-permute-start.2 = (f32[16,2048]{1,0:T(8,128)S(1)}, f32[16,2048]{1,0:T(8,128)S(1)}, u32[]{:S(2)}, u32[]{:S(2)}) collective-permute-start(f32[16,2048]{1,0:T(8,128)S(1)} %fusion.23), channel_id=1, source_target_pairs={{0,2},{2,0},{1,3},{3,1},{4,6},{6,4},{5,7},{7,5},{8,10},{10,8},{9,1... | collective-permute-start | bytes 393224 | tf_op jit(solution)/shard_map/ppermute | solution.py:40
  15.2 7.1 %collective-permute-start.3 = (bf16[20,256]{1,0:T(8,128)(2,1)S(1)}, bf16[20,256]{1,0:T(8,128)(2,1)S(1)}, u32[]{:S(2)}, u32[]{:S(2)}) collective-permute-start(bf16[20,256]{1,0:T(8,128)(2,1)S(1)} %pad_maximum_fusion.4), channel_id=1, source_target_pairs={{0,2},{2,0},{1,3},{3,1},{4,6},{6,4},{5,7},{7,5},{8,10},{10,8},{9,1... | collective-permute-start | bytes 30728 | tf_op jit(solution)/shard_map/ppermute | solution.py:41
  22.3 7.0 %collective-permute-start.5 = (bf16[40,256]{1,0:T(8,128)(2,1)S(1)}, bf16[40,256]{1,0:T(8,128)(2,1)S(1)}, u32[]{:S(2)}, u32[]{:S(2)}) collective-permute-start(bf16[40,256]{1,0:T(8,128)(2,1)S(1)} %pad_maximum_fusion.3), channel_id=1, source_target_pairs={{0,4},{4,0},{8,12},{12,8},{16,20},{20,16},{24,28},{28,24},{1,5},{5... | collective-permute-start | bytes 61448 | tf_op jit(solution)/shard_map/ppermute | solution.py:41
  27.4 6.9 %collective-permute-start.4 = (f32[16,2048]{1,0:T(8,128)S(1)}, f32[16,2048]{1,0:T(8,128)S(1)}, u32[]{:S(2)}, u32[]{:S(2)}) collective-permute-start(f32[16,2048]{1,0:T(8,128)S(1)} %add.106), channel_id=1, source_target_pairs={{0,4},{4,0},{8,12},{12,8},{16,20},{20,16},{24,28},{28,24},{1,5},{5... | collective-permute-start | bytes 393224 | tf_op jit(solution)/shard_map/ppermute | solution.py:40
  34.3 8.6 %collective-permute-start.7 = (bf16[80,256]{1,0:T(8,128)(2,1)S(1)}, bf16[80,256]{1,0:T(8,128)(2,1)S(1)}, u32[]{:S(2)}, u32[]{:S(2)}) collective-permute-start(bf16[80,256]{1,0:T(8,128)(2,1)S(1)} %pad_maximum_fusion.2), channel_id=1, source_target_pairs={{0,8},{4,12},{8,0},{12,4},{16,24},{20,28},{24,16},{28,20},{1,9},{5... | collective-permute-start | bytes 122888 | tf_op jit(solution)/shard_map/ppermute | solution.py:41
  36.2 8.1 %collective-permute-start.6 = (f32[16,2048]{1,0:T(8,128)S(1)}, f32[16,2048]{1,0:T(8,128)S(1)}, u32[]{:S(2)}, u32[]{:S(2)}) collective-permute-start(f32[16,2048]{1,0:T(8,128)S(1)} %add.107), channel_id=1, source_target_pairs={{0,8},{4,12},{8,0},{12,4},{16,24},{20,28},{24,16},{28,20},{1,9},{5... | collective-permute-start | bytes 393224 | tf_op jit(solution)/shard_map/ppermute | solution.py:40
  41.1 37.9 %copy-start.1 = (s32[24]{0:T(128)S(1)}, s32[24]{0:T(128)}, u32[]{:S(2)}) copy-start(s32[24]{0:T(128)} %param.19) | copy-start | bytes 292
  44.4 10.0 %collective-permute-start.9 = (bf16[160,256]{1,0:T(8,128)(2,1)S(1)}, bf16[160,256]{1,0:T(8,128)(2,1)S(1)}, u32[]{:S(2)}, u32[]{:S(2)}) collective-permute-start(bf16[160,256]{1,0:T(8,128)(2,1)S(1)} %pad_maximum_fusion.1), channel_id=1, source_target_pairs={{0,28},{4,24},{8,20},{12,16},{16,12},{20,8},{24,4},{28,0},{1,29},{... | collective-permute-start | bytes 245768 | tf_op jit(solution)/shard_map/ppermute | solution.py:41
  49.8 10.0 %collective-permute-start.8 = (f32[16,2048]{1,0:T(8,128)S(1)}, f32[16,2048]{1,0:T(8,128)S(1)}, u32[]{:S(2)}, u32[]{:S(2)}) collective-permute-start(f32[16,2048]{1,0:T(8,128)S(1)} %add.108), channel_id=1, source_target_pairs={{0,28},{4,24},{8,20},{12,16},{16,12},{20,8},{24,4},{28,0},{1,29},{... | collective-permute-start | bytes 393224 | tf_op jit(solution)/shard_map/ppermute | solution.py:40
  60.2 3.1 %collective-permute-start.10 = (f32[16,48]{1,0:T(8,128)S(1)}, f32[16,48]{1,0:T(8,128)S(1)}, u32[]{:S(2)}, u32[]{:S(2)}) collective-permute-start(f32[16,48]{1,0:T(8,128)S(1)} %convolution_multiply_fusion.1), channel_id=1, source_target_pairs={{0,1},{1,0},{2,3},{3,2},{4,5},{5,4},{6,7},{7,6},{8,9},{9,8},{10,11... | collective-permute-start | bytes 9224 | tf_op jit(solution)/shard_map/ppermute | solution.py:30
  63.3 7.0 %collective-permute-start.11 = (f32[16,48]{1,0:T(8,128)S(1)}, f32[16,48]{1,0:T(8,128)S(1)}, u32[]{:S(2)}, u32[]{:S(2)}) collective-permute-start(f32[16,48]{1,0:T(8,128)S(1)} %add.110), channel_id=1, source_target_pairs={{0,2},{2,0},{1,3},{3,1},{4,6},{6,4},{5,7},{7,5},{8,10},{10,8},{9,1... | collective-permute-start | bytes 9224 | tf_op jit(solution)/shard_map/ppermute | solution.py:30
  70.4 5.5 %collective-permute-start.12 = (f32[16,48]{1,0:T(8,128)S(1)}, f32[16,48]{1,0:T(8,128)S(1)}, u32[]{:S(2)}, u32[]{:S(2)}) collective-permute-start(f32[16,48]{1,0:T(8,128)S(1)} %add.111), channel_id=1, source_target_pairs={{0,4},{4,0},{8,12},{12,8},{16,20},{20,16},{24,28},{28,24},{1,5},{5... | collective-permute-start | bytes 9224 | tf_op jit(solution)/shard_map/ppermute | solution.py:30
  75.9 6.4 %collective-permute-start.13 = (f32[16,48]{1,0:T(8,128)S(1)}, f32[16,48]{1,0:T(8,128)S(1)}, u32[]{:S(2)}, u32[]{:S(2)}) collective-permute-start(f32[16,48]{1,0:T(8,128)S(1)} %add.112), channel_id=1, source_target_pairs={{0,8},{4,12},{8,0},{12,4},{16,24},{20,28},{24,16},{28,20},{1,9},{5... | collective-permute-start | bytes 9224 | tf_op jit(solution)/shard_map/ppermute | solution.py:30
  82.3 8.5 %collective-permute-start.14 = (f32[16,48]{1,0:T(8,128)S(1)}, f32[16,48]{1,0:T(8,128)S(1)}, u32[]{:S(2)}, u32[]{:S(2)}) collective-permute-start(f32[16,48]{1,0:T(8,128)S(1)} %add.113), channel_id=1, source_target_pairs={{0,28},{4,24},{8,20},{12,16},{16,12},{20,8},{24,4},{28,0},{1,29},{... | collective-permute-start | bytes 9224 | tf_op jit(solution)/shard_map/ppermute | solution.py:30
  90.9 5.5 %collective-permute-start.15 = (f32[16,48]{1,0:T(8,128)S(1)}, f32[16,48]{1,0:T(8,128)S(1)}, u32[]{:S(2)}, u32[]{:S(2)}) collective-permute-start(f32[16,48]{1,0:T(8,128)S(1)} %add.114), channel_id=1, source_target_pairs={{0,32},{32,0},{1,33},{33,1},{2,34},{34,2},{3,35},{35,3},{4,36},{36... | collective-permute-start | bytes 9224 | tf_op jit(solution)/shard_map/ppermute | solution.py:30
  96.4 5.9 %collective-permute-start.16 = (f32[16,48]{1,0:T(8,128)S(1)}, f32[16,48]{1,0:T(8,128)S(1)}, u32[]{:S(2)}, u32[]{:S(2)}) collective-permute-start(f32[16,48]{1,0:T(8,128)S(1)} %add.115), channel_id=1, source_target_pairs={{0,64},{64,0},{128,192},{192,128},{256,320},{320,256},{384,448},{4... | collective-permute-start | bytes 9224 | tf_op jit(solution)/shard_map/ppermute | solution.py:30
  102.3 7.7 %collective-permute-start.17 = (f32[16,48]{1,0:T(8,128)S(1)}, f32[16,48]{1,0:T(8,128)S(1)}, u32[]{:S(2)}, u32[]{:S(2)}) collective-permute-start(f32[16,48]{1,0:T(8,128)S(1)} %add.116), channel_id=1, source_target_pairs={{0,128},{64,192},{128,0},{192,64},{256,384},{320,448},{384,256},{4... | collective-permute-start | bytes 9224 | tf_op jit(solution)/shard_map/ppermute | solution.py:30
  110.0 11.0 %collective-permute-start.18 = (f32[16,48]{1,0:T(8,128)S(1)}, f32[16,48]{1,0:T(8,128)S(1)}, u32[]{:S(2)}, u32[]{:S(2)}) collective-permute-start(f32[16,48]{1,0:T(8,128)S(1)} %add.117), channel_id=1, source_target_pairs={{0,448},{64,384},{128,320},{192,256},{256,192},{320,128},{384,64},... | collective-permute-start | bytes 9224 | tf_op jit(solution)/shard_map/ppermute | solution.py:30

commit v7 on v6

--- a/solution.py
+++ b/solution.py
@@ -13,9 +13,9 @@
 
 
 def ring_label(position, size):
-    if size < 8:
+    if size != 8:
         return position
-    return position if position < size // 2 else 3 * size // 2 - 1 - position
+    return position if position < 4 else position ^ 2
 
 
 def partners(size, step):
@@ -29,6 +29,12 @@
         while step < size:
             value = value + lax.ppermute(value, axis, partners(size, step))
             step *= 2
+    return value
+
+
+def x_ring_sum(value):
+    for pairs in ([(i, i ^ 2) for i in range(4)], [(i, 3 - i) for i in range(4)]):
+        value = value + lax.ppermute(value, ("xlo", "xhi"), pairs)
     return value
 
 
@@ -62,11 +68,13 @@
         "vn,pkn->vpk", coef_t, soc_ints.reshape(rows, 3 * width, -1), preferred_element_type=jnp.float32
     ).reshape(width * rows, 3 * width)
     field_part = jnp.dot(weight, soc_part, precision=HIGH) * scale
-    field = butterfly_sum(field_part, AO_ROUNDS + AUX_ROUNDS)
+    field = butterfly_sum(field_part, (("core", 2),))
+    field = x_ring_sum(field)
+    field = butterfly_sum(field, (("y", 8), ("z", 8)))
 
     def labelled(device):
         y = device // 4
-        return jnp.where(y < 4, y, 11 - y) * 4 + device % 4
+        return jnp.where(y < 4, y, y ^ 2) * 4 + device % 4
 
     me = (lax.axis_index("y") * 4 + lax.axis_index("xhi") * 2 + lax.axis_index("core")).astype(jnp.int32)
     block = spin_dens.shape[0]

time: 123 us -> 122 us (level)
  starting transfers between devices: 70.5 us -> 67.8 us
  waiting for transfers between devices: 39.3 us -> 41.1 us
    ppermute x9 -> x7, starting transfers between devices: 36.2 us -> 28.4 us  [butterfly_sum(): value = value + lax.ppermute(value, axis, partners(size, step))]
    ppermute x0 -> x2, starting transfers between devices: none -> 5.52 us  [x_ring_sum(): value = value + lax.ppermute(value, ('xlo', 'xhi'), pairs)]
    ppermute x0 -> x2, waiting for transfers between devices: none -> 5.37 us  [x_ring_sum(): value = value + lax.ppermute(value, ('xlo', 'xhi'), pairs)]
    ppermute x9 -> x7, waiting for transfers between devices: 20.7 us -> 16.4 us  [butterfly_sum(): value = value + lax.ppermute(value, axis, partners(size, step))]
    ppermute x5, waiting for transfers between devices: 6.76 us -> 8.99 us  [butterfly_sum_gather(): lax.ppermute(blocks, axis, pairs)]
    ppermute x5, starting transfers between devices: 17.1 us -> 15.5 us  [butterfly_sum_gather(): total = total + lax.ppermute(total, axis, pairs)]
    ppermute x5, waiting for transfers between devices: 11.8 us -> 10.3 us  [butterfly_sum_gather(): total = total + lax.ppermute(total, axis, pairs)]
where the time goes in v7:
time: 122 us; the launch traced here: 121 us
  starting transfers between devices  67.8 us (56%)
  waiting for transfers between devices  41.1 us (34%)
  matrix products  7.1 us (6%)
  local copies, waits for them, and re-layouts  3.63 us (3%)
    ppermute x7, starting transfers between devices, butterfly_sum(): value = value + lax.ppermute(value, axis, partners(size, step))  28.4 us
    ppermute x5, starting transfers between devices, butterfly_sum_gather(): lax.ppermute(blocks, axis, pairs)  18.4 us
    ppermute x7, waiting for transfers between devices, butterfly_sum(): value = value + lax.ppermute(value, axis, partners(size, step))  16.4 us
    ppermute x5, starting transfers between devices, butterfly_sum_gather(): total = total + lax.ppermute(total, axis, pairs)  15.5 us
    ppermute x5, waiting for transfers between devices, butterfly_sum_gather(): total = total + lax.ppermute(total, axis, pairs)  10.3 us
    ppermute x5, waiting for transfers between devices, butterfly_sum_gather(): lax.ppermute(blocks, axis, pairs)  8.99 us
    ppermute x2, starting transfers between devices, x_ring_sum(): value = value + lax.ppermute(value, ('xlo', 'xhi'), pairs)  5.52 us
    ppermute x2, waiting for transfers between devices, x_ring_sum(): value = value + lax.ppermute(value, ('xlo', 'xhi'), pairs)  5.37 us
  transfers between devices with their start and end apart: 19, of which 15 were waited for; matrix products, arithmetic and copies ran while one was open for 5% of the time, Pallas kernels for 0%

profile of v7, /device:TPU:8, one launch (start us, length us, event | category | flops | bytes accessed | tf_op | source)
XLA Modules:
  0.0 121.1 jit_solution(11140698823136248996)
XLA Ops:
  0.0 2.1 %fusion.5 = f32[16,128,16]{1,0,2:T(8,128)S(1)} fusion(bf16[128,16,256]{2,1,0:T(8,128)(2,1)} %param.13, bf16[16,256]{1,0:T(8,128)(2,1)} %param.14), kind=kOutput, calls=%fused_computation.14 | convolution fusion | flops 16777216 | bytes 1187840 | tf_op jit(solution)/shard_map/un,ptn->upt/dot_general | solution.py:60
  4.1 1.9 %collective-permute-start = (f32[16,2048]{1,0:T(8,128)S(1)}, f32[16,2048]{1,0:T(8,128)S(1)}, u32[]{:S(2)}, u32[]{:S(2)}) collective-permute-start(f32[16,2048]{1,0:T(8,128)S(1)} %bitcast.42), channel_id=1, source_target_pairs={{0,1},{1,0},{2,3},{3,2},{4,5},{5,4},{6,7},{7,6},{8,9},{9,8},{10,11... | collective-permute-start | bytes 393224 | tf_op jit(solution)/shard_map/ppermute | solution.py:46
  6.0 2.4 %collective-permute-start.1 = (bf16[10,256]{1,0:T(8,128)(2,1)}, bf16[10,256]{1,0:T(8,128)(2,1)S(1)}, u32[]{:S(2)}, u32[]{:S(2)}) collective-permute-start(bf16[10,256]{1,0:T(8,128)(2,1)} %param.16), channel_id=1, source_target_pairs={{0,1},{1,0},{2,3},{3,2},{4,5},{5,4},{6,7},{7,6},{8,9},{9,8},{10,11... | collective-permute-start | bytes 15368 | tf_op jit(solution)/shard_map/ppermute | solution.py:47
  10.2 4.9 %collective-permute-start.2 = (f32[16,2048]{1,0:T(8,128)S(1)}, f32[16,2048]{1,0:T(8,128)S(1)}, u32[]{:S(2)}, u32[]{:S(2)}) collective-permute-start(f32[16,2048]{1,0:T(8,128)S(1)} %fusion.23), channel_id=1, source_target_pairs={{0,2},{2,0},{1,3},{3,1},{4,6},{6,4},{5,7},{7,5},{8,10},{10,8},{9,1... | collective-permute-start | bytes 393224 | tf_op jit(solution)/shard_map/ppermute | solution.py:46
  15.2 2.4 %collective-permute-start.3 = (bf16[20,256]{1,0:T(8,128)(2,1)S(1)}, bf16[20,256]{1,0:T(8,128)(2,1)S(1)}, u32[]{:S(2)}, u32[]{:S(2)}) collective-permute-start(bf16[20,256]{1,0:T(8,128)(2,1)S(1)} %pad_maximum_fusion.4), channel_id=1, source_target_pairs={{0,2},{2,0},{1,3},{3,1},{4,6},{6,4},{5,7},{7,5},{8,10},{10,8},{9,1... | collective-permute-start | bytes 30728 | tf_op jit(solution)/shard_map/ppermute | solution.py:47
  17.6 4.7 %collective-permute-done.3 = bf16[20,256]{1,0:T(8,128)(2,1)S(1)} collective-permute-done((bf16[20,256]{1,0:T(8,128)(2,1)S(1)}, bf16[20,256]{1,0:T(8,128)(2,1)S(1)}, u32[]{:S(2)}, u32[]{:S(2)}) %collective-permute-start.3) | collective-permute-done | bytes 10272 | tf_op jit(solution)/shard_map/ppermute | solution.py:47
  22.3 5.1 %collective-permute-start.5 = (bf16[40,256]{1,0:T(8,128)(2,1)S(1)}, bf16[40,256]{1,0:T(8,128)(2,1)S(1)}, u32[]{:S(2)}, u32[]{:S(2)}) collective-permute-start(bf16[40,256]{1,0:T(8,128)(2,1)S(1)} %pad_maximum_fusion.3), channel_id=1, source_target_pairs={{0,4},{4,0},{8,12},{12,8},{16,20},{20,16},{24,28},{28,24},{1,5},{5... | collective-permute-start | bytes 61448 | tf_op jit(solution)/shard_map/ppermute | solution.py:47
  27.4 1.9 %collective-permute-start.4 = (f32[16,2048]{1,0:T(8,128)S(1)}, f32[16,2048]{1,0:T(8,128)S(1)}, u32[]{:S(2)}, u32[]{:S(2)}) collective-permute-start(f32[16,2048]{1,0:T(8,128)S(1)} %add.106), channel_id=1, source_target_pairs={{0,4},{4,0},{8,12},{12,8},{16,20},{20,16},{24,28},{28,24},{1,5},{5... | collective-permute-start | bytes 393224 | tf_op jit(solution)/shard_map/ppermute | solution.py:46
  29.3 4.9 %collective-permute-done.4 = f32[16,2048]{1,0:T(8,128)S(1)} collective-permute-done((f32[16,2048]{1,0:T(8,128)S(1)}, f32[16,2048]{1,0:T(8,128)S(1)}, u32[]{:S(2)}, u32[]{:S(2)}) %collective-permute-start.4) | collective-permute-done | bytes 131104 | tf_op jit(solution)/shard_map/ppermute | solution.py:46
  34.3 1.9 %collective-permute-start.7 = (bf16[80,256]{1,0:T(8,128)(2,1)S(1)}, bf16[80,256]{1,0:T(8,128)(2,1)S(1)}, u32[]{:S(2)}, u32[]{:S(2)}) collective-permute-start(bf16[80,256]{1,0:T(8,128)(2,1)S(1)} %pad_maximum_fusion.2), channel_id=1, source_target_pairs={{0,8},{4,12},{8,0},{12,4},{16,24},{20,28},{24,16},{28,20},{1,9},{5... | collective-permute-start | bytes 122888 | tf_op jit(solution)/shard_map/ppermute | solution.py:47
  36.2 4.8 %collective-permute-start.6 = (f32[16,2048]{1,0:T(8,128)S(1)}, f32[16,2048]{1,0:T(8,128)S(1)}, u32[]{:S(2)}, u32[]{:S(2)}) collective-permute-start(f32[16,2048]{1,0:T(8,128)S(1)} %add.107), channel_id=1, source_target_pairs={{0,8},{4,12},{8,0},{12,4},{16,24},{20,28},{24,16},{28,20},{1,9},{5... | collective-permute-start | bytes 393224 | tf_op jit(solution)/shard_map/ppermute | solution.py:46
  41.1 1.8 %fusion = f32[16,128,48]{1,0,2:T(8,128)S(1)} fusion(bf16[128,48,256]{2,1,0:T(8,128)(2,1)S(1)} %bitcast.38, bf16[16,256]{1,0:T(8,128)(2,1)S(1)} %copy-done.2), kind=kOutput, calls=%fused_computation.5 | convolution fusion | flops 50331648 | bytes 3547136 | tf_op jit(solution)/shard_map/vn,pkn->vpk/dot_general | solution.py:67
  42.8 1.5 %collective-permute-done.6 = f32[16,2048]{1,0:T(8,128)S(1)} collective-permute-done((f32[16,2048]{1,0:T(8,128)S(1)}, f32[16,2048]{1,0:T(8,128)S(1)}, u32[]{:S(2)}, u32[]{:S(2)}) %collective-permute-start.6) | collective-permute-done | bytes 131104 | tf_op jit(solution)/shard_map/ppermute | solution.py:46
  44.4 6.6 %collective-permute-start.9 = (bf16[160,256]{1,0:T(8,128)(2,1)S(1)}, bf16[160,256]{1,0:T(8,128)(2,1)S(1)}, u32[]{:S(2)}, u32[]{:S(2)}) collective-permute-start(bf16[160,256]{1,0:T(8,128)(2,1)S(1)} %pad_maximum_fusion.1), channel_id=1, source_target_pairs={{0,24},{4,28},{8,16},{12,20},{16,8},{20,12},{24,0},{28,4},{1,25},{... | collective-permute-start | bytes 245768 | tf_op jit(solution)/shard_map/ppermute | solution.py:47
  51.0 1.9 %collective-permute-start.8 = (f32[16,2048]{1,0:T(8,128)S(1)}, f32[16,2048]{1,0:T(8,128)S(1)}, u32[]{:S(2)}, u32[]{:S(2)}) collective-permute-start(f32[16,2048]{1,0:T(8,128)S(1)} %add.108), channel_id=1, source_target_pairs={{0,24},{4,28},{8,16},{12,20},{16,8},{20,12},{24,0},{28,4},{1,25},{... | collective-permute-start | bytes 393224 | tf_op jit(solution)/shard_map/ppermute | solution.py:46
  52.9 3.3 %collective-permute-done.9 = bf16[160,256]{1,0:T(8,128)(2,1)S(1)} collective-permute-done((bf16[160,256]{1,0:T(8,128)(2,1)S(1)}, bf16[160,256]{1,0:T(8,128)(2,1)S(1)}, u32[]{:S(2)}, u32[]{:S(2)}) %collective-permute-start.9) | collective-permute-done | bytes 81952 | tf_op jit(solution)/shard_map/ppermute | solution.py:47
  56.2 3.9 %collective-permute-done.8 = f32[16,2048]{1,0:T(8,128)S(1)} collective-permute-done((f32[16,2048]{1,0:T(8,128)S(1)}, f32[16,2048]{1,0:T(8,128)S(1)}, u32[]{:S(2)}, u32[]{:S(2)}) %collective-permute-start.8) | collective-permute-done | bytes 131104 | tf_op jit(solution)/shard_map/ppermute | solution.py:46
  60.6 1.9 %collective-permute-start.10 = (f32[16,48]{1,0:T(8,128)S(1)}, f32[16,48]{1,0:T(8,128)S(1)}, u32[]{:S(2)}, u32[]{:S(2)}) collective-permute-start(f32[16,48]{1,0:T(8,128)S(1)} %convolution_multiply_fusion.1), channel_id=1, source_target_pairs={{0,1},{1,0},{2,3},{3,2},{4,5},{5,4},{6,7},{7,6},{8,9},{9,8},{10,11... | collective-permute-start | bytes 9224 | tf_op jit(solution)/shard_map/ppermute | solution.py:30
  63.7 2.5 %collective-permute-start.11 = (f32[16,48]{1,0:T(8,128)S(1)}, f32[16,48]{1,0:T(8,128)S(1)}, u32[]{:S(2)}, u32[]{:S(2)}) collective-permute-start(f32[16,48]{1,0:T(8,128)S(1)} %add.110), channel_id=1, source_target_pairs={{0,32},{2,34},{32,0},{34,2},{1,33},{3,35},{33,1},{35,3},{4,36},{6,... | collective-permute-start | bytes 9224 | tf_op jit(solution)/shard_map/ppermute | solution.py:37
  67.6 1.7 %collective-permute-done.11 = f32[16,48]{1,0:T(8,128)S(1)} collective-permute-done((f32[16,48]{1,0:T(8,128)S(1)}, f32[16,48]{1,0:T(8,128)S(1)}, u32[]{:S(2)}, u32[]{:S(2)}) %collective-permute-start.11) | collective-permute-done | bytes 3104 | tf_op jit(solution)/shard_map/ppermute | solution.py:37
  69.3 3.0 %collective-permute-start.12 = (f32[16,48]{1,0:T(8,128)S(1)}, f32[16,48]{1,0:T(8,128)S(1)}, u32[]{:S(2)}, u32[]{:S(2)}) collective-permute-start(f32[16,48]{1,0:T(8,128)S(1)} %add.111), channel_id=1, source_target_pairs={{0,34},{2,32},{32,2},{34,0},{1,35},{3,33},{33,3},{35,1},{4,38},{6,... | collective-permute-start | bytes 9224 | tf_op jit(solution)/shard_map/ppermute | solution.py:37
  72.3 3.7 %collective-permute-done.12 = f32[16,48]{1,0:T(8,128)S(1)} collective-permute-done((f32[16,48]{1,0:T(8,128)S(1)}, f32[16,48]{1,0:T(8,128)S(1)}, u32[]{:S(2)}, u32[]{:S(2)}) %collective-permute-start.12) | collective-permute-done | bytes 3104 | tf_op jit(solution)/shard_map/ppermute | solution.py:37
  76.0 1.9 %collective-permute-start.13 = (f32[16,48]{1,0:T(8,128)S(1)}, f32[16,48]{1,0:T(8,128)S(1)}, u32[]{:S(2)}, u32[]{:S(2)}) collective-permute-start(f32[16,48]{1,0:T(8,128)S(1)} %add.112), channel_id=1, source_target_pairs={{0,4},{4,0},{8,12},{12,8},{16,20},{20,16},{24,28},{28,24},{1,5},{5... | collective-permute-start | bytes 9224 | tf_op jit(solution)/shard_map/ppermute | solution.py:30
  79.3 2.3 %collective-permute-done.13 = f32[16,48]{1,0:T(8,128)S(1)} collective-permute-done((f32[16,48]{1,0:T(8,128)S(1)}, f32[16,48]{1,0:T(8,128)S(1)}, u32[]{:S(2)}, u32[]{:S(2)}) %collective-permute-start.13) | collective-permute-done | bytes 3104 | tf_op jit(solution)/shard_map/ppermute | solution.py:30
  81.5 2.1 %collective-permute-start.14 = (f32[16,48]{1,0:T(8,128)S(1)}, f32[16,48]{1,0:T(8,128)S(1)}, u32[]{:S(2)}, u32[]{:S(2)}) collective-permute-start(f32[16,48]{1,0:T(8,128)S(1)} %add.113), channel_id=1, source_target_pairs={{0,8},{4,12},{8,0},{12,4},{16,24},{20,28},{24,16},{28,20},{1,9},{5... | collective-permute-start | bytes 9224 | tf_op jit(solution)/shard_map/ppermute | solution.py:30
  83.7 4.3 %collective-permute-done.14 = f32[16,48]{1,0:T(8,128)S(1)} collective-permute-done((f32[16,48]{1,0:T(8,128)S(1)}, f32[16,48]{1,0:T(8,128)S(1)}, u32[]{:S(2)}, u32[]{:S(2)}) %collective-permute-start.14) | collective-permute-done | bytes 3104 | tf_op jit(solution)/shard_map/ppermute | solution.py:30
  88.0 2.8 %collective-permute-start.15 = (f32[16,48]{1,0:T(8,128)S(1)}, f32[16,48]{1,0:T(8,128)S(1)}, u32[]{:S(2)}, u32[]{:S(2)}) collective-permute-start(f32[16,48]{1,0:T(8,128)S(1)} %add.114), channel_id=1, source_target_pairs={{0,24},{4,28},{8,16},{12,20},{16,8},{20,12},{24,0},{28,4},{1,25},{... | collective-permute-start | bytes 9224 | tf_op jit(solution)/shard_map/ppermute | solution.py:30
  90.8 4.8 %collective-permute-done.15 = f32[16,48]{1,0:T(8,128)S(1)} collective-permute-done((f32[16,48]{1,0:T(8,128)S(1)}, f32[16,48]{1,0:T(8,128)S(1)}, u32[]{:S(2)}, u32[]{:S(2)}) %collective-permute-start.15) | collective-permute-done | bytes 3104 | tf_op jit(solution)/shard_map/ppermute | solution.py:30
  95.6 4.3 %collective-permute-start.16 = (f32[16,48]{1,0:T(8,128)S(1)}, f32[16,48]{1,0:T(8,128)S(1)}, u32[]{:S(2)}, u32[]{:S(2)}) collective-permute-start(f32[16,48]{1,0:T(8,128)S(1)} %add.115), channel_id=1, source_target_pairs={{0,64},{64,0},{128,192},{192,128},{256,320},{320,256},{384,448},{4... | collective-permute-start | bytes 9224 | tf_op jit(solution)/shard_map/ppermute | solution.py:30
  99.9 1.6 %collective-permute-done.16 = f32[16,48]{1,0:T(8,128)S(1)} collective-permute-done((f32[16,48]{1,0:T(8,128)S(1)}, f32[16,48]{1,0:T(8,128)S(1)}, u32[]{:S(2)}, u32[]{:S(2)}) %collective-permute-start.16) | collective-permute-done | bytes 3104 | tf_op jit(solution)/shard_map/ppermute | solution.py:30
  101.5 6.1 %collective-permute-start.17 = (f32[16,48]{1,0:T(8,128)S(1)}, f32[16,48]{1,0:T(8,128)S(1)}, u32[]{:S(2)}, u32[]{:S(2)}) collective-permute-start(f32[16,48]{1,0:T(8,128)S(1)} %add.116), channel_id=1, source_target_pairs={{0,128},{64,192},{128,0},{192,64},{256,384},{320,448},{384,256},{4... | collective-permute-start | bytes 9224 | tf_op jit(solution)/shard_map/ppermute | solution.py:30
  109.2 9.3 %collective-permute-start.18 = (f32[16,48]{1,0:T(8,128)S(1)}, f32[16,48]{1,0:T(8,128)S(1)}, u32[]{:S(2)}, u32[]{:S(2)}) collective-permute-start(f32[16,48]{1,0:T(8,128)S(1)} %add.117), channel_id=1, source_target_pairs={{0,384},{64,448},{128,256},{192,320},{256,128},{320,192},{384,0},{... | collective-permute-start | bytes 9224 | tf_op jit(solution)/shard_map/ppermute | solution.py:30
  (61 shorter events, 12.4 us)
Async XLA Ops:
  0.0 41.0 %copy-start = (bf16[128,3,16,256]{3,2,1,0:T(8,128)(2,1)S(1)}, bf16[128,3,16,256]{3,2,1,0:T(8,128)(2,1)}, u32[]{:S(2)}) copy-start(bf16[128,3,16,256]{3,2,1,0:T(8,128)(2,1)} %param.12) | copy-start | bytes 9437188
  0.0 41.0 %copy-start.2 = (bf16[16,256]{1,0:T(8,128)(2,1)S(1)}, bf16[16,256]{1,0:T(8,128)(2,1)}, u32[]{:S(2)}) copy-start(bf16[16,256]{1,0:T(8,128)(2,1)} %param.14) | copy-start | bytes 24580
  2.1 50.8 %copy-start.4 = (s32[10]{0:T(128)S(1)}, s32[10]{0:T(128)}, u32[]{:S(2)}) copy-start(s32[10]{0:T(128)} %param.18) | copy-start | bytes 124
  4.1 6.1 %collective-permute-start = (f32[16,2048]{1,0:T(8,128)S(1)}, f32[16,2048]{1,0:T(8,128)S(1)}, u32[]{:S(2)}, u32[]{:S(2)}) collective-permute-start(f32[16,2048]{1,0:T(8,128)S(1)} %bitcast.42), channel_id=1, source_target_pairs={{0,1},{1,0},{2,3},{3,2},{4,5},{5,4},{6,7},{7,6},{8,9},{9,8},{10,11... | collective-permute-start | bytes 393224 | tf_op jit(solution)/shard_map/ppermute | solution.py:46
  6.0 3.4 %collective-permute-start.1 = (bf16[10,256]{1,0:T(8,128)(2,1)}, bf16[10,256]{1,0:T(8,128)(2,1)S(1)}, u32[]{:S(2)}, u32[]{:S(2)}) collective-permute-start(bf16[10,256]{1,0:T(8,128)(2,1)} %param.16), channel_id=1, source_target_pairs={{0,1},{1,0},{2,3},{3,2},{4,5},{5,4},{6,7},{7,6},{8,9},{9,8},{10,11... | collective-permute-start | bytes 15368 | tf_op jit(solution)/shard_map/ppermute | solution.py:47
  10.2 52.4 %copy-start.3 = (s32[320,2]{0,1:T(2,128)S(1)}, s32[320,2]{0,1:T(2,128)}, u32[]{:S(2)}) copy-start(s32[320,2]{0,1:T(2,128)} %param.17) | copy-start | bytes 7684
  10.2 12.0 %collective-permute-start.2 = (f32[16,2048]{1,0:T(8,128)S(1)}, f32[16,2048]{1,0:T(8,128)S(1)}, u32[]{:S(2)}, u32[]{:S(2)}) collective-permute-start(f32[16,2048]{1,0:T(8,128)S(1)} %fusion.23), channel_id=1, source_target_pairs={{0,2},{2,0},{1,3},{3,1},{4,6},{6,4},{5,7},{7,5},{8,10},{10,8},{9,1... | collective-permute-start | bytes 393224 | tf_op jit(solution)/shard_map/ppermute | solution.py:46
  15.2 7.1 %collective-permute-start.3 = (bf16[20,256]{1,0:T(8,128)(2,1)S(1)}, bf16[20,256]{1,0:T(8,128)(2,1)S(1)}, u32[]{:S(2)}, u32[]{:S(2)}) collective-permute-start(bf16[20,256]{1,0:T(8,128)(2,1)S(1)} %pad_maximum_fusion.4), channel_id=1, source_target_pairs={{0,2},{2,0},{1,3},{3,1},{4,6},{6,4},{5,7},{7,5},{8,10},{10,8},{9,1... | collective-permute-start | bytes 30728 | tf_op jit(solution)/shard_map/ppermute | solution.py:47
  22.3 7.0 %collective-permute-start.5 = (bf16[40,256]{1,0:T(8,128)(2,1)S(1)}, bf16[40,256]{1,0:T(8,128)(2,1)S(1)}, u32[]{:S(2)}, u32[]{:S(2)}) collective-permute-start(bf16[40,256]{1,0:T(8,128)(2,1)S(1)} %pad_maximum_fusion.3), channel_id=1, source_target_pairs={{0,4},{4,0},{8,12},{12,8},{16,20},{20,16},{24,28},{28,24},{1,5},{5... | collective-permute-start | bytes 61448 | tf_op jit(solution)/shard_map/ppermute | solution.py:47
  27.4 6.9 %collective-permute-start.4 = (f32[16,2048]{1,0:T(8,128)S(1)}, f32[16,2048]{1,0:T(8,128)S(1)}, u32[]{:S(2)}, u32[]{:S(2)}) collective-permute-start(f32[16,2048]{1,0:T(8,128)S(1)} %add.106), channel_id=1, source_target_pairs={{0,4},{4,0},{8,12},{12,8},{16,20},{20,16},{24,28},{28,24},{1,5},{5... | collective-permute-start | bytes 393224 | tf_op jit(solution)/shard_map/ppermute | solution.py:46
  34.3 8.6 %collective-permute-start.7 = (bf16[80,256]{1,0:T(8,128)(2,1)S(1)}, bf16[80,256]{1,0:T(8,128)(2,1)S(1)}, u32[]{:S(2)}, u32[]{:S(2)}) collective-permute-start(bf16[80,256]{1,0:T(8,128)(2,1)S(1)} %pad_maximum_fusion.2), channel_id=1, source_target_pairs={{0,8},{4,12},{8,0},{12,4},{16,24},{20,28},{24,16},{28,20},{1,9},{5... | collective-permute-start | bytes 122888 | tf_op jit(solution)/shard_map/ppermute | solution.py:47
  36.2 8.1 %collective-permute-start.6 = (f32[16,2048]{1,0:T(8,128)S(1)}, f32[16,2048]{1,0:T(8,128)S(1)}, u32[]{:S(2)}, u32[]{:S(2)}) collective-permute-start(f32[16,2048]{1,0:T(8,128)S(1)} %add.107), channel_id=1, source_target_pairs={{0,8},{4,12},{8,0},{12,4},{16,24},{20,28},{24,16},{28,20},{1,9},{5... | collective-permute-start | bytes 393224 | tf_op jit(solution)/shard_map/ppermute | solution.py:46
  41.1 36.9 %copy-start.1 = (s32[24]{0:T(128)S(1)}, s32[24]{0:T(128)}, u32[]{:S(2)}) copy-start(s32[24]{0:T(128)} %param.19) | copy-start | bytes 292
  44.4 11.8 %collective-permute-start.9 = (bf16[160,256]{1,0:T(8,128)(2,1)S(1)}, bf16[160,256]{1,0:T(8,128)(2,1)S(1)}, u32[]{:S(2)}, u32[]{:S(2)}) collective-permute-start(bf16[160,256]{1,0:T(8,128)(2,1)S(1)} %pad_maximum_fusion.1), channel_id=1, source_target_pairs={{0,24},{4,28},{8,16},{12,20},{16,8},{20,12},{24,0},{28,4},{1,25},{... | collective-permute-start | bytes 245768 | tf_op jit(solution)/shard_map/ppermute | solution.py:47
  51.0 9.2 %collective-permute-start.8 = (f32[16,2048]{1,0:T(8,128)S(1)}, f32[16,2048]{1,0:T(8,128)S(1)}, u32[]{:S(2)}, u32[]{:S(2)}) collective-permute-start(f32[16,2048]{1,0:T(8,128)S(1)} %add.108), channel_id=1, source_target_pairs={{0,24},{4,28},{8,16},{12,20},{16,8},{20,12},{24,0},{28,4},{1,25},{... | collective-permute-start | bytes 393224 | tf_op jit(solution)/shard_map/ppermute | solution.py:46
  60.6 3.1 %collective-permute-start.10 = (f32[16,48]{1,0:T(8,128)S(1)}, f32[16,48]{1,0:T(8,128)S(1)}, u32[]{:S(2)}, u32[]{:S(2)}) collective-permute-start(f32[16,48]{1,0:T(8,128)S(1)} %convolution_multiply_fusion.1), channel_id=1, source_target_pairs={{0,1},{1,0},{2,3},{3,2},{4,5},{5,4},{6,7},{7,6},{8,9},{9,8},{10,11... | collective-permute-start | bytes 9224 | tf_op jit(solution)/shard_map/ppermute | solution.py:30
  63.7 5.5 %collective-permute-start.11 = (f32[16,48]{1,0:T(8,128)S(1)}, f32[16,48]{1,0:T(8,128)S(1)}, u32[]{:S(2)}, u32[]{:S(2)}) collective-permute-start(f32[16,48]{1,0:T(8,128)S(1)} %add.110), channel_id=1, source_target_pairs={{0,32},{2,34},{32,0},{34,2},{1,33},{3,35},{33,1},{35,3},{4,36},{6,... | collective-permute-start | bytes 9224 | tf_op jit(solution)/shard_map/ppermute | solution.py:37
  69.3 6.7 %collective-permute-start.12 = (f32[16,48]{1,0:T(8,128)S(1)}, f32[16,48]{1,0:T(8,128)S(1)}, u32[]{:S(2)}, u32[]{:S(2)}) collective-permute-start(f32[16,48]{1,0:T(8,128)S(1)} %add.111), channel_id=1, source_target_pairs={{0,34},{2,32},{32,2},{34,0},{1,35},{3,33},{33,3},{35,1},{4,38},{6,... | collective-permute-start | bytes 9224 | tf_op jit(solution)/shard_map/ppermute | solution.py:37
  76.0 5.5 %collective-permute-start.13 = (f32[16,48]{1,0:T(8,128)S(1)}, f32[16,48]{1,0:T(8,128)S(1)}, u32[]{:S(2)}, u32[]{:S(2)}) collective-permute-start(f32[16,48]{1,0:T(8,128)S(1)} %add.112), channel_id=1, source_target_pairs={{0,4},{4,0},{8,12},{12,8},{16,20},{20,16},{24,28},{28,24},{1,5},{5... | collective-permute-start | bytes 9224 | tf_op jit(solution)/shard_map/ppermute | solution.py:30
  81.5 6.4 %collective-permute-start.14 = (f32[16,48]{1,0:T(8,128)S(1)}, f32[16,48]{1,0:T(8,128)S(1)}, u32[]{:S(2)}, u32[]{:S(2)}) collective-permute-start(f32[16,48]{1,0:T(8,128)S(1)} %add.113), channel_id=1, source_target_pairs={{0,8},{4,12},{8,0},{12,4},{16,24},{20,28},{24,16},{28,20},{1,9},{5... | collective-permute-start | bytes 9224 | tf_op jit(solution)/shard_map/ppermute | solution.py:30
  88.0 7.6 %collective-permute-start.15 = (f32[16,48]{1,0:T(8,128)S(1)}, f32[16,48]{1,0:T(8,128)S(1)}, u32[]{:S(2)}, u32[]{:S(2)}) collective-permute-start(f32[16,48]{1,0:T(8,128)S(1)} %add.114), channel_id=1, source_target_pairs={{0,24},{4,28},{8,16},{12,20},{16,8},{20,12},{24,0},{28,4},{1,25},{... | collective-permute-start | bytes 9224 | tf_op jit(solution)/shard_map/ppermute | solution.py:30
  95.6 5.9 %collective-permute-start.16 = (f32[16,48]{1,0:T(8,128)S(1)}, f32[16,48]{1,0:T(8,128)S(1)}, u32[]{:S(2)}, u32[]{:S(2)}) collective-permute-start(f32[16,48]{1,0:T(8,128)S(1)} %add.115), channel_id=1, source_target_pairs={{0,64},{64,0},{128,192},{192,128},{256,320},{320,256},{384,448},{4... | collective-permute-start | bytes 9224 | tf_op jit(solution)/shard_map/ppermute | solution.py:30
  101.5 7.7 %collective-permute-start.17 = (f32[16,48]{1,0:T(8,128)S(1)}, f32[16,48]{1,0:T(8,128)S(1)}, u32[]{:S(2)}, u32[]{:S(2)}) collective-permute-start(f32[16,48]{1,0:T(8,128)S(1)} %add.116), channel_id=1, source_target_pairs={{0,128},{64,192},{128,0},{192,64},{256,384},{320,448},{384,256},{4... | collective-permute-start | bytes 9224 | tf_op jit(solution)/shard_map/ppermute | solution.py:30
  109.2 10.9 %collective-permute-start.18 = (f32[16,48]{1,0:T(8,128)S(1)}, f32[16,48]{1,0:T(8,128)S(1)}, u32[]{:S(2)}, u32[]{:S(2)}) collective-permute-start(f32[16,48]{1,0:T(8,128)S(1)} %add.117), channel_id=1, source_target_pairs={{0,384},{64,448},{128,256},{192,320},{256,128},{320,192},{384,0},{... | collective-permute-start | bytes 9224 | tf_op jit(solution)/shard_map/ppermute | solution.py:30

commit v8 on v7

--- a/solution.py
+++ b/solution.py
@@ -62,7 +62,7 @@
     folded = jnp.einsum("upw,vw->uvp", cou_part, active_rdm, precision=HIGH)
     eye = jnp.eye(width, dtype=jnp.float32)
     weight = (eye[:, :, None] * fitted[None, None, :] - 1.5 * folded).reshape(width, width * rows)
-    weight, every_dens = butterfly_sum_gather(weight, spin_dens, AO_ROUNDS)
+    weight, every_dens = butterfly_sum_gather(weight, spin_dens, (("y", 8), ("xhi", 2), ("core", 2)))
 
     soc_part = jnp.einsum(
         "vn,pkn->vpk", coef_t, soc_ints.reshape(rows, 3 * width, -1), preferred_element_type=jnp.float32
@@ -74,7 +74,7 @@
 
     def labelled(device):
         y = device // 4
-        return jnp.where(y < 4, y, y ^ 2) * 4 + device % 4
+        return (device % 2) * 16 + (device // 2 % 2) * 8 + jnp.where(y < 4, y, y ^ 2)
 
     me = (lax.axis_index("y") * 4 + lax.axis_index("xhi") * 2 + lax.axis_index("core")).astype(jnp.int32)
     block = spin_dens.shape[0]

time: 122 us -> 121 us (level)
  waiting for transfers between devices: 41.1 us -> 37.7 us
  starting transfers between devices: 67.8 us -> 69.7 us
    ppermute x5, starting transfers between devices: 15.5 us -> 19.4 us  [butterfly_sum_gather(): total = total + lax.ppermute(total, axis, pairs)]
    ppermute x5, waiting for transfers between devices: 8.99 us -> 5.94 us  [butterfly_sum_gather(): lax.ppermute(blocks, axis, pairs)]
    ppermute x5, starting transfers between devices: 18.4 us -> 16.6 us  [butterfly_sum_gather(): lax.ppermute(blocks, axis, pairs)]
  transfers between devices with their start and end apart: 19 -> 19, of which waited for: 15 -> 14; matrix products, arithmetic and copies ran while one was open for 5% -> 6% of each run, Pallas kernels for 0% -> 0%
where the time goes in v8:
time: 121 us; the launch traced here: 120 us
  starting transfers between devices  69.7 us (58%)
  waiting for transfers between devices  37.7 us (31%)
  matrix products  7.8 us (6%)
  local copies, waits for them, and re-layouts  3.62 us (3%)
    ppermute x7, starting transfers between devices, butterfly_sum(): value = value + lax.ppermute(value, axis, partners(size, step))  28.2 us
    ppermute x5, starting transfers between devices, butterfly_sum_gather(): total = total + lax.ppermute(total, axis, pairs)  19.4 us
    ppermute x7, waiting for transfers between devices, butterfly_sum(): value = value + lax.ppermute(value, axis, partners(size, step))  17.1 us
    ppermute x5, starting transfers between devices, butterfly_sum_gather(): lax.ppermute(blocks, axis, pairs)  16.6 us
    ppermute x5, waiting for transfers between devices, butterfly_sum_gather(): total = total + lax.ppermute(total, axis, pairs)  9.25 us
    ppermute x5, waiting for transfers between devices, butterfly_sum_gather(): lax.ppermute(blocks, axis, pairs)  5.94 us
    ppermute x2, starting transfers between devices, x_ring_sum(): value = value + lax.ppermute(value, ('xlo', 'xhi'), pairs)  5.54 us
    ppermute x2, waiting for transfers between devices, x_ring_sum(): value = value + lax.ppermute(value, ('xlo', 'xhi'), pairs)  5.37 us
  transfers between devices with their start and end apart: 19, of which 14 were waited for; matrix products, arithmetic and copies ran while one was open for 6% of the time, Pallas kernels for 0%

profile of v8, /device:TPU:8, one launch (start us, length us, event | category | flops | bytes accessed | tf_op | source)
XLA Modules:
  0.0 120.3 jit_solution(18054462270126199277)
XLA Ops:
  0.0 2.1 %fusion.5 = f32[16,128,16]{1,0,2:T(8,128)S(1)} fusion(bf16[128,16,256]{2,1,0:T(8,128)(2,1)} %param.13, bf16[16,256]{1,0:T(8,128)(2,1)} %param.14), kind=kOutput, calls=%fused_computation.14 | convolution fusion | flops 16777216 | bytes 1187840 | tf_op jit(solution)/shard_map/un,ptn->upt/dot_general | solution.py:60
  4.1 7.7 %collective-permute-start = (f32[16,2048]{1,0:T(8,128)S(1)}, f32[16,2048]{1,0:T(8,128)S(1)}, u32[]{:S(2)}, u32[]{:S(2)}) collective-permute-start(f32[16,2048]{1,0:T(8,128)S(1)} %bitcast.42), channel_id=1, source_target_pairs={{0,4},{4,0},{8,12},{12,8},{16,20},{20,16},{24,28},{28,24},{1,5},{5... | collective-permute-start | bytes 393224 | tf_op jit(solution)/shard_map/ppermute | solution.py:46
  11.8 1.9 %collective-permute-start.1 = (bf16[10,256]{1,0:T(8,128)(2,1)}, bf16[10,256]{1,0:T(8,128)(2,1)S(1)}, u32[]{:S(2)}, u32[]{:S(2)}) collective-permute-start(bf16[10,256]{1,0:T(8,128)(2,1)} %param.16), channel_id=1, source_target_pairs={{0,4},{4,0},{8,12},{12,8},{16,20},{20,16},{24,28},{28,24},{1,5},{5... | collective-permute-start | bytes 15368 | tf_op jit(solution)/shard_map/ppermute | solution.py:47
  13.7 3.8 %collective-permute-done.1 = bf16[10,256]{1,0:T(8,128)(2,1)S(1)} collective-permute-done((bf16[10,256]{1,0:T(8,128)(2,1)}, bf16[10,256]{1,0:T(8,128)(2,1)S(1)}, u32[]{:S(2)}, u32[]{:S(2)}) %collective-permute-start.1) | collective-permute-done | bytes 5152 | tf_op jit(solution)/shard_map/ppermute | solution.py:47
  18.3 1.9 %collective-permute-start.2 = (f32[16,2048]{1,0:T(8,128)S(1)}, f32[16,2048]{1,0:T(8,128)S(1)}, u32[]{:S(2)}, u32[]{:S(2)}) collective-permute-start(f32[16,2048]{1,0:T(8,128)S(1)} %fusion.26), channel_id=1, source_target_pairs={{0,8},{4,12},{8,0},{12,4},{16,24},{20,28},{24,16},{28,20},{1,9},{5... | collective-permute-start | bytes 393224 | tf_op jit(solution)/shard_map/ppermute | solution.py:46
  20.3 4.8 %collective-permute-start.3 = (bf16[20,256]{1,0:T(8,128)(2,1)S(1)}, bf16[20,256]{1,0:T(8,128)(2,1)S(1)}, u32[]{:S(2)}, u32[]{:S(2)}) collective-permute-start(bf16[20,256]{1,0:T(8,128)(2,1)S(1)} %pad_maximum_fusion.4), channel_id=1, source_target_pairs={{0,8},{4,12},{8,0},{12,4},{16,24},{20,28},{24,16},{28,20},{1,9},{5... | collective-permute-start | bytes 30728 | tf_op jit(solution)/shard_map/ppermute | solution.py:47
  25.1 1.7 %collective-permute-done.3 = bf16[20,256]{1,0:T(8,128)(2,1)S(1)} collective-permute-done((bf16[20,256]{1,0:T(8,128)(2,1)S(1)}, bf16[20,256]{1,0:T(8,128)(2,1)S(1)}, u32[]{:S(2)}, u32[]{:S(2)}) %collective-permute-start.3) | collective-permute-done | bytes 10272 | tf_op jit(solution)/shard_map/ppermute | solution.py:47
  26.8 3.0 %collective-permute-start.5 = (bf16[40,256]{1,0:T(8,128)(2,1)S(1)}, bf16[40,256]{1,0:T(8,128)(2,1)S(1)}, u32[]{:S(2)}, u32[]{:S(2)}) collective-permute-start(bf16[40,256]{1,0:T(8,128)(2,1)S(1)} %pad_maximum_fusion.3), channel_id=1, source_target_pairs={{0,24},{4,28},{8,16},{12,20},{16,8},{20,12},{24,0},{28,4},{1,25},{... | collective-permute-start | bytes 61448 | tf_op jit(solution)/shard_map/ppermute | solution.py:47
  29.8 5.0 %collective-permute-start.4 = (f32[16,2048]{1,0:T(8,128)S(1)}, f32[16,2048]{1,0:T(8,128)S(1)}, u32[]{:S(2)}, u32[]{:S(2)}) collective-permute-start(f32[16,2048]{1,0:T(8,128)S(1)} %add.121), channel_id=1, source_target_pairs={{0,24},{4,28},{8,16},{12,20},{16,8},{20,12},{24,0},{28,4},{1,25},{... | collective-permute-start | bytes 393224 | tf_op jit(solution)/shard_map/ppermute | solution.py:46
  34.8 2.5 %fusion = f32[16,128,48]{1,0,2:T(8,128)S(1)} fusion(bf16[128,48,256]{2,1,0:T(8,128)(2,1)S(1)} %bitcast.38, bf16[16,256]{1,0:T(8,128)(2,1)} %param.14), kind=kOutput, calls=%fused_computation.5 | convolution fusion | flops 50331648 | bytes 3547136 | tf_op jit(solution)/shard_map/vn,pkn->vpk/dot_general | solution.py:67
  37.3 2.9 %collective-permute-done.4 = f32[16,2048]{1,0:T(8,128)S(1)} collective-permute-done((f32[16,2048]{1,0:T(8,128)S(1)}, f32[16,2048]{1,0:T(8,128)S(1)}, u32[]{:S(2)}, u32[]{:S(2)}) %collective-permute-start.4) | collective-permute-done | bytes 131104 | tf_op jit(solution)/shard_map/ppermute | solution.py:46
  40.1 4.9 %collective-permute-start.7 = (bf16[80,256]{1,0:T(8,128)(2,1)S(1)}, bf16[80,256]{1,0:T(8,128)(2,1)S(1)}, u32[]{:S(2)}, u32[]{:S(2)}) collective-permute-start(bf16[80,256]{1,0:T(8,128)(2,1)S(1)} %pad_maximum_fusion.2), channel_id=1, source_target_pairs={{0,2},{2,0},{1,3},{3,1},{4,6},{6,4},{5,7},{7,5},{8,10},{10,8},{9,1... | collective-permute-start | bytes 122888 | tf_op jit(solution)/shard_map/ppermute | solution.py:47
  45.1 2.4 %collective-permute-start.6 = (f32[16,2048]{1,0:T(8,128)S(1)}, f32[16,2048]{1,0:T(8,128)S(1)}, u32[]{:S(2)}, u32[]{:S(2)}) collective-permute-start(f32[16,2048]{1,0:T(8,128)S(1)} %add.122), channel_id=1, source_target_pairs={{0,2},{2,0},{1,3},{3,1},{4,6},{6,4},{5,7},{7,5},{8,10},{10,8},{9,1... | collective-permute-start | bytes 393224 | tf_op jit(solution)/shard_map/ppermute | solution.py:46
  48.0 5.5 %collective-permute-done.6 = f32[16,2048]{1,0:T(8,128)S(1)} collective-permute-done((f32[16,2048]{1,0:T(8,128)S(1)}, f32[16,2048]{1,0:T(8,128)S(1)}, u32[]{:S(2)}, u32[]{:S(2)}) %collective-permute-start.6) | collective-permute-done | bytes 131104 | tf_op jit(solution)/shard_map/ppermute | solution.py:46
  53.5 1.9 %collective-permute-start.9 = (bf16[160,256]{1,0:T(8,128)(2,1)S(1)}, bf16[160,256]{1,0:T(8,128)(2,1)S(1)}, u32[]{:S(2)}, u32[]{:S(2)}) collective-permute-start(bf16[160,256]{1,0:T(8,128)(2,1)S(1)} %pad_maximum_fusion.1), channel_id=1, source_target_pairs={{0,1},{1,0},{2,3},{3,2},{4,5},{5,4},{6,7},{7,6},{8,9},{9,8},{10,11... | collective-permute-start | bytes 245768 | tf_op jit(solution)/shard_map/ppermute | solution.py:47
  55.4 2.4 %collective-permute-start.8 = (f32[16,2048]{1,0:T(8,128)S(1)}, f32[16,2048]{1,0:T(8,128)S(1)}, u32[]{:S(2)}, u32[]{:S(2)}) collective-permute-start(f32[16,2048]{1,0:T(8,128)S(1)} %add.123), channel_id=1, source_target_pairs={{0,1},{1,0},{2,3},{3,2},{4,5},{5,4},{6,7},{7,6},{8,9},{9,8},{10,11... | collective-permute-start | bytes 393224 | tf_op jit(solution)/shard_map/ppermute | solution.py:46
  59.3 2.3 %collective-permute-start.10 = (f32[16,48]{1,0:T(8,128)S(1)}, f32[16,48]{1,0:T(8,128)S(1)}, u32[]{:S(2)}, u32[]{:S(2)}) collective-permute-start(f32[16,48]{1,0:T(8,128)S(1)} %convolution_multiply_fusion.1), channel_id=1, source_target_pairs={{0,1},{1,0},{2,3},{3,2},{4,5},{5,4},{6,7},{7,6},{8,9},{9,8},{10,11... | collective-permute-start | bytes 9224 | tf_op jit(solution)/shard_map/ppermute | solution.py:30
  62.9 2.5 %collective-permute-start.11 = (f32[16,48]{1,0:T(8,128)S(1)}, f32[16,48]{1,0:T(8,128)S(1)}, u32[]{:S(2)}, u32[]{:S(2)}) collective-permute-start(f32[16,48]{1,0:T(8,128)S(1)} %add.125), channel_id=1, source_target_pairs={{0,32},{2,34},{32,0},{34,2},{1,33},{3,35},{33,1},{35,3},{4,36},{6,... | collective-permute-start | bytes 9224 | tf_op jit(solution)/shard_map/ppermute | solution.py:37
  65.4 3.0 %collective-permute-done.11 = f32[16,48]{1,0:T(8,128)S(1)} collective-permute-done((f32[16,48]{1,0:T(8,128)S(1)}, f32[16,48]{1,0:T(8,128)S(1)}, u32[]{:S(2)}, u32[]{:S(2)}) %collective-permute-start.11) | collective-permute-done | bytes 3104 | tf_op jit(solution)/shard_map/ppermute | solution.py:37
  68.5 3.0 %collective-permute-start.12 = (f32[16,48]{1,0:T(8,128)S(1)}, f32[16,48]{1,0:T(8,128)S(1)}, u32[]{:S(2)}, u32[]{:S(2)}) collective-permute-start(f32[16,48]{1,0:T(8,128)S(1)} %add.126), channel_id=1, source_target_pairs={{0,34},{2,32},{32,2},{34,0},{1,35},{3,33},{33,3},{35,1},{4,38},{6,... | collective-permute-start | bytes 9224 | tf_op jit(solution)/shard_map/ppermute | solution.py:37
  72.9 2.3 %collective-permute-done.12 = f32[16,48]{1,0:T(8,128)S(1)} collective-permute-done((f32[16,48]{1,0:T(8,128)S(1)}, f32[16,48]{1,0:T(8,128)S(1)}, u32[]{:S(2)}, u32[]{:S(2)}) %collective-permute-start.12) | collective-permute-done | bytes 3104 | tf_op jit(solution)/shard_map/ppermute | solution.py:37
  75.2 1.9 %collective-permute-start.13 = (f32[16,48]{1,0:T(8,128)S(1)}, f32[16,48]{1,0:T(8,128)S(1)}, u32[]{:S(2)}, u32[]{:S(2)}) collective-permute-start(f32[16,48]{1,0:T(8,128)S(1)} %add.127), channel_id=1, source_target_pairs={{0,4},{4,0},{8,12},{12,8},{16,20},{20,16},{24,28},{28,24},{1,5},{5... | collective-permute-start | bytes 9224 | tf_op jit(solution)/shard_map/ppermute | solution.py:30
  77.2 3.6 %collective-permute-done.13 = f32[16,48]{1,0:T(8,128)S(1)} collective-permute-done((f32[16,48]{1,0:T(8,128)S(1)}, f32[16,48]{1,0:T(8,128)S(1)}, u32[]{:S(2)}, u32[]{:S(2)}) %collective-permute-start.13) | collective-permute-done | bytes 3104 | tf_op jit(solution)/shard_map/ppermute | solution.py:30
  80.8 2.2 %collective-permute-start.14 = (f32[16,48]{1,0:T(8,128)S(1)}, f32[16,48]{1,0:T(8,128)S(1)}, u32[]{:S(2)}, u32[]{:S(2)}) collective-permute-start(f32[16,48]{1,0:T(8,128)S(1)} %add.128), channel_id=1, source_target_pairs={{0,8},{4,12},{8,0},{12,4},{16,24},{20,28},{24,16},{28,20},{1,9},{5... | collective-permute-start | bytes 9224 | tf_op jit(solution)/shard_map/ppermute | solution.py:30
  83.0 4.1 %collective-permute-done.14 = f32[16,48]{1,0:T(8,128)S(1)} collective-permute-done((f32[16,48]{1,0:T(8,128)S(1)}, f32[16,48]{1,0:T(8,128)S(1)}, u32[]{:S(2)}, u32[]{:S(2)}) %collective-permute-start.14) | collective-permute-done | bytes 3104 | tf_op jit(solution)/shard_map/ppermute | solution.py:30
  87.2 2.1 %collective-permute-start.15 = (f32[16,48]{1,0:T(8,128)S(1)}, f32[16,48]{1,0:T(8,128)S(1)}, u32[]{:S(2)}, u32[]{:S(2)}) collective-permute-start(f32[16,48]{1,0:T(8,128)S(1)} %add.129), channel_id=1, source_target_pairs={{0,24},{4,28},{8,16},{12,20},{16,8},{20,12},{24,0},{28,4},{1,25},{... | collective-permute-start | bytes 9224 | tf_op jit(solution)/shard_map/ppermute | solution.py:30
  89.4 5.5 %collective-permute-done.15 = f32[16,48]{1,0:T(8,128)S(1)} collective-permute-done((f32[16,48]{1,0:T(8,128)S(1)}, f32[16,48]{1,0:T(8,128)S(1)}, u32[]{:S(2)}, u32[]{:S(2)}) %collective-permute-start.15) | collective-permute-done | bytes 3104 | tf_op jit(solution)/shard_map/ppermute | solution.py:30
  94.8 4.3 %collective-permute-start.16 = (f32[16,48]{1,0:T(8,128)S(1)}, f32[16,48]{1,0:T(8,128)S(1)}, u32[]{:S(2)}, u32[]{:S(2)}) collective-permute-start(f32[16,48]{1,0:T(8,128)S(1)} %add.130), channel_id=1, source_target_pairs={{0,64},{64,0},{128,192},{192,128},{256,320},{320,256},{384,448},{4... | collective-permute-start | bytes 9224 | tf_op jit(solution)/shard_map/ppermute | solution.py:30
  99.1 1.6 %collective-permute-done.16 = f32[16,48]{1,0:T(8,128)S(1)} collective-permute-done((f32[16,48]{1,0:T(8,128)S(1)}, f32[16,48]{1,0:T(8,128)S(1)}, u32[]{:S(2)}, u32[]{:S(2)}) %collective-permute-start.16) | collective-permute-done | bytes 3104 | tf_op jit(solution)/shard_map/ppermute | solution.py:30
  100.7 6.1 %collective-permute-start.17 = (f32[16,48]{1,0:T(8,128)S(1)}, f32[16,48]{1,0:T(8,128)S(1)}, u32[]{:S(2)}, u32[]{:S(2)}) collective-permute-start(f32[16,48]{1,0:T(8,128)S(1)} %add.131), channel_id=1, source_target_pairs={{0,128},{64,192},{128,0},{192,64},{256,384},{320,448},{384,256},{4... | collective-permute-start | bytes 9224 | tf_op jit(solution)/shard_map/ppermute | solution.py:30
  108.4 9.3 %collective-permute-start.18 = (f32[16,48]{1,0:T(8,128)S(1)}, f32[16,48]{1,0:T(8,128)S(1)}, u32[]{:S(2)}, u32[]{:S(2)}) collective-permute-start(f32[16,48]{1,0:T(8,128)S(1)} %add.132), channel_id=1, source_target_pairs={{0,384},{64,448},{128,256},{192,320},{256,128},{320,192},{384,0},{... | collective-permute-start | bytes 9224 | tf_op jit(solution)/shard_map/ppermute | solution.py:30
  118.0 1.4 %collective-permute-done.18 = f32[16,48]{1,0:T(8,128)S(1)} collective-permute-done((f32[16,48]{1,0:T(8,128)S(1)}, f32[16,48]{1,0:T(8,128)S(1)}, u32[]{:S(2)}, u32[]{:S(2)}) %collective-permute-start.18) | collective-permute-done | bytes 3104 | tf_op jit(solution)/shard_map/ppermute | solution.py:30
  (59 shorter events, 10.3 us)
Async XLA Ops:
  0.0 34.8 %copy-start = (bf16[128,3,16,256]{3,2,1,0:T(8,128)(2,1)S(1)}, bf16[128,3,16,256]{3,2,1,0:T(8,128)(2,1)}, u32[]{:S(2)}) copy-start(bf16[128,3,16,256]{3,2,1,0:T(8,128)(2,1)} %param.12) | copy-start | bytes 9437188
  0.0 47.5 %copy-start.3 = (s32[10]{0:T(128)S(1)}, s32[10]{0:T(128)}, u32[]{:S(2)}) copy-start(s32[10]{0:T(128)} %param.18) | copy-start | bytes 124
  2.1 55.7 %copy-start.2 = (s32[320,2]{0,1:T(2,128)S(1)}, s32[320,2]{0,1:T(2,128)}, u32[]{:S(2)}) copy-start(s32[320,2]{0,1:T(2,128)} %param.17) | copy-start | bytes 7684
  4.1 14.2 %collective-permute-start = (f32[16,2048]{1,0:T(8,128)S(1)}, f32[16,2048]{1,0:T(8,128)S(1)}, u32[]{:S(2)}, u32[]{:S(2)}) collective-permute-start(f32[16,2048]{1,0:T(8,128)S(1)} %bitcast.42), channel_id=1, source_target_pairs={{0,4},{4,0},{8,12},{12,8},{16,20},{20,16},{24,28},{28,24},{1,5},{5... | collective-permute-start | bytes 393224 | tf_op jit(solution)/shard_map/ppermute | solution.py:46
  11.8 5.8 %collective-permute-start.1 = (bf16[10,256]{1,0:T(8,128)(2,1)}, bf16[10,256]{1,0:T(8,128)(2,1)S(1)}, u32[]{:S(2)}, u32[]{:S(2)}) collective-permute-start(bf16[10,256]{1,0:T(8,128)(2,1)} %param.16), channel_id=1, source_target_pairs={{0,4},{4,0},{8,12},{12,8},{16,20},{20,16},{24,28},{28,24},{1,5},{5... | collective-permute-start | bytes 15368 | tf_op jit(solution)/shard_map/ppermute | solution.py:47
  18.3 8.4 %collective-permute-start.2 = (f32[16,2048]{1,0:T(8,128)S(1)}, f32[16,2048]{1,0:T(8,128)S(1)}, u32[]{:S(2)}, u32[]{:S(2)}) collective-permute-start(f32[16,2048]{1,0:T(8,128)S(1)} %fusion.26), channel_id=1, source_target_pairs={{0,8},{4,12},{8,0},{12,4},{16,24},{20,28},{24,16},{28,20},{1,9},{5... | collective-permute-start | bytes 393224 | tf_op jit(solution)/shard_map/ppermute | solution.py:46
  20.3 6.5 %collective-permute-start.3 = (bf16[20,256]{1,0:T(8,128)(2,1)S(1)}, bf16[20,256]{1,0:T(8,128)(2,1)S(1)}, u32[]{:S(2)}, u32[]{:S(2)}) collective-permute-start(bf16[20,256]{1,0:T(8,128)(2,1)S(1)} %pad_maximum_fusion.4), channel_id=1, source_target_pairs={{0,8},{4,12},{8,0},{12,4},{16,24},{20,28},{24,16},{28,20},{1,9},{5... | collective-permute-start | bytes 30728 | tf_op jit(solution)/shard_map/ppermute | solution.py:47
  26.8 10.5 %collective-permute-start.5 = (bf16[40,256]{1,0:T(8,128)(2,1)S(1)}, bf16[40,256]{1,0:T(8,128)(2,1)S(1)}, u32[]{:S(2)}, u32[]{:S(2)}) collective-permute-start(bf16[40,256]{1,0:T(8,128)(2,1)S(1)} %pad_maximum_fusion.3), channel_id=1, source_target_pairs={{0,24},{4,28},{8,16},{12,20},{16,8},{20,12},{24,0},{28,4},{1,25},{... | collective-permute-start | bytes 61448 | tf_op jit(solution)/shard_map/ppermute | solution.py:47
  29.8 10.4 %collective-permute-start.4 = (f32[16,2048]{1,0:T(8,128)S(1)}, f32[16,2048]{1,0:T(8,128)S(1)}, u32[]{:S(2)}, u32[]{:S(2)}) collective-permute-start(f32[16,2048]{1,0:T(8,128)S(1)} %add.121), channel_id=1, source_target_pairs={{0,24},{4,28},{8,16},{12,20},{16,8},{20,12},{24,0},{28,4},{1,25},{... | collective-permute-start | bytes 393224 | tf_op jit(solution)/shard_map/ppermute | solution.py:46
  34.8 36.8 %copy-start.1 = (s32[24]{0:T(128)S(1)}, s32[24]{0:T(128)}, u32[]{:S(2)}) copy-start(s32[24]{0:T(128)} %param.19) | copy-start | bytes 292
  40.1 7.8 %collective-permute-start.7 = (bf16[80,256]{1,0:T(8,128)(2,1)S(1)}, bf16[80,256]{1,0:T(8,128)(2,1)S(1)}, u32[]{:S(2)}, u32[]{:S(2)}) collective-permute-start(bf16[80,256]{1,0:T(8,128)(2,1)S(1)} %pad_maximum_fusion.2), channel_id=1, source_target_pairs={{0,2},{2,0},{1,3},{3,1},{4,6},{6,4},{5,7},{7,5},{8,10},{10,8},{9,1... | collective-permute-start | bytes 122888 | tf_op jit(solution)/shard_map/ppermute | solution.py:47
  45.1 8.4 %collective-permute-start.6 = (f32[16,2048]{1,0:T(8,128)S(1)}, f32[16,2048]{1,0:T(8,128)S(1)}, u32[]{:S(2)}, u32[]{:S(2)}) collective-permute-start(f32[16,2048]{1,0:T(8,128)S(1)} %add.122), channel_id=1, source_target_pairs={{0,2},{2,0},{1,3},{3,1},{4,6},{6,4},{5,7},{7,5},{8,10},{10,8},{9,1... | collective-permute-start | bytes 393224 | tf_op jit(solution)/shard_map/ppermute | solution.py:46
  53.5 4.4 %collective-permute-start.9 = (bf16[160,256]{1,0:T(8,128)(2,1)S(1)}, bf16[160,256]{1,0:T(8,128)(2,1)S(1)}, u32[]{:S(2)}, u32[]{:S(2)}) collective-permute-start(bf16[160,256]{1,0:T(8,128)(2,1)S(1)} %pad_maximum_fusion.1), channel_id=1, source_target_pairs={{0,1},{1,0},{2,3},{3,2},{4,5},{5,4},{6,7},{7,6},{8,9},{9,8},{10,11... | collective-permute-start | bytes 245768 | tf_op jit(solution)/shard_map/ppermute | solution.py:47
  55.4 3.4 %collective-permute-start.8 = (f32[16,2048]{1,0:T(8,128)S(1)}, f32[16,2048]{1,0:T(8,128)S(1)}, u32[]{:S(2)}, u32[]{:S(2)}) collective-permute-start(f32[16,2048]{1,0:T(8,128)S(1)} %add.123), channel_id=1, source_target_pairs={{0,1},{1,0},{2,3},{3,2},{4,5},{5,4},{6,7},{7,6},{8,9},{9,8},{10,11... | collective-permute-start | bytes 393224 | tf_op jit(solution)/shard_map/ppermute | solution.py:46
  59.3 3.6 %collective-permute-start.10 = (f32[16,48]{1,0:T(8,128)S(1)}, f32[16,48]{1,0:T(8,128)S(1)}, u32[]{:S(2)}, u32[]{:S(2)}) collective-permute-start(f32[16,48]{1,0:T(8,128)S(1)} %convolution_multiply_fusion.1), channel_id=1, source_target_pairs={{0,1},{1,0},{2,3},{3,2},{4,5},{5,4},{6,7},{7,6},{8,9},{9,8},{10,11... | collective-permute-start | bytes 9224 | tf_op jit(solution)/shard_map/ppermute | solution.py:30
  62.9 5.5 %collective-permute-start.11 = (f32[16,48]{1,0:T(8,128)S(1)}, f32[16,48]{1,0:T(8,128)S(1)}, u32[]{:S(2)}, u32[]{:S(2)}) collective-permute-start(f32[16,48]{1,0:T(8,128)S(1)} %add.125), channel_id=1, source_target_pairs={{0,32},{2,34},{32,0},{34,2},{1,33},{3,35},{33,1},{35,3},{4,36},{6,... | collective-permute-start | bytes 9224 | tf_op jit(solution)/shard_map/ppermute | solution.py:37
  68.5 6.7 %collective-permute-start.12 = (f32[16,48]{1,0:T(8,128)S(1)}, f32[16,48]{1,0:T(8,128)S(1)}, u32[]{:S(2)}, u32[]{:S(2)}) collective-permute-start(f32[16,48]{1,0:T(8,128)S(1)} %add.126), channel_id=1, source_target_pairs={{0,34},{2,32},{32,2},{34,0},{1,35},{3,33},{33,3},{35,1},{4,38},{6,... | collective-permute-start | bytes 9224 | tf_op jit(solution)/shard_map/ppermute | solution.py:37
  75.2 5.5 %collective-permute-start.13 = (f32[16,48]{1,0:T(8,128)S(1)}, f32[16,48]{1,0:T(8,128)S(1)}, u32[]{:S(2)}, u32[]{:S(2)}) collective-permute-start(f32[16,48]{1,0:T(8,128)S(1)} %add.127), channel_id=1, source_target_pairs={{0,4},{4,0},{8,12},{12,8},{16,20},{20,16},{24,28},{28,24},{1,5},{5... | collective-permute-start | bytes 9224 | tf_op jit(solution)/shard_map/ppermute | solution.py:30
  80.8 6.4 %collective-permute-start.14 = (f32[16,48]{1,0:T(8,128)S(1)}, f32[16,48]{1,0:T(8,128)S(1)}, u32[]{:S(2)}, u32[]{:S(2)}) collective-permute-start(f32[16,48]{1,0:T(8,128)S(1)} %add.128), channel_id=1, source_target_pairs={{0,8},{4,12},{8,0},{12,4},{16,24},{20,28},{24,16},{28,20},{1,9},{5... | collective-permute-start | bytes 9224 | tf_op jit(solution)/shard_map/ppermute | solution.py:30
  87.2 7.6 %collective-permute-start.15 = (f32[16,48]{1,0:T(8,128)S(1)}, f32[16,48]{1,0:T(8,128)S(1)}, u32[]{:S(2)}, u32[]{:S(2)}) collective-permute-start(f32[16,48]{1,0:T(8,128)S(1)} %add.129), channel_id=1, source_target_pairs={{0,24},{4,28},{8,16},{12,20},{16,8},{20,12},{24,0},{28,4},{1,25},{... | collective-permute-start | bytes 9224 | tf_op jit(solution)/shard_map/ppermute | solution.py:30
  94.8 5.9 %collective-permute-start.16 = (f32[16,48]{1,0:T(8,128)S(1)}, f32[16,48]{1,0:T(8,128)S(1)}, u32[]{:S(2)}, u32[]{:S(2)}) collective-permute-start(f32[16,48]{1,0:T(8,128)S(1)} %add.130), channel_id=1, source_target_pairs={{0,64},{64,0},{128,192},{192,128},{256,320},{320,256},{384,448},{4... | collective-permute-start | bytes 9224 | tf_op jit(solution)/shard_map/ppermute | solution.py:30
  100.7 7.7 %collective-permute-start.17 = (f32[16,48]{1,0:T(8,128)S(1)}, f32[16,48]{1,0:T(8,128)S(1)}, u32[]{:S(2)}, u32[]{:S(2)}) collective-permute-start(f32[16,48]{1,0:T(8,128)S(1)} %add.131), channel_id=1, source_target_pairs={{0,128},{64,192},{128,0},{192,64},{256,384},{320,448},{384,256},{4... | collective-permute-start | bytes 9224 | tf_op jit(solution)/shard_map/ppermute | solution.py:30
  108.4 10.9 %collective-permute-start.18 = (f32[16,48]{1,0:T(8,128)S(1)}, f32[16,48]{1,0:T(8,128)S(1)}, u32[]{:S(2)}, u32[]{:S(2)}) collective-permute-start(f32[16,48]{1,0:T(8,128)S(1)} %add.132), channel_id=1, source_target_pairs={{0,384},{64,448},{128,256},{192,320},{256,128},{320,192},{384,0},{... | collective-permute-start | bytes 9224 | tf_op jit(solution)/shard_map/ppermute | solution.py:30

commit v9 on v8

--- a/solution.py
+++ b/solution.py
@@ -68,9 +68,9 @@
         "vn,pkn->vpk", coef_t, soc_ints.reshape(rows, 3 * width, -1), preferred_element_type=jnp.float32
     ).reshape(width * rows, 3 * width)
     field_part = jnp.dot(weight, soc_part, precision=HIGH) * scale
-    field = butterfly_sum(field_part, (("core", 2),))
+    field = butterfly_sum(field_part, (("z", 8), ("y", 8)))
     field = x_ring_sum(field)
-    field = butterfly_sum(field, (("y", 8), ("z", 8)))
+    field = butterfly_sum(field, (("core", 2),))
 
     def labelled(device):
         y = device // 4

time: 121 us -> 121 us (level)
  the two profiles are of different devices: /device:TPU:8 before, /device:TPU:1 now
where the time goes in v9:
time: 121 us; the launch traced here: 120 us
  starting transfers between devices  79.5 us (66%)
  waiting for transfers between devices  28 us (23%)
  matrix products  7.8 us (6%)
  local copies, waits for them, and re-layouts  3.62 us (3%)
    ppermute x7, starting transfers between devices, butterfly_sum(): value = value + lax.ppermute(value, axis, partners(size, step))  39 us
    ppermute x5, starting transfers between devices, butterfly_sum_gather(): lax.ppermute(blocks, axis, pairs)  20.7 us
    ppermute x5, starting transfers between devices, butterfly_sum_gather(): total = total + lax.ppermute(total, axis, pairs)  14.8 us
    ppermute x5, waiting for transfers between devices, butterfly_sum_gather(): total = total + lax.ppermute(total, axis, pairs)  9.87 us
    ppermute x7, waiting for transfers between devices, butterfly_sum(): value = value + lax.ppermute(value, axis, partners(size, step))  7.48 us
    ppermute x5, waiting for transfers between devices, butterfly_sum_gather(): lax.ppermute(blocks, axis, pairs)  6.05 us
    ppermute x2, starting transfers between devices, x_ring_sum(): value = value + lax.ppermute(value, ('xlo', 'xhi'), pairs)  4.96 us
    ppermute x2, waiting for transfers between devices, x_ring_sum(): value = value + lax.ppermute(value, ('xlo', 'xhi'), pairs)  4.58 us
  transfers between devices with their start and end apart: 19, of which 12 were waited for; matrix products, arithmetic and copies ran while one was open for 6% of the time, Pallas kernels for 0%

profile of v9, /device:TPU:1, one launch (start us, length us, event | category | flops | bytes accessed | tf_op | source)
XLA Modules:
  0.0 120.4 jit_solution(7210680255009695919)
XLA Ops:
  0.0 2.1 %fusion.5 = f32[16,128,16]{1,0,2:T(8,128)S(1)} fusion(bf16[128,16,256]{2,1,0:T(8,128)(2,1)} %param.13, bf16[16,256]{1,0:T(8,128)(2,1)} %param.14), kind=kOutput, calls=%fused_computation.14 | convolution fusion | flops 16777216 | bytes 1187840 | tf_op jit(solution)/shard_map/un,ptn->upt/dot_general | solution.py:60
  4.1 4.0 %collective-permute-start = (f32[16,2048]{1,0:T(8,128)S(1)}, f32[16,2048]{1,0:T(8,128)S(1)}, u32[]{:S(2)}, u32[]{:S(2)}) collective-permute-start(f32[16,2048]{1,0:T(8,128)S(1)} %bitcast.42), channel_id=1, source_target_pairs={{0,4},{4,0},{8,12},{12,8},{16,20},{20,16},{24,28},{28,24},{1,5},{5... | collective-permute-start | bytes 393224 | tf_op jit(solution)/shard_map/ppermute | solution.py:46
  8.1 1.9 %collective-permute-start.1 = (bf16[10,256]{1,0:T(8,128)(2,1)}, bf16[10,256]{1,0:T(8,128)(2,1)S(1)}, u32[]{:S(2)}, u32[]{:S(2)}) collective-permute-start(bf16[10,256]{1,0:T(8,128)(2,1)} %param.16), channel_id=1, source_target_pairs={{0,4},{4,0},{8,12},{12,8},{16,20},{20,16},{24,28},{28,24},{1,5},{5... | collective-permute-start | bytes 15368 | tf_op jit(solution)/shard_map/ppermute | solution.py:47
  10.1 2.7 %collective-permute-done.1 = bf16[10,256]{1,0:T(8,128)(2,1)S(1)} collective-permute-done((bf16[10,256]{1,0:T(8,128)(2,1)}, bf16[10,256]{1,0:T(8,128)(2,1)S(1)}, u32[]{:S(2)}, u32[]{:S(2)}) %collective-permute-start.1) | collective-permute-done | bytes 5152 | tf_op jit(solution)/shard_map/ppermute | solution.py:47
  13.5 4.2 %collective-permute-start.2 = (f32[16,2048]{1,0:T(8,128)S(1)}, f32[16,2048]{1,0:T(8,128)S(1)}, u32[]{:S(2)}, u32[]{:S(2)}) collective-permute-start(f32[16,2048]{1,0:T(8,128)S(1)} %fusion.26), channel_id=1, source_target_pairs={{0,8},{4,12},{8,0},{12,4},{16,24},{20,28},{24,16},{28,20},{1,9},{5... | collective-permute-start | bytes 393224 | tf_op jit(solution)/shard_map/ppermute | solution.py:46
  17.7 2.0 %collective-permute-start.3 = (bf16[20,256]{1,0:T(8,128)(2,1)S(1)}, bf16[20,256]{1,0:T(8,128)(2,1)S(1)}, u32[]{:S(2)}, u32[]{:S(2)}) collective-permute-start(bf16[20,256]{1,0:T(8,128)(2,1)S(1)} %pad_maximum_fusion.4), channel_id=1, source_target_pairs={{0,8},{4,12},{8,0},{12,4},{16,24},{20,28},{24,16},{28,20},{1,9},{5... | collective-permute-start | bytes 30728 | tf_op jit(solution)/shard_map/ppermute | solution.py:47
  19.7 3.4 %collective-permute-done.3 = bf16[20,256]{1,0:T(8,128)(2,1)S(1)} collective-permute-done((bf16[20,256]{1,0:T(8,128)(2,1)S(1)}, bf16[20,256]{1,0:T(8,128)(2,1)S(1)}, u32[]{:S(2)}, u32[]{:S(2)}) %collective-permute-start.3) | collective-permute-done | bytes 10272 | tf_op jit(solution)/shard_map/ppermute | solution.py:47
  23.1 5.1 %collective-permute-start.5 = (bf16[40,256]{1,0:T(8,128)(2,1)S(1)}, bf16[40,256]{1,0:T(8,128)(2,1)S(1)}, u32[]{:S(2)}, u32[]{:S(2)}) collective-permute-start(bf16[40,256]{1,0:T(8,128)(2,1)S(1)} %pad_maximum_fusion.3), channel_id=1, source_target_pairs={{0,24},{4,28},{8,16},{12,20},{16,8},{20,12},{24,0},{28,4},{1,25},{... | collective-permute-start | bytes 61448 | tf_op jit(solution)/shard_map/ppermute | solution.py:47
  28.3 2.3 %collective-permute-start.4 = (f32[16,2048]{1,0:T(8,128)S(1)}, f32[16,2048]{1,0:T(8,128)S(1)}, u32[]{:S(2)}, u32[]{:S(2)}) collective-permute-start(f32[16,2048]{1,0:T(8,128)S(1)} %add.121), channel_id=1, source_target_pairs={{0,24},{4,28},{8,16},{12,20},{16,8},{20,12},{24,0},{28,4},{1,25},{... | collective-permute-start | bytes 393224 | tf_op jit(solution)/shard_map/ppermute | solution.py:46
  30.5 2.5 %fusion = f32[16,128,48]{1,0,2:T(8,128)S(1)} fusion(bf16[128,48,256]{2,1,0:T(8,128)(2,1)S(1)} %bitcast.38, bf16[16,256]{1,0:T(8,128)(2,1)} %param.14), kind=kOutput, calls=%fused_computation.5 | convolution fusion | flops 50331648 | bytes 3547136 | tf_op jit(solution)/shard_map/vn,pkn->vpk/dot_general | solution.py:67
  33.0 3.4 %collective-permute-done.4 = f32[16,2048]{1,0:T(8,128)S(1)} collective-permute-done((f32[16,2048]{1,0:T(8,128)S(1)}, f32[16,2048]{1,0:T(8,128)S(1)}, u32[]{:S(2)}, u32[]{:S(2)}) %collective-permute-start.4) | collective-permute-done | bytes 131104 | tf_op jit(solution)/shard_map/ppermute | solution.py:46
  36.4 4.4 %collective-permute-start.7 = (bf16[80,256]{1,0:T(8,128)(2,1)S(1)}, bf16[80,256]{1,0:T(8,128)(2,1)S(1)}, u32[]{:S(2)}, u32[]{:S(2)}) collective-permute-start(bf16[80,256]{1,0:T(8,128)(2,1)S(1)} %pad_maximum_fusion.2), channel_id=1, source_target_pairs={{0,2},{2,0},{1,3},{3,1},{4,6},{6,4},{5,7},{7,5},{8,10},{10,8},{9,1... | collective-permute-start | bytes 122888 | tf_op jit(solution)/shard_map/ppermute | solution.py:47
  40.8 2.4 %collective-permute-start.6 = (f32[16,2048]{1,0:T(8,128)S(1)}, f32[16,2048]{1,0:T(8,128)S(1)}, u32[]{:S(2)}, u32[]{:S(2)}) collective-permute-start(f32[16,2048]{1,0:T(8,128)S(1)} %add.122), channel_id=1, source_target_pairs={{0,2},{2,0},{1,3},{3,1},{4,6},{6,4},{5,7},{7,5},{8,10},{10,8},{9,1... | collective-permute-start | bytes 393224 | tf_op jit(solution)/shard_map/ppermute | solution.py:46
  43.3 5.2 %collective-permute-done.6 = f32[16,2048]{1,0:T(8,128)S(1)} collective-permute-done((f32[16,2048]{1,0:T(8,128)S(1)}, f32[16,2048]{1,0:T(8,128)S(1)}, u32[]{:S(2)}, u32[]{:S(2)}) %collective-permute-start.6) | collective-permute-done | bytes 131104 | tf_op jit(solution)/shard_map/ppermute | solution.py:46
  48.5 7.3 %collective-permute-start.9 = (bf16[160,256]{1,0:T(8,128)(2,1)S(1)}, bf16[160,256]{1,0:T(8,128)(2,1)S(1)}, u32[]{:S(2)}, u32[]{:S(2)}) collective-permute-start(bf16[160,256]{1,0:T(8,128)(2,1)S(1)} %pad_maximum_fusion.1), channel_id=1, source_target_pairs={{0,1},{1,0},{2,3},{3,2},{4,5},{5,4},{6,7},{7,6},{8,9},{9,8},{10,11... | collective-permute-start | bytes 245768 | tf_op jit(solution)/shard_map/ppermute | solution.py:47
  55.8 1.9 %collective-permute-start.8 = (f32[16,2048]{1,0:T(8,128)S(1)}, f32[16,2048]{1,0:T(8,128)S(1)}, u32[]{:S(2)}, u32[]{:S(2)}) collective-permute-start(f32[16,2048]{1,0:T(8,128)S(1)} %add.123), channel_id=1, source_target_pairs={{0,1},{1,0},{2,3},{3,2},{4,5},{5,4},{6,7},{7,6},{8,9},{9,8},{10,11... | collective-permute-start | bytes 393224 | tf_op jit(solution)/shard_map/ppermute | solution.py:46
  57.8 1.2 %collective-permute-done.8 = f32[16,2048]{1,0:T(8,128)S(1)} collective-permute-done((f32[16,2048]{1,0:T(8,128)S(1)}, f32[16,2048]{1,0:T(8,128)S(1)}, u32[]{:S(2)}, u32[]{:S(2)}) %collective-permute-start.8) | collective-permute-done | bytes 131104 | tf_op jit(solution)/shard_map/ppermute | solution.py:46
  59.5 4.0 %collective-permute-start.10 = (f32[16,48]{1,0:T(8,128)S(1)}, f32[16,48]{1,0:T(8,128)S(1)}, u32[]{:S(2)}, u32[]{:S(2)}) collective-permute-start(f32[16,48]{1,0:T(8,128)S(1)} %convolution_multiply_fusion.1), channel_id=1, source_target_pairs={{0,64},{64,0},{128,192},{192,128},{256,320},{320,256},{384,448},{4... | collective-permute-start | bytes 9224 | tf_op jit(solution)/shard_map/ppermute | solution.py:30
  64.9 5.8 %collective-permute-start.11 = (f32[16,48]{1,0:T(8,128)S(1)}, f32[16,48]{1,0:T(8,128)S(1)}, u32[]{:S(2)}, u32[]{:S(2)}) collective-permute-start(f32[16,48]{1,0:T(8,128)S(1)} %add.125), channel_id=1, source_target_pairs={{0,128},{64,192},{128,0},{192,64},{256,384},{320,448},{384,256},{4... | collective-permute-start | bytes 9224 | tf_op jit(solution)/shard_map/ppermute | solution.py:30
  70.8 1.0 collective-permute-done.11
  71.8 8.2 %collective-permute-start.12 = (f32[16,48]{1,0:T(8,128)S(1)}, f32[16,48]{1,0:T(8,128)S(1)}, u32[]{:S(2)}, u32[]{:S(2)}) collective-permute-start(f32[16,48]{1,0:T(8,128)S(1)} %add.126), channel_id=1, source_target_pairs={{0,384},{64,448},{128,256},{192,320},{256,128},{320,192},{384,0},{... | collective-permute-start | bytes 9224 | tf_op jit(solution)/shard_map/ppermute | solution.py:30
  81.4 4.3 %collective-permute-start.13 = (f32[16,48]{1,0:T(8,128)S(1)}, f32[16,48]{1,0:T(8,128)S(1)}, u32[]{:S(2)}, u32[]{:S(2)}) collective-permute-start(f32[16,48]{1,0:T(8,128)S(1)} %add.127), channel_id=1, source_target_pairs={{0,4},{4,0},{8,12},{12,8},{16,20},{20,16},{24,28},{28,24},{1,5},{5... | collective-permute-start | bytes 9224 | tf_op jit(solution)/shard_map/ppermute | solution.py:30
  85.7 1.0 collective-permute-done.13
  86.7 3.7 %collective-permute-start.14 = (f32[16,48]{1,0:T(8,128)S(1)}, f32[16,48]{1,0:T(8,128)S(1)}, u32[]{:S(2)}, u32[]{:S(2)}) collective-permute-start(f32[16,48]{1,0:T(8,128)S(1)} %add.128), channel_id=1, source_target_pairs={{0,8},{4,12},{8,0},{12,4},{16,24},{20,28},{24,16},{28,20},{1,9},{5... | collective-permute-start | bytes 9224 | tf_op jit(solution)/shard_map/ppermute | solution.py:30
  90.4 1.6 %collective-permute-done.14 = f32[16,48]{1,0:T(8,128)S(1)} collective-permute-done((f32[16,48]{1,0:T(8,128)S(1)}, f32[16,48]{1,0:T(8,128)S(1)}, u32[]{:S(2)}, u32[]{:S(2)}) %collective-permute-start.14) | collective-permute-done | bytes 3104 | tf_op jit(solution)/shard_map/ppermute | solution.py:30
  92.0 3.1 %collective-permute-start.15 = (f32[16,48]{1,0:T(8,128)S(1)}, f32[16,48]{1,0:T(8,128)S(1)}, u32[]{:S(2)}, u32[]{:S(2)}) collective-permute-start(f32[16,48]{1,0:T(8,128)S(1)} %add.129), channel_id=1, source_target_pairs={{0,24},{4,28},{8,16},{12,20},{16,8},{20,12},{24,0},{28,4},{1,25},{... | collective-permute-start | bytes 9224 | tf_op jit(solution)/shard_map/ppermute | solution.py:30
  95.1 3.3 %collective-permute-done.15 = f32[16,48]{1,0:T(8,128)S(1)} collective-permute-done((f32[16,48]{1,0:T(8,128)S(1)}, f32[16,48]{1,0:T(8,128)S(1)}, u32[]{:S(2)}, u32[]{:S(2)}) %collective-permute-start.15) | collective-permute-done | bytes 3104 | tf_op jit(solution)/shard_map/ppermute | solution.py:30
  98.5 2.2 %collective-permute-start.16 = (f32[16,48]{1,0:T(8,128)S(1)}, f32[16,48]{1,0:T(8,128)S(1)}, u32[]{:S(2)}, u32[]{:S(2)}) collective-permute-start(f32[16,48]{1,0:T(8,128)S(1)} %add.130), channel_id=1, source_target_pairs={{0,32},{2,34},{32,0},{34,2},{1,33},{3,35},{33,1},{35,3},{4,36},{6,... | collective-permute-start | bytes 9224 | tf_op jit(solution)/shard_map/ppermute | solution.py:37
  100.7 2.4 %collective-permute-done.16 = f32[16,48]{1,0:T(8,128)S(1)} collective-permute-done((f32[16,48]{1,0:T(8,128)S(1)}, f32[16,48]{1,0:T(8,128)S(1)}, u32[]{:S(2)}, u32[]{:S(2)}) %collective-permute-start.16) | collective-permute-done | bytes 3104 | tf_op jit(solution)/shard_map/ppermute | solution.py:37
  103.1 2.8 %collective-permute-start.17 = (f32[16,48]{1,0:T(8,128)S(1)}, f32[16,48]{1,0:T(8,128)S(1)}, u32[]{:S(2)}, u32[]{:S(2)}) collective-permute-start(f32[16,48]{1,0:T(8,128)S(1)} %add.131), channel_id=1, source_target_pairs={{0,34},{2,32},{32,2},{34,0},{1,35},{3,33},{33,3},{35,1},{4,38},{6,... | collective-permute-start | bytes 9224 | tf_op jit(solution)/shard_map/ppermute | solution.py:37
  106.6 2.1 %collective-permute-done.17 = f32[16,48]{1,0:T(8,128)S(1)} collective-permute-done((f32[16,48]{1,0:T(8,128)S(1)}, f32[16,48]{1,0:T(8,128)S(1)}, u32[]{:S(2)}, u32[]{:S(2)}) %collective-permute-start.17) | collective-permute-done | bytes 3104 | tf_op jit(solution)/shard_map/ppermute | solution.py:37
  108.7 9.9 %collective-permute-start.18 = (f32[16,48]{1,0:T(8,128)S(1)}, f32[16,48]{1,0:T(8,128)S(1)}, u32[]{:S(2)}, u32[]{:S(2)}) collective-permute-start(f32[16,48]{1,0:T(8,128)S(1)} %add.132), channel_id=1, source_target_pairs={{0,1},{1,0},{2,3},{3,2},{4,5},{5,4},{6,7},{7,6},{8,9},{9,8},{10,11... | collective-permute-start | bytes 9224 | tf_op jit(solution)/shard_map/ppermute | solution.py:30
  (59 shorter events, 8.6 us)
Async XLA Ops:
  0.0 30.5 %copy-start = (bf16[128,3,16,256]{3,2,1,0:T(8,128)(2,1)S(1)}, bf16[128,3,16,256]{3,2,1,0:T(8,128)(2,1)}, u32[]{:S(2)}) copy-start(bf16[128,3,16,256]{3,2,1,0:T(8,128)(2,1)} %param.12) | copy-start | bytes 9437188
  0.0 43.2 %copy-start.3 = (s32[10]{0:T(128)S(1)}, s32[10]{0:T(128)}, u32[]{:S(2)}) copy-start(s32[10]{0:T(128)} %param.18) | copy-start | bytes 124
  2.1 55.7 %copy-start.2 = (s32[320,2]{0,1:T(2,128)S(1)}, s32[320,2]{0,1:T(2,128)}, u32[]{:S(2)}) copy-start(s32[320,2]{0,1:T(2,128)} %param.17) | copy-start | bytes 7684
  4.1 9.3 %collective-permute-start = (f32[16,2048]{1,0:T(8,128)S(1)}, f32[16,2048]{1,0:T(8,128)S(1)}, u32[]{:S(2)}, u32[]{:S(2)}) collective-permute-start(f32[16,2048]{1,0:T(8,128)S(1)} %bitcast.42), channel_id=1, source_target_pairs={{0,4},{4,0},{8,12},{12,8},{16,20},{20,16},{24,28},{28,24},{1,5},{5... | collective-permute-start | bytes 393224 | tf_op jit(solution)/shard_map/ppermute | solution.py:46
  8.1 4.6 %collective-permute-start.1 = (bf16[10,256]{1,0:T(8,128)(2,1)}, bf16[10,256]{1,0:T(8,128)(2,1)S(1)}, u32[]{:S(2)}, u32[]{:S(2)}) collective-permute-start(bf16[10,256]{1,0:T(8,128)(2,1)} %param.16), channel_id=1, source_target_pairs={{0,4},{4,0},{8,12},{12,8},{16,20},{20,16},{24,28},{28,24},{1,5},{5... | collective-permute-start | bytes 15368 | tf_op jit(solution)/shard_map/ppermute | solution.py:47
  13.5 9.6 %collective-permute-start.2 = (f32[16,2048]{1,0:T(8,128)S(1)}, f32[16,2048]{1,0:T(8,128)S(1)}, u32[]{:S(2)}, u32[]{:S(2)}) collective-permute-start(f32[16,2048]{1,0:T(8,128)S(1)} %fusion.26), channel_id=1, source_target_pairs={{0,8},{4,12},{8,0},{12,4},{16,24},{20,28},{24,16},{28,20},{1,9},{5... | collective-permute-start | bytes 393224 | tf_op jit(solution)/shard_map/ppermute | solution.py:46
  17.7 5.3 %collective-permute-start.3 = (bf16[20,256]{1,0:T(8,128)(2,1)S(1)}, bf16[20,256]{1,0:T(8,128)(2,1)S(1)}, u32[]{:S(2)}, u32[]{:S(2)}) collective-permute-start(bf16[20,256]{1,0:T(8,128)(2,1)S(1)} %pad_maximum_fusion.4), channel_id=1, source_target_pairs={{0,8},{4,12},{8,0},{12,4},{16,24},{20,28},{24,16},{28,20},{1,9},{5... | collective-permute-start | bytes 30728 | tf_op jit(solution)/shard_map/ppermute | solution.py:47
  23.1 9.9 %collective-permute-start.5 = (bf16[40,256]{1,0:T(8,128)(2,1)S(1)}, bf16[40,256]{1,0:T(8,128)(2,1)S(1)}, u32[]{:S(2)}, u32[]{:S(2)}) collective-permute-start(bf16[40,256]{1,0:T(8,128)(2,1)S(1)} %pad_maximum_fusion.3), channel_id=1, source_target_pairs={{0,24},{4,28},{8,16},{12,20},{16,8},{20,12},{24,0},{28,4},{1,25},{... | collective-permute-start | bytes 61448 | tf_op jit(solution)/shard_map/ppermute | solution.py:47
  28.3 8.1 %collective-permute-start.4 = (f32[16,2048]{1,0:T(8,128)S(1)}, f32[16,2048]{1,0:T(8,128)S(1)}, u32[]{:S(2)}, u32[]{:S(2)}) collective-permute-start(f32[16,2048]{1,0:T(8,128)S(1)} %add.121), channel_id=1, source_target_pairs={{0,24},{4,28},{8,16},{12,20},{16,8},{20,12},{24,0},{28,4},{1,25},{... | collective-permute-start | bytes 393224 | tf_op jit(solution)/shard_map/ppermute | solution.py:46
  30.5 49.5 %copy-start.1 = (s32[24]{0:T(128)S(1)}, s32[24]{0:T(128)}, u32[]{:S(2)}) copy-start(s32[24]{0:T(128)} %param.19) | copy-start | bytes 292
  36.4 6.8 %collective-permute-start.7 = (bf16[80,256]{1,0:T(8,128)(2,1)S(1)}, bf16[80,256]{1,0:T(8,128)(2,1)S(1)}, u32[]{:S(2)}, u32[]{:S(2)}) collective-permute-start(bf16[80,256]{1,0:T(8,128)(2,1)S(1)} %pad_maximum_fusion.2), channel_id=1, source_target_pairs={{0,2},{2,0},{1,3},{3,1},{4,6},{6,4},{5,7},{7,5},{8,10},{10,8},{9,1... | collective-permute-start | bytes 122888 | tf_op jit(solution)/shard_map/ppermute | solution.py:47
  40.8 7.7 %collective-permute-start.6 = (f32[16,2048]{1,0:T(8,128)S(1)}, f32[16,2048]{1,0:T(8,128)S(1)}, u32[]{:S(2)}, u32[]{:S(2)}) collective-permute-start(f32[16,2048]{1,0:T(8,128)S(1)} %add.122), channel_id=1, source_target_pairs={{0,2},{2,0},{1,3},{3,1},{4,6},{6,4},{5,7},{7,5},{8,10},{10,8},{9,1... | collective-permute-start | bytes 393224 | tf_op jit(solution)/shard_map/ppermute | solution.py:46
  48.5 9.3 %collective-permute-start.9 = (bf16[160,256]{1,0:T(8,128)(2,1)S(1)}, bf16[160,256]{1,0:T(8,128)(2,1)S(1)}, u32[]{:S(2)}, u32[]{:S(2)}) collective-permute-start(bf16[160,256]{1,0:T(8,128)(2,1)S(1)} %pad_maximum_fusion.1), channel_id=1, source_target_pairs={{0,1},{1,0},{2,3},{3,2},{4,5},{5,4},{6,7},{7,6},{8,9},{9,8},{10,11... | collective-permute-start | bytes 245768 | tf_op jit(solution)/shard_map/ppermute | solution.py:47
  55.8 3.2 %collective-permute-start.8 = (f32[16,2048]{1,0:T(8,128)S(1)}, f32[16,2048]{1,0:T(8,128)S(1)}, u32[]{:S(2)}, u32[]{:S(2)}) collective-permute-start(f32[16,2048]{1,0:T(8,128)S(1)} %add.123), channel_id=1, source_target_pairs={{0,1},{1,0},{2,3},{3,2},{4,5},{5,4},{6,7},{7,6},{8,9},{9,8},{10,11... | collective-permute-start | bytes 393224 | tf_op jit(solution)/shard_map/ppermute | solution.py:46
  59.5 5.4 %collective-permute-start.10 = (f32[16,48]{1,0:T(8,128)S(1)}, f32[16,48]{1,0:T(8,128)S(1)}, u32[]{:S(2)}, u32[]{:S(2)}) collective-permute-start(f32[16,48]{1,0:T(8,128)S(1)} %convolution_multiply_fusion.1), channel_id=1, source_target_pairs={{0,64},{64,0},{128,192},{192,128},{256,320},{320,256},{384,448},{4... | collective-permute-start | bytes 9224 | tf_op jit(solution)/shard_map/ppermute | solution.py:30
  64.9 6.8 %collective-permute-start.11 = (f32[16,48]{1,0:T(8,128)S(1)}, f32[16,48]{1,0:T(8,128)S(1)}, u32[]{:S(2)}, u32[]{:S(2)}) collective-permute-start(f32[16,48]{1,0:T(8,128)S(1)} %add.125), channel_id=1, source_target_pairs={{0,128},{64,192},{128,0},{192,64},{256,384},{320,448},{384,256},{4... | collective-permute-start | bytes 9224 | tf_op jit(solution)/shard_map/ppermute | solution.py:30
  71.8 9.6 %collective-permute-start.12 = (f32[16,48]{1,0:T(8,128)S(1)}, f32[16,48]{1,0:T(8,128)S(1)}, u32[]{:S(2)}, u32[]{:S(2)}) collective-permute-start(f32[16,48]{1,0:T(8,128)S(1)} %add.126), channel_id=1, source_target_pairs={{0,384},{64,448},{128,256},{192,320},{256,128},{320,192},{384,0},{... | collective-permute-start | bytes 9224 | tf_op jit(solution)/shard_map/ppermute | solution.py:30
  81.4 5.3 %collective-permute-start.13 = (f32[16,48]{1,0:T(8,128)S(1)}, f32[16,48]{1,0:T(8,128)S(1)}, u32[]{:S(2)}, u32[]{:S(2)}) collective-permute-start(f32[16,48]{1,0:T(8,128)S(1)} %add.127), channel_id=1, source_target_pairs={{0,4},{4,0},{8,12},{12,8},{16,20},{20,16},{24,28},{28,24},{1,5},{5... | collective-permute-start | bytes 9224 | tf_op jit(solution)/shard_map/ppermute | solution.py:30
  86.7 5.3 %collective-permute-start.14 = (f32[16,48]{1,0:T(8,128)S(1)}, f32[16,48]{1,0:T(8,128)S(1)}, u32[]{:S(2)}, u32[]{:S(2)}) collective-permute-start(f32[16,48]{1,0:T(8,128)S(1)} %add.128), channel_id=1, source_target_pairs={{0,8},{4,12},{8,0},{12,4},{16,24},{20,28},{24,16},{28,20},{1,9},{5... | collective-permute-start | bytes 9224 | tf_op jit(solution)/shard_map/ppermute | solution.py:30
  92.0 6.5 %collective-permute-start.15 = (f32[16,48]{1,0:T(8,128)S(1)}, f32[16,48]{1,0:T(8,128)S(1)}, u32[]{:S(2)}, u32[]{:S(2)}) collective-permute-start(f32[16,48]{1,0:T(8,128)S(1)} %add.129), channel_id=1, source_target_pairs={{0,24},{4,28},{8,16},{12,20},{16,8},{20,12},{24,0},{28,4},{1,25},{... | collective-permute-start | bytes 9224 | tf_op jit(solution)/shard_map/ppermute | solution.py:30
  98.5 4.7 %collective-permute-start.16 = (f32[16,48]{1,0:T(8,128)S(1)}, f32[16,48]{1,0:T(8,128)S(1)}, u32[]{:S(2)}, u32[]{:S(2)}) collective-permute-start(f32[16,48]{1,0:T(8,128)S(1)} %add.130), channel_id=1, source_target_pairs={{0,32},{2,34},{32,0},{34,2},{1,33},{3,35},{33,1},{35,3},{4,36},{6,... | collective-permute-start | bytes 9224 | tf_op jit(solution)/shard_map/ppermute | solution.py:37
  103.1 5.6 %collective-permute-start.17 = (f32[16,48]{1,0:T(8,128)S(1)}, f32[16,48]{1,0:T(8,128)S(1)}, u32[]{:S(2)}, u32[]{:S(2)}) collective-permute-start(f32[16,48]{1,0:T(8,128)S(1)} %add.131), channel_id=1, source_target_pairs={{0,34},{2,32},{32,2},{34,0},{1,35},{3,33},{33,3},{35,1},{4,38},{6,... | collective-permute-start | bytes 9224 | tf_op jit(solution)/shard_map/ppermute | solution.py:37
  108.7 10.8 %collective-permute-start.18 = (f32[16,48]{1,0:T(8,128)S(1)}, f32[16,48]{1,0:T(8,128)S(1)}, u32[]{:S(2)}, u32[]{:S(2)}) collective-permute-start(f32[16,48]{1,0:T(8,128)S(1)} %add.132), channel_id=1, source_target_pairs={{0,1},{1,0},{2,3},{3,2},{4,5},{5,4},{6,7},{7,6},{8,9},{9,8},{10,11... | collective-permute-start | bytes 9224 | tf_op jit(solution)/shard_map/ppermute | solution.py:30

commit v10 on v8

--- a/solution.py
+++ b/solution.py
@@ -38,15 +38,21 @@
     return value
 
 
-def butterfly_sum_gather(total, blocks, rounds):
-    for axis, size in rounds:
-        step = 1
-        while step < size:
-            pairs = partners(size, step)
-            total = total + lax.ppermute(total, axis, pairs)
-            blocks = jnp.concatenate([blocks, lax.ppermute(blocks, axis, pairs)], axis=0)
-            total, blocks = lax.optimization_barrier((total, blocks))
-            step *= 2
+def steps_of(rounds):
+    return [(axis, size, 1 << k) for axis, size in rounds for k in range(size.bit_length() - 1)]
+
+
+def gather_round(blocks, step):
+    axis, size, distance = step
+    return jnp.concatenate([blocks, lax.ppermute(blocks, axis, partners(size, distance))], axis=0)
+
+
+def butterfly_sum_gather(total, blocks, steps):
+    for i, (axis, size, distance) in enumerate(steps):
+        total = total + lax.ppermute(total, axis, partners(size, distance))
+        if i + 1 < len(steps):
+            blocks = gather_round(blocks, steps[i + 1])
+        total, blocks = lax.optimization_barrier((total, blocks))
     return total, blocks
 
 
@@ -57,12 +63,15 @@
     n_aux = lax.axis_size("z") * lax.axis_size("xlo")
     scale = 1.0 / (8.0 * jnp.sqrt(jnp.float32(rows * n_aux)))
 
+    steps = steps_of((("y", 8), ("xhi", 2), ("core", 2)))
+    first = gather_round(spin_dens, steps[0])
     cou_part = jnp.einsum("un,ptn->upt", coef_t, cou_ints, preferred_element_type=jnp.float32)
+    cou_part, first = lax.optimization_barrier((cou_part, first))
     fitted = jnp.einsum("upt,tu->p", cou_part, active_rdm, precision=HIGH)
     folded = jnp.einsum("upw,vw->uvp", cou_part, active_rdm, precision=HIGH)
     eye = jnp.eye(width, dtype=jnp.float32)
     weight = (eye[:, :, None] * fitted[None, None, :] - 1.5 * folded).reshape(width, width * rows)
-    weight, every_dens = butterfly_sum_gather(weight, spin_dens, (("y", 8), ("xhi", 2), ("core", 2)))
+    weight, every_dens = butterfly_sum_gather(weight, first, steps)
 
     soc_part = jnp.einsum(
         "vn,pkn->vpk", coef_t, soc_ints.reshape(rows, 3 * width, -1), preferred_element_type=jnp.float32

time: 121 us -> 123 us (1.017)
  the two profiles are of different devices: /device:TPU:8 before, /device:TPU:24 now
where the time goes in v10:
time: 123 us; the launch traced here: 122 us
  starting transfers between devices  66.8 us (54%)
  waiting for transfers between devices  43.4 us (35%)
  matrix products  6.96 us (6%)
  local copies, waits for them, and re-layouts  3.63 us (3%)
    ppermute x7, starting transfers between devices, butterfly_sum(): value = value + lax.ppermute(value, axis, partners(size, step))  28.8 us
    ppermute x5, starting transfers between devices, gather_round(): lax.ppermute(blocks, axis, partners(size, distance))  20 us
    ppermute x5, waiting for transfers between devices, butterfly_sum_gather(): total = total + lax.ppermute(total, axis, partners(size, distance))  16.7 us
    ppermute x7, waiting for transfers between devices, butterfly_sum(): value = value + lax.ppermute(value, axis, partners(size, step))  16.2 us
    ppermute x5, starting transfers between devices, butterfly_sum_gather(): total = total + lax.ppermute(total, axis, partners(size, distance))  12.4 us
    ppermute x2, starting transfers between devices, x_ring_sum(): value = value + lax.ppermute(value, ('xlo', 'xhi'), pairs)  5.54 us
    ppermute x2, waiting for transfers between devices, x_ring_sum(): value = value + lax.ppermute(value, ('xlo', 'xhi'), pairs)  5.37 us
    ppermute x5, waiting for transfers between devices, gather_round(): lax.ppermute(blocks, axis, partners(size, distance))  5.13 us
  transfers between devices with their start and end apart: 19, of which 16 were waited for; matrix products, arithmetic and copies ran while one was open for 6% of the time, Pallas kernels for 0%

profile of v10, /device:TPU:24, one launch (start us, length us, event | category | flops | bytes accessed | tf_op | source)
XLA Modules:
  0.0 122.3 jit_solution(7925124607793794304)
XLA Ops:
  0.0 2.6 %collective-permute-start = (bf16[10,256]{1,0:T(8,128)(2,1)}, bf16[10,256]{1,0:T(8,128)(2,1)S(1)}, u32[]{:S(2)}, u32[]{:S(2)}) collective-permute-start(bf16[10,256]{1,0:T(8,128)(2,1)} %param.16), channel_id=1, source_target_pairs={{0,4},{4,0},{8,12},{12,8},{16,20},{20,16},{24,28},{28,24},{1,5},{5... | collective-permute-start | bytes 15368 | tf_op jit(solution)/shard_map/ppermute | solution.py:47
  2.6 1.9 %fusion.5 = f32[16,128,16]{1,0,2:T(8,128)S(1)} fusion(bf16[128,16,256]{2,1,0:T(8,128)(2,1)} %param.13, bf16[16,256]{1,0:T(8,128)(2,1)} %param.14), kind=kOutput, calls=%fused_computation.14 | convolution fusion | flops 16777216 | bytes 1187840 | tf_op jit(solution)/shard_map/un,ptn->upt/dot_general | solution.py:68
  4.5 1.5 %collective-permute-done = bf16[10,256]{1,0:T(8,128)(2,1)S(1)} collective-permute-done((bf16[10,256]{1,0:T(8,128)(2,1)}, bf16[10,256]{1,0:T(8,128)(2,1)S(1)}, u32[]{:S(2)}, u32[]{:S(2)}) %collective-permute-start) | collective-permute-done | bytes 5152 | tf_op jit(solution)/shard_map/ppermute | solution.py:47
  8.8 2.4 %collective-permute-start.1 = (f32[16,2048]{1,0:T(8,128)S(1)}, f32[16,2048]{1,0:T(8,128)S(1)}, u32[]{:S(2)}, u32[]{:S(2)}) collective-permute-start(f32[16,2048]{1,0:T(8,128)S(1)} %bitcast.42), channel_id=1, source_target_pairs={{0,4},{4,0},{8,12},{12,8},{16,20},{20,16},{24,28},{28,24},{1,5},{5... | collective-permute-start | bytes 393224 | tf_op jit(solution)/shard_map/ppermute | solution.py:52
  11.1 7.6 %collective-permute-start.2 = (bf16[20,256]{1,0:T(8,128)(2,1)S(1)}, bf16[20,256]{1,0:T(8,128)(2,1)S(1)}, u32[]{:S(2)}, u32[]{:S(2)}) collective-permute-start(bf16[20,256]{1,0:T(8,128)(2,1)S(1)} %pad_maximum_fusion.4), channel_id=1, source_target_pairs={{0,8},{4,12},{8,0},{12,4},{16,24},{20,28},{24,16},{28,20},{1,9},{5... | collective-permute-start | bytes 30728 | tf_op jit(solution)/shard_map/ppermute | solution.py:47
  18.7 1.7 %collective-permute-done.2 = bf16[20,256]{1,0:T(8,128)(2,1)S(1)} collective-permute-done((bf16[20,256]{1,0:T(8,128)(2,1)S(1)}, bf16[20,256]{1,0:T(8,128)(2,1)S(1)}, u32[]{:S(2)}, u32[]{:S(2)}) %collective-permute-start.2) | collective-permute-done | bytes 10272 | tf_op jit(solution)/shard_map/ppermute | solution.py:47
  20.4 2.9 %collective-permute-start.4 = (bf16[40,256]{1,0:T(8,128)(2,1)S(1)}, bf16[40,256]{1,0:T(8,128)(2,1)S(1)}, u32[]{:S(2)}, u32[]{:S(2)}) collective-permute-start(bf16[40,256]{1,0:T(8,128)(2,1)S(1)} %pad_maximum_fusion.3), channel_id=1, source_target_pairs={{0,24},{4,28},{8,16},{12,20},{16,8},{20,12},{24,0},{28,4},{1,25},{... | collective-permute-start | bytes 61448 | tf_op jit(solution)/shard_map/ppermute | solution.py:47
  23.4 3.8 %collective-permute-start.3 = (f32[16,2048]{1,0:T(8,128)S(1)}, f32[16,2048]{1,0:T(8,128)S(1)}, u32[]{:S(2)}, u32[]{:S(2)}) collective-permute-start(f32[16,2048]{1,0:T(8,128)S(1)} %fusion.26), channel_id=1, source_target_pairs={{0,8},{4,12},{8,0},{12,4},{16,24},{20,28},{24,16},{28,20},{1,9},{5... | collective-permute-start | bytes 393224 | tf_op jit(solution)/shard_map/ppermute | solution.py:52
  28.7 3.9 %collective-permute-done.3 = f32[16,2048]{1,0:T(8,128)S(1)} collective-permute-done((f32[16,2048]{1,0:T(8,128)S(1)}, f32[16,2048]{1,0:T(8,128)S(1)}, u32[]{:S(2)}, u32[]{:S(2)}) %collective-permute-start.3) | collective-permute-done | bytes 131104 | tf_op jit(solution)/shard_map/ppermute | solution.py:52
  32.6 4.9 %collective-permute-start.6 = (bf16[80,256]{1,0:T(8,128)(2,1)S(1)}, bf16[80,256]{1,0:T(8,128)(2,1)S(1)}, u32[]{:S(2)}, u32[]{:S(2)}) collective-permute-start(bf16[80,256]{1,0:T(8,128)(2,1)S(1)} %pad_maximum_fusion.2), channel_id=1, source_target_pairs={{0,2},{2,0},{1,3},{3,1},{4,6},{6,4},{5,7},{7,5},{8,10},{10,8},{9,1... | collective-permute-start | bytes 122888 | tf_op jit(solution)/shard_map/ppermute | solution.py:47
  37.5 1.9 %collective-permute-start.5 = (f32[16,2048]{1,0:T(8,128)S(1)}, f32[16,2048]{1,0:T(8,128)S(1)}, u32[]{:S(2)}, u32[]{:S(2)}) collective-permute-start(f32[16,2048]{1,0:T(8,128)S(1)} %add.121), channel_id=1, source_target_pairs={{0,24},{4,28},{8,16},{12,20},{16,8},{20,12},{24,0},{28,4},{1,25},{... | collective-permute-start | bytes 393224 | tf_op jit(solution)/shard_map/ppermute | solution.py:52
  40.0 6.5 %collective-permute-done.5 = f32[16,2048]{1,0:T(8,128)S(1)} collective-permute-done((f32[16,2048]{1,0:T(8,128)S(1)}, f32[16,2048]{1,0:T(8,128)S(1)}, u32[]{:S(2)}, u32[]{:S(2)}) %collective-permute-start.5) | collective-permute-done | bytes 131104 | tf_op jit(solution)/shard_map/ppermute | solution.py:52
  46.5 1.9 %collective-permute-start.8 = (bf16[160,256]{1,0:T(8,128)(2,1)S(1)}, bf16[160,256]{1,0:T(8,128)(2,1)S(1)}, u32[]{:S(2)}, u32[]{:S(2)}) collective-permute-start(bf16[160,256]{1,0:T(8,128)(2,1)S(1)} %pad_maximum_fusion.1), channel_id=1, source_target_pairs={{0,1},{1,0},{2,3},{3,2},{4,5},{5,4},{6,7},{7,6},{8,9},{9,8},{10,11... | collective-permute-start | bytes 245768 | tf_op jit(solution)/shard_map/ppermute | solution.py:47
  48.4 2.4 %collective-permute-start.7 = (f32[16,2048]{1,0:T(8,128)S(1)}, f32[16,2048]{1,0:T(8,128)S(1)}, u32[]{:S(2)}, u32[]{:S(2)}) collective-permute-start(f32[16,2048]{1,0:T(8,128)S(1)} %add.122), channel_id=1, source_target_pairs={{0,2},{2,0},{1,3},{3,1},{4,6},{6,4},{5,7},{7,5},{8,10},{10,8},{9,1... | collective-permute-start | bytes 393224 | tf_op jit(solution)/shard_map/ppermute | solution.py:52
  50.9 1.8 %fusion = f32[16,128,48]{1,0,2:T(8,128)S(1)} fusion(bf16[128,48,256]{2,1,0:T(8,128)(2,1)S(1)} %bitcast.38, bf16[16,256]{1,0:T(8,128)(2,1)S(1)} %copy-done.2), kind=kOutput, calls=%fused_computation.5 | convolution fusion | flops 50331648 | bytes 3547136 | tf_op jit(solution)/shard_map/vn,pkn->vpk/dot_general | solution.py:76
  52.7 5.1 %collective-permute-done.7 = f32[16,2048]{1,0:T(8,128)S(1)} collective-permute-done((f32[16,2048]{1,0:T(8,128)S(1)}, f32[16,2048]{1,0:T(8,128)S(1)}, u32[]{:S(2)}, u32[]{:S(2)}) %collective-permute-start.7) | collective-permute-done | bytes 131104 | tf_op jit(solution)/shard_map/ppermute | solution.py:52
  57.8 1.9 %collective-permute-start.9 = (f32[16,2048]{1,0:T(8,128)S(1)}, f32[16,2048]{1,0:T(8,128)S(1)}, u32[]{:S(2)}, u32[]{:S(2)}) collective-permute-start(f32[16,2048]{1,0:T(8,128)S(1)} %add.123), channel_id=1, source_target_pairs={{0,1},{1,0},{2,3},{3,2},{4,5},{5,4},{6,7},{7,6},{8,9},{9,8},{10,11... | collective-permute-start | bytes 393224 | tf_op jit(solution)/shard_map/ppermute | solution.py:52
  61.5 2.1 %collective-permute-start.10 = (f32[16,48]{1,0:T(8,128)S(1)}, f32[16,48]{1,0:T(8,128)S(1)}, u32[]{:S(2)}, u32[]{:S(2)}) collective-permute-start(f32[16,48]{1,0:T(8,128)S(1)} %convolution_multiply_fusion.1), channel_id=1, source_target_pairs={{0,1},{1,0},{2,3},{3,2},{4,5},{5,4},{6,7},{7,6},{8,9},{9,8},{10,11... | collective-permute-start | bytes 9224 | tf_op jit(solution)/shard_map/ppermute | solution.py:30
  64.9 2.5 %collective-permute-start.11 = (f32[16,48]{1,0:T(8,128)S(1)}, f32[16,48]{1,0:T(8,128)S(1)}, u32[]{:S(2)}, u32[]{:S(2)}) collective-permute-start(f32[16,48]{1,0:T(8,128)S(1)} %add.125), channel_id=1, source_target_pairs={{0,32},{2,34},{32,0},{34,2},{1,33},{3,35},{33,1},{35,3},{4,36},{6,... | collective-permute-start | bytes 9224 | tf_op jit(solution)/shard_map/ppermute | solution.py:37
  67.5 3.0 %collective-permute-done.11 = f32[16,48]{1,0:T(8,128)S(1)} collective-permute-done((f32[16,48]{1,0:T(8,128)S(1)}, f32[16,48]{1,0:T(8,128)S(1)}, u32[]{:S(2)}, u32[]{:S(2)}) %collective-permute-start.11) | collective-permute-done | bytes 3104 | tf_op jit(solution)/shard_map/ppermute | solution.py:37
  70.5 3.0 %collective-permute-start.12 = (f32[16,48]{1,0:T(8,128)S(1)}, f32[16,48]{1,0:T(8,128)S(1)}, u32[]{:S(2)}, u32[]{:S(2)}) collective-permute-start(f32[16,48]{1,0:T(8,128)S(1)} %add.126), channel_id=1, source_target_pairs={{0,34},{2,32},{32,2},{34,0},{1,35},{3,33},{33,3},{35,1},{4,38},{6,... | collective-permute-start | bytes 9224 | tf_op jit(solution)/shard_map/ppermute | solution.py:37
  74.9 2.3 %collective-permute-done.12 = f32[16,48]{1,0:T(8,128)S(1)} collective-permute-done((f32[16,48]{1,0:T(8,128)S(1)}, f32[16,48]{1,0:T(8,128)S(1)}, u32[]{:S(2)}, u32[]{:S(2)}) %collective-permute-start.12) | collective-permute-done | bytes 3104 | tf_op jit(solution)/shard_map/ppermute | solution.py:37
  77.2 1.9 %collective-permute-start.13 = (f32[16,48]{1,0:T(8,128)S(1)}, f32[16,48]{1,0:T(8,128)S(1)}, u32[]{:S(2)}, u32[]{:S(2)}) collective-permute-start(f32[16,48]{1,0:T(8,128)S(1)} %add.127), channel_id=1, source_target_pairs={{0,4},{4,0},{8,12},{12,8},{16,20},{20,16},{24,28},{28,24},{1,5},{5... | collective-permute-start | bytes 9224 | tf_op jit(solution)/shard_map/ppermute | solution.py:30
  79.2 3.6 %collective-permute-done.13 = f32[16,48]{1,0:T(8,128)S(1)} collective-permute-done((f32[16,48]{1,0:T(8,128)S(1)}, f32[16,48]{1,0:T(8,128)S(1)}, u32[]{:S(2)}, u32[]{:S(2)}) %collective-permute-start.13) | collective-permute-done | bytes 3104 | tf_op jit(solution)/shard_map/ppermute | solution.py:30
  82.8 1.9 %collective-permute-start.14 = (f32[16,48]{1,0:T(8,128)S(1)}, f32[16,48]{1,0:T(8,128)S(1)}, u32[]{:S(2)}, u32[]{:S(2)}) collective-permute-start(f32[16,48]{1,0:T(8,128)S(1)} %add.128), channel_id=1, source_target_pairs={{0,8},{4,12},{8,0},{12,4},{16,24},{20,28},{24,16},{28,20},{1,9},{5... | collective-permute-start | bytes 9224 | tf_op jit(solution)/shard_map/ppermute | solution.py:30
  84.7 4.5 %collective-permute-done.14 = f32[16,48]{1,0:T(8,128)S(1)} collective-permute-done((f32[16,48]{1,0:T(8,128)S(1)}, f32[16,48]{1,0:T(8,128)S(1)}, u32[]{:S(2)}, u32[]{:S(2)}) %collective-permute-start.14) | collective-permute-done | bytes 3104 | tf_op jit(solution)/shard_map/ppermute | solution.py:30
  89.2 3.3 %collective-permute-start.15 = (f32[16,48]{1,0:T(8,128)S(1)}, f32[16,48]{1,0:T(8,128)S(1)}, u32[]{:S(2)}, u32[]{:S(2)}) collective-permute-start(f32[16,48]{1,0:T(8,128)S(1)} %add.129), channel_id=1, source_target_pairs={{0,24},{4,28},{8,16},{12,20},{16,8},{20,12},{24,0},{28,4},{1,25},{... | collective-permute-start | bytes 9224 | tf_op jit(solution)/shard_map/ppermute | solution.py:30
  92.6 4.3 %collective-permute-done.15 = f32[16,48]{1,0:T(8,128)S(1)} collective-permute-done((f32[16,48]{1,0:T(8,128)S(1)}, f32[16,48]{1,0:T(8,128)S(1)}, u32[]{:S(2)}, u32[]{:S(2)}) %collective-permute-start.15) | collective-permute-done | bytes 3104 | tf_op jit(solution)/shard_map/ppermute | solution.py:30
  96.8 4.3 %collective-permute-start.16 = (f32[16,48]{1,0:T(8,128)S(1)}, f32[16,48]{1,0:T(8,128)S(1)}, u32[]{:S(2)}, u32[]{:S(2)}) collective-permute-start(f32[16,48]{1,0:T(8,128)S(1)} %add.130), channel_id=1, source_target_pairs={{0,64},{64,0},{128,192},{192,128},{256,320},{320,256},{384,448},{4... | collective-permute-start | bytes 9224 | tf_op jit(solution)/shard_map/ppermute | solution.py:30
  101.1 1.6 %collective-permute-done.16 = f32[16,48]{1,0:T(8,128)S(1)} collective-permute-done((f32[16,48]{1,0:T(8,128)S(1)}, f32[16,48]{1,0:T(8,128)S(1)}, u32[]{:S(2)}, u32[]{:S(2)}) %collective-permute-start.16) | collective-permute-done | bytes 3104 | tf_op jit(solution)/shard_map/ppermute | solution.py:30
  102.7 6.1 %collective-permute-start.17 = (f32[16,48]{1,0:T(8,128)S(1)}, f32[16,48]{1,0:T(8,128)S(1)}, u32[]{:S(2)}, u32[]{:S(2)}) collective-permute-start(f32[16,48]{1,0:T(8,128)S(1)} %add.131), channel_id=1, source_target_pairs={{0,128},{64,192},{128,0},{192,64},{256,384},{320,448},{384,256},{4... | collective-permute-start | bytes 9224 | tf_op jit(solution)/shard_map/ppermute | solution.py:30
  110.4 9.3 %collective-permute-start.18 = (f32[16,48]{1,0:T(8,128)S(1)}, f32[16,48]{1,0:T(8,128)S(1)}, u32[]{:S(2)}, u32[]{:S(2)}) collective-permute-start(f32[16,48]{1,0:T(8,128)S(1)} %add.132), channel_id=1, source_target_pairs={{0,384},{64,448},{128,256},{192,320},{256,128},{320,192},{384,0},{... | collective-permute-start | bytes 9224 | tf_op jit(solution)/shard_map/ppermute | solution.py:30
  (61 shorter events, 13.6 us)
Async XLA Ops:
  0.0 50.9 %copy-start = (bf16[128,3,16,256]{3,2,1,0:T(8,128)(2,1)S(1)}, bf16[128,3,16,256]{3,2,1,0:T(8,128)(2,1)}, u32[]{:S(2)}) copy-start(bf16[128,3,16,256]{3,2,1,0:T(8,128)(2,1)} %param.12) | copy-start | bytes 9437188
  0.0 50.9 %copy-start.2 = (bf16[16,256]{1,0:T(8,128)(2,1)S(1)}, bf16[16,256]{1,0:T(8,128)(2,1)}, u32[]{:S(2)}) copy-start(bf16[16,256]{1,0:T(8,128)(2,1)} %param.14) | copy-start | bytes 24580
  0.0 6.0 %collective-permute-start = (bf16[10,256]{1,0:T(8,128)(2,1)}, bf16[10,256]{1,0:T(8,128)(2,1)S(1)}, u32[]{:S(2)}, u32[]{:S(2)}) collective-permute-start(bf16[10,256]{1,0:T(8,128)(2,1)} %param.16), channel_id=1, source_target_pairs={{0,4},{4,0},{8,12},{12,8},{16,20},{20,16},{24,28},{28,24},{1,5},{5... | collective-permute-start | bytes 15368 | tf_op jit(solution)/shard_map/ppermute | solution.py:47
  7.7 52.0 %copy-start.4 = (s32[10]{0:T(128)S(1)}, s32[10]{0:T(128)}, u32[]{:S(2)}) copy-start(s32[10]{0:T(128)} %param.18) | copy-start | bytes 124
  7.7 52.0 %copy-start.3 = (s32[320,2]{0,1:T(2,128)S(1)}, s32[320,2]{0,1:T(2,128)}, u32[]{:S(2)}) copy-start(s32[320,2]{0,1:T(2,128)} %param.17) | copy-start | bytes 7684
  8.8 11.6 %collective-permute-start.1 = (f32[16,2048]{1,0:T(8,128)S(1)}, f32[16,2048]{1,0:T(8,128)S(1)}, u32[]{:S(2)}, u32[]{:S(2)}) collective-permute-start(f32[16,2048]{1,0:T(8,128)S(1)} %bitcast.42), channel_id=1, source_target_pairs={{0,4},{4,0},{8,12},{12,8},{16,20},{20,16},{24,28},{28,24},{1,5},{5... | collective-permute-start | bytes 393224 | tf_op jit(solution)/shard_map/ppermute | solution.py:52
  11.1 9.3 %collective-permute-start.2 = (bf16[20,256]{1,0:T(8,128)(2,1)S(1)}, bf16[20,256]{1,0:T(8,128)(2,1)S(1)}, u32[]{:S(2)}, u32[]{:S(2)}) collective-permute-start(bf16[20,256]{1,0:T(8,128)(2,1)S(1)} %pad_maximum_fusion.4), channel_id=1, source_target_pairs={{0,8},{4,12},{8,0},{12,4},{16,24},{20,28},{24,16},{28,20},{1,9},{5... | collective-permute-start | bytes 30728 | tf_op jit(solution)/shard_map/ppermute | solution.py:47
  20.4 8.2 %collective-permute-start.4 = (bf16[40,256]{1,0:T(8,128)(2,1)S(1)}, bf16[40,256]{1,0:T(8,128)(2,1)S(1)}, u32[]{:S(2)}, u32[]{:S(2)}) collective-permute-start(bf16[40,256]{1,0:T(8,128)(2,1)S(1)} %pad_maximum_fusion.3), channel_id=1, source_target_pairs={{0,24},{4,28},{8,16},{12,20},{16,8},{20,12},{24,0},{28,4},{1,25},{... | collective-permute-start | bytes 61448 | tf_op jit(solution)/shard_map/ppermute | solution.py:47
  23.4 9.2 %collective-permute-start.3 = (f32[16,2048]{1,0:T(8,128)S(1)}, f32[16,2048]{1,0:T(8,128)S(1)}, u32[]{:S(2)}, u32[]{:S(2)}) collective-permute-start(f32[16,2048]{1,0:T(8,128)S(1)} %fusion.26), channel_id=1, source_target_pairs={{0,8},{4,12},{8,0},{12,4},{16,24},{20,28},{24,16},{28,20},{1,9},{5... | collective-permute-start | bytes 393224 | tf_op jit(solution)/shard_map/ppermute | solution.py:52
  32.6 7.4 %collective-permute-start.6 = (bf16[80,256]{1,0:T(8,128)(2,1)S(1)}, bf16[80,256]{1,0:T(8,128)(2,1)S(1)}, u32[]{:S(2)}, u32[]{:S(2)}) collective-permute-start(bf16[80,256]{1,0:T(8,128)(2,1)S(1)} %pad_maximum_fusion.2), channel_id=1, source_target_pairs={{0,2},{2,0},{1,3},{3,1},{4,6},{6,4},{5,7},{7,5},{8,10},{10,8},{9,1... | collective-permute-start | bytes 122888 | tf_op jit(solution)/shard_map/ppermute | solution.py:47
  37.5 9.0 %collective-permute-start.5 = (f32[16,2048]{1,0:T(8,128)S(1)}, f32[16,2048]{1,0:T(8,128)S(1)}, u32[]{:S(2)}, u32[]{:S(2)}) collective-permute-start(f32[16,2048]{1,0:T(8,128)S(1)} %add.121), channel_id=1, source_target_pairs={{0,24},{4,28},{8,16},{12,20},{16,8},{20,12},{24,0},{28,4},{1,25},{... | collective-permute-start | bytes 393224 | tf_op jit(solution)/shard_map/ppermute | solution.py:52
  46.5 6.1 %collective-permute-start.8 = (bf16[160,256]{1,0:T(8,128)(2,1)S(1)}, bf16[160,256]{1,0:T(8,128)(2,1)S(1)}, u32[]{:S(2)}, u32[]{:S(2)}) collective-permute-start(bf16[160,256]{1,0:T(8,128)(2,1)S(1)} %pad_maximum_fusion.1), channel_id=1, source_target_pairs={{0,1},{1,0},{2,3},{3,2},{4,5},{5,4},{6,7},{7,6},{8,9},{9,8},{10,11... | collective-permute-start | bytes 245768 | tf_op jit(solution)/shard_map/ppermute | solution.py:47
  48.4 9.3 %collective-permute-start.7 = (f32[16,2048]{1,0:T(8,128)S(1)}, f32[16,2048]{1,0:T(8,128)S(1)}, u32[]{:S(2)}, u32[]{:S(2)}) collective-permute-start(f32[16,2048]{1,0:T(8,128)S(1)} %add.122), channel_id=1, source_target_pairs={{0,2},{2,0},{1,3},{3,1},{4,6},{6,4},{5,7},{7,5},{8,10},{10,8},{9,1... | collective-permute-start | bytes 393224 | tf_op jit(solution)/shard_map/ppermute | solution.py:52
  50.9 22.7 %copy-start.1 = (s32[24]{0:T(128)S(1)}, s32[24]{0:T(128)}, u32[]{:S(2)}) copy-start(s32[24]{0:T(128)} %param.19) | copy-start | bytes 292
  57.8 3.2 %collective-permute-start.9 = (f32[16,2048]{1,0:T(8,128)S(1)}, f32[16,2048]{1,0:T(8,128)S(1)}, u32[]{:S(2)}, u32[]{:S(2)}) collective-permute-start(f32[16,2048]{1,0:T(8,128)S(1)} %add.123), channel_id=1, source_target_pairs={{0,1},{1,0},{2,3},{3,2},{4,5},{5,4},{6,7},{7,6},{8,9},{9,8},{10,11... | collective-permute-start | bytes 393224 | tf_op jit(solution)/shard_map/ppermute | solution.py:52
  61.5 3.4 %collective-permute-start.10 = (f32[16,48]{1,0:T(8,128)S(1)}, f32[16,48]{1,0:T(8,128)S(1)}, u32[]{:S(2)}, u32[]{:S(2)}) collective-permute-start(f32[16,48]{1,0:T(8,128)S(1)} %convolution_multiply_fusion.1), channel_id=1, source_target_pairs={{0,1},{1,0},{2,3},{3,2},{4,5},{5,4},{6,7},{7,6},{8,9},{9,8},{10,11... | collective-permute-start | bytes 9224 | tf_op jit(solution)/shard_map/ppermute | solution.py:30
  64.9 5.5 %collective-permute-start.11 = (f32[16,48]{1,0:T(8,128)S(1)}, f32[16,48]{1,0:T(8,128)S(1)}, u32[]{:S(2)}, u32[]{:S(2)}) collective-permute-start(f32[16,48]{1,0:T(8,128)S(1)} %add.125), channel_id=1, source_target_pairs={{0,32},{2,34},{32,0},{34,2},{1,33},{3,35},{33,1},{35,3},{4,36},{6,... | collective-permute-start | bytes 9224 | tf_op jit(solution)/shard_map/ppermute | solution.py:37
  70.5 6.7 %collective-permute-start.12 = (f32[16,48]{1,0:T(8,128)S(1)}, f32[16,48]{1,0:T(8,128)S(1)}, u32[]{:S(2)}, u32[]{:S(2)}) collective-permute-start(f32[16,48]{1,0:T(8,128)S(1)} %add.126), channel_id=1, source_target_pairs={{0,34},{2,32},{32,2},{34,0},{1,35},{3,33},{33,3},{35,1},{4,38},{6,... | collective-permute-start | bytes 9224 | tf_op jit(solution)/shard_map/ppermute | solution.py:37
  77.2 5.5 %collective-permute-start.13 = (f32[16,48]{1,0:T(8,128)S(1)}, f32[16,48]{1,0:T(8,128)S(1)}, u32[]{:S(2)}, u32[]{:S(2)}) collective-permute-start(f32[16,48]{1,0:T(8,128)S(1)} %add.127), channel_id=1, source_target_pairs={{0,4},{4,0},{8,12},{12,8},{16,20},{20,16},{24,28},{28,24},{1,5},{5... | collective-permute-start | bytes 9224 | tf_op jit(solution)/shard_map/ppermute | solution.py:30
  82.8 6.4 %collective-permute-start.14 = (f32[16,48]{1,0:T(8,128)S(1)}, f32[16,48]{1,0:T(8,128)S(1)}, u32[]{:S(2)}, u32[]{:S(2)}) collective-permute-start(f32[16,48]{1,0:T(8,128)S(1)} %add.128), channel_id=1, source_target_pairs={{0,8},{4,12},{8,0},{12,4},{16,24},{20,28},{24,16},{28,20},{1,9},{5... | collective-permute-start | bytes 9224 | tf_op jit(solution)/shard_map/ppermute | solution.py:30
  89.2 7.6 %collective-permute-start.15 = (f32[16,48]{1,0:T(8,128)S(1)}, f32[16,48]{1,0:T(8,128)S(1)}, u32[]{:S(2)}, u32[]{:S(2)}) collective-permute-start(f32[16,48]{1,0:T(8,128)S(1)} %add.129), channel_id=1, source_target_pairs={{0,24},{4,28},{8,16},{12,20},{16,8},{20,12},{24,0},{28,4},{1,25},{... | collective-permute-start | bytes 9224 | tf_op jit(solution)/shard_map/ppermute | solution.py:30
  96.8 5.9 %collective-permute-start.16 = (f32[16,48]{1,0:T(8,128)S(1)}, f32[16,48]{1,0:T(8,128)S(1)}, u32[]{:S(2)}, u32[]{:S(2)}) collective-permute-start(f32[16,48]{1,0:T(8,128)S(1)} %add.130), channel_id=1, source_target_pairs={{0,64},{64,0},{128,192},{192,128},{256,320},{320,256},{384,448},{4... | collective-permute-start | bytes 9224 | tf_op jit(solution)/shard_map/ppermute | solution.py:30
  102.7 7.7 %collective-permute-start.17 = (f32[16,48]{1,0:T(8,128)S(1)}, f32[16,48]{1,0:T(8,128)S(1)}, u32[]{:S(2)}, u32[]{:S(2)}) collective-permute-start(f32[16,48]{1,0:T(8,128)S(1)} %add.131), channel_id=1, source_target_pairs={{0,128},{64,192},{128,0},{192,64},{256,384},{320,448},{384,256},{4... | collective-permute-start | bytes 9224 | tf_op jit(solution)/shard_map/ppermute | solution.py:30
  110.4 10.9 %collective-permute-start.18 = (f32[16,48]{1,0:T(8,128)S(1)}, f32[16,48]{1,0:T(8,128)S(1)}, u32[]{:S(2)}, u32[]{:S(2)}) collective-permute-start(f32[16,48]{1,0:T(8,128)S(1)} %add.132), channel_id=1, source_target_pairs={{0,384},{64,448},{128,256},{192,320},{256,128},{320,192},{384,0},{... | collective-permute-start | bytes 9224 | tf_op jit(solution)/shard_map/ppermute | solution.py:30

commit v11 on v8

--- a/solution.py
+++ b/solution.py
@@ -58,10 +58,9 @@
     scale = 1.0 / (8.0 * jnp.sqrt(jnp.float32(rows * n_aux)))
 
     cou_part = jnp.einsum("un,ptn->upt", coef_t, cou_ints, preferred_element_type=jnp.float32)
-    fitted = jnp.einsum("upt,tu->p", cou_part, active_rdm, precision=HIGH)
-    folded = jnp.einsum("upw,vw->uvp", cou_part, active_rdm, precision=HIGH)
     eye = jnp.eye(width, dtype=jnp.float32)
-    weight = (eye[:, :, None] * fitted[None, None, :] - 1.5 * folded).reshape(width, width * rows)
+    table = jnp.einsum("ta,uv->atuv", active_rdm, eye) - 1.5 * jnp.einsum("vt,au->atuv", active_rdm, eye)
+    weight = jnp.einsum("apt,atuv->uvp", cou_part, table, precision=HIGH).reshape(width, width * rows)
     weight, every_dens = butterfly_sum_gather(weight, spin_dens, (("y", 8), ("xhi", 2), ("core", 2)))
 
     soc_part = jnp.einsum(

time: 121 us -> 127 us (1.050)
  local copies, waits for them, and re-layouts: 3.62 us -> 6.71 us
  other arithmetic: 1.07 us -> 2.9 us
    transpose x0 -> x1, local copies, waits for them, and re-layouts: none -> 3.07 us  [on_device(): jnp.einsum('ta,uv->atuv', active_rdm, eye)]
    transpose x0 -> x1, other arithmetic: none -> 2.52 us  [on_device(): jnp.einsum('ta,uv->atuv', active_rdm, eye)]
    dot_general x2 -> x1, matrix products: 1.95 us -> 3.67 us  [on_device(): jnp.einsum('apt,atuv->uvp', cou_part, table, precision=HIGH)]
  transfers between devices with their start and end apart: 19 -> 19, of which waited for: 14 -> 14; matrix products, arithmetic and copies ran while one was open for 6% -> 4% of each run, Pallas kernels for 0% -> 0%
where the time goes in v11:
time: 127 us
  starting transfers between devices  69.7 us (55%)
  waiting for transfers between devices  38.2 us (30%)
  matrix products  8.65 us (7%)
  local copies, waits for them, and re-layouts  6.71 us (5%)
  other arithmetic  2.9 us (2%)
    ppermute x7, starting transfers between devices, butterfly_sum(): value = value + lax.ppermute(value, axis, partners(size, step))  28.2 us
    ppermute x5, starting transfers between devices, butterfly_sum_gather(): total = total + lax.ppermute(total, axis, pairs)  19.5 us
    ppermute x7, waiting for transfers between devices, butterfly_sum(): value = value + lax.ppermute(value, axis, partners(size, step))  17.1 us
    ppermute x5, starting transfers between devices, butterfly_sum_gather(): lax.ppermute(blocks, axis, pairs)  16.5 us
    ppermute x5, waiting for transfers between devices, butterfly_sum_gather(): total = total + lax.ppermute(total, axis, pairs)  9.84 us
    ppermute x5, waiting for transfers between devices, butterfly_sum_gather(): lax.ppermute(blocks, axis, pairs)  5.82 us
    ppermute x2, starting transfers between devices, x_ring_sum(): value = value + lax.ppermute(value, ('xlo', 'xhi'), pairs)  5.54 us
    ppermute x2, waiting for transfers between devices, x_ring_sum(): value = value + lax.ppermute(value, ('xlo', 'xhi'), pairs)  5.37 us
  transfers between devices with their start and end apart: 19, of which 14 were waited for; matrix products, arithmetic and copies ran while one was open for 4% of the time, Pallas kernels for 0%

profile of v11, /device:TPU:8, one launch (start us, length us, event | category | flops | bytes accessed | tf_op | source)
XLA Modules:
  0.0 126.6 jit_solution(763769859300792585)
XLA Ops:
  0.0 2.5 %multiply_bitcast_fusion = f32[16,16,16,16]{0,1,2,3:T(8,128)} fusion(f32[16,16]{1,0:T(8,128)} %param.15, f32[16,16]{0,1:T(8,128)S(1)} %fusion.23), kind=kLoop, calls=%fused_computation.8 | loop fusion | flops 65536 | bytes 264192 | tf_op jit(solution)/shard_map/ta,uv->atuv/transpose | solution.py:62
  2.5 3.1 %copy.13 = f32[16,16,16,16]{1,3,0,2:T(8,128)} copy(f32[16,16,16,16]{0,1,2,3:T(8,128)} %multiply_bitcast_fusion) | data formatting | bytes 524288 | tf_op jit(solution)/shard_map/ta,uv->atuv/transpose | solution.py:62
  5.6 1.9 %fusion.7 = f32[16,128,16]{1,0,2:T(8,128)S(1)} fusion(bf16[128,16,256]{2,1,0:T(8,128)(2,1)} %param.13, bf16[16,256]{1,0:T(8,128)(2,1)S(1)} %copy-done.3), kind=kOutput, calls=%fused_computation.15 | convolution fusion | flops 16777216 | bytes 1187840 | tf_op jit(solution)/shard_map/un,ptn->upt/dot_general | solution.py:60
  7.5 3.7 %fusion.4 = f32[16,16,128,1]{2,1,3,0:T(8,128)S(1)} fusion(f32[16,16,16,16]{1,3,0,2:T(8,128)} %copy.13, f32[16,16]{1,0:T(8,128)S(1)} %copy-done.2, f32[16,16]{0,1:T(8,128)S(1)} %fusion.23, f32[16,128,16]{1,0,2:T(8,128)S(1)} %fusion.7), kind=kOutput, calls=%fused_computation.11 | convolution fusion | flops 100859904 | bytes 526336 | tf_op jit(solution)/shard_map/apt,atuv->uvp/dot_general | solution.py:63
  11.2 7.7 %collective-permute-start = (f32[16,2048]{1,0:T(8,128)S(1)}, f32[16,2048]{1,0:T(8,128)S(1)}, u32[]{:S(2)}, u32[]{:S(2)}) collective-permute-start(f32[16,2048]{1,0:T(8,128)S(1)} %bitcast.41), channel_id=1, source_target_pairs={{0,4},{4,0},{8,12},{12,8},{16,20},{20,16},{24,28},{28,24},{1,5},{5... | collective-permute-start | bytes 393224 | tf_op jit(solution)/shard_map/ppermute | solution.py:46
  19.0 1.9 %collective-permute-start.1 = (bf16[10,256]{1,0:T(8,128)(2,1)S(1)}, bf16[10,256]{1,0:T(8,128)(2,1)S(1)}, u32[]{:S(2)}, u32[]{:S(2)}) collective-permute-start(bf16[10,256]{1,0:T(8,128)(2,1)S(1)} %copy-done.4), channel_id=1, source_target_pairs={{0,4},{4,0},{8,12},{12,8},{16,20},{20,16},{24,28},{28,24},{1,5},{5... | collective-permute-start | bytes 15368 | tf_op jit(solution)/shard_map/ppermute | solution.py:47
  20.9 3.7 %collective-permute-done.1 = bf16[10,256]{1,0:T(8,128)(2,1)S(1)} collective-permute-done((bf16[10,256]{1,0:T(8,128)(2,1)S(1)}, bf16[10,256]{1,0:T(8,128)(2,1)S(1)}, u32[]{:S(2)}, u32[]{:S(2)}) %collective-permute-start.1) | collective-permute-done | bytes 5152 | tf_op jit(solution)/shard_map/ppermute | solution.py:47
  24.7 1.9 %collective-permute-start.2 = (f32[16,2048]{1,0:T(8,128)S(1)}, f32[16,2048]{1,0:T(8,128)S(1)}, u32[]{:S(2)}, u32[]{:S(2)}) collective-permute-start(f32[16,2048]{1,0:T(8,128)S(1)} %fusion.32), channel_id=1, source_target_pairs={{0,8},{4,12},{8,0},{12,4},{16,24},{20,28},{24,16},{28,20},{1,9},{5... | collective-permute-start | bytes 393224 | tf_op jit(solution)/shard_map/ppermute | solution.py:46
  26.6 4.8 %collective-permute-start.3 = (bf16[20,256]{1,0:T(8,128)(2,1)S(1)}, bf16[20,256]{1,0:T(8,128)(2,1)S(1)}, u32[]{:S(2)}, u32[]{:S(2)}) collective-permute-start(bf16[20,256]{1,0:T(8,128)(2,1)S(1)} %pad_maximum_fusion.4), channel_id=1, source_target_pairs={{0,8},{4,12},{8,0},{12,4},{16,24},{20,28},{24,16},{28,20},{1,9},{5... | collective-permute-start | bytes 30728 | tf_op jit(solution)/shard_map/ppermute | solution.py:47
  33.1 2.9 %collective-permute-start.5 = (bf16[40,256]{1,0:T(8,128)(2,1)S(1)}, bf16[40,256]{1,0:T(8,128)(2,1)S(1)}, u32[]{:S(2)}, u32[]{:S(2)}) collective-permute-start(bf16[40,256]{1,0:T(8,128)(2,1)S(1)} %pad_maximum_fusion.3), channel_id=1, source_target_pairs={{0,24},{4,28},{8,16},{12,20},{16,8},{20,12},{24,0},{28,4},{1,25},{... | collective-permute-start | bytes 61448 | tf_op jit(solution)/shard_map/ppermute | solution.py:47
  36.0 5.1 %collective-permute-start.4 = (f32[16,2048]{1,0:T(8,128)S(1)}, f32[16,2048]{1,0:T(8,128)S(1)}, u32[]{:S(2)}, u32[]{:S(2)}) collective-permute-start(f32[16,2048]{1,0:T(8,128)S(1)} %add.121), channel_id=1, source_target_pairs={{0,24},{4,28},{8,16},{12,20},{16,8},{20,12},{24,0},{28,4},{1,25},{... | collective-permute-start | bytes 393224 | tf_op jit(solution)/shard_map/ppermute | solution.py:46
  41.1 1.8 %fusion = f32[16,128,48]{1,0,2:T(8,128)S(1)} fusion(bf16[128,48,256]{2,1,0:T(8,128)(2,1)S(1)} %bitcast.37, bf16[16,256]{1,0:T(8,128)(2,1)S(1)} %copy-done.3), kind=kOutput, calls=%fused_computation.5 | convolution fusion | flops 50331648 | bytes 3547136 | tf_op jit(solution)/shard_map/vn,pkn->vpk/dot_general | solution.py:66
  42.9 3.5 %collective-permute-done.4 = f32[16,2048]{1,0:T(8,128)S(1)} collective-permute-done((f32[16,2048]{1,0:T(8,128)S(1)}, f32[16,2048]{1,0:T(8,128)S(1)}, u32[]{:S(2)}, u32[]{:S(2)}) %collective-permute-start.4) | collective-permute-done | bytes 131104 | tf_op jit(solution)/shard_map/ppermute | solution.py:46
  46.4 4.9 %collective-permute-start.7 = (bf16[80,256]{1,0:T(8,128)(2,1)S(1)}, bf16[80,256]{1,0:T(8,128)(2,1)S(1)}, u32[]{:S(2)}, u32[]{:S(2)}) collective-permute-start(bf16[80,256]{1,0:T(8,128)(2,1)S(1)} %pad_maximum_fusion.2), channel_id=1, source_target_pairs={{0,2},{2,0},{1,3},{3,1},{4,6},{6,4},{5,7},{7,5},{8,10},{10,8},{9,1... | collective-permute-start | bytes 122888 | tf_op jit(solution)/shard_map/ppermute | solution.py:47
  51.4 2.4 %collective-permute-start.6 = (f32[16,2048]{1,0:T(8,128)S(1)}, f32[16,2048]{1,0:T(8,128)S(1)}, u32[]{:S(2)}, u32[]{:S(2)}) collective-permute-start(f32[16,2048]{1,0:T(8,128)S(1)} %add.122), channel_id=1, source_target_pairs={{0,2},{2,0},{1,3},{3,1},{4,6},{6,4},{5,7},{7,5},{8,10},{10,8},{9,1... | collective-permute-start | bytes 393224 | tf_op jit(solution)/shard_map/ppermute | solution.py:46
  54.3 5.5 %collective-permute-done.6 = f32[16,2048]{1,0:T(8,128)S(1)} collective-permute-done((f32[16,2048]{1,0:T(8,128)S(1)}, f32[16,2048]{1,0:T(8,128)S(1)}, u32[]{:S(2)}, u32[]{:S(2)}) %collective-permute-start.6) | collective-permute-done | bytes 131104 | tf_op jit(solution)/shard_map/ppermute | solution.py:46
  59.7 1.9 %collective-permute-start.9 = (bf16[160,256]{1,0:T(8,128)(2,1)S(1)}, bf16[160,256]{1,0:T(8,128)(2,1)S(1)}, u32[]{:S(2)}, u32[]{:S(2)}) collective-permute-start(bf16[160,256]{1,0:T(8,128)(2,1)S(1)} %pad_maximum_fusion.1), channel_id=1, source_target_pairs={{0,1},{1,0},{2,3},{3,2},{4,5},{5,4},{6,7},{7,6},{8,9},{9,8},{10,11... | collective-permute-start | bytes 245768 | tf_op jit(solution)/shard_map/ppermute | solution.py:47
  61.7 2.4 %collective-permute-start.8 = (f32[16,2048]{1,0:T(8,128)S(1)}, f32[16,2048]{1,0:T(8,128)S(1)}, u32[]{:S(2)}, u32[]{:S(2)}) collective-permute-start(f32[16,2048]{1,0:T(8,128)S(1)} %add.123), channel_id=1, source_target_pairs={{0,1},{1,0},{2,3},{3,2},{4,5},{5,4},{6,7},{7,6},{8,9},{9,8},{10,11... | collective-permute-start | bytes 393224 | tf_op jit(solution)/shard_map/ppermute | solution.py:46
  65.5 2.3 %collective-permute-start.10 = (f32[16,48]{1,0:T(8,128)S(1)}, f32[16,48]{1,0:T(8,128)S(1)}, u32[]{:S(2)}, u32[]{:S(2)}) collective-permute-start(f32[16,48]{1,0:T(8,128)S(1)} %convolution_multiply_fusion), channel_id=1, source_target_pairs={{0,1},{1,0},{2,3},{3,2},{4,5},{5,4},{6,7},{7,6},{8,9},{9,8},{10,11... | collective-permute-start | bytes 9224 | tf_op jit(solution)/shard_map/ppermute | solution.py:30
  69.2 2.5 %collective-permute-start.11 = (f32[16,48]{1,0:T(8,128)S(1)}, f32[16,48]{1,0:T(8,128)S(1)}, u32[]{:S(2)}, u32[]{:S(2)}) collective-permute-start(f32[16,48]{1,0:T(8,128)S(1)} %add.125), channel_id=1, source_target_pairs={{0,32},{2,34},{32,0},{34,2},{1,33},{3,35},{33,1},{35,3},{4,36},{6,... | collective-permute-start | bytes 9224 | tf_op jit(solution)/shard_map/ppermute | solution.py:37
  71.7 3.0 %collective-permute-done.11 = f32[16,48]{1,0:T(8,128)S(1)} collective-permute-done((f32[16,48]{1,0:T(8,128)S(1)}, f32[16,48]{1,0:T(8,128)S(1)}, u32[]{:S(2)}, u32[]{:S(2)}) %collective-permute-start.11) | collective-permute-done | bytes 3104 | tf_op jit(solution)/shard_map/ppermute | solution.py:37
  74.7 3.0 %collective-permute-start.12 = (f32[16,48]{1,0:T(8,128)S(1)}, f32[16,48]{1,0:T(8,128)S(1)}, u32[]{:S(2)}, u32[]{:S(2)}) collective-permute-start(f32[16,48]{1,0:T(8,128)S(1)} %add.126), channel_id=1, source_target_pairs={{0,34},{2,32},{32,2},{34,0},{1,35},{3,33},{33,3},{35,1},{4,38},{6,... | collective-permute-start | bytes 9224 | tf_op jit(solution)/shard_map/ppermute | solution.py:37
  79.1 2.4 %collective-permute-done.12 = f32[16,48]{1,0:T(8,128)S(1)} collective-permute-done((f32[16,48]{1,0:T(8,128)S(1)}, f32[16,48]{1,0:T(8,128)S(1)}, u32[]{:S(2)}, u32[]{:S(2)}) %collective-permute-start.12) | collective-permute-done | bytes 3104 | tf_op jit(solution)/shard_map/ppermute | solution.py:37
  81.5 1.9 %collective-permute-start.13 = (f32[16,48]{1,0:T(8,128)S(1)}, f32[16,48]{1,0:T(8,128)S(1)}, u32[]{:S(2)}, u32[]{:S(2)}) collective-permute-start(f32[16,48]{1,0:T(8,128)S(1)} %add.127), channel_id=1, source_target_pairs={{0,4},{4,0},{8,12},{12,8},{16,20},{20,16},{24,28},{28,24},{1,5},{5... | collective-permute-start | bytes 9224 | tf_op jit(solution)/shard_map/ppermute | solution.py:30
  83.4 3.6 %collective-permute-done.13 = f32[16,48]{1,0:T(8,128)S(1)} collective-permute-done((f32[16,48]{1,0:T(8,128)S(1)}, f32[16,48]{1,0:T(8,128)S(1)}, u32[]{:S(2)}, u32[]{:S(2)}) %collective-permute-start.13) | collective-permute-done | bytes 3104 | tf_op jit(solution)/shard_map/ppermute | solution.py:30
  87.0 2.2 %collective-permute-start.14 = (f32[16,48]{1,0:T(8,128)S(1)}, f32[16,48]{1,0:T(8,128)S(1)}, u32[]{:S(2)}, u32[]{:S(2)}) collective-permute-start(f32[16,48]{1,0:T(8,128)S(1)} %add.128), channel_id=1, source_target_pairs={{0,8},{4,12},{8,0},{12,4},{16,24},{20,28},{24,16},{28,20},{1,9},{5... | collective-permute-start | bytes 9224 | tf_op jit(solution)/shard_map/ppermute | solution.py:30
  89.3 4.1 %collective-permute-done.14 = f32[16,48]{1,0:T(8,128)S(1)} collective-permute-done((f32[16,48]{1,0:T(8,128)S(1)}, f32[16,48]{1,0:T(8,128)S(1)}, u32[]{:S(2)}, u32[]{:S(2)}) %collective-permute-start.14) | collective-permute-done | bytes 3104 | tf_op jit(solution)/shard_map/ppermute | solution.py:30
  93.5 2.1 %collective-permute-start.15 = (f32[16,48]{1,0:T(8,128)S(1)}, f32[16,48]{1,0:T(8,128)S(1)}, u32[]{:S(2)}, u32[]{:S(2)}) collective-permute-start(f32[16,48]{1,0:T(8,128)S(1)} %add.129), channel_id=1, source_target_pairs={{0,24},{4,28},{8,16},{12,20},{16,8},{20,12},{24,0},{28,4},{1,25},{... | collective-permute-start | bytes 9224 | tf_op jit(solution)/shard_map/ppermute | solution.py:30
  95.6 5.5 %collective-permute-done.15 = f32[16,48]{1,0:T(8,128)S(1)} collective-permute-done((f32[16,48]{1,0:T(8,128)S(1)}, f32[16,48]{1,0:T(8,128)S(1)}, u32[]{:S(2)}, u32[]{:S(2)}) %collective-permute-start.15) | collective-permute-done | bytes 3104 | tf_op jit(solution)/shard_map/ppermute | solution.py:30
  101.1 4.3 %collective-permute-start.16 = (f32[16,48]{1,0:T(8,128)S(1)}, f32[16,48]{1,0:T(8,128)S(1)}, u32[]{:S(2)}, u32[]{:S(2)}) collective-permute-start(f32[16,48]{1,0:T(8,128)S(1)} %add.130), channel_id=1, source_target_pairs={{0,64},{64,0},{128,192},{192,128},{256,320},{320,256},{384,448},{4... | collective-permute-start | bytes 9224 | tf_op jit(solution)/shard_map/ppermute | solution.py:30
  107.0 6.1 %collective-permute-start.17 = (f32[16,48]{1,0:T(8,128)S(1)}, f32[16,48]{1,0:T(8,128)S(1)}, u32[]{:S(2)}, u32[]{:S(2)}) collective-permute-start(f32[16,48]{1,0:T(8,128)S(1)} %add.131), channel_id=1, source_target_pairs={{0,128},{64,192},{128,0},{192,64},{256,384},{320,448},{384,256},{4... | collective-permute-start | bytes 9224 | tf_op jit(solution)/shard_map/ppermute | solution.py:30
  114.7 9.3 %collective-permute-start.18 = (f32[16,48]{1,0:T(8,128)S(1)}, f32[16,48]{1,0:T(8,128)S(1)}, u32[]{:S(2)}, u32[]{:S(2)}) collective-permute-start(f32[16,48]{1,0:T(8,128)S(1)} %add.132), channel_id=1, source_target_pairs={{0,384},{64,448},{128,256},{192,320},{256,128},{320,192},{384,0},{... | collective-permute-start | bytes 9224 | tf_op jit(solution)/shard_map/ppermute | solution.py:30
  (66 shorter events, 12.3 us)
Async XLA Ops:
  0.0 41.1 %copy-start = (bf16[128,3,16,256]{3,2,1,0:T(8,128)(2,1)S(1)}, bf16[128,3,16,256]{3,2,1,0:T(8,128)(2,1)}, u32[]{:S(2)}) copy-start(bf16[128,3,16,256]{3,2,1,0:T(8,128)(2,1)} %param.12) | copy-start | bytes 9437188
  2.5 3.1 %copy-start.3 = (bf16[16,256]{1,0:T(8,128)(2,1)S(1)}, bf16[16,256]{1,0:T(8,128)(2,1)}, u32[]{:S(2)}) copy-start(bf16[16,256]{1,0:T(8,128)(2,1)} %param.14) | copy-start | bytes 24580
  2.5 5.0 %copy-start.2 = (f32[16,16]{1,0:T(8,128)S(1)}, f32[16,16]{1,0:T(8,128)}, u32[]{:S(2)}) copy-start(f32[16,16]{1,0:T(8,128)} %param.15) | copy-start | bytes 3076
  5.6 13.3 %copy-start.4 = (bf16[10,256]{1,0:T(8,128)(2,1)S(1)}, bf16[10,256]{1,0:T(8,128)(2,1)}, u32[]{:S(2)}) copy-start(bf16[10,256]{1,0:T(8,128)(2,1)} %param.16) | copy-start | bytes 15364
  11.2 13.4 %collective-permute-start = (f32[16,2048]{1,0:T(8,128)S(1)}, f32[16,2048]{1,0:T(8,128)S(1)}, u32[]{:S(2)}, u32[]{:S(2)}) collective-permute-start(f32[16,2048]{1,0:T(8,128)S(1)} %bitcast.41), channel_id=1, source_target_pairs={{0,4},{4,0},{8,12},{12,8},{16,20},{20,16},{24,28},{28,24},{1,5},{5... | collective-permute-start | bytes 393224 | tf_op jit(solution)/shard_map/ppermute | solution.py:46
  19.0 5.6 %collective-permute-start.1 = (bf16[10,256]{1,0:T(8,128)(2,1)S(1)}, bf16[10,256]{1,0:T(8,128)(2,1)S(1)}, u32[]{:S(2)}, u32[]{:S(2)}) collective-permute-start(bf16[10,256]{1,0:T(8,128)(2,1)S(1)} %copy-done.4), channel_id=1, source_target_pairs={{0,4},{4,0},{8,12},{12,8},{16,20},{20,16},{24,28},{28,24},{1,5},{5... | collective-permute-start | bytes 15368 | tf_op jit(solution)/shard_map/ppermute | solution.py:47
  24.7 8.4 %collective-permute-start.2 = (f32[16,2048]{1,0:T(8,128)S(1)}, f32[16,2048]{1,0:T(8,128)S(1)}, u32[]{:S(2)}, u32[]{:S(2)}) collective-permute-start(f32[16,2048]{1,0:T(8,128)S(1)} %fusion.32), channel_id=1, source_target_pairs={{0,8},{4,12},{8,0},{12,4},{16,24},{20,28},{24,16},{28,20},{1,9},{5... | collective-permute-start | bytes 393224 | tf_op jit(solution)/shard_map/ppermute | solution.py:46
  26.6 6.5 %collective-permute-start.3 = (bf16[20,256]{1,0:T(8,128)(2,1)S(1)}, bf16[20,256]{1,0:T(8,128)(2,1)S(1)}, u32[]{:S(2)}, u32[]{:S(2)}) collective-permute-start(bf16[20,256]{1,0:T(8,128)(2,1)S(1)} %pad_maximum_fusion.4), channel_id=1, source_target_pairs={{0,8},{4,12},{8,0},{12,4},{16,24},{20,28},{24,16},{28,20},{1,9},{5... | collective-permute-start | bytes 30728 | tf_op jit(solution)/shard_map/ppermute | solution.py:47
  33.1 20.6 %copy-start.6 = (s32[10]{0:T(128)S(1)}, s32[10]{0:T(128)}, u32[]{:S(2)}) copy-start(s32[10]{0:T(128)} %param.18) | copy-start | bytes 124
  33.1 9.8 %collective-permute-start.5 = (bf16[40,256]{1,0:T(8,128)(2,1)S(1)}, bf16[40,256]{1,0:T(8,128)(2,1)S(1)}, u32[]{:S(2)}, u32[]{:S(2)}) collective-permute-start(bf16[40,256]{1,0:T(8,128)(2,1)S(1)} %pad_maximum_fusion.3), channel_id=1, source_target_pairs={{0,24},{4,28},{8,16},{12,20},{16,8},{20,12},{24,0},{28,4},{1,25},{... | collective-permute-start | bytes 61448 | tf_op jit(solution)/shard_map/ppermute | solution.py:47
  36.0 10.4 %collective-permute-start.4 = (f32[16,2048]{1,0:T(8,128)S(1)}, f32[16,2048]{1,0:T(8,128)S(1)}, u32[]{:S(2)}, u32[]{:S(2)}) collective-permute-start(f32[16,2048]{1,0:T(8,128)S(1)} %add.121), channel_id=1, source_target_pairs={{0,24},{4,28},{8,16},{12,20},{16,8},{20,12},{24,0},{28,4},{1,25},{... | collective-permute-start | bytes 393224 | tf_op jit(solution)/shard_map/ppermute | solution.py:46
  41.1 23.0 %copy-start.5 = (s32[320,2]{0,1:T(2,128)S(1)}, s32[320,2]{0,1:T(2,128)}, u32[]{:S(2)}) copy-start(s32[320,2]{0,1:T(2,128)} %param.17) | copy-start | bytes 7684
  42.9 34.9 %copy-start.1 = (s32[24]{0:T(128)S(1)}, s32[24]{0:T(128)}, u32[]{:S(2)}) copy-start(s32[24]{0:T(128)} %param.19) | copy-start | bytes 292
  46.4 7.8 %collective-permute-start.7 = (bf16[80,256]{1,0:T(8,128)(2,1)S(1)}, bf16[80,256]{1,0:T(8,128)(2,1)S(1)}, u32[]{:S(2)}, u32[]{:S(2)}) collective-permute-start(bf16[80,256]{1,0:T(8,128)(2,1)S(1)} %pad_maximum_fusion.2), channel_id=1, source_target_pairs={{0,2},{2,0},{1,3},{3,1},{4,6},{6,4},{5,7},{7,5},{8,10},{10,8},{9,1... | collective-permute-start | bytes 122888 | tf_op jit(solution)/shard_map/ppermute | solution.py:47
  51.4 8.4 %collective-permute-start.6 = (f32[16,2048]{1,0:T(8,128)S(1)}, f32[16,2048]{1,0:T(8,128)S(1)}, u32[]{:S(2)}, u32[]{:S(2)}) collective-permute-start(f32[16,2048]{1,0:T(8,128)S(1)} %add.122), channel_id=1, source_target_pairs={{0,2},{2,0},{1,3},{3,1},{4,6},{6,4},{5,7},{7,5},{8,10},{10,8},{9,1... | collective-permute-start | bytes 393224 | tf_op jit(solution)/shard_map/ppermute | solution.py:46
  59.7 4.4 %collective-permute-start.9 = (bf16[160,256]{1,0:T(8,128)(2,1)S(1)}, bf16[160,256]{1,0:T(8,128)(2,1)S(1)}, u32[]{:S(2)}, u32[]{:S(2)}) collective-permute-start(bf16[160,256]{1,0:T(8,128)(2,1)S(1)} %pad_maximum_fusion.1), channel_id=1, source_target_pairs={{0,1},{1,0},{2,3},{3,2},{4,5},{5,4},{6,7},{7,6},{8,9},{9,8},{10,11... | collective-permute-start | bytes 245768 | tf_op jit(solution)/shard_map/ppermute | solution.py:47
  61.7 3.4 %collective-permute-start.8 = (f32[16,2048]{1,0:T(8,128)S(1)}, f32[16,2048]{1,0:T(8,128)S(1)}, u32[]{:S(2)}, u32[]{:S(2)}) collective-permute-start(f32[16,2048]{1,0:T(8,128)S(1)} %add.123), channel_id=1, source_target_pairs={{0,1},{1,0},{2,3},{3,2},{4,5},{5,4},{6,7},{7,6},{8,9},{9,8},{10,11... | collective-permute-start | bytes 393224 | tf_op jit(solution)/shard_map/ppermute | solution.py:46
  65.5 3.6 %collective-permute-start.10 = (f32[16,48]{1,0:T(8,128)S(1)}, f32[16,48]{1,0:T(8,128)S(1)}, u32[]{:S(2)}, u32[]{:S(2)}) collective-permute-start(f32[16,48]{1,0:T(8,128)S(1)} %convolution_multiply_fusion), channel_id=1, source_target_pairs={{0,1},{1,0},{2,3},{3,2},{4,5},{5,4},{6,7},{7,6},{8,9},{9,8},{10,11... | collective-permute-start | bytes 9224 | tf_op jit(solution)/shard_map/ppermute | solution.py:30
  69.2 5.5 %collective-permute-start.11 = (f32[16,48]{1,0:T(8,128)S(1)}, f32[16,48]{1,0:T(8,128)S(1)}, u32[]{:S(2)}, u32[]{:S(2)}) collective-permute-start(f32[16,48]{1,0:T(8,128)S(1)} %add.125), channel_id=1, source_target_pairs={{0,32},{2,34},{32,0},{34,2},{1,33},{3,35},{33,1},{35,3},{4,36},{6,... | collective-permute-start | bytes 9224 | tf_op jit(solution)/shard_map/ppermute | solution.py:37
  74.7 6.7 %collective-permute-start.12 = (f32[16,48]{1,0:T(8,128)S(1)}, f32[16,48]{1,0:T(8,128)S(1)}, u32[]{:S(2)}, u32[]{:S(2)}) collective-permute-start(f32[16,48]{1,0:T(8,128)S(1)} %add.126), channel_id=1, source_target_pairs={{0,34},{2,32},{32,2},{34,0},{1,35},{3,33},{33,3},{35,1},{4,38},{6,... | collective-permute-start | bytes 9224 | tf_op jit(solution)/shard_map/ppermute | solution.py:37
  81.5 5.5 %collective-permute-start.13 = (f32[16,48]{1,0:T(8,128)S(1)}, f32[16,48]{1,0:T(8,128)S(1)}, u32[]{:S(2)}, u32[]{:S(2)}) collective-permute-start(f32[16,48]{1,0:T(8,128)S(1)} %add.127), channel_id=1, source_target_pairs={{0,4},{4,0},{8,12},{12,8},{16,20},{20,16},{24,28},{28,24},{1,5},{5... | collective-permute-start | bytes 9224 | tf_op jit(solution)/shard_map/ppermute | solution.py:30
  87.0 6.4 %collective-permute-start.14 = (f32[16,48]{1,0:T(8,128)S(1)}, f32[16,48]{1,0:T(8,128)S(1)}, u32[]{:S(2)}, u32[]{:S(2)}) collective-permute-start(f32[16,48]{1,0:T(8,128)S(1)} %add.128), channel_id=1, source_target_pairs={{0,8},{4,12},{8,0},{12,4},{16,24},{20,28},{24,16},{28,20},{1,9},{5... | collective-permute-start | bytes 9224 | tf_op jit(solution)/shard_map/ppermute | solution.py:30
  93.5 7.6 %collective-permute-start.15 = (f32[16,48]{1,0:T(8,128)S(1)}, f32[16,48]{1,0:T(8,128)S(1)}, u32[]{:S(2)}, u32[]{:S(2)}) collective-permute-start(f32[16,48]{1,0:T(8,128)S(1)} %add.129), channel_id=1, source_target_pairs={{0,24},{4,28},{8,16},{12,20},{16,8},{20,12},{24,0},{28,4},{1,25},{... | collective-permute-start | bytes 9224 | tf_op jit(solution)/shard_map/ppermute | solution.py:30
  101.1 5.9 %collective-permute-start.16 = (f32[16,48]{1,0:T(8,128)S(1)}, f32[16,48]{1,0:T(8,128)S(1)}, u32[]{:S(2)}, u32[]{:S(2)}) collective-permute-start(f32[16,48]{1,0:T(8,128)S(1)} %add.130), channel_id=1, source_target_pairs={{0,64},{64,0},{128,192},{192,128},{256,320},{320,256},{384,448},{4... | collective-permute-start | bytes 9224 | tf_op jit(solution)/shard_map/ppermute | solution.py:30
  107.0 7.7 %collective-permute-start.17 = (f32[16,48]{1,0:T(8,128)S(1)}, f32[16,48]{1,0:T(8,128)S(1)}, u32[]{:S(2)}, u32[]{:S(2)}) collective-permute-start(f32[16,48]{1,0:T(8,128)S(1)} %add.131), channel_id=1, source_target_pairs={{0,128},{64,192},{128,0},{192,64},{256,384},{320,448},{384,256},{4... | collective-permute-start | bytes 9224 | tf_op jit(solution)/shard_map/ppermute | solution.py:30
  114.7 10.9 %collective-permute-start.18 = (f32[16,48]{1,0:T(8,128)S(1)}, f32[16,48]{1,0:T(8,128)S(1)}, u32[]{:S(2)}, u32[]{:S(2)}) collective-permute-start(f32[16,48]{1,0:T(8,128)S(1)} %add.132), channel_id=1, source_target_pairs={{0,384},{64,448},{128,256},{192,320},{256,128},{320,192},{384,0},{... | collective-permute-start | bytes 9224 | tf_op jit(solution)/shard_map/ppermute | solution.py:30

commit v12 on v8

--- a/solution.py
+++ b/solution.py
@@ -62,7 +62,7 @@
     folded = jnp.einsum("upw,vw->uvp", cou_part, active_rdm, precision=HIGH)
     eye = jnp.eye(width, dtype=jnp.float32)
     weight = (eye[:, :, None] * fitted[None, None, :] - 1.5 * folded).reshape(width, width * rows)
-    weight, every_dens = butterfly_sum_gather(weight, spin_dens, (("y", 8), ("xhi", 2), ("core", 2)))
+    weight, every_dens = butterfly_sum_gather(weight, spin_dens, (("xhi", 2), ("y", 8), ("core", 2)))
 
     soc_part = jnp.einsum(
         "vn,pkn->vpk", coef_t, soc_ints.reshape(rows, 3 * width, -1), preferred_element_type=jnp.float32
@@ -74,7 +74,7 @@
 
     def labelled(device):
         y = device // 4
-        return (device % 2) * 16 + (device // 2 % 2) * 8 + jnp.where(y < 4, y, y ^ 2)
+        return (device % 2) * 16 + jnp.where(y < 4, y, y ^ 2) * 2 + device // 2 % 2
 
     me = (lax.axis_index("y") * 4 + lax.axis_index("xhi") * 2 + lax.axis_index("core")).astype(jnp.int32)
     block = spin_dens.shape[0]

time: 121 us -> 121 us (level)
  waiting for transfers between devices: 37.7 us -> 39.7 us
  starting transfers between devices: 69.7 us -> 67.9 us
    ppermute x5, waiting for transfers between devices: 5.94 us -> 10 us  [butterfly_sum_gather(): lax.ppermute(blocks, axis, pairs)]
    ppermute x5, waiting for transfers between devices: 9.25 us -> 7.42 us  [butterfly_sum_gather(): total = total + lax.ppermute(total, axis, pairs)]
where the time goes in v12:
time: 121 us
  starting transfers between devices  67.9 us (56%)
  waiting for transfers between devices  39.7 us (33%)
  matrix products  7.8 us (6%)
  local copies, waits for them, and re-layouts  3.62 us (3%)
    ppermute x7, starting transfers between devices, butterfly_sum(): value = value + lax.ppermute(value, axis, partners(size, step))  28.5 us
    ppermute x5, starting transfers between devices, butterfly_sum_gather(): total = total + lax.ppermute(total, axis, pairs)  18.5 us
    ppermute x7, waiting for transfers between devices, butterfly_sum(): value = value + lax.ppermute(value, axis, partners(size, step))  16.8 us
    ppermute x5, starting transfers between devices, butterfly_sum_gather(): lax.ppermute(blocks, axis, pairs)  15.4 us
    ppermute x5, waiting for transfers between devices, butterfly_sum_gather(): lax.ppermute(blocks, axis, pairs)  10 us
    ppermute x5, waiting for transfers between devices, butterfly_sum_gather(): total = total + lax.ppermute(total, axis, pairs)  7.42 us
    ppermute x2, starting transfers between devices, x_ring_sum(): value = value + lax.ppermute(value, ('xlo', 'xhi'), pairs)  5.53 us
    ppermute x2, waiting for transfers between devices, x_ring_sum(): value = value + lax.ppermute(value, ('xlo', 'xhi'), pairs)  5.38 us
  transfers between devices with their start and end apart: 19, of which 14 were waited for; matrix products, arithmetic and copies ran while one was open for 6% of the time, Pallas kernels for 0%

profile of v12, /device:TPU:8, one launch (start us, length us, event | category | flops | bytes accessed | tf_op | source)
XLA Modules:
  0.0 120.5 jit_solution(15790458796999836329)
XLA Ops:
  0.0 2.1 %fusion.5 = f32[16,128,16]{1,0,2:T(8,128)S(1)} fusion(bf16[128,16,256]{2,1,0:T(8,128)(2,1)} %param.13, bf16[16,256]{1,0:T(8,128)(2,1)} %param.14), kind=kOutput, calls=%fused_computation.14 | convolution fusion | flops 16777216 | bytes 1187840 | tf_op jit(solution)/shard_map/un,ptn->upt/dot_general | solution.py:60
  4.1 4.9 %collective-permute-start = (f32[16,2048]{1,0:T(8,128)S(1)}, f32[16,2048]{1,0:T(8,128)S(1)}, u32[]{:S(2)}, u32[]{:S(2)}) collective-permute-start(f32[16,2048]{1,0:T(8,128)S(1)} %bitcast.42), channel_id=1, source_target_pairs={{0,2},{2,0},{1,3},{3,1},{4,6},{6,4},{5,7},{7,5},{8,10},{10,8},{9,1... | collective-permute-start | bytes 393224 | tf_op jit(solution)/shard_map/ppermute | solution.py:46
  9.0 2.4 %collective-permute-start.1 = (bf16[10,256]{1,0:T(8,128)(2,1)}, bf16[10,256]{1,0:T(8,128)(2,1)S(1)}, u32[]{:S(2)}, u32[]{:S(2)}) collective-permute-start(bf16[10,256]{1,0:T(8,128)(2,1)} %param.16), channel_id=1, source_target_pairs={{0,2},{2,0},{1,3},{3,1},{4,6},{6,4},{5,7},{7,5},{8,10},{10,8},{9,1... | collective-permute-start | bytes 15368 | tf_op jit(solution)/shard_map/ppermute | solution.py:47
  11.5 4.8 %collective-permute-done.1 = bf16[10,256]{1,0:T(8,128)(2,1)S(1)} collective-permute-done((bf16[10,256]{1,0:T(8,128)(2,1)}, bf16[10,256]{1,0:T(8,128)(2,1)S(1)}, u32[]{:S(2)}, u32[]{:S(2)}) %collective-permute-start.1) | collective-permute-done | bytes 5152 | tf_op jit(solution)/shard_map/ppermute | solution.py:47
  17.1 4.7 %collective-permute-start.2 = (f32[16,2048]{1,0:T(8,128)S(1)}, f32[16,2048]{1,0:T(8,128)S(1)}, u32[]{:S(2)}, u32[]{:S(2)}) collective-permute-start(f32[16,2048]{1,0:T(8,128)S(1)} %fusion.26), channel_id=1, source_target_pairs={{0,4},{4,0},{8,12},{12,8},{16,20},{20,16},{24,28},{28,24},{1,5},{5... | collective-permute-start | bytes 393224 | tf_op jit(solution)/shard_map/ppermute | solution.py:46
  21.8 1.9 %collective-permute-start.3 = (bf16[20,256]{1,0:T(8,128)(2,1)S(1)}, bf16[20,256]{1,0:T(8,128)(2,1)S(1)}, u32[]{:S(2)}, u32[]{:S(2)}) collective-permute-start(bf16[20,256]{1,0:T(8,128)(2,1)S(1)} %pad_maximum_fusion.4), channel_id=1, source_target_pairs={{0,4},{4,0},{8,12},{12,8},{16,20},{20,16},{24,28},{28,24},{1,5},{5... | collective-permute-start | bytes 30728 | tf_op jit(solution)/shard_map/ppermute | solution.py:47
  23.7 3.7 %collective-permute-done.3 = bf16[20,256]{1,0:T(8,128)(2,1)S(1)} collective-permute-done((bf16[20,256]{1,0:T(8,128)(2,1)S(1)}, bf16[20,256]{1,0:T(8,128)(2,1)S(1)}, u32[]{:S(2)}, u32[]{:S(2)}) %collective-permute-start.3) | collective-permute-done | bytes 10272 | tf_op jit(solution)/shard_map/ppermute | solution.py:47
  27.4 2.2 %collective-permute-start.5 = (bf16[40,256]{1,0:T(8,128)(2,1)S(1)}, bf16[40,256]{1,0:T(8,128)(2,1)S(1)}, u32[]{:S(2)}, u32[]{:S(2)}) collective-permute-start(bf16[40,256]{1,0:T(8,128)(2,1)S(1)} %pad_maximum_fusion.3), channel_id=1, source_target_pairs={{0,8},{4,12},{8,0},{12,4},{16,24},{20,28},{24,16},{28,20},{1,9},{5... | collective-permute-start | bytes 61448 | tf_op jit(solution)/shard_map/ppermute | solution.py:47
  29.6 4.6 %collective-permute-start.4 = (f32[16,2048]{1,0:T(8,128)S(1)}, f32[16,2048]{1,0:T(8,128)S(1)}, u32[]{:S(2)}, u32[]{:S(2)}) collective-permute-start(f32[16,2048]{1,0:T(8,128)S(1)} %add.121), channel_id=1, source_target_pairs={{0,8},{4,12},{8,0},{12,4},{16,24},{20,28},{24,16},{28,20},{1,9},{5... | collective-permute-start | bytes 393224 | tf_op jit(solution)/shard_map/ppermute | solution.py:46
  34.2 2.5 %fusion = f32[16,128,48]{1,0,2:T(8,128)S(1)} fusion(bf16[128,48,256]{2,1,0:T(8,128)(2,1)S(1)} %bitcast.38, bf16[16,256]{1,0:T(8,128)(2,1)} %param.14), kind=kOutput, calls=%fused_computation.5 | convolution fusion | flops 50331648 | bytes 3547136 | tf_op jit(solution)/shard_map/vn,pkn->vpk/dot_general | solution.py:67
  37.5 7.0 %collective-permute-start.7 = (bf16[80,256]{1,0:T(8,128)(2,1)S(1)}, bf16[80,256]{1,0:T(8,128)(2,1)S(1)}, u32[]{:S(2)}, u32[]{:S(2)}) collective-permute-start(bf16[80,256]{1,0:T(8,128)(2,1)S(1)} %pad_maximum_fusion.2), channel_id=1, source_target_pairs={{0,24},{4,28},{8,16},{12,20},{16,8},{20,12},{24,0},{28,4},{1,25},{... | collective-permute-start | bytes 122888 | tf_op jit(solution)/shard_map/ppermute | solution.py:47
  44.5 1.9 %collective-permute-start.6 = (f32[16,2048]{1,0:T(8,128)S(1)}, f32[16,2048]{1,0:T(8,128)S(1)}, u32[]{:S(2)}, u32[]{:S(2)}) collective-permute-start(f32[16,2048]{1,0:T(8,128)S(1)} %add.122), channel_id=1, source_target_pairs={{0,24},{4,28},{8,16},{12,20},{16,8},{20,12},{24,0},{28,4},{1,25},{... | collective-permute-start | bytes 393224 | tf_op jit(solution)/shard_map/ppermute | solution.py:46
  46.4 1.5 %collective-permute-done.7 = bf16[80,256]{1,0:T(8,128)(2,1)S(1)} collective-permute-done((bf16[80,256]{1,0:T(8,128)(2,1)S(1)}, bf16[80,256]{1,0:T(8,128)(2,1)S(1)}, u32[]{:S(2)}, u32[]{:S(2)}) %collective-permute-start.7) | collective-permute-done | bytes 40992 | tf_op jit(solution)/shard_map/ppermute | solution.py:47
  48.0 5.7 %collective-permute-done.6 = f32[16,2048]{1,0:T(8,128)S(1)} collective-permute-done((f32[16,2048]{1,0:T(8,128)S(1)}, f32[16,2048]{1,0:T(8,128)S(1)}, u32[]{:S(2)}, u32[]{:S(2)}) %collective-permute-start.6) | collective-permute-done | bytes 131104 | tf_op jit(solution)/shard_map/ppermute | solution.py:46
  53.7 1.9 %collective-permute-start.9 = (bf16[160,256]{1,0:T(8,128)(2,1)S(1)}, bf16[160,256]{1,0:T(8,128)(2,1)S(1)}, u32[]{:S(2)}, u32[]{:S(2)}) collective-permute-start(bf16[160,256]{1,0:T(8,128)(2,1)S(1)} %pad_maximum_fusion.1), channel_id=1, source_target_pairs={{0,1},{1,0},{2,3},{3,2},{4,5},{5,4},{6,7},{7,6},{8,9},{9,8},{10,11... | collective-permute-start | bytes 245768 | tf_op jit(solution)/shard_map/ppermute | solution.py:47
  55.6 2.4 %collective-permute-start.8 = (f32[16,2048]{1,0:T(8,128)S(1)}, f32[16,2048]{1,0:T(8,128)S(1)}, u32[]{:S(2)}, u32[]{:S(2)}) collective-permute-start(f32[16,2048]{1,0:T(8,128)S(1)} %add.123), channel_id=1, source_target_pairs={{0,1},{1,0},{2,3},{3,2},{4,5},{5,4},{6,7},{7,6},{8,9},{9,8},{10,11... | collective-permute-start | bytes 393224 | tf_op jit(solution)/shard_map/ppermute | solution.py:46
  59.5 2.3 %collective-permute-start.10 = (f32[16,48]{1,0:T(8,128)S(1)}, f32[16,48]{1,0:T(8,128)S(1)}, u32[]{:S(2)}, u32[]{:S(2)}) collective-permute-start(f32[16,48]{1,0:T(8,128)S(1)} %convolution_multiply_fusion.1), channel_id=1, source_target_pairs={{0,1},{1,0},{2,3},{3,2},{4,5},{5,4},{6,7},{7,6},{8,9},{9,8},{10,11... | collective-permute-start | bytes 9224 | tf_op jit(solution)/shard_map/ppermute | solution.py:30
  63.1 2.5 %collective-permute-start.11 = (f32[16,48]{1,0:T(8,128)S(1)}, f32[16,48]{1,0:T(8,128)S(1)}, u32[]{:S(2)}, u32[]{:S(2)}) collective-permute-start(f32[16,48]{1,0:T(8,128)S(1)} %add.125), channel_id=1, source_target_pairs={{0,32},{2,34},{32,0},{34,2},{1,33},{3,35},{33,1},{35,3},{4,36},{6,... | collective-permute-start | bytes 9224 | tf_op jit(solution)/shard_map/ppermute | solution.py:37
  65.6 3.0 %collective-permute-done.11 = f32[16,48]{1,0:T(8,128)S(1)} collective-permute-done((f32[16,48]{1,0:T(8,128)S(1)}, f32[16,48]{1,0:T(8,128)S(1)}, u32[]{:S(2)}, u32[]{:S(2)}) %collective-permute-start.11) | collective-permute-done | bytes 3104 | tf_op jit(solution)/shard_map/ppermute | solution.py:37
  68.7 3.0 %collective-permute-start.12 = (f32[16,48]{1,0:T(8,128)S(1)}, f32[16,48]{1,0:T(8,128)S(1)}, u32[]{:S(2)}, u32[]{:S(2)}) collective-permute-start(f32[16,48]{1,0:T(8,128)S(1)} %add.126), channel_id=1, source_target_pairs={{0,34},{2,32},{32,2},{34,0},{1,35},{3,33},{33,3},{35,1},{4,38},{6,... | collective-permute-start | bytes 9224 | tf_op jit(solution)/shard_map/ppermute | solution.py:37
  73.1 2.4 %collective-permute-done.12 = f32[16,48]{1,0:T(8,128)S(1)} collective-permute-done((f32[16,48]{1,0:T(8,128)S(1)}, f32[16,48]{1,0:T(8,128)S(1)}, u32[]{:S(2)}, u32[]{:S(2)}) %collective-permute-start.12) | collective-permute-done | bytes 3104 | tf_op jit(solution)/shard_map/ppermute | solution.py:37
  75.4 1.9 %collective-permute-start.13 = (f32[16,48]{1,0:T(8,128)S(1)}, f32[16,48]{1,0:T(8,128)S(1)}, u32[]{:S(2)}, u32[]{:S(2)}) collective-permute-start(f32[16,48]{1,0:T(8,128)S(1)} %add.127), channel_id=1, source_target_pairs={{0,4},{4,0},{8,12},{12,8},{16,20},{20,16},{24,28},{28,24},{1,5},{5... | collective-permute-start | bytes 9224 | tf_op jit(solution)/shard_map/ppermute | solution.py:30
  77.4 3.6 %collective-permute-done.13 = f32[16,48]{1,0:T(8,128)S(1)} collective-permute-done((f32[16,48]{1,0:T(8,128)S(1)}, f32[16,48]{1,0:T(8,128)S(1)}, u32[]{:S(2)}, u32[]{:S(2)}) %collective-permute-start.13) | collective-permute-done | bytes 3104 | tf_op jit(solution)/shard_map/ppermute | solution.py:30
  81.0 2.1 %collective-permute-start.14 = (f32[16,48]{1,0:T(8,128)S(1)}, f32[16,48]{1,0:T(8,128)S(1)}, u32[]{:S(2)}, u32[]{:S(2)}) collective-permute-start(f32[16,48]{1,0:T(8,128)S(1)} %add.128), channel_id=1, source_target_pairs={{0,8},{4,12},{8,0},{12,4},{16,24},{20,28},{24,16},{28,20},{1,9},{5... | collective-permute-start | bytes 9224 | tf_op jit(solution)/shard_map/ppermute | solution.py:30
  83.1 4.3 %collective-permute-done.14 = f32[16,48]{1,0:T(8,128)S(1)} collective-permute-done((f32[16,48]{1,0:T(8,128)S(1)}, f32[16,48]{1,0:T(8,128)S(1)}, u32[]{:S(2)}, u32[]{:S(2)}) %collective-permute-start.14) | collective-permute-done | bytes 3104 | tf_op jit(solution)/shard_map/ppermute | solution.py:30
  87.4 2.5 %collective-permute-start.15 = (f32[16,48]{1,0:T(8,128)S(1)}, f32[16,48]{1,0:T(8,128)S(1)}, u32[]{:S(2)}, u32[]{:S(2)}) collective-permute-start(f32[16,48]{1,0:T(8,128)S(1)} %add.129), channel_id=1, source_target_pairs={{0,24},{4,28},{8,16},{12,20},{16,8},{20,12},{24,0},{28,4},{1,25},{... | collective-permute-start | bytes 9224 | tf_op jit(solution)/shard_map/ppermute | solution.py:30
  90.0 5.0 %collective-permute-done.15 = f32[16,48]{1,0:T(8,128)S(1)} collective-permute-done((f32[16,48]{1,0:T(8,128)S(1)}, f32[16,48]{1,0:T(8,128)S(1)}, u32[]{:S(2)}, u32[]{:S(2)}) %collective-permute-start.15) | collective-permute-done | bytes 3104 | tf_op jit(solution)/shard_map/ppermute | solution.py:30
  95.0 4.3 %collective-permute-start.16 = (f32[16,48]{1,0:T(8,128)S(1)}, f32[16,48]{1,0:T(8,128)S(1)}, u32[]{:S(2)}, u32[]{:S(2)}) collective-permute-start(f32[16,48]{1,0:T(8,128)S(1)} %add.130), channel_id=1, source_target_pairs={{0,64},{64,0},{128,192},{192,128},{256,320},{320,256},{384,448},{4... | collective-permute-start | bytes 9224 | tf_op jit(solution)/shard_map/ppermute | solution.py:30
  99.3 1.6 %collective-permute-done.16 = f32[16,48]{1,0:T(8,128)S(1)} collective-permute-done((f32[16,48]{1,0:T(8,128)S(1)}, f32[16,48]{1,0:T(8,128)S(1)}, u32[]{:S(2)}, u32[]{:S(2)}) %collective-permute-start.16) | collective-permute-done | bytes 3104 | tf_op jit(solution)/shard_map/ppermute | solution.py:30
  100.9 6.1 %collective-permute-start.17 = (f32[16,48]{1,0:T(8,128)S(1)}, f32[16,48]{1,0:T(8,128)S(1)}, u32[]{:S(2)}, u32[]{:S(2)}) collective-permute-start(f32[16,48]{1,0:T(8,128)S(1)} %add.131), channel_id=1, source_target_pairs={{0,128},{64,192},{128,0},{192,64},{256,384},{320,448},{384,256},{4... | collective-permute-start | bytes 9224 | tf_op jit(solution)/shard_map/ppermute | solution.py:30
  108.6 9.3 %collective-permute-start.18 = (f32[16,48]{1,0:T(8,128)S(1)}, f32[16,48]{1,0:T(8,128)S(1)}, u32[]{:S(2)}, u32[]{:S(2)}) collective-permute-start(f32[16,48]{1,0:T(8,128)S(1)} %add.132), channel_id=1, source_target_pairs={{0,384},{64,448},{128,256},{192,320},{256,128},{320,192},{384,0},{... | collective-permute-start | bytes 9224 | tf_op jit(solution)/shard_map/ppermute | solution.py:30
  118.2 1.4 %collective-permute-done.18 = f32[16,48]{1,0:T(8,128)S(1)} collective-permute-done((f32[16,48]{1,0:T(8,128)S(1)}, f32[16,48]{1,0:T(8,128)S(1)}, u32[]{:S(2)}, u32[]{:S(2)}) %collective-permute-start.18) | collective-permute-done | bytes 3104 | tf_op jit(solution)/shard_map/ppermute | solution.py:30
  (59 shorter events, 10.6 us)
Async XLA Ops:
  0.0 34.1 %copy-start = (bf16[128,3,16,256]{3,2,1,0:T(8,128)(2,1)S(1)}, bf16[128,3,16,256]{3,2,1,0:T(8,128)(2,1)}, u32[]{:S(2)}) copy-start(bf16[128,3,16,256]{3,2,1,0:T(8,128)(2,1)} %param.12) | copy-start | bytes 9437188
  0.0 46.4 %copy-start.3 = (s32[10]{0:T(128)S(1)}, s32[10]{0:T(128)}, u32[]{:S(2)}) copy-start(s32[10]{0:T(128)} %param.18) | copy-start | bytes 124
  2.1 55.9 %copy-start.2 = (s32[320,2]{0,1:T(2,128)S(1)}, s32[320,2]{0,1:T(2,128)}, u32[]{:S(2)}) copy-start(s32[320,2]{0,1:T(2,128)} %param.17) | copy-start | bytes 7684
  4.1 12.9 %collective-permute-start = (f32[16,2048]{1,0:T(8,128)S(1)}, f32[16,2048]{1,0:T(8,128)S(1)}, u32[]{:S(2)}, u32[]{:S(2)}) collective-permute-start(f32[16,2048]{1,0:T(8,128)S(1)} %bitcast.42), channel_id=1, source_target_pairs={{0,2},{2,0},{1,3},{3,1},{4,6},{6,4},{5,7},{7,5},{8,10},{10,8},{9,1... | collective-permute-start | bytes 393224 | tf_op jit(solution)/shard_map/ppermute | solution.py:46
  9.0 7.3 %collective-permute-start.1 = (bf16[10,256]{1,0:T(8,128)(2,1)}, bf16[10,256]{1,0:T(8,128)(2,1)S(1)}, u32[]{:S(2)}, u32[]{:S(2)}) collective-permute-start(bf16[10,256]{1,0:T(8,128)(2,1)} %param.16), channel_id=1, source_target_pairs={{0,2},{2,0},{1,3},{3,1},{4,6},{6,4},{5,7},{7,5},{8,10},{10,8},{9,1... | collective-permute-start | bytes 15368 | tf_op jit(solution)/shard_map/ppermute | solution.py:47
  17.1 10.3 %collective-permute-start.2 = (f32[16,2048]{1,0:T(8,128)S(1)}, f32[16,2048]{1,0:T(8,128)S(1)}, u32[]{:S(2)}, u32[]{:S(2)}) collective-permute-start(f32[16,2048]{1,0:T(8,128)S(1)} %fusion.26), channel_id=1, source_target_pairs={{0,4},{4,0},{8,12},{12,8},{16,20},{20,16},{24,28},{28,24},{1,5},{5... | collective-permute-start | bytes 393224 | tf_op jit(solution)/shard_map/ppermute | solution.py:46
  21.8 5.6 %collective-permute-start.3 = (bf16[20,256]{1,0:T(8,128)(2,1)S(1)}, bf16[20,256]{1,0:T(8,128)(2,1)S(1)}, u32[]{:S(2)}, u32[]{:S(2)}) collective-permute-start(bf16[20,256]{1,0:T(8,128)(2,1)S(1)} %pad_maximum_fusion.4), channel_id=1, source_target_pairs={{0,4},{4,0},{8,12},{12,8},{16,20},{20,16},{24,28},{28,24},{1,5},{5... | collective-permute-start | bytes 30728 | tf_op jit(solution)/shard_map/ppermute | solution.py:47
  27.4 9.2 %collective-permute-start.5 = (bf16[40,256]{1,0:T(8,128)(2,1)S(1)}, bf16[40,256]{1,0:T(8,128)(2,1)S(1)}, u32[]{:S(2)}, u32[]{:S(2)}) collective-permute-start(bf16[40,256]{1,0:T(8,128)(2,1)S(1)} %pad_maximum_fusion.3), channel_id=1, source_target_pairs={{0,8},{4,12},{8,0},{12,4},{16,24},{20,28},{24,16},{28,20},{1,9},{5... | collective-permute-start | bytes 61448 | tf_op jit(solution)/shard_map/ppermute | solution.py:47
  29.6 7.9 %collective-permute-start.4 = (f32[16,2048]{1,0:T(8,128)S(1)}, f32[16,2048]{1,0:T(8,128)S(1)}, u32[]{:S(2)}, u32[]{:S(2)}) collective-permute-start(f32[16,2048]{1,0:T(8,128)S(1)} %add.121), channel_id=1, source_target_pairs={{0,8},{4,12},{8,0},{12,4},{16,24},{20,28},{24,16},{28,20},{1,9},{5... | collective-permute-start | bytes 393224 | tf_op jit(solution)/shard_map/ppermute | solution.py:46
  34.2 37.6 %copy-start.1 = (s32[24]{0:T(128)S(1)}, s32[24]{0:T(128)}, u32[]{:S(2)}) copy-start(s32[24]{0:T(128)} %param.19) | copy-start | bytes 292
  37.5 10.5 %collective-permute-start.7 = (bf16[80,256]{1,0:T(8,128)(2,1)S(1)}, bf16[80,256]{1,0:T(8,128)(2,1)S(1)}, u32[]{:S(2)}, u32[]{:S(2)}) collective-permute-start(bf16[80,256]{1,0:T(8,128)(2,1)S(1)} %pad_maximum_fusion.2), channel_id=1, source_target_pairs={{0,24},{4,28},{8,16},{12,20},{16,8},{20,12},{24,0},{28,4},{1,25},{... | collective-permute-start | bytes 122888 | tf_op jit(solution)/shard_map/ppermute | solution.py:47
  44.5 9.2 %collective-permute-start.6 = (f32[16,2048]{1,0:T(8,128)S(1)}, f32[16,2048]{1,0:T(8,128)S(1)}, u32[]{:S(2)}, u32[]{:S(2)}) collective-permute-start(f32[16,2048]{1,0:T(8,128)S(1)} %add.122), channel_id=1, source_target_pairs={{0,24},{4,28},{8,16},{12,20},{16,8},{20,12},{24,0},{28,4},{1,25},{... | collective-permute-start | bytes 393224 | tf_op jit(solution)/shard_map/ppermute | solution.py:46
  53.7 4.4 %collective-permute-start.9 = (bf16[160,256]{1,0:T(8,128)(2,1)S(1)}, bf16[160,256]{1,0:T(8,128)(2,1)S(1)}, u32[]{:S(2)}, u32[]{:S(2)}) collective-permute-start(bf16[160,256]{1,0:T(8,128)(2,1)S(1)} %pad_maximum_fusion.1), channel_id=1, source_target_pairs={{0,1},{1,0},{2,3},{3,2},{4,5},{5,4},{6,7},{7,6},{8,9},{9,8},{10,11... | collective-permute-start | bytes 245768 | tf_op jit(solution)/shard_map/ppermute | solution.py:47
  55.6 3.4 %collective-permute-start.8 = (f32[16,2048]{1,0:T(8,128)S(1)}, f32[16,2048]{1,0:T(8,128)S(1)}, u32[]{:S(2)}, u32[]{:S(2)}) collective-permute-start(f32[16,2048]{1,0:T(8,128)S(1)} %add.123), channel_id=1, source_target_pairs={{0,1},{1,0},{2,3},{3,2},{4,5},{5,4},{6,7},{7,6},{8,9},{9,8},{10,11... | collective-permute-start | bytes 393224 | tf_op jit(solution)/shard_map/ppermute | solution.py:46
  59.5 3.6 %collective-permute-start.10 = (f32[16,48]{1,0:T(8,128)S(1)}, f32[16,48]{1,0:T(8,128)S(1)}, u32[]{:S(2)}, u32[]{:S(2)}) collective-permute-start(f32[16,48]{1,0:T(8,128)S(1)} %convolution_multiply_fusion.1), channel_id=1, source_target_pairs={{0,1},{1,0},{2,3},{3,2},{4,5},{5,4},{6,7},{7,6},{8,9},{9,8},{10,11... | collective-permute-start | bytes 9224 | tf_op jit(solution)/shard_map/ppermute | solution.py:30
  63.1 5.5 %collective-permute-start.11 = (f32[16,48]{1,0:T(8,128)S(1)}, f32[16,48]{1,0:T(8,128)S(1)}, u32[]{:S(2)}, u32[]{:S(2)}) collective-permute-start(f32[16,48]{1,0:T(8,128)S(1)} %add.125), channel_id=1, source_target_pairs={{0,32},{2,34},{32,0},{34,2},{1,33},{3,35},{33,1},{35,3},{4,36},{6,... | collective-permute-start | bytes 9224 | tf_op jit(solution)/shard_map/ppermute | solution.py:37
  68.7 6.7 %collective-permute-start.12 = (f32[16,48]{1,0:T(8,128)S(1)}, f32[16,48]{1,0:T(8,128)S(1)}, u32[]{:S(2)}, u32[]{:S(2)}) collective-permute-start(f32[16,48]{1,0:T(8,128)S(1)} %add.126), channel_id=1, source_target_pairs={{0,34},{2,32},{32,2},{34,0},{1,35},{3,33},{33,3},{35,1},{4,38},{6,... | collective-permute-start | bytes 9224 | tf_op jit(solution)/shard_map/ppermute | solution.py:37
  75.4 5.5 %collective-permute-start.13 = (f32[16,48]{1,0:T(8,128)S(1)}, f32[16,48]{1,0:T(8,128)S(1)}, u32[]{:S(2)}, u32[]{:S(2)}) collective-permute-start(f32[16,48]{1,0:T(8,128)S(1)} %add.127), channel_id=1, source_target_pairs={{0,4},{4,0},{8,12},{12,8},{16,20},{20,16},{24,28},{28,24},{1,5},{5... | collective-permute-start | bytes 9224 | tf_op jit(solution)/shard_map/ppermute | solution.py:30
  81.0 6.4 %collective-permute-start.14 = (f32[16,48]{1,0:T(8,128)S(1)}, f32[16,48]{1,0:T(8,128)S(1)}, u32[]{:S(2)}, u32[]{:S(2)}) collective-permute-start(f32[16,48]{1,0:T(8,128)S(1)} %add.128), channel_id=1, source_target_pairs={{0,8},{4,12},{8,0},{12,4},{16,24},{20,28},{24,16},{28,20},{1,9},{5... | collective-permute-start | bytes 9224 | tf_op jit(solution)/shard_map/ppermute | solution.py:30
  87.4 7.6 %collective-permute-start.15 = (f32[16,48]{1,0:T(8,128)S(1)}, f32[16,48]{1,0:T(8,128)S(1)}, u32[]{:S(2)}, u32[]{:S(2)}) collective-permute-start(f32[16,48]{1,0:T(8,128)S(1)} %add.129), channel_id=1, source_target_pairs={{0,24},{4,28},{8,16},{12,20},{16,8},{20,12},{24,0},{28,4},{1,25},{... | collective-permute-start | bytes 9224 | tf_op jit(solution)/shard_map/ppermute | solution.py:30
  95.0 5.9 %collective-permute-start.16 = (f32[16,48]{1,0:T(8,128)S(1)}, f32[16,48]{1,0:T(8,128)S(1)}, u32[]{:S(2)}, u32[]{:S(2)}) collective-permute-start(f32[16,48]{1,0:T(8,128)S(1)} %add.130), channel_id=1, source_target_pairs={{0,64},{64,0},{128,192},{192,128},{256,320},{320,256},{384,448},{4... | collective-permute-start | bytes 9224 | tf_op jit(solution)/shard_map/ppermute | solution.py:30
  100.9 7.7 %collective-permute-start.17 = (f32[16,48]{1,0:T(8,128)S(1)}, f32[16,48]{1,0:T(8,128)S(1)}, u32[]{:S(2)}, u32[]{:S(2)}) collective-permute-start(f32[16,48]{1,0:T(8,128)S(1)} %add.131), channel_id=1, source_target_pairs={{0,128},{64,192},{128,0},{192,64},{256,384},{320,448},{384,256},{4... | collective-permute-start | bytes 9224 | tf_op jit(solution)/shard_map/ppermute | solution.py:30
  108.6 10.9 %collective-permute-start.18 = (f32[16,48]{1,0:T(8,128)S(1)}, f32[16,48]{1,0:T(8,128)S(1)}, u32[]{:S(2)}, u32[]{:S(2)}) collective-permute-start(f32[16,48]{1,0:T(8,128)S(1)} %add.132), channel_id=1, source_target_pairs={{0,384},{64,448},{128,256},{192,320},{256,128},{320,192},{384,0},{... | collective-permute-start | bytes 9224 | tf_op jit(solution)/shard_map/ppermute | solution.py:30

commit v13 on v8

--- a/solution.py
+++ b/solution.py
@@ -70,7 +70,7 @@
     field_part = jnp.dot(weight, soc_part, precision=HIGH) * scale
     field = butterfly_sum(field_part, (("core", 2),))
     field = x_ring_sum(field)
-    field = butterfly_sum(field, (("y", 8), ("z", 8)))
+    field = butterfly_sum(field, (("z", 8), ("y", 8)))
 
     def labelled(device):
         y = device // 4

time: 121 us -> 121 us (level)
  no operation moved by 1% of the time
where the time goes in v13:
time: 121 us; the launch traced here: 120 us
  starting transfers between devices  69.7 us (58%)
  waiting for transfers between devices  37.7 us (31%)
  matrix products  7.8 us (6%)
  local copies, waits for them, and re-layouts  3.62 us (3%)
    ppermute x7, starting transfers between devices, butterfly_sum(): value = value + lax.ppermute(value, axis, partners(size, step))  28.2 us
    ppermute x5, starting transfers between devices, butterfly_sum_gather(): total = total + lax.ppermute(total, axis, pairs)  19.4 us
    ppermute x7, waiting for transfers between devices, butterfly_sum(): value = value + lax.ppermute(value, axis, partners(size, step))  17.1 us
    ppermute x5, starting transfers between devices, butterfly_sum_gather(): lax.ppermute(blocks, axis, pairs)  16.6 us
    ppermute x5, waiting for transfers between devices, butterfly_sum_gather(): total = total + lax.ppermute(total, axis, pairs)  9.25 us
    ppermute x5, waiting for transfers between devices, butterfly_sum_gather(): lax.ppermute(blocks, axis, pairs)  5.94 us
    ppermute x2, starting transfers between devices, x_ring_sum(): value = value + lax.ppermute(value, ('xlo', 'xhi'), pairs)  5.54 us
    ppermute x2, waiting for transfers between devices, x_ring_sum(): value = value + lax.ppermute(value, ('xlo', 'xhi'), pairs)  5.37 us
  transfers between devices with their start and end apart: 19, of which 14 were waited for; matrix products, arithmetic and copies ran while one was open for 6% of the time, Pallas kernels for 0%

profile of v13, /device:TPU:8, one launch (start us, length us, event | category | flops | bytes accessed | tf_op | source)
XLA Modules:
  0.0 120.3 jit_solution(7457478682946659512)
XLA Ops:
  0.0 2.1 %fusion.5 = f32[16,128,16]{1,0,2:T(8,128)S(1)} fusion(bf16[128,16,256]{2,1,0:T(8,128)(2,1)} %param.13, bf16[16,256]{1,0:T(8,128)(2,1)} %param.14), kind=kOutput, calls=%fused_computation.14 | convolution fusion | flops 16777216 | bytes 1187840 | tf_op jit(solution)/shard_map/un,ptn->upt/dot_general | solution.py:60
  4.1 7.7 %collective-permute-start = (f32[16,2048]{1,0:T(8,128)S(1)}, f32[16,2048]{1,0:T(8,128)S(1)}, u32[]{:S(2)}, u32[]{:S(2)}) collective-permute-start(f32[16,2048]{1,0:T(8,128)S(1)} %bitcast.42), channel_id=1, source_target_pairs={{0,4},{4,0},{8,12},{12,8},{16,20},{20,16},{24,28},{28,24},{1,5},{5... | collective-permute-start | bytes 393224 | tf_op jit(solution)/shard_map/ppermute | solution.py:46
  11.8 1.9 %collective-permute-start.1 = (bf16[10,256]{1,0:T(8,128)(2,1)}, bf16[10,256]{1,0:T(8,128)(2,1)S(1)}, u32[]{:S(2)}, u32[]{:S(2)}) collective-permute-start(bf16[10,256]{1,0:T(8,128)(2,1)} %param.16), channel_id=1, source_target_pairs={{0,4},{4,0},{8,12},{12,8},{16,20},{20,16},{24,28},{28,24},{1,5},{5... | collective-permute-start | bytes 15368 | tf_op jit(solution)/shard_map/ppermute | solution.py:47
  13.7 3.8 %collective-permute-done.1 = bf16[10,256]{1,0:T(8,128)(2,1)S(1)} collective-permute-done((bf16[10,256]{1,0:T(8,128)(2,1)}, bf16[10,256]{1,0:T(8,128)(2,1)S(1)}, u32[]{:S(2)}, u32[]{:S(2)}) %collective-permute-start.1) | collective-permute-done | bytes 5152 | tf_op jit(solution)/shard_map/ppermute | solution.py:47
  18.3 1.9 %collective-permute-start.2 = (f32[16,2048]{1,0:T(8,128)S(1)}, f32[16,2048]{1,0:T(8,128)S(1)}, u32[]{:S(2)}, u32[]{:S(2)}) collective-permute-start(f32[16,2048]{1,0:T(8,128)S(1)} %fusion.26), channel_id=1, source_target_pairs={{0,8},{4,12},{8,0},{12,4},{16,24},{20,28},{24,16},{28,20},{1,9},{5... | collective-permute-start | bytes 393224 | tf_op jit(solution)/shard_map/ppermute | solution.py:46
  20.3 4.8 %collective-permute-start.3 = (bf16[20,256]{1,0:T(8,128)(2,1)S(1)}, bf16[20,256]{1,0:T(8,128)(2,1)S(1)}, u32[]{:S(2)}, u32[]{:S(2)}) collective-permute-start(bf16[20,256]{1,0:T(8,128)(2,1)S(1)} %pad_maximum_fusion.4), channel_id=1, source_target_pairs={{0,8},{4,12},{8,0},{12,4},{16,24},{20,28},{24,16},{28,20},{1,9},{5... | collective-permute-start | bytes 30728 | tf_op jit(solution)/shard_map/ppermute | solution.py:47
  25.1 1.7 %collective-permute-done.3 = bf16[20,256]{1,0:T(8,128)(2,1)S(1)} collective-permute-done((bf16[20,256]{1,0:T(8,128)(2,1)S(1)}, bf16[20,256]{1,0:T(8,128)(2,1)S(1)}, u32[]{:S(2)}, u32[]{:S(2)}) %collective-permute-start.3) | collective-permute-done | bytes 10272 | tf_op jit(solution)/shard_map/ppermute | solution.py:47
  26.8 3.0 %collective-permute-start.5 = (bf16[40,256]{1,0:T(8,128)(2,1)S(1)}, bf16[40,256]{1,0:T(8,128)(2,1)S(1)}, u32[]{:S(2)}, u32[]{:S(2)}) collective-permute-start(bf16[40,256]{1,0:T(8,128)(2,1)S(1)} %pad_maximum_fusion.3), channel_id=1, source_target_pairs={{0,24},{4,28},{8,16},{12,20},{16,8},{20,12},{24,0},{28,4},{1,25},{... | collective-permute-start | bytes 61448 | tf_op jit(solution)/shard_map/ppermute | solution.py:47
  29.8 5.0 %collective-permute-start.4 = (f32[16,2048]{1,0:T(8,128)S(1)}, f32[16,2048]{1,0:T(8,128)S(1)}, u32[]{:S(2)}, u32[]{:S(2)}) collective-permute-start(f32[16,2048]{1,0:T(8,128)S(1)} %add.121), channel_id=1, source_target_pairs={{0,24},{4,28},{8,16},{12,20},{16,8},{20,12},{24,0},{28,4},{1,25},{... | collective-permute-start | bytes 393224 | tf_op jit(solution)/shard_map/ppermute | solution.py:46
  34.8 2.5 %fusion = f32[16,128,48]{1,0,2:T(8,128)S(1)} fusion(bf16[128,48,256]{2,1,0:T(8,128)(2,1)S(1)} %bitcast.38, bf16[16,256]{1,0:T(8,128)(2,1)} %param.14), kind=kOutput, calls=%fused_computation.5 | convolution fusion | flops 50331648 | bytes 3547136 | tf_op jit(solution)/shard_map/vn,pkn->vpk/dot_general | solution.py:67
  37.3 2.9 %collective-permute-done.4 = f32[16,2048]{1,0:T(8,128)S(1)} collective-permute-done((f32[16,2048]{1,0:T(8,128)S(1)}, f32[16,2048]{1,0:T(8,128)S(1)}, u32[]{:S(2)}, u32[]{:S(2)}) %collective-permute-start.4) | collective-permute-done | bytes 131104 | tf_op jit(solution)/shard_map/ppermute | solution.py:46
  40.1 4.9 %collective-permute-start.7 = (bf16[80,256]{1,0:T(8,128)(2,1)S(1)}, bf16[80,256]{1,0:T(8,128)(2,1)S(1)}, u32[]{:S(2)}, u32[]{:S(2)}) collective-permute-start(bf16[80,256]{1,0:T(8,128)(2,1)S(1)} %pad_maximum_fusion.2), channel_id=1, source_target_pairs={{0,2},{2,0},{1,3},{3,1},{4,6},{6,4},{5,7},{7,5},{8,10},{10,8},{9,1... | collective-permute-start | bytes 122888 | tf_op jit(solution)/shard_map/ppermute | solution.py:47
  45.1 2.4 %collective-permute-start.6 = (f32[16,2048]{1,0:T(8,128)S(1)}, f32[16,2048]{1,0:T(8,128)S(1)}, u32[]{:S(2)}, u32[]{:S(2)}) collective-permute-start(f32[16,2048]{1,0:T(8,128)S(1)} %add.122), channel_id=1, source_target_pairs={{0,2},{2,0},{1,3},{3,1},{4,6},{6,4},{5,7},{7,5},{8,10},{10,8},{9,1... | collective-permute-start | bytes 393224 | tf_op jit(solution)/shard_map/ppermute | solution.py:46
  48.0 5.5 %collective-permute-done.6 = f32[16,2048]{1,0:T(8,128)S(1)} collective-permute-done((f32[16,2048]{1,0:T(8,128)S(1)}, f32[16,2048]{1,0:T(8,128)S(1)}, u32[]{:S(2)}, u32[]{:S(2)}) %collective-permute-start.6) | collective-permute-done | bytes 131104 | tf_op jit(solution)/shard_map/ppermute | solution.py:46
  53.5 1.9 %collective-permute-start.9 = (bf16[160,256]{1,0:T(8,128)(2,1)S(1)}, bf16[160,256]{1,0:T(8,128)(2,1)S(1)}, u32[]{:S(2)}, u32[]{:S(2)}) collective-permute-start(bf16[160,256]{1,0:T(8,128)(2,1)S(1)} %pad_maximum_fusion.1), channel_id=1, source_target_pairs={{0,1},{1,0},{2,3},{3,2},{4,5},{5,4},{6,7},{7,6},{8,9},{9,8},{10,11... | collective-permute-start | bytes 245768 | tf_op jit(solution)/shard_map/ppermute | solution.py:47
  55.4 2.4 %collective-permute-start.8 = (f32[16,2048]{1,0:T(8,128)S(1)}, f32[16,2048]{1,0:T(8,128)S(1)}, u32[]{:S(2)}, u32[]{:S(2)}) collective-permute-start(f32[16,2048]{1,0:T(8,128)S(1)} %add.123), channel_id=1, source_target_pairs={{0,1},{1,0},{2,3},{3,2},{4,5},{5,4},{6,7},{7,6},{8,9},{9,8},{10,11... | collective-permute-start | bytes 393224 | tf_op jit(solution)/shard_map/ppermute | solution.py:46
  59.3 2.3 %collective-permute-start.10 = (f32[16,48]{1,0:T(8,128)S(1)}, f32[16,48]{1,0:T(8,128)S(1)}, u32[]{:S(2)}, u32[]{:S(2)}) collective-permute-start(f32[16,48]{1,0:T(8,128)S(1)} %convolution_multiply_fusion.1), channel_id=1, source_target_pairs={{0,1},{1,0},{2,3},{3,2},{4,5},{5,4},{6,7},{7,6},{8,9},{9,8},{10,11... | collective-permute-start | bytes 9224 | tf_op jit(solution)/shard_map/ppermute | solution.py:30
  62.9 2.5 %collective-permute-start.11 = (f32[16,48]{1,0:T(8,128)S(1)}, f32[16,48]{1,0:T(8,128)S(1)}, u32[]{:S(2)}, u32[]{:S(2)}) collective-permute-start(f32[16,48]{1,0:T(8,128)S(1)} %add.125), channel_id=1, source_target_pairs={{0,32},{2,34},{32,0},{34,2},{1,33},{3,35},{33,1},{35,3},{4,36},{6,... | collective-permute-start | bytes 9224 | tf_op jit(solution)/shard_map/ppermute | solution.py:37
  65.4 3.0 %collective-permute-done.11 = f32[16,48]{1,0:T(8,128)S(1)} collective-permute-done((f32[16,48]{1,0:T(8,128)S(1)}, f32[16,48]{1,0:T(8,128)S(1)}, u32[]{:S(2)}, u32[]{:S(2)}) %collective-permute-start.11) | collective-permute-done | bytes 3104 | tf_op jit(solution)/shard_map/ppermute | solution.py:37
  68.5 3.0 %collective-permute-start.12 = (f32[16,48]{1,0:T(8,128)S(1)}, f32[16,48]{1,0:T(8,128)S(1)}, u32[]{:S(2)}, u32[]{:S(2)}) collective-permute-start(f32[16,48]{1,0:T(8,128)S(1)} %add.126), channel_id=1, source_target_pairs={{0,34},{2,32},{32,2},{34,0},{1,35},{3,33},{33,3},{35,1},{4,38},{6,... | collective-permute-start | bytes 9224 | tf_op jit(solution)/shard_map/ppermute | solution.py:37
  72.9 2.3 %collective-permute-done.12 = f32[16,48]{1,0:T(8,128)S(1)} collective-permute-done((f32[16,48]{1,0:T(8,128)S(1)}, f32[16,48]{1,0:T(8,128)S(1)}, u32[]{:S(2)}, u32[]{:S(2)}) %collective-permute-start.12) | collective-permute-done | bytes 3104 | tf_op jit(solution)/shard_map/ppermute | solution.py:37
  75.2 4.3 %collective-permute-start.13 = (f32[16,48]{1,0:T(8,128)S(1)}, f32[16,48]{1,0:T(8,128)S(1)}, u32[]{:S(2)}, u32[]{:S(2)}) collective-permute-start(f32[16,48]{1,0:T(8,128)S(1)} %add.127), channel_id=1, source_target_pairs={{0,64},{64,0},{128,192},{192,128},{256,320},{320,256},{384,448},{4... | collective-permute-start | bytes 9224 | tf_op jit(solution)/shard_map/ppermute | solution.py:30
  79.5 1.6 %collective-permute-done.13 = f32[16,48]{1,0:T(8,128)S(1)} collective-permute-done((f32[16,48]{1,0:T(8,128)S(1)}, f32[16,48]{1,0:T(8,128)S(1)}, u32[]{:S(2)}, u32[]{:S(2)}) %collective-permute-start.13) | collective-permute-done | bytes 3104 | tf_op jit(solution)/shard_map/ppermute | solution.py:30
  81.1 6.1 %collective-permute-start.14 = (f32[16,48]{1,0:T(8,128)S(1)}, f32[16,48]{1,0:T(8,128)S(1)}, u32[]{:S(2)}, u32[]{:S(2)}) collective-permute-start(f32[16,48]{1,0:T(8,128)S(1)} %add.128), channel_id=1, source_target_pairs={{0,128},{64,192},{128,0},{192,64},{256,384},{320,448},{384,256},{4... | collective-permute-start | bytes 9224 | tf_op jit(solution)/shard_map/ppermute | solution.py:30
  88.8 9.3 %collective-permute-start.15 = (f32[16,48]{1,0:T(8,128)S(1)}, f32[16,48]{1,0:T(8,128)S(1)}, u32[]{:S(2)}, u32[]{:S(2)}) collective-permute-start(f32[16,48]{1,0:T(8,128)S(1)} %add.129), channel_id=1, source_target_pairs={{0,384},{64,448},{128,256},{192,320},{256,128},{320,192},{384,0},{... | collective-permute-start | bytes 9224 | tf_op jit(solution)/shard_map/ppermute | solution.py:30
  98.2 1.6 %collective-permute-done.15 = f32[16,48]{1,0:T(8,128)S(1)} collective-permute-done((f32[16,48]{1,0:T(8,128)S(1)}, f32[16,48]{1,0:T(8,128)S(1)}, u32[]{:S(2)}, u32[]{:S(2)}) %collective-permute-start.15) | collective-permute-done | bytes 3104 | tf_op jit(solution)/shard_map/ppermute | solution.py:30
  99.7 1.9 %collective-permute-start.16 = (f32[16,48]{1,0:T(8,128)S(1)}, f32[16,48]{1,0:T(8,128)S(1)}, u32[]{:S(2)}, u32[]{:S(2)}) collective-permute-start(f32[16,48]{1,0:T(8,128)S(1)} %add.130), channel_id=1, source_target_pairs={{0,4},{4,0},{8,12},{12,8},{16,20},{20,16},{24,28},{28,24},{1,5},{5... | collective-permute-start | bytes 9224 | tf_op jit(solution)/shard_map/ppermute | solution.py:30
  101.7 3.6 %collective-permute-done.16 = f32[16,48]{1,0:T(8,128)S(1)} collective-permute-done((f32[16,48]{1,0:T(8,128)S(1)}, f32[16,48]{1,0:T(8,128)S(1)}, u32[]{:S(2)}, u32[]{:S(2)}) %collective-permute-start.16) | collective-permute-done | bytes 3104 | tf_op jit(solution)/shard_map/ppermute | solution.py:30
  105.3 2.2 %collective-permute-start.17 = (f32[16,48]{1,0:T(8,128)S(1)}, f32[16,48]{1,0:T(8,128)S(1)}, u32[]{:S(2)}, u32[]{:S(2)}) collective-permute-start(f32[16,48]{1,0:T(8,128)S(1)} %add.131), channel_id=1, source_target_pairs={{0,8},{4,12},{8,0},{12,4},{16,24},{20,28},{24,16},{28,20},{1,9},{5... | collective-permute-start | bytes 9224 | tf_op jit(solution)/shard_map/ppermute | solution.py:30
  108.2 3.5 %collective-permute-done.17 = f32[16,48]{1,0:T(8,128)S(1)} collective-permute-done((f32[16,48]{1,0:T(8,128)S(1)}, f32[16,48]{1,0:T(8,128)S(1)}, u32[]{:S(2)}, u32[]{:S(2)}) %collective-permute-start.17) | collective-permute-done | bytes 3104 | tf_op jit(solution)/shard_map/ppermute | solution.py:30
  111.7 2.1 %collective-permute-start.18 = (f32[16,48]{1,0:T(8,128)S(1)}, f32[16,48]{1,0:T(8,128)S(1)}, u32[]{:S(2)}, u32[]{:S(2)}) collective-permute-start(f32[16,48]{1,0:T(8,128)S(1)} %add.132), channel_id=1, source_target_pairs={{0,24},{4,28},{8,16},{12,20},{16,8},{20,12},{24,0},{28,4},{1,25},{... | collective-permute-start | bytes 9224 | tf_op jit(solution)/shard_map/ppermute | solution.py:30
  114.1 5.3 %collective-permute-done.18 = f32[16,48]{1,0:T(8,128)S(1)} collective-permute-done((f32[16,48]{1,0:T(8,128)S(1)}, f32[16,48]{1,0:T(8,128)S(1)}, u32[]{:S(2)}, u32[]{:S(2)}) %collective-permute-start.18) | collective-permute-done | bytes 3104 | tf_op jit(solution)/shard_map/ppermute | solution.py:30
  (59 shorter events, 10.9 us)
Async XLA Ops:
  0.0 34.8 %copy-start = (bf16[128,3,16,256]{3,2,1,0:T(8,128)(2,1)S(1)}, bf16[128,3,16,256]{3,2,1,0:T(8,128)(2,1)}, u32[]{:S(2)}) copy-start(bf16[128,3,16,256]{3,2,1,0:T(8,128)(2,1)} %param.12) | copy-start | bytes 9437188
  0.0 47.5 %copy-start.3 = (s32[10]{0:T(128)S(1)}, s32[10]{0:T(128)}, u32[]{:S(2)}) copy-start(s32[10]{0:T(128)} %param.18) | copy-start | bytes 124
  2.1 55.7 %copy-start.2 = (s32[320,2]{0,1:T(2,128)S(1)}, s32[320,2]{0,1:T(2,128)}, u32[]{:S(2)}) copy-start(s32[320,2]{0,1:T(2,128)} %param.17) | copy-start | bytes 7684
  4.1 14.2 %collective-permute-start = (f32[16,2048]{1,0:T(8,128)S(1)}, f32[16,2048]{1,0:T(8,128)S(1)}, u32[]{:S(2)}, u32[]{:S(2)}) collective-permute-start(f32[16,2048]{1,0:T(8,128)S(1)} %bitcast.42), channel_id=1, source_target_pairs={{0,4},{4,0},{8,12},{12,8},{16,20},{20,16},{24,28},{28,24},{1,5},{5... | collective-permute-start | bytes 393224 | tf_op jit(solution)/shard_map/ppermute | solution.py:46
  11.8 5.8 %collective-permute-start.1 = (bf16[10,256]{1,0:T(8,128)(2,1)}, bf16[10,256]{1,0:T(8,128)(2,1)S(1)}, u32[]{:S(2)}, u32[]{:S(2)}) collective-permute-start(bf16[10,256]{1,0:T(8,128)(2,1)} %param.16), channel_id=1, source_target_pairs={{0,4},{4,0},{8,12},{12,8},{16,20},{20,16},{24,28},{28,24},{1,5},{5... | collective-permute-start | bytes 15368 | tf_op jit(solution)/shard_map/ppermute | solution.py:47
  18.3 8.4 %collective-permute-start.2 = (f32[16,2048]{1,0:T(8,128)S(1)}, f32[16,2048]{1,0:T(8,128)S(1)}, u32[]{:S(2)}, u32[]{:S(2)}) collective-permute-start(f32[16,2048]{1,0:T(8,128)S(1)} %fusion.26), channel_id=1, source_target_pairs={{0,8},{4,12},{8,0},{12,4},{16,24},{20,28},{24,16},{28,20},{1,9},{5... | collective-permute-start | bytes 393224 | tf_op jit(solution)/shard_map/ppermute | solution.py:46
  20.3 6.5 %collective-permute-start.3 = (bf16[20,256]{1,0:T(8,128)(2,1)S(1)}, bf16[20,256]{1,0:T(8,128)(2,1)S(1)}, u32[]{:S(2)}, u32[]{:S(2)}) collective-permute-start(bf16[20,256]{1,0:T(8,128)(2,1)S(1)} %pad_maximum_fusion.4), channel_id=1, source_target_pairs={{0,8},{4,12},{8,0},{12,4},{16,24},{20,28},{24,16},{28,20},{1,9},{5... | collective-permute-start | bytes 30728 | tf_op jit(solution)/shard_map/ppermute | solution.py:47
  26.8 10.5 %collective-permute-start.5 = (bf16[40,256]{1,0:T(8,128)(2,1)S(1)}, bf16[40,256]{1,0:T(8,128)(2,1)S(1)}, u32[]{:S(2)}, u32[]{:S(2)}) collective-permute-start(bf16[40,256]{1,0:T(8,128)(2,1)S(1)} %pad_maximum_fusion.3), channel_id=1, source_target_pairs={{0,24},{4,28},{8,16},{12,20},{16,8},{20,12},{24,0},{28,4},{1,25},{... | collective-permute-start | bytes 61448 | tf_op jit(solution)/shard_map/ppermute | solution.py:47
  29.8 10.4 %collective-permute-start.4 = (f32[16,2048]{1,0:T(8,128)S(1)}, f32[16,2048]{1,0:T(8,128)S(1)}, u32[]{:S(2)}, u32[]{:S(2)}) collective-permute-start(f32[16,2048]{1,0:T(8,128)S(1)} %add.121), channel_id=1, source_target_pairs={{0,24},{4,28},{8,16},{12,20},{16,8},{20,12},{24,0},{28,4},{1,25},{... | collective-permute-start | bytes 393224 | tf_op jit(solution)/shard_map/ppermute | solution.py:46
  34.8 36.8 %copy-start.1 = (s32[24]{0:T(128)S(1)}, s32[24]{0:T(128)}, u32[]{:S(2)}) copy-start(s32[24]{0:T(128)} %param.19) | copy-start | bytes 292
  40.1 7.8 %collective-permute-start.7 = (bf16[80,256]{1,0:T(8,128)(2,1)S(1)}, bf16[80,256]{1,0:T(8,128)(2,1)S(1)}, u32[]{:S(2)}, u32[]{:S(2)}) collective-permute-start(bf16[80,256]{1,0:T(8,128)(2,1)S(1)} %pad_maximum_fusion.2), channel_id=1, source_target_pairs={{0,2},{2,0},{1,3},{3,1},{4,6},{6,4},{5,7},{7,5},{8,10},{10,8},{9,1... | collective-permute-start | bytes 122888 | tf_op jit(solution)/shard_map/ppermute | solution.py:47
  45.1 8.4 %collective-permute-start.6 = (f32[16,2048]{1,0:T(8,128)S(1)}, f32[16,2048]{1,0:T(8,128)S(1)}, u32[]{:S(2)}, u32[]{:S(2)}) collective-permute-start(f32[16,2048]{1,0:T(8,128)S(1)} %add.122), channel_id=1, source_target_pairs={{0,2},{2,0},{1,3},{3,1},{4,6},{6,4},{5,7},{7,5},{8,10},{10,8},{9,1... | collective-permute-start | bytes 393224 | tf_op jit(solution)/shard_map/ppermute | solution.py:46
  53.5 4.4 %collective-permute-start.9 = (bf16[160,256]{1,0:T(8,128)(2,1)S(1)}, bf16[160,256]{1,0:T(8,128)(2,1)S(1)}, u32[]{:S(2)}, u32[]{:S(2)}) collective-permute-start(bf16[160,256]{1,0:T(8,128)(2,1)S(1)} %pad_maximum_fusion.1), channel_id=1, source_target_pairs={{0,1},{1,0},{2,3},{3,2},{4,5},{5,4},{6,7},{7,6},{8,9},{9,8},{10,11... | collective-permute-start | bytes 245768 | tf_op jit(solution)/shard_map/ppermute | solution.py:47
  55.4 3.4 %collective-permute-start.8 = (f32[16,2048]{1,0:T(8,128)S(1)}, f32[16,2048]{1,0:T(8,128)S(1)}, u32[]{:S(2)}, u32[]{:S(2)}) collective-permute-start(f32[16,2048]{1,0:T(8,128)S(1)} %add.123), channel_id=1, source_target_pairs={{0,1},{1,0},{2,3},{3,2},{4,5},{5,4},{6,7},{7,6},{8,9},{9,8},{10,11... | collective-permute-start | bytes 393224 | tf_op jit(solution)/shard_map/ppermute | solution.py:46
  59.3 3.6 %collective-permute-start.10 = (f32[16,48]{1,0:T(8,128)S(1)}, f32[16,48]{1,0:T(8,128)S(1)}, u32[]{:S(2)}, u32[]{:S(2)}) collective-permute-start(f32[16,48]{1,0:T(8,128)S(1)} %convolution_multiply_fusion.1), channel_id=1, source_target_pairs={{0,1},{1,0},{2,3},{3,2},{4,5},{5,4},{6,7},{7,6},{8,9},{9,8},{10,11... | collective-permute-start | bytes 9224 | tf_op jit(solution)/shard_map/ppermute | solution.py:30
  62.9 5.5 %collective-permute-start.11 = (f32[16,48]{1,0:T(8,128)S(1)}, f32[16,48]{1,0:T(8,128)S(1)}, u32[]{:S(2)}, u32[]{:S(2)}) collective-permute-start(f32[16,48]{1,0:T(8,128)S(1)} %add.125), channel_id=1, source_target_pairs={{0,32},{2,34},{32,0},{34,2},{1,33},{3,35},{33,1},{35,3},{4,36},{6,... | collective-permute-start | bytes 9224 | tf_op jit(solution)/shard_map/ppermute | solution.py:37
  68.5 6.7 %collective-permute-start.12 = (f32[16,48]{1,0:T(8,128)S(1)}, f32[16,48]{1,0:T(8,128)S(1)}, u32[]{:S(2)}, u32[]{:S(2)}) collective-permute-start(f32[16,48]{1,0:T(8,128)S(1)} %add.126), channel_id=1, source_target_pairs={{0,34},{2,32},{32,2},{34,0},{1,35},{3,33},{33,3},{35,1},{4,38},{6,... | collective-permute-start | bytes 9224 | tf_op jit(solution)/shard_map/ppermute | solution.py:37
  75.2 5.9 %collective-permute-start.13 = (f32[16,48]{1,0:T(8,128)S(1)}, f32[16,48]{1,0:T(8,128)S(1)}, u32[]{:S(2)}, u32[]{:S(2)}) collective-permute-start(f32[16,48]{1,0:T(8,128)S(1)} %add.127), channel_id=1, source_target_pairs={{0,64},{64,0},{128,192},{192,128},{256,320},{320,256},{384,448},{4... | collective-permute-start | bytes 9224 | tf_op jit(solution)/shard_map/ppermute | solution.py:30
  81.1 7.7 %collective-permute-start.14 = (f32[16,48]{1,0:T(8,128)S(1)}, f32[16,48]{1,0:T(8,128)S(1)}, u32[]{:S(2)}, u32[]{:S(2)}) collective-permute-start(f32[16,48]{1,0:T(8,128)S(1)} %add.128), channel_id=1, source_target_pairs={{0,128},{64,192},{128,0},{192,64},{256,384},{320,448},{384,256},{4... | collective-permute-start | bytes 9224 | tf_op jit(solution)/shard_map/ppermute | solution.py:30
  88.8 10.9 %collective-permute-start.15 = (f32[16,48]{1,0:T(8,128)S(1)}, f32[16,48]{1,0:T(8,128)S(1)}, u32[]{:S(2)}, u32[]{:S(2)}) collective-permute-start(f32[16,48]{1,0:T(8,128)S(1)} %add.129), channel_id=1, source_target_pairs={{0,384},{64,448},{128,256},{192,320},{256,128},{320,192},{384,0},{... | collective-permute-start | bytes 9224 | tf_op jit(solution)/shard_map/ppermute | solution.py:30
  99.7 5.5 %collective-permute-start.16 = (f32[16,48]{1,0:T(8,128)S(1)}, f32[16,48]{1,0:T(8,128)S(1)}, u32[]{:S(2)}, u32[]{:S(2)}) collective-permute-start(f32[16,48]{1,0:T(8,128)S(1)} %add.130), channel_id=1, source_target_pairs={{0,4},{4,0},{8,12},{12,8},{16,20},{20,16},{24,28},{28,24},{1,5},{5... | collective-permute-start | bytes 9224 | tf_op jit(solution)/shard_map/ppermute | solution.py:30
  105.3 6.4 %collective-permute-start.17 = (f32[16,48]{1,0:T(8,128)S(1)}, f32[16,48]{1,0:T(8,128)S(1)}, u32[]{:S(2)}, u32[]{:S(2)}) collective-permute-start(f32[16,48]{1,0:T(8,128)S(1)} %add.131), channel_id=1, source_target_pairs={{0,8},{4,12},{8,0},{12,4},{16,24},{20,28},{24,16},{28,20},{1,9},{5... | collective-permute-start | bytes 9224 | tf_op jit(solution)/shard_map/ppermute | solution.py:30
  111.7 7.6 %collective-permute-start.18 = (f32[16,48]{1,0:T(8,128)S(1)}, f32[16,48]{1,0:T(8,128)S(1)}, u32[]{:S(2)}, u32[]{:S(2)}) collective-permute-start(f32[16,48]{1,0:T(8,128)S(1)} %add.132), channel_id=1, source_target_pairs={{0,24},{4,28},{8,16},{12,20},{16,8},{20,12},{24,0},{28,4},{1,25},{... | collective-permute-start | bytes 9224 | tf_op jit(solution)/shard_map/ppermute | solution.py:30
